TPU v7x, 32 devices: a whole 2x2x4 slice. The times are simulated.
32 devices in a mesh: space: 4 (over y, x), chan: 8 (over z, core).
Axes of the slice: x: 2, y: 2, z: 4, core: 2. Of those that a mesh axis runs over, the one named last changes fastest.
Arguments:
- inputs: bfloat16 [256, 16, 1024], P('chan', 'space'), may hold values from -6 to 6
- weight: bfloat16 [27, 256, 256], P(None, None, 'chan'), may hold values from -0.078125 to 0.078125
- bias_term: float32 [256], P('chan'), may hold values from -1 to 1
- output_grad: bfloat16 [256, 16, 1024], P('chan', 'space'), may hold values from -6 to 6
Outputs:
- outputs: bfloat16 [256, 16, 1024], P('chan', 'space')
- input_grad: bfloat16 [256, 16, 1024], P('chan', 'space')
- weight_grad: float32 [27, 256, 256], P(None, None, 'chan')
- bias_grad: float32 [256], P('chan')
All inputs are finite; a program needn't handle non-finite values.
Results may differ from a plain program's by a relative error of at most 0.001.
Values may be sent and summed in bfloat16 or wider, within the bound.
No kernel may reach another device: no remote copies, remote signals or barrier semaphores. Data moves between devices by JAX's collectives and lax.ppermute only.
A program may use at most 128 MiB of HBM per device.

v0:
```python
import math

import jax
import jax.numpy as jnp
from jax import lax
from jax.sharding import PartitionSpec as P

W = 64


tap_offsets = tuple(
    (
        (depth_step, row_step, column_step)
        for depth_step in (-1, 0, 1)
        for row_step in (-1, 0, 1)
        for column_step in (-1, 0, 1)
    )
)


def padded_2(array, sides, width):
    for axis, dim in sides:
        devices, length = (lax.axis_size(axis), array.shape[dim])
        up = [(i, (i + 1) % devices) for i in range(devices - 1)]
        down = [(j, i) for i, j in up]
        last = lax.slice_in_dim(array, length - width, length, axis=dim)
        first = lax.slice_in_dim(array, 0, width, axis=dim)
        before = lax.ppermute(last, axis, up)
        after = lax.ppermute(first, axis, down)
        array = jnp.concatenate([before, array, after], axis=dim)
    return array


def shift_cells(field, row_step, column_step):
    length_flat = field.shape[-1]
    pad_width = W + 1
    widths = [(0, 0)] * (field.ndim - 1) + [(pad_width, pad_width)]
    padded = jnp.pad(field, widths)
    first_index = pad_width + row_step * W + column_step
    shifted = lax.slice_in_dim(padded, first_index, first_index + length_flat, axis=field.ndim - 1)
    column = jnp.arange(length_flat, dtype=jnp.int32) % W
    inside = (column + column_step >= 0) & (column + column_step < W)
    return jnp.where(inside, shifted, jnp.zeros_like(shifted))


def outer_planes(field):
    return jnp.concatenate([field[:, :1], field[:, -1:]], axis=1)


def attach_rims(field, rims):
    return jnp.concatenate([rims[:, :1], field, rims[:, 3:]], axis=1)


def all_reduce_rows(block, axis):
    devices = lax.axis_size(axis)
    steps = devices.bit_length() - 1
    assert 1 << steps == devices
    current = block
    index = lax.axis_index(axis)
    for step in range(steps):
        half = current.shape[0] // 2
        bit = (index >> step) & 1
        keep = lax.dynamic_slice_in_dim(current, bit * half, half)
        send = lax.dynamic_slice_in_dim(current, (1 - bit) * half, half)
        pairs = [(i, i ^ (1 << step)) for i in range(devices)]
        current = keep + lax.ppermute(send, axis, pairs)
    for step in reversed(range(steps)):
        half = current.shape[0]
        bit = (index >> step) & 1
        pairs = [(i, i ^ (1 << step)) for i in range(devices)]
        other = lax.ppermute(current, axis, pairs)
        both = jnp.zeros((2 * half,) + current.shape[1:], current.dtype)
        both = lax.dynamic_update_slice_in_dim(both, current, bit * half, 0)
        current = lax.dynamic_update_slice_in_dim(both, other, (1 - bit) * half, 0)
    return current


def shift_volume(field, row_step, column_step, rows):
    length_flat = field.shape[-1]
    pad_width = W + 1
    widths = [(0, 0)] * (field.ndim - 1) + [(pad_width, pad_width)]
    padded = jnp.pad(field, widths)
    first_index = pad_width + row_step * W + column_step
    shifted = lax.slice_in_dim(padded, first_index, first_index + length_flat, axis=field.ndim - 1)
    cell = jnp.arange(length_flat, dtype=jnp.int32)
    column = cell % W
    row = (cell // W) % rows
    inside = (column + column_step >= 0) & (column + column_step < W)
    inside = inside & (row + row_step >= 0) & (row + row_step < rows)
    return jnp.where(inside, shifted, jnp.zeros_like(shifted))


plane_offsets = tuple((row_step, column_step) for row_step in (-1, 0, 1) for column_step in (-1, 0, 1))


def body(inputs, weight, bias_term, output_grad):
    taps_total = weight.shape[0]
    channels_in = weight.shape[1]
    block_out = weight.shape[2]
    block_in = inputs.shape[0]
    depth_cells = inputs.shape[1]
    plane_cells = inputs.shape[2]
    grad_scale = 1.0 / math.sqrt(lax.axis_size("space") * depth_cells * plane_cells)
    inputs_planes = jnp.transpose(inputs, (1, 0, 2))
    grad_planes = jnp.transpose(output_grad, (1, 0, 2))
    rimmed = padded_2(inputs_planes, (("space", 0),), 1)
    gathered = lax.all_gather(rimmed, "chan", axis=1, tiled=True)

    weight_grid = weight.reshape(3, 9, channels_in, block_out)
    forward_weight = jnp.transpose(weight_grid, (0, 1, 3, 2)).reshape(3, 9 * block_out, channels_in)
    in_plane = None
    for depth_index in range(3):
        part = jnp.einsum(
            "ki,zin->zkn",
            forward_weight[depth_index],
            gathered[depth_index : depth_index + depth_cells],
            preferred_element_type=jnp.float32,
        )
        in_plane = part if in_plane is None else in_plane + part
    in_plane = in_plane.reshape(depth_cells, 9, block_out, plane_cells)
    forward = None
    for shift_index, (row_step, column_step) in enumerate(plane_offsets):
        term = shift_cells(in_plane[:, shift_index], row_step, column_step)
        forward = term if forward is None else forward + term
    outputs = jnp.transpose(
        (forward + bias_term[None, :, None]).astype(jnp.bfloat16), (1, 0, 2)
    )

    grad_rimmed = padded_2(grad_planes, (("space", 0),), 1)
    grad_shifted = jnp.stack(
        [shift_cells(grad_rimmed, -row_step, -column_step) for row_step, column_step in plane_offsets],
        axis=1,
    ).reshape(depth_cells + 2, 9 * block_out, plane_cells)
    placed = grad_shifted[1 : 1 + depth_cells]
    weight_part = jnp.stack(
        [
            jnp.einsum(
                "zkn,zin->ki",
                placed,
                gathered[depth_index : depth_index + depth_cells],
                preferred_element_type=jnp.float32,
            )
            for depth_index in range(3)
        ]
    ).reshape(taps_total * block_out, channels_in)
    bias_part = jnp.sum(output_grad.astype(jnp.float32), axis=(1, 2))
    space_devices = lax.axis_size("space")
    unit = 8 * space_devices
    total_rows = -(-(taps_total * block_out + 1) // unit) * unit
    bias_rows = jnp.zeros((total_rows - taps_total * block_out, channels_in), jnp.float32)
    bias_rows = bias_rows.at[0, :block_out].set(bias_part)
    reduced = all_reduce_rows(
        jnp.concatenate([weight_part, bias_rows]) * grad_scale, "space"
    )
    weight_grad = jnp.transpose(
        reduced[: taps_total * block_out].reshape(taps_total, block_out, channels_in), (0, 2, 1)
    )
    bias_grad = reduced[taps_total * block_out, :block_out]

    chan_devices = lax.axis_size("chan")
    backward_weight = jnp.transpose(weight_grid, (0, 2, 1, 3)).reshape(
        3, chan_devices, channels_in // chan_devices, 9 * block_out
    )
    spread = None
    for depth_index in range(3):
        part = jnp.einsum(
            "bjk,zkn->bjzn",
            backward_weight[depth_index],
            grad_shifted[2 - depth_index : 2 - depth_index + depth_cells],
            preferred_element_type=jnp.float32,
        )
        spread = part if spread is None else spread + part
    summed = lax.psum_scatter(
        spread.reshape(channels_in, depth_cells * plane_cells), "chan", scatter_dimension=0, tiled=True
    )
    input_grad = summed.astype(jnp.bfloat16).reshape(block_in, depth_cells, plane_cells)
    return (outputs, input_grad, weight_grad, bias_grad)


def solution(mesh):
    placed = (P("chan", "space", None), P(None, None, "chan"), P("chan"), P("chan", "space", None))
    return jax.shard_map(
        body,
        mesh=mesh,
        in_specs=placed,
        out_specs=(
            P("chan", "space", None),
            P("chan", "space", None),
            P(None, None, "chan"),
            P("chan"),
        ),
        check_vma=False,
    )
```

profile of v0, /device:TPU:0, one launch (start us, length us, event | category | flops | bytes accessed | tf_op | source)
XLA Modules:
  0.0 119.7 jit_solution(10059584985586090883)
XLA Ops:
  7.2 1.0 copy.79
  8.3 4.8 %collective-permute-start = (bf16[1,32,1024]{2,1,0:T(8,128)(2,1)S(1)}, bf16[1,32,1024]{2,1,0:T(8,128)(2,1)S(1)}, u32[]{:S(2)}, u32[]{:S(2)}) collective-permute-start(bf16[1,32,1024]{2,1,0:T(8,128)(2,1)S(1)} %get-tuple-element.40), channel_id=1, source_target_pairs={{0,8},{8,16},{16,24},{1,9},{9,17},{17,25},{2,10},{10,18},{18,26},{... | collective-permute-start | bytes 196616 | tf_op jit(solution)/shard_map/ppermute | solution.py:28
  13.1 1.3 %collective-permute-start.1 = (bf16[1,32,1024]{2,1,0:T(8,128)(2,1)S(1)}, bf16[1,32,1024]{2,1,0:T(8,128)(2,1)S(1)}, u32[]{:S(2)}, u32[]{:S(2)}) collective-permute-start(bf16[1,32,1024]{2,1,0:T(8,128)(2,1)S(1)} %get-tuple-element.41), channel_id=1, source_target_pairs={{8,0},{16,8},{24,16},{9,1},{17,9},{25,17},{10,2},{18,10},{26,18},{... | collective-permute-start | bytes 196616 | tf_op jit(solution)/shard_map/ppermute | solution.py:29
  14.4 0.6 collective-permute-done
  15.0 4.3 %collective-permute-done.1 = bf16[1,32,1024]{2,1,0:T(8,128)(2,1)S(1)} collective-permute-done((bf16[1,32,1024]{2,1,0:T(8,128)(2,1)S(1)}, bf16[1,32,1024]{2,1,0:T(8,128)(2,1)S(1)}, u32[]{:S(2)}, u32[]{:S(2)}) %collective-permute-start.1) | collective-permute-done | bytes 65568 | tf_op jit(solution)/shard_map/ppermute | solution.py:29
  19.3 0.8 pad_maximum_fusion.1
  20.1 1.0 copy.80
  21.2 4.3 %collective-permute-start.2 = (bf16[1,32,1024]{2,1,0:T(8,128)(2,1)S(1)}, bf16[1,32,1024]{2,1,0:T(8,128)(2,1)S(1)}, u32[]{:S(2)}, u32[]{:S(2)}) collective-permute-start(bf16[1,32,1024]{2,1,0:T(8,128)(2,1)S(1)} %get-tuple-element.38), channel_id=1, source_target_pairs={{0,8},{8,16},{16,24},{1,9},{9,17},{17,25},{2,10},{10,18},{18,26},{... | collective-permute-start | bytes 196616 | tf_op jit(solution)/shard_map/ppermute | solution.py:28
  25.5 1.3 %collective-permute-start.3 = (bf16[1,32,1024]{2,1,0:T(8,128)(2,1)S(1)}, bf16[1,32,1024]{2,1,0:T(8,128)(2,1)S(1)}, u32[]{:S(2)}, u32[]{:S(2)}) collective-permute-start(bf16[1,32,1024]{2,1,0:T(8,128)(2,1)S(1)} %get-tuple-element.39), channel_id=1, source_target_pairs={{8,0},{16,8},{24,16},{9,1},{17,9},{25,17},{10,2},{18,10},{26,18},{... | collective-permute-start | bytes 196616 | tf_op jit(solution)/shard_map/ppermute | solution.py:29
  26.8 1.1 fusion.83
  28.2 0.4 copy.42
  28.8 0.4 copy.40
  29.5 0.4 copy.44
  29.9 1.8 %collective-permute-done.3 = bf16[1,32,1024]{2,1,0:T(8,128)(2,1)S(1)} collective-permute-done((bf16[1,32,1024]{2,1,0:T(8,128)(2,1)S(1)}, bf16[1,32,1024]{2,1,0:T(8,128)(2,1)S(1)}, u32[]{:S(2)}, u32[]{:S(2)}) %collective-permute-start.3) | collective-permute-done | bytes 65568 | tf_op jit(solution)/shard_map/ppermute | solution.py:29
  33.3 1.0 fusion.82
  34.9 1.7 %fusion.63 = f32[4,1024,8,32]{1,3,2,0:T(8,128)S(1)} fusion(bf16[4,288,1024,1]{2,1,3,0:T(8,128)(2,1)S(1)} %bitcast.162, bf16[8,32,288]{2,1,0:T(8,128)(2,1)S(1)} %copy.42), kind=kOutput, calls=%fused_computation.98 | convolution fusion | flops 603979776 | bytes 6701056 | tf_op jit(solution)/shard_map/bjk,zkn->bjzn/dot_general | solution.py:166
  36.7 1.7 %fusion.65 = f32[4,1024,8,32]{1,3,2,0:T(8,128)S(1)} fusion(bf16[4,288,1024,1]{2,1,3,0:T(8,128)(2,1)S(1)} %bitcast.166, bf16[8,32,288]{2,1,0:T(8,128)(2,1)S(1)} %copy.40), kind=kOutput, calls=%fused_computation.100 | convolution fusion | flops 603979776 | bytes 6701056 | tf_op jit(solution)/shard_map/bjk,zkn->bjzn/dot_general | solution.py:166
  38.4 2.3 %add_bitcast_fusion = f32[8,32,4,1024]{3,1,0,2:T(8,128)S(1)} fusion(f32[4,1024,8,32]{1,3,2,0:T(8,128)S(1)} %fusion.65, f32[4,1024,8,32]{1,3,2,0:T(8,128)S(1)} %fusion.63, bf16[4,288,1024,1]{2,1,3,0:T(8,128)(2,1)S(1)} %bitcast.158, bf16[8,32,288]{2,1,0:T(8,128)(2,1)S(1)} %copy.44), kind=kOutput, calls=%fused_computation.1 | convolution fusion | flops 606076928 | bytes 15089664 | tf_op jit(solution)/shard_map/bjk,zkn->bjzn/dot_general | solution.py:166
  40.8 2.9 %copy.45 = f32[8,32,4,1024]{3,2,1,0:T(4,128)S(1)} copy(f32[8,32,4,1024]{3,1,0,2:T(8,128)S(1)} %add_bitcast_fusion) | data formatting | bytes 8388608 | tf_op jit(solution)/shard_map/add | solution.py:172
  43.7 5.7 %copy.58 = f32[32,8,4,1024]{3,1,2,0:T(8,128)} copy(f32[32,8,4,1024]{3,2,1,0:T(4,128)S(1)} %bitcast.161) | data formatting | bytes 8388608
  49.4 0.9 copy-done.2
  50.4 0.3 convert_reduce_fusion
  50.7 9.0 %all-gather.2.cloned.1.call-done = bf16[6,256,1024]{2,1,0:T(8,128)(2,1)} async-done(((bf16[6,32,1024]{2,1,0:T(8,128)(2,1)}), bf16[6,256,1024]{2,1,0:T(8,128)(2,1)}) %all-gather.2.cloned.1.call-update) | async-done | bytes 3145744 | tf_op jit(solution)/shard_map/all_gather | solution.py:107
  59.7 2.5 %fusion.11 = f32[1,288,256]{2,1,0:T(8,128)S(1)} fusion(bf16[4,288,1024]{2,1,0:T(8,128)(2,1)S(1)} %bitcast.163, bf16[6,256,1024]{2,1,0:T(8,128)(2,1)} %all-gather.2.cloned.1.call-done), kind=kOutput, calls=%fused_computation.15 | convolution fusion | flops 603979776 | bytes 4751360 | tf_op jit(solution)/shard_map/zkn,zin->ki/dot_general | solution.py:137
  62.3 0.8 fusion.14
  63.1 0.8 fusion.17
  64.1 1.5 %collective-permute-start.4 = (f32[448,256]{1,0:T(8,128)S(1)}, f32[448,256]{1,0:T(8,128)S(1)}, u32[]{:S(2)}, u32[]{:S(2)}) collective-permute-start(f32[448,256]{1,0:T(8,128)S(1)} %constant_dynamic-slice_fusion.1), channel_id=1, source_target_pairs={{0,8},{8,0},{16,24},{24,16},{1,9},{9,1},{17,25},{25,17},{2,10},{10... | collective-permute-start | bytes 1376264 | tf_op jit(solution)/shard_map/ppermute | solution.py:66
  65.6 0.8 fusion.5
  66.4 0.8 fusion.9
  67.2 0.8 add_add_fusion
  68.0 0.7 fusion.81
  68.8 0.7 copy_bitcast_fusion.7
  69.5 0.7 copy_bitcast_fusion.5
  70.1 6.7 %collective-permute-done.4 = f32[448,256]{1,0:T(8,128)S(1)} collective-permute-done((f32[448,256]{1,0:T(8,128)S(1)}, f32[448,256]{1,0:T(8,128)S(1)}, u32[]{:S(2)}, u32[]{:S(2)}) %collective-permute-start.4) | collective-permute-done | bytes 458784 | tf_op jit(solution)/shard_map/ppermute | solution.py:66
  77.0 1.5 %collective-permute-start.5 = (f32[224,256]{1,0:T(8,128)S(1)}, f32[224,256]{1,0:T(8,128)S(1)}, u32[]{:S(2)}, u32[]{:S(2)}) collective-permute-start(f32[224,256]{1,0:T(8,128)S(1)} %constant_dynamic-slice_fusion), channel_id=1, source_target_pairs={{0,16},{8,24},{16,0},{24,8},{1,17},{9,25},{17,1},{25,9},{2,18},{10... | collective-permute-start | bytes 688136 | tf_op jit(solution)/shard_map/ppermute | solution.py:66
  78.5 0.7 copy_bitcast_fusion.2
  79.2 4.9 %collective-permute-done.5 = f32[224,256]{1,0:T(8,128)S(1)} collective-permute-done((f32[224,256]{1,0:T(8,128)S(1)}, f32[224,256]{1,0:T(8,128)S(1)}, u32[]{:S(2)}, u32[]{:S(2)}) %collective-permute-start.5) | collective-permute-done | bytes 229408 | tf_op jit(solution)/shard_map/ppermute | solution.py:66
  84.4 1.5 %collective-permute-start.6 = (f32[224,256]{1,0:T(8,128)S(1)}, f32[224,256]{1,0:T(8,128)S(1)}, u32[]{:S(2)}, u32[]{:S(2)}) collective-permute-start(f32[224,256]{1,0:T(8,128)S(1)} %get-tuple-element.17), channel_id=1, source_target_pairs={{0,16},{8,24},{16,0},{24,8},{1,17},{9,25},{17,1},{25,9},{2,18},{10... | collective-permute-start | bytes 688136 | tf_op jit(solution)/shard_map/ppermute | solution.py:71
  85.9 0.7 copy_bitcast_fusion
  86.6 4.1 %collective-permute-done.6 = f32[224,256]{1,0:T(8,128)S(1)} collective-permute-done((f32[224,256]{1,0:T(8,128)S(1)}, f32[224,256]{1,0:T(8,128)S(1)}, u32[]{:S(2)}, u32[]{:S(2)}) %collective-permute-start.6) | collective-permute-done | bytes 229408 | tf_op jit(solution)/shard_map/ppermute | solution.py:71
  90.7 1.5 %collective-permute-start.7 = (f32[448,256]{1,0:T(8,128)S(1)}, f32[448,256]{1,0:T(8,128)S(1)}, u32[]{:S(2)}, u32[]{:S(2)}) collective-permute-start(f32[448,256]{1,0:T(8,128)S(1)} %constant_dynamic-update-slice_fusion.2), channel_id=1, source_target_pairs={{0,8},{8,0},{16,24},{24,16},{1,9},{9,1},{17,25},{25,17},{2,10},{10... | collective-permute-start | bytes 1376264 | tf_op jit(solution)/shard_map/ppermute | solution.py:71
  92.2 3.0 %fusion.61 = bf16[32,4,1024]{2,1,0:T(4,128)(2,1)} fusion(f32[32]{0:T(128)S(1)} %copy-done.3, f32[4,32,1024]{2,0,1:T(4,128)S(1)} %get-tuple-element.42, f32[4,32,1024]{2,0,1:T(4,128)S(1)} %get-tuple-element.43, f32[4,32,1024]{2,0,1:T(4,128)S(1)} %get-tuple-element.44, f32[4,32,1024]{2,0,1:T(4,128)S(1)} %get-tuple-element.45, ...), kind=kLoop, calls=%fused_computation.93 | loop fusion | flops 2490368 | bytes 4983936 | tf_op jit(solution)/shard_map/transpose | solution.py:125
  95.3 5.8 %collective-permute-done.7 = f32[448,256]{1,0:T(8,128)S(1)} collective-permute-done((f32[448,256]{1,0:T(8,128)S(1)}, f32[448,256]{1,0:T(8,128)S(1)}, u32[]{:S(2)}, u32[]{:S(2)}) %collective-permute-start.7) | collective-permute-done | bytes 458784 | tf_op jit(solution)/shard_map/ppermute | solution.py:71
  101.1 1.0 slice.245
  102.1 0.5 slice_bitcast_fusion
  102.6 8.3 %reduce-scatter.2.cloned.1.call-done = f32[32,4096]{1,0:T(8,128)} async-done(((f32[256,4096]{1,0:T(8,128)}), f32[32,4096]{1,0:T(8,128)}) %reduce-scatter.2.cloned.1.call-update) | async-done | bytes 524304 | tf_op jit(solution)/shard_map/reduce_scatter | solution.py:173
  110.9 1.1 convert_element_type.30
  112.0 0.9 reshape.120
  (44 shorter events, 3.8 us)
Async XLA Ops:
  7.2 52.6 %all-gather.2.cloned.1.call-start = ((), (), s32[]{:S(2)}) async-start(), calls=%async_computation.1 | async-start | bytes 3538944 | tf_op jit(solution)/shard_map/all_gather | solution.py:107
  8.3 6.7 %collective-permute-start = (bf16[1,32,1024]{2,1,0:T(8,128)(2,1)S(1)}, bf16[1,32,1024]{2,1,0:T(8,128)(2,1)S(1)}, u32[]{:S(2)}, u32[]{:S(2)}) collective-permute-start(bf16[1,32,1024]{2,1,0:T(8,128)(2,1)S(1)} %get-tuple-element.40), channel_id=1, source_target_pairs={{0,8},{8,16},{16,24},{1,9},{9,17},{17,25},{2,10},{10,18},{18,26},{... | collective-permute-start | bytes 196616 | tf_op jit(solution)/shard_map/ppermute | solution.py:28
  13.1 6.2 %collective-permute-start.1 = (bf16[1,32,1024]{2,1,0:T(8,128)(2,1)S(1)}, bf16[1,32,1024]{2,1,0:T(8,128)(2,1)S(1)}, u32[]{:S(2)}, u32[]{:S(2)}) collective-permute-start(bf16[1,32,1024]{2,1,0:T(8,128)(2,1)S(1)} %get-tuple-element.41), channel_id=1, source_target_pairs={{8,0},{16,8},{24,16},{9,1},{17,9},{25,17},{10,2},{18,10},{26,18},{... | collective-permute-start | bytes 196616 | tf_op jit(solution)/shard_map/ppermute | solution.py:29
  20.1 90.8 %reduce-scatter.2.cloned.1.call-start = ((), (), s32[]{:S(2)}) async-start(), calls=%async_computation.2 | async-start | bytes 4718592 | tf_op jit(solution)/shard_map/reduce_scatter | solution.py:173
  21.2 8.7 %collective-permute-start.2 = (bf16[1,32,1024]{2,1,0:T(8,128)(2,1)S(1)}, bf16[1,32,1024]{2,1,0:T(8,128)(2,1)S(1)}, u32[]{:S(2)}, u32[]{:S(2)}) collective-permute-start(bf16[1,32,1024]{2,1,0:T(8,128)(2,1)S(1)} %get-tuple-element.38), channel_id=1, source_target_pairs={{0,8},{8,16},{16,24},{1,9},{9,17},{17,25},{2,10},{10,18},{18,26},{... | collective-permute-start | bytes 196616 | tf_op jit(solution)/shard_map/ppermute | solution.py:28
  25.5 6.2 %collective-permute-start.3 = (bf16[1,32,1024]{2,1,0:T(8,128)(2,1)S(1)}, bf16[1,32,1024]{2,1,0:T(8,128)(2,1)S(1)}, u32[]{:S(2)}, u32[]{:S(2)}) collective-permute-start(bf16[1,32,1024]{2,1,0:T(8,128)(2,1)S(1)} %get-tuple-element.39), channel_id=1, source_target_pairs={{8,0},{16,8},{24,16},{9,1},{17,9},{25,17},{10,2},{18,10},{26,18},{... | collective-permute-start | bytes 196616 | tf_op jit(solution)/shard_map/ppermute | solution.py:29
  49.4 0.9 copy-start.2
  49.4 1.3 %copy-start.1 = (bf16[27,256,32]{1,2,0:T(8,128)(2,1)S(1)}, bf16[27,256,32]{1,2,0:T(8,128)(2,1)}, u32[]{:S(2)}) copy-start(bf16[27,256,32]{1,2,0:T(8,128)(2,1)} %param.7) | copy-start | bytes 1327108
  59.7 2.6 %copy-start = (bf16[6,256,1024]{2,1,0:T(8,128)(2,1)S(1)}, bf16[6,256,1024]{2,1,0:T(8,128)(2,1)}, u32[]{:S(2)}) copy-start(bf16[6,256,1024]{2,1,0:T(8,128)(2,1)} %all-gather.2.cloned.1.call-done) | copy-start | bytes 9437188
  64.1 12.7 %collective-permute-start.4 = (f32[448,256]{1,0:T(8,128)S(1)}, f32[448,256]{1,0:T(8,128)S(1)}, u32[]{:S(2)}, u32[]{:S(2)}) collective-permute-start(f32[448,256]{1,0:T(8,128)S(1)} %constant_dynamic-slice_fusion.1), channel_id=1, source_target_pairs={{0,8},{8,0},{16,24},{24,16},{1,9},{9,1},{17,25},{25,17},{2,10},{10... | collective-permute-start | bytes 1376264 | tf_op jit(solution)/shard_map/ppermute | solution.py:66
  76.9 15.3 %copy-start.3 = (f32[32]{0:T(128)S(1)}, f32[32]{0:T(128)}, u32[]{:S(2)}) copy-start(f32[32]{0:T(128)} %param.8) | copy-start | bytes 388
  77.0 7.1 %collective-permute-start.5 = (f32[224,256]{1,0:T(8,128)S(1)}, f32[224,256]{1,0:T(8,128)S(1)}, u32[]{:S(2)}, u32[]{:S(2)}) collective-permute-start(f32[224,256]{1,0:T(8,128)S(1)} %constant_dynamic-slice_fusion), channel_id=1, source_target_pairs={{0,16},{8,24},{16,0},{24,8},{1,17},{9,25},{17,1},{25,9},{2,18},{10... | collective-permute-start | bytes 688136 | tf_op jit(solution)/shard_map/ppermute | solution.py:66
  84.4 6.3 %collective-permute-start.6 = (f32[224,256]{1,0:T(8,128)S(1)}, f32[224,256]{1,0:T(8,128)S(1)}, u32[]{:S(2)}, u32[]{:S(2)}) collective-permute-start(f32[224,256]{1,0:T(8,128)S(1)} %get-tuple-element.17), channel_id=1, source_target_pairs={{0,16},{8,24},{16,0},{24,8},{1,17},{9,25},{17,1},{25,9},{2,18},{10... | collective-permute-start | bytes 688136 | tf_op jit(solution)/shard_map/ppermute | solution.py:71
  90.7 10.4 %collective-permute-start.7 = (f32[448,256]{1,0:T(8,128)S(1)}, f32[448,256]{1,0:T(8,128)S(1)}, u32[]{:S(2)}, u32[]{:S(2)}) collective-permute-start(f32[448,256]{1,0:T(8,128)S(1)} %constant_dynamic-update-slice_fusion.2), channel_id=1, source_target_pairs={{0,8},{8,0},{16,24},{24,16},{1,9},{9,1},{17,25},{25,17},{2,10},{10... | collective-permute-start | bytes 1376264 | tf_op jit(solution)/shard_map/ppermute | solution.py:71
Sparse Core Ops, SparseCore 0:
  20.2 39.4 all-gather.1
  62.0 48.8 reduce-scatter.1
where the time goes:
time: 120 us
  waiting for transfers between devices  45.5 us (38%)
  local copies, waits for them, and re-layouts  22.4 us (19%)
  starting transfers between devices  17.9 us (15%)
  between operations  14.5 us (12%)
  matrix products  12.4 us (10%)
  other arithmetic  7.14 us (6%)
    ppermute x2, waiting for transfers between devices, all_reduce_rows(): current = keep + lax.ppermute(send, axis, pairs)  11.6 us
    ppermute x2, waiting for transfers between devices, all_reduce_rows(): other = lax.ppermute(current, axis, pairs)  9.88 us
    ppermute x2, starting transfers between devices, padded_2(): before = lax.ppermute(last, axis, up)  9.14 us
    all_gather x1, waiting for transfers between devices, body(): gathered = lax.all_gather(rimmed, 'chan', axis=1, tiled=True)  9.01 us
    unnamed x11, local copies, waits for them, and re-layouts  8.73 us
    reduce_scatter x1, waiting for transfers between devices, body(): lax.psum_scatter(spread.reshape(channels_in, depth_cells * plane_cells),...  8.32 us
    ppermute x2, waiting for transfers between devices, padded_2(): after = lax.ppermute(first, axis, down)  6.03 us
    dot_general x3, matrix products, body(): jnp.einsum('bjk,zkn->bjzn', backward_weight[depth_index], grad_shifted[2...  5.81 us
  transfers between devices with their start and end apart: 10, of which 9 were waited for; matrix products, arithmetic and copies ran while one was open for 31% of the time, Pallas kernels for 0%

commit v1 on v0

--- a/solution.py
+++ b/solution.py
@@ -103,8 +103,7 @@
     grad_scale = 1.0 / math.sqrt(lax.axis_size("space") * depth_cells * plane_cells)
     inputs_planes = jnp.transpose(inputs, (1, 0, 2))
     grad_planes = jnp.transpose(output_grad, (1, 0, 2))
-    rimmed = padded_2(inputs_planes, (("space", 0),), 1)
-    gathered = lax.all_gather(rimmed, "chan", axis=1, tiled=True)
+    gathered = lax.all_gather(inputs_planes, "chan", axis=1, tiled=True)
 
     weight_grid = weight.reshape(3, 9, channels_in, block_out)
     forward_weight = jnp.transpose(weight_grid, (0, 1, 3, 2)).reshape(3, 9 * block_out, channels_in)
@@ -113,15 +112,24 @@
         part = jnp.einsum(
             "ki,zin->zkn",
             forward_weight[depth_index],
-            gathered[depth_index : depth_index + depth_cells],
+            gathered,
             preferred_element_type=jnp.float32,
         )
+        part = jnp.pad(part, ((2 - depth_index, depth_index), (0, 0), (0, 0)))
         in_plane = part if in_plane is None else in_plane + part
-    in_plane = in_plane.reshape(depth_cells, 9, block_out, plane_cells)
+    in_plane = in_plane.reshape(depth_cells + 2, 9, block_out, plane_cells)
     forward = None
     for shift_index, (row_step, column_step) in enumerate(plane_offsets):
         term = shift_cells(in_plane[:, shift_index], row_step, column_step)
         forward = term if forward is None else forward + term
+    space_devices = lax.axis_size("space")
+    up = [(i, i + 1) for i in range(space_devices - 1)]
+    down = [(i + 1, i) for i in range(space_devices - 1)]
+    from_below = lax.ppermute(forward[depth_cells + 1 :], "space", up)
+    from_above = lax.ppermute(forward[:1], "space", down)
+    forward = forward[1 : depth_cells + 1] + jnp.concatenate(
+        [from_below, jnp.zeros((depth_cells - 2, block_out, plane_cells), jnp.float32), from_above]
+    )
     outputs = jnp.transpose(
         (forward + bias_term[None, :, None]).astype(jnp.bfloat16), (1, 0, 2)
     )
@@ -131,20 +139,18 @@
         [shift_cells(grad_rimmed, -row_step, -column_step) for row_step, column_step in plane_offsets],
         axis=1,
     ).reshape(depth_cells + 2, 9 * block_out, plane_cells)
-    placed = grad_shifted[1 : 1 + depth_cells]
     weight_part = jnp.stack(
         [
             jnp.einsum(
                 "zkn,zin->ki",
-                placed,
-                gathered[depth_index : depth_index + depth_cells],
+                grad_shifted[2 - depth_index : 2 - depth_index + depth_cells],
+                gathered,
                 preferred_element_type=jnp.float32,
             )
             for depth_index in range(3)
         ]
     ).reshape(taps_total * block_out, channels_in)
     bias_part = jnp.sum(output_grad.astype(jnp.float32), axis=(1, 2))
-    space_devices = lax.axis_size("space")
     unit = 8 * space_devices
     total_rows = -(-(taps_total * block_out + 1) // unit) * unit
     bias_rows = jnp.zeros((total_rows - taps_total * block_out, channels_in), jnp.float32)

time: 120 us -> 109 us (0.908)
  waiting for transfers between devices: 45.5 us -> 34.2 us
    ppermute x2 -> x1, waiting for transfers between devices: 6.03 us -> 0.01 us  [padded_2(): after = lax.ppermute(first, axis, down)]
    ppermute x0 -> x2, starting transfers between devices: none -> 4.67 us  [the longest x1 3.38 us: body(): from_below = lax.ppermute(forward[depth_cells + 1:], 'space', up)]
    reduce_scatter x1, waiting for transfers between devices: 8.32 us -> 3.95 us  [body(): lax.psum_scatter(spread.reshape(channels_in, depth_cells * plane_cells),...]
    ppermute x2 -> x1, starting transfers between devices: 9.14 us -> 4.85 us  [padded_2(): before = lax.ppermute(last, axis, up)]
    ppermute x0 -> x2, waiting for transfers between devices: none -> 4.2 us  [the longest x1 4.19 us: body(): from_above = lax.ppermute(forward[:1], 'space', down)]
    add x0 -> x2, other arithmetic: none -> 4.18 us  [the longest x1 2.5 us: body(): in_plane = part if in_plane is None else in_plane + part]
    transpose x1, other arithmetic: 2.98 us -> 0.13 us  [body(): jnp.transpose((forward + bias_term[None, :, None]).astype(jnp.bfloat16),...]
    unnamed x11 -> x20, local copies, waits for them, and re-layouts: 8.73 us -> 11.6 us
  transfers between devices with their start and end apart: 10 -> 10, of which waited for: 9 -> 7; matrix products, arithmetic and copies ran while one was open for 31% -> 35% of each run, Pallas kernels for 0% -> 0%
where the time goes in v1:
time: 109 us; the launch traced here: 108 us
  waiting for transfers between devices  34.2 us (31%)
  local copies, waits for them, and re-layouts  23.2 us (21%)
  starting transfers between devices  16.7 us (15%)
  between operations  14.5 us (13%)
  matrix products  12.4 us (11%)
  other arithmetic  7.47 us (7%)
    unnamed x20, local copies, waits for them, and re-layouts  11.6 us
    ppermute x2, waiting for transfers between devices, all_reduce_rows(): current = keep + lax.ppermute(send, axis, pairs)  9.03 us
    all_gather x1, waiting for transfers between devices, body(): gathered = lax.all_gather(inputs_planes, 'chan', axis=1, tiled=True)  8.86 us
    ppermute x2, waiting for transfers between devices, all_reduce_rows(): other = lax.ppermute(current, axis, pairs)  8.11 us
    dot_general x3, matrix products, body(): jnp.einsum('bjk,zkn->bjzn', backward_weight[depth_index], grad_shifted[2...  5.86 us
    ppermute x1, starting transfers between devices, padded_2(): before = lax.ppermute(last, axis, up)  4.85 us
    ppermute x1, waiting for transfers between devices, body(): from_above = lax.ppermute(forward[:1], 'space', down)  4.19 us
    dot_general x3, matrix products, body(): jnp.einsum('zkn,zin->ki', grad_shifted[2 - depth_index:2 - depth_index +...  4.15 us
  transfers between devices with their start and end apart: 10, of which 7 were waited for; matrix products, arithmetic and copies ran while one was open for 35% of the time, Pallas kernels for 0%

profile of v1, /device:TPU:0, one launch (start us, length us, event | category | flops | bytes accessed | tf_op | source)
XLA Modules:
  0.0 108.5 jit_solution(17551314630763585014)
XLA Ops:
  7.2 1.0 copy.65
  8.3 4.8 %collective-permute-start.2 = (bf16[1,32,1024]{2,1,0:T(8,128)(2,1)S(1)}, bf16[1,32,1024]{2,1,0:T(8,128)(2,1)S(1)}, u32[]{:S(2)}, u32[]{:S(2)}) collective-permute-start(bf16[1,32,1024]{2,1,0:T(8,128)(2,1)S(1)} %get-tuple-element.43), channel_id=1, source_target_pairs={{0,8},{8,16},{16,24},{1,9},{9,17},{17,25},{2,10},{10,18},{18,26},{... | collective-permute-start | bytes 196616 | tf_op jit(solution)/shard_map/ppermute | solution.py:28
  13.1 1.3 %collective-permute-start.3 = (bf16[1,32,1024]{2,1,0:T(8,128)(2,1)S(1)}, bf16[1,32,1024]{2,1,0:T(8,128)(2,1)S(1)}, u32[]{:S(2)}, u32[]{:S(2)}) collective-permute-start(bf16[1,32,1024]{2,1,0:T(8,128)(2,1)S(1)} %get-tuple-element.44), channel_id=1, source_target_pairs={{8,0},{16,8},{24,16},{9,1},{17,9},{25,17},{10,2},{18,10},{26,18},{... | collective-permute-start | bytes 196616 | tf_op jit(solution)/shard_map/ppermute | solution.py:29
  14.4 1.7 %copy.64 = bf16[32,4,1024]{2,0,1:T(8,128)(2,1)} copy(bf16[32,4,1024]{2,1,0:T(4,128)(2,1)} %param.6) | data formatting | bytes 524288 | tf_op args[0]
  16.2 1.1 %fusion.65 = (bf16[1,256,9,32]{1,3,2,0:T(8,128)(2,1)S(1)}, bf16[1,256,9,32]{1,3,2,0:T(8,128)(2,1)S(1)}, bf16[1,256,9,32]{1,3,2,0:T(8,128)(2,1)S(1)}) fusion(bf16[3,256,9,32]{1,3,2,0:T(8,128)(2,1)} %bitcast.196), kind=kLoop, calls=%fused_computation.120 | loop fusion | bytes 884736 | tf_op jit(solution)/shard_map/slice | solution.py:174
  17.6 0.4 copy.43
  18.2 0.4 copy.41
  18.9 0.4 copy.45
  20.9 1.0 fusion.63
  22.1 0.3 copy.42
  22.5 0.3 copy.40
  22.8 1.8 %fusion.45 = f32[4,1024,8,32]{1,3,2,0:T(8,128)S(1)} fusion(bf16[4,288,1024,1]{2,1,3,0:T(8,128)(2,1)S(1)} %bitcast.188, bf16[8,32,288]{2,1,0:T(8,128)(2,1)S(1)} %copy.43), kind=kOutput, calls=%fused_computation.91 | convolution fusion | flops 603979776 | bytes 6701056 | tf_op jit(solution)/shard_map/bjk,zkn->bjzn/dot_general | solution.py:172
  24.6 0.3 copy-done.3
  24.9 1.8 %fusion.47 = f32[4,1024,8,32]{1,3,2,0:T(8,128)S(1)} fusion(bf16[4,288,1024,1]{2,1,3,0:T(8,128)(2,1)S(1)} %bitcast.190, bf16[8,32,288]{2,1,0:T(8,128)(2,1)S(1)} %copy.41), kind=kOutput, calls=%fused_computation.93 | convolution fusion | flops 603979776 | bytes 6701056 | tf_op jit(solution)/shard_map/bjk,zkn->bjzn/dot_general | solution.py:172
  26.7 2.3 %add_bitcast_fusion = f32[8,32,4,1024]{3,1,0,2:T(8,128)S(1)} fusion(f32[4,1024,8,32]{1,3,2,0:T(8,128)S(1)} %fusion.47, f32[4,1024,8,32]{1,3,2,0:T(8,128)S(1)} %fusion.45, bf16[4,288,1024,1]{2,1,3,0:T(8,128)(2,1)S(1)} %bitcast.184, bf16[8,32,288]{2,1,0:T(8,128)(2,1)S(1)} %copy.45), kind=kOutput, calls=%fused_computation.1 | convolution fusion | flops 606076928 | bytes 15089664 | tf_op jit(solution)/shard_map/bjk,zkn->bjzn/dot_general | solution.py:172
  29.0 2.9 %copy.46 = f32[8,32,4,1024]{3,2,1,0:T(4,128)S(1)} copy(f32[8,32,4,1024]{3,1,0,2:T(8,128)S(1)} %add_bitcast_fusion) | data formatting | bytes 8388608 | tf_op jit(solution)/shard_map/add | solution.py:178
  31.9 5.7 %copy.60 = f32[32,8,4,1024]{3,1,2,0:T(8,128)} copy(f32[32,8,4,1024]{3,2,1,0:T(4,128)S(1)} %bitcast.187) | data formatting | bytes 8388608
  37.7 0.9 copy-done.6
  38.6 0.3 convert_reduce_fusion
  39.0 8.9 %all-gather.2.cloned.1.call-done = bf16[4,256,1024]{2,1,0:T(8,128)(2,1)} async-done(((bf16[4,32,1024]{2,1,0:T(8,128)(2,1)}), bf16[4,256,1024]{2,1,0:T(8,128)(2,1)}) %all-gather.2.cloned.1.call-update) | async-done | bytes 2097168 | tf_op jit(solution)/shard_map/all_gather | solution.py:106
  47.8 2.5 %convolution_bitcast_fusion.3 = f32[1,288,256]{2,1,0:T(8,128)S(1)} fusion(bf16[4,288,1024]{2,1,0:T(8,128)(2,1)S(1)} %bitcast.185, bf16[4,256,1024]{2,1,0:T(8,128)(2,1)} %all-gather.2.cloned.1.call-done), kind=kOutput, calls=%fused_computation.7 | convolution fusion | flops 603979776 | bytes 4751360 | tf_op jit(solution)/shard_map/zkn,zin->ki/dot_general | solution.py:144
  50.4 0.3 copy-done.2
  50.8 0.8 convolution_bitcast_fusion.4
  51.6 0.6 copy-done.4
  52.2 0.8 convolution_bitcast_fusion.5
  53.2 1.5 %collective-permute-start.4 = (f32[448,256]{1,0:T(8,128)S(1)}, f32[448,256]{1,0:T(8,128)S(1)}, u32[]{:S(2)}, u32[]{:S(2)}) collective-permute-start(f32[448,256]{1,0:T(8,128)S(1)} %constant_dynamic-slice_fusion.1), channel_id=1, source_target_pairs={{0,8},{8,0},{16,24},{24,16},{1,9},{9,1},{17,25},{25,17},{2,10},{10... | collective-permute-start | bytes 1376264 | tf_op jit(solution)/shard_map/ppermute | solution.py:66
  54.7 0.8 convolution_bitcast_fusion
  55.5 0.8 convolution_bitcast_fusion.1
  56.3 0.8 convolution_bitcast_fusion.2
  57.1 2.5 %pad_add_fusion = f32[6,288,1024]{2,1,0:T(8,128)S(1)} fusion(f32[4,288,1024]{2,1,0:T(8,128)S(1)} %convolution_bitcast_fusion, f32[4,288,1024]{2,1,0:T(8,128)S(1)} %convolution_bitcast_fusion.1, f32[4,288,1024]{2,1,0:T(8,128)S(1)} %convolution_bitcast_fusion.2), kind=kLoop, calls=%fused_computation | loop fusion | flops 3538944 | bytes 21233664 | tf_op jit(solution)/shard_map/add | solution.py:119
  59.6 1.1 %slice_bitcast_fusion = (f32[6,32,1024]{2,1,0:T(8,128)S(1)}, f32[6,32,1024]{2,1,0:T(8,128)S(1)}, f32[6,32,1024]{2,1,0:T(8,128)S(1)}, f32[6,32,1024]{2,1,0:T(8,12...) fusion(f32[6,9,32,1024]{3,2,1,0:T(8,128)S(1)} %bitcast.182), kind=kLoop, calls=%fused_computation.39 | loop fusion | bytes 12582912 | tf_op jit(solution)/shard_map/squeeze | solution.py:123
  60.7 5.2 %collective-permute-done.4 = f32[448,256]{1,0:T(8,128)S(1)} collective-permute-done((f32[448,256]{1,0:T(8,128)S(1)}, f32[448,256]{1,0:T(8,128)S(1)}, u32[]{:S(2)}, u32[]{:S(2)}) %collective-permute-start.4) | collective-permute-done | bytes 458784 | tf_op jit(solution)/shard_map/ppermute | solution.py:66
  66.0 1.5 %collective-permute-start.5 = (f32[224,256]{1,0:T(8,128)S(1)}, f32[224,256]{1,0:T(8,128)S(1)}, u32[]{:S(2)}, u32[]{:S(2)}) collective-permute-start(f32[224,256]{1,0:T(8,128)S(1)} %constant_dynamic-slice_fusion), channel_id=1, source_target_pairs={{0,16},{8,24},{16,0},{24,8},{1,17},{9,25},{17,1},{25,9},{2,18},{10... | collective-permute-start | bytes 688136 | tf_op jit(solution)/shard_map/ppermute | solution.py:66
  67.5 1.7 %fusion.10 = f32[6,32,1024]{2,1,0:T(8,128)S(1)} fusion(f32[6,32,1024]{2,1,0:T(8,128)S(1)} %get-tuple-element.29, f32[6,32,1024]{2,1,0:T(8,128)S(1)} %get-tuple-element.28, f32[6,32,1024]{2,1,0:T(8,128)S(1)} %get-tuple-element.27, f32[6,32,1024]{2,1,0:T(8,128)S(1)} %get-tuple-element.26, f32[6,32,1024]{2,1,0:T(8,128)S(1)} %get-tuple-element.25, ...), kind=kLoop, calls=%fused_computation.31 | loop fusion | flops 3342336 | bytes 7867392 | tf_op jit(solution)/shard_map/add | solution.py:124
  69.2 3.9 %collective-permute-done.5 = f32[224,256]{1,0:T(8,128)S(1)} collective-permute-done((f32[224,256]{1,0:T(8,128)S(1)}, f32[224,256]{1,0:T(8,128)S(1)}, u32[]{:S(2)}, u32[]{:S(2)}) %collective-permute-start.5) | collective-permute-done | bytes 229408 | tf_op jit(solution)/shard_map/ppermute | solution.py:66
  73.2 1.5 %collective-permute-start.6 = (f32[224,256]{1,0:T(8,128)S(1)}, f32[224,256]{1,0:T(8,128)S(1)}, u32[]{:S(2)}, u32[]{:S(2)}) collective-permute-start(f32[224,256]{1,0:T(8,128)S(1)} %get-tuple-element.21), channel_id=1, source_target_pairs={{0,16},{8,24},{16,0},{24,8},{1,17},{9,25},{17,1},{25,9},{2,18},{10... | collective-permute-start | bytes 688136 | tf_op jit(solution)/shard_map/ppermute | solution.py:71
  74.7 3.4 %collective-permute-start = (f32[1,32,1024]{2,1,0:T(8,128)S(1)}, f32[1,32,1024]{2,1,0:T(8,128)S(1)}, u32[]{:S(2)}, u32[]{:S(2)}) collective-permute-start(f32[1,32,1024]{2,1,0:T(8,128)S(1)} %get-tuple-element.33), channel_id=1, source_target_pairs={{0,8},{8,16},{16,24},{1,9},{9,17},{17,25},{2,10},{10,18},{18,26},{... | collective-permute-start | bytes 393224 | tf_op jit(solution)/shard_map/ppermute | solution.py:128
  78.1 1.3 %collective-permute-start.1 = (f32[1,32,1024]{2,1,0:T(8,128)S(1)}, f32[1,32,1024]{2,1,0:T(8,128)S(1)}, u32[]{:S(2)}, u32[]{:S(2)}) collective-permute-start(f32[1,32,1024]{2,1,0:T(8,128)S(1)} %get-tuple-element.34), channel_id=1, source_target_pairs={{8,0},{16,8},{24,16},{9,1},{17,9},{25,17},{10,2},{18,10},{26,18},{... | collective-permute-start | bytes 393224 | tf_op jit(solution)/shard_map/ppermute | solution.py:129
  79.4 1.5 %collective-permute-done.6 = f32[224,256]{1,0:T(8,128)S(1)} collective-permute-done((f32[224,256]{1,0:T(8,128)S(1)}, f32[224,256]{1,0:T(8,128)S(1)}, u32[]{:S(2)}, u32[]{:S(2)}) %collective-permute-start.6) | collective-permute-done | bytes 229408 | tf_op jit(solution)/shard_map/ppermute | solution.py:71
  80.9 1.2 %collective-permute-start.7 = (f32[448,256]{1,0:T(8,128)S(1)}, f32[448,256]{1,0:T(8,128)S(1)}, u32[]{:S(2)}, u32[]{:S(2)}) collective-permute-start(f32[448,256]{1,0:T(8,128)S(1)} %constant_dynamic-update-slice_fusion.2), channel_id=1, source_target_pairs={{0,8},{8,0},{16,24},{24,16},{1,9},{9,1},{17,25},{25,17},{2,10},{10... | collective-permute-start | bytes 1376264 | tf_op jit(solution)/shard_map/ppermute | solution.py:71
  82.2 4.2 %collective-permute-done.1 = f32[1,32,1024]{2,1,0:T(8,128)S(1)} collective-permute-done((f32[1,32,1024]{2,1,0:T(8,128)S(1)}, f32[1,32,1024]{2,1,0:T(8,128)S(1)}, u32[]{:S(2)}, u32[]{:S(2)}) %collective-permute-start.1) | collective-permute-done | bytes 131104 | tf_op jit(solution)/shard_map/ppermute | solution.py:129
  86.6 0.9 copy.47
  87.6 6.6 %collective-permute-done.7 = f32[448,256]{1,0:T(8,128)S(1)} collective-permute-done((f32[448,256]{1,0:T(8,128)S(1)}, f32[448,256]{1,0:T(8,128)S(1)}, u32[]{:S(2)}, u32[]{:S(2)}) %collective-permute-start.7) | collective-permute-done | bytes 458784 | tf_op jit(solution)/shard_map/ppermute | solution.py:71
  94.2 1.0 slice.234
  95.2 0.5 slice_bitcast_fusion.9
  95.7 4.0 %reduce-scatter.2.cloned.1.call-done = f32[32,4096]{1,0:T(8,128)} async-done(((f32[256,4096]{1,0:T(8,128)}), f32[32,4096]{1,0:T(8,128)}) %reduce-scatter.2.cloned.1.call-update) | async-done | bytes 524304 | tf_op jit(solution)/shard_map/reduce_scatter | solution.py:179
  99.7 1.1 convert_element_type.36
  100.7 0.9 reshape.120
  (52 shorter events, 3.4 us)
Async XLA Ops:
  7.2 40.7 %all-gather.2.cloned.1.call-start = ((), (), s32[]{:S(2)}) async-start(), calls=%async_computation.1 | async-start | bytes 2359296 | tf_op jit(solution)/shard_map/all_gather | solution.py:106
  8.3 11.0 %collective-permute-start.2 = (bf16[1,32,1024]{2,1,0:T(8,128)(2,1)S(1)}, bf16[1,32,1024]{2,1,0:T(8,128)(2,1)S(1)}, u32[]{:S(2)}, u32[]{:S(2)}) collective-permute-start(bf16[1,32,1024]{2,1,0:T(8,128)(2,1)S(1)} %get-tuple-element.43), channel_id=1, source_target_pairs={{0,8},{8,16},{16,24},{1,9},{9,17},{17,25},{2,10},{10,18},{18,26},{... | collective-permute-start | bytes 196616 | tf_op jit(solution)/shard_map/ppermute | solution.py:28
  13.1 6.2 %collective-permute-start.3 = (bf16[1,32,1024]{2,1,0:T(8,128)(2,1)S(1)}, bf16[1,32,1024]{2,1,0:T(8,128)(2,1)S(1)}, u32[]{:S(2)}, u32[]{:S(2)}) collective-permute-start(bf16[1,32,1024]{2,1,0:T(8,128)(2,1)S(1)} %get-tuple-element.44), channel_id=1, source_target_pairs={{8,0},{16,8},{24,16},{9,1},{17,9},{25,17},{10,2},{18,10},{26,18},{... | collective-permute-start | bytes 196616 | tf_op jit(solution)/shard_map/ppermute | solution.py:29
  16.2 83.5 %reduce-scatter.2.cloned.1.call-start = ((), (), s32[]{:S(2)}) async-start(), calls=%async_computation.2 | async-start | bytes 4718592 | tf_op jit(solution)/shard_map/reduce_scatter | solution.py:179
  22.5 2.1 %copy-start.1 = (bf16[4,9,32,1024]{3,2,1,0:T(8,128)(2,1)}, bf16[4,9,32,1024]{3,2,1,0:T(8,128)(2,1)S(1)}, u32[]{:S(2)}) copy-start(bf16[4,9,32,1024]{3,2,1,0:T(8,128)(2,1)S(1)} %copy.42) | copy-start | bytes 7077892
  22.8 2.1 %copy-start.3 = (bf16[4,9,32,1024]{3,2,1,0:T(8,128)(2,1)}, bf16[4,9,32,1024]{3,2,1,0:T(8,128)(2,1)S(1)}, u32[]{:S(2)}) copy-start(bf16[4,9,32,1024]{3,2,1,0:T(8,128)(2,1)S(1)} %copy.40) | copy-start | bytes 7077892
  37.7 1.0 copy-start.6
  37.7 1.3 %copy-start.5 = (bf16[27,256,32]{1,2,0:T(8,128)(2,1)S(1)}, bf16[27,256,32]{1,2,0:T(8,128)(2,1)}, u32[]{:S(2)}) copy-start(bf16[27,256,32]{1,2,0:T(8,128)(2,1)} %param.7) | copy-start | bytes 1327108
  47.8 2.6 %copy-start = (bf16[4,256,1024]{2,1,0:T(8,128)(2,1)S(1)}, bf16[4,256,1024]{2,1,0:T(8,128)(2,1)}, u32[]{:S(2)}) copy-start(bf16[4,256,1024]{2,1,0:T(8,128)(2,1)} %all-gather.2.cloned.1.call-done) | copy-start | bytes 6291460
  47.8 2.9 %copy-start.2 = (bf16[4,9,32,1024]{3,2,1,0:T(8,128)(2,1)S(1)}, bf16[4,9,32,1024]{3,2,1,0:T(8,128)(2,1)}, u32[]{:S(2)}) copy-start(bf16[4,9,32,1024]{3,2,1,0:T(8,128)(2,1)} %copy-done.1) | copy-start | bytes 7077892
  50.4 1.8 %copy-start.4 = (bf16[4,9,32,1024]{3,2,1,0:T(8,128)(2,1)S(1)}, bf16[4,9,32,1024]{3,2,1,0:T(8,128)(2,1)}, u32[]{:S(2)}) copy-start(bf16[4,9,32,1024]{3,2,1,0:T(8,128)(2,1)} %copy-done.3) | copy-start | bytes 7077892
  53.2 12.7 %collective-permute-start.4 = (f32[448,256]{1,0:T(8,128)S(1)}, f32[448,256]{1,0:T(8,128)S(1)}, u32[]{:S(2)}, u32[]{:S(2)}) collective-permute-start(f32[448,256]{1,0:T(8,128)S(1)} %constant_dynamic-slice_fusion.1), channel_id=1, source_target_pairs={{0,8},{8,0},{16,24},{24,16},{1,9},{9,1},{17,25},{25,17},{2,10},{10... | collective-permute-start | bytes 1376264 | tf_op jit(solution)/shard_map/ppermute | solution.py:66
  66.0 7.1 %collective-permute-start.5 = (f32[224,256]{1,0:T(8,128)S(1)}, f32[224,256]{1,0:T(8,128)S(1)}, u32[]{:S(2)}, u32[]{:S(2)}) collective-permute-start(f32[224,256]{1,0:T(8,128)S(1)} %constant_dynamic-slice_fusion), channel_id=1, source_target_pairs={{0,16},{8,24},{16,0},{24,8},{1,17},{9,25},{17,1},{25,9},{2,18},{10... | collective-permute-start | bytes 688136 | tf_op jit(solution)/shard_map/ppermute | solution.py:66
  67.5 18.9 %copy-start.7 = (f32[32]{0:T(128)S(1)}, f32[32]{0:T(128)}, u32[]{:S(2)}) copy-start(f32[32]{0:T(128)} %param.8) | copy-start | bytes 388
  73.2 7.7 %collective-permute-start.6 = (f32[224,256]{1,0:T(8,128)S(1)}, f32[224,256]{1,0:T(8,128)S(1)}, u32[]{:S(2)}, u32[]{:S(2)}) collective-permute-start(f32[224,256]{1,0:T(8,128)S(1)} %get-tuple-element.21), channel_id=1, source_target_pairs={{0,16},{8,24},{16,0},{24,8},{1,17},{9,25},{17,1},{25,9},{2,18},{10... | collective-permute-start | bytes 688136 | tf_op jit(solution)/shard_map/ppermute | solution.py:71
  74.7 7.5 %collective-permute-start = (f32[1,32,1024]{2,1,0:T(8,128)S(1)}, f32[1,32,1024]{2,1,0:T(8,128)S(1)}, u32[]{:S(2)}, u32[]{:S(2)}) collective-permute-start(f32[1,32,1024]{2,1,0:T(8,128)S(1)} %get-tuple-element.33), channel_id=1, source_target_pairs={{0,8},{8,16},{16,24},{1,9},{9,17},{17,25},{2,10},{10,18},{18,26},{... | collective-permute-start | bytes 393224 | tf_op jit(solution)/shard_map/ppermute | solution.py:128
  78.1 8.3 %collective-permute-start.1 = (f32[1,32,1024]{2,1,0:T(8,128)S(1)}, f32[1,32,1024]{2,1,0:T(8,128)S(1)}, u32[]{:S(2)}, u32[]{:S(2)}) collective-permute-start(f32[1,32,1024]{2,1,0:T(8,128)S(1)} %get-tuple-element.34), channel_id=1, source_target_pairs={{8,0},{16,8},{24,16},{9,1},{17,9},{25,17},{10,2},{18,10},{26,18},{... | collective-permute-start | bytes 393224 | tf_op jit(solution)/shard_map/ppermute | solution.py:129
  80.9 13.3 %collective-permute-start.7 = (f32[448,256]{1,0:T(8,128)S(1)}, f32[448,256]{1,0:T(8,128)S(1)}, u32[]{:S(2)}, u32[]{:S(2)}) collective-permute-start(f32[448,256]{1,0:T(8,128)S(1)} %constant_dynamic-update-slice_fusion.2), channel_id=1, source_target_pairs={{0,8},{8,0},{16,24},{24,16},{1,9},{9,1},{17,25},{25,17},{2,10},{10... | collective-permute-start | bytes 1376264 | tf_op jit(solution)/shard_map/ppermute | solution.py:71
Sparse Core Ops, SparseCore 0:
  16.3 31.4 all-gather.1
  50.1 49.4 reduce-scatter.1

commit v2 on v1

--- a/solution.py
+++ b/solution.py
@@ -91,6 +91,22 @@
 
 
 plane_offsets = tuple((row_step, column_step) for row_step in (-1, 0, 1) for column_step in (-1, 0, 1))
+
+
+def reduce_scatter_blocks(blocks, axis):
+    devices = lax.axis_size(axis)
+    steps = devices.bit_length() - 1
+    assert 1 << steps == devices
+    current = blocks.reshape((2,) * steps + blocks.shape[1:])
+    index = lax.axis_index(axis)
+    for step in range(steps):
+        bit = (index >> step) & 1
+        position = steps - 1 - step
+        keep = lax.dynamic_index_in_dim(current, bit, axis=position, keepdims=False)
+        send = lax.dynamic_index_in_dim(current, 1 - bit, axis=position, keepdims=False)
+        pairs = [(i, i ^ (1 << step)) for i in range(devices)]
+        current = keep + lax.ppermute(send, axis, pairs)
+    return current
 
 
 def body(inputs, weight, bias_term, output_grad):
@@ -176,8 +192,8 @@
             preferred_element_type=jnp.float32,
         )
         spread = part if spread is None else spread + part
-    summed = lax.psum_scatter(
-        spread.reshape(channels_in, depth_cells * plane_cells), "chan", scatter_dimension=0, tiled=True
+    summed = reduce_scatter_blocks(
+        spread.reshape(chan_devices, channels_in // chan_devices, depth_cells * plane_cells), "chan"
     )
     input_grad = summed.astype(jnp.bfloat16).reshape(block_in, depth_cells, plane_cells)
     return (outputs, input_grad, weight_grad, bias_grad)

time: 109 us -> 153 us (1.40)
  waiting for transfers between devices: 34.2 us -> 62.7 us
  local copies, waits for them, and re-layouts: 23.2 us -> 31.3 us
  other arithmetic: 7.47 us -> 11.9 us
  starting transfers between devices: 16.7 us -> 19.7 us
    ppermute x0 -> x3, waiting for transfers between devices: none -> 42.3 us  [reduce_scatter_blocks(): current = keep + lax.ppermute(send, axis, pairs)]
    all_gather x1, waiting for transfers between devices: 8.86 us -> 0.01 us  [body(): gathered = lax.all_gather(inputs_planes, 'chan', axis=1, tiled=True)]
    unnamed x20 -> x43, local copies, waits for them, and re-layouts: 11.6 us -> 5.4 us
    another operation x0 -> x1, local copies, waits for them, and re-layouts: none -> 6.07 us  [reduce_scatter_blocks(): current = blocks.reshape((2,) * steps + blocks.shape[1:])]
    squeeze x0 -> x3, local copies, waits for them, and re-layouts: none -> 5.02 us  [reduce_scatter_blocks(): lax.dynamic_index_in_dim(current, 1 - bit, axis=position, keepdims=False)]
    add x0 -> x2, other arithmetic: none -> 4.11 us  [reduce_scatter_blocks(): current = keep + lax.ppermute(send, axis, pairs)]
    ppermute x0 -> x3, starting transfers between devices: none -> 4.07 us  [reduce_scatter_blocks(): current = keep + lax.ppermute(send, axis, pairs)]
    reduce_scatter x1 -> x0, waiting for transfers between devices: 3.95 us -> none  [body(): lax.psum_scatter(spread.reshape(channels_in, depth_cells * plane_cells),...]
  transfers between devices with their start and end apart: 10 -> 12, of which waited for: 7 -> 8; matrix products, arithmetic and copies ran while one was open for 35% -> 18% of each run, Pallas kernels for 0% -> 0%
where the time goes in v2:
time: 153 us; the launch traced here: 152 us
  waiting for transfers between devices  62.7 us (41%)
  local copies, waits for them, and re-layouts  31.3 us (20%)
  starting transfers between devices  19.7 us (13%)
  between operations  14.6 us (10%)
  matrix products  12.4 us (8%)
  other arithmetic  11.9 us (8%)
    ppermute x3, waiting for transfers between devices, reduce_scatter_blocks(): current = keep + lax.ppermute(send, axis, pairs)  42.3 us
    ppermute x2, waiting for transfers between devices, all_reduce_rows(): current = keep + lax.ppermute(send, axis, pairs)  8.36 us
    ppermute x2, waiting for transfers between devices, all_reduce_rows(): other = lax.ppermute(current, axis, pairs)  7.34 us
    another operation x1, local copies, waits for them, and re-layouts, reduce_scatter_blocks(): current = blocks.reshape((2,) * steps + blocks.shape[1:])  6.07 us
    dot_general x3, matrix products, body(): jnp.einsum('bjk,zkn->bjzn', backward_weight[depth_index], grad_shifted[2...  5.85 us
    unnamed x43, local copies, waits for them, and re-layouts  5.4 us
    squeeze x3, local copies, waits for them, and re-layouts, reduce_scatter_blocks(): lax.dynamic_index_in_dim(current, 1 - bit, axis=position, keepdims=False)  5.02 us
    add x1, local copies, waits for them, and re-layouts, body(): spread = part if spread is None else spread + part  4.93 us
  transfers between devices with their start and end apart: 12, of which 8 were waited for; matrix products, arithmetic and copies ran while one was open for 18% of the time, Pallas kernels for 0%

profile of v2, /device:TPU:0, one launch (start us, length us, event | category | flops | bytes accessed | tf_op | source)
XLA Modules:
  0.0 152.4 jit_solution(14739577389658618446)
XLA Ops:
  7.2 1.0 copy.64
  8.3 4.8 %collective-permute-start.2 = (bf16[1,32,1024]{2,1,0:T(8,128)(2,1)S(1)}, bf16[1,32,1024]{2,1,0:T(8,128)(2,1)S(1)}, u32[]{:S(2)}, u32[]{:S(2)}) collective-permute-start(bf16[1,32,1024]{2,1,0:T(8,128)(2,1)S(1)} %get-tuple-element.43), channel_id=1, source_target_pairs={{0,8},{8,16},{16,24},{1,9},{9,17},{17,25},{2,10},{10,18},{18,26},{... | collective-permute-start | bytes 196616 | tf_op jit(solution)/shard_map/ppermute | solution.py:28
  13.1 1.3 collective-permute-start.3
  14.5 1.1 fusion.66
  17.5 1.7 %collective-permute-done.3 = bf16[1,32,1024]{2,1,0:T(8,128)(2,1)S(1)} collective-permute-done((bf16[1,32,1024]{2,1,0:T(8,128)(2,1)S(1)}, bf16[1,32,1024]{2,1,0:T(8,128)(2,1)S(1)}, u32[]{:S(2)}, u32[]{:S(2)}) %collective-permute-start.3) | collective-permute-done | bytes 65568 | tf_op jit(solution)/shard_map/ppermute | solution.py:29
  20.9 1.0 fusion.64
  22.8 1.8 %fusion.46 = f32[4,1024,8,32]{1,3,2,0:T(8,128)S(1)} fusion(bf16[4,288,1024,1]{2,1,3,0:T(8,128)(2,1)S(1)} %bitcast.197, bf16[8,32,288]{2,1,0:T(8,128)(2,1)S(1)} %copy.43), kind=kOutput, calls=%fused_computation.98 | convolution fusion | flops 603979776 | bytes 6701056 | tf_op jit(solution)/shard_map/bjk,zkn->bjzn/dot_general | solution.py:188
  24.9 1.8 %fusion.48 = f32[4,1024,8,32]{1,3,2,0:T(8,128)S(1)} fusion(bf16[4,288,1024,1]{2,1,3,0:T(8,128)(2,1)S(1)} %bitcast.199, bf16[8,32,288]{2,1,0:T(8,128)(2,1)S(1)} %copy.41), kind=kOutput, calls=%fused_computation.100 | convolution fusion | flops 603979776 | bytes 6701056 | tf_op jit(solution)/shard_map/bjk,zkn->bjzn/dot_general | solution.py:188
  26.7 2.3 %add_bitcast_fusion = f32[8,32,4,1024]{3,1,0,2:T(8,128)S(1)} fusion(f32[4,1024,8,32]{1,3,2,0:T(8,128)S(1)} %fusion.48, f32[4,1024,8,32]{1,3,2,0:T(8,128)S(1)} %fusion.46, bf16[4,288,1024,1]{2,1,3,0:T(8,128)(2,1)S(1)} %bitcast.195, bf16[8,32,288]{2,1,0:T(8,128)(2,1)S(1)} %copy.45), kind=kOutput, calls=%fused_computation.1 | convolution fusion | flops 606076928 | bytes 15089664 | tf_op jit(solution)/shard_map/bjk,zkn->bjzn/dot_general | solution.py:188
  29.0 4.9 %copy.46 = f32[8,32,4,1024]{3,2,1,0:T(4,128)} copy(f32[8,32,4,1024]{3,1,0,2:T(8,128)S(1)} %add_bitcast_fusion) | data formatting | bytes 8388608 | tf_op jit(solution)/shard_map/add | solution.py:194
  33.9 6.1 %reshape_reshape.3 = f32[2,2,2,32,4096]{4,3,2,1,0:T(8,128)} reshape(f32[8,32,4,1024]{3,2,1,0:T(4,128)} %copy.46) | data formatting | bytes 8388608 | tf_op jit(solution)/shard_map/reshape;reshape | solution.py:100
  40.0 3.1 %dynamic-slice_bitcast_fusion = f32[2,2,32,4096]{3,2,1,0:T(8,128)} fusion(f32[2,2,2,32,4096]{4,3,2,1,0:T(8,128)} %reshape_reshape.3, s32[]{:T(128)S(6)} %select_n.195), kind=kLoop, calls=%fused_computation.6 | loop fusion | bytes 4194308 | tf_op jit(solution)/shard_map/jit(dynamic_index_in_dim)/squeeze | solution.py:106
  43.1 0.8 copy.63
  44.0 3.7 %collective-permute-done.4 = f32[2,2,32,4096]{3,2,1,0:T(8,128)} collective-permute-done((f32[2,2,32,4096]{3,2,1,0:T(8,128)}, f32[2,2,32,4096]{3,2,1,0:T(8,128)}, u32[]{:S(2)}, u32[]{:S(2)}) %collective-permute-start.4) | collective-permute-done | bytes 2097184 | tf_op jit(solution)/shard_map/ppermute | solution.py:108
  47.6 2.5 %bitcast_add_fusion = f32[2,2,32,4096]{3,2,1,0:T(8,128)S(1)} fusion(f32[2,2,32,4096]{3,2,1,0:T(8,128)} %collective-permute-done.4, f32[2,2,2,32,4096]{4,3,2,1,0:T(8,128)} %reshape_reshape.3, s32[]{:T(128)S(6)} %select_n.194), kind=kLoop, calls=%fused_computation.5 | loop fusion | flops 524288 | bytes 6291460 | tf_op jit(solution)/shard_map/add | solution.py:108
  50.1 1.4 copy-done.5
  51.5 1.0 dynamic-slice_bitcast_fusion.1
  52.6 1.5 %collective-permute-start.5 = (f32[2,32,4096]{2,1,0:T(8,128)}, f32[2,32,4096]{2,1,0:T(8,128)}, u32[]{:S(2)}, u32[]{:S(2)}) collective-permute-start(f32[2,32,4096]{2,1,0:T(8,128)} %dynamic-slice_bitcast_fusion.1), channel_id=1, source_target_pairs={{0,2},{1,3},{2,0},{3,1},{4,6},{5,7},{6,4},{7,5},{8,10},{9,11},{10,... | collective-permute-start | bytes 3145736 | tf_op jit(solution)/shard_map/ppermute | solution.py:108
  54.7 0.8 convert_reduce_fusion
  55.5 0.7 fusion.67
  56.3 38.7 %collective-permute-done.5 = f32[2,32,4096]{2,1,0:T(8,128)} collective-permute-done((f32[2,32,4096]{2,1,0:T(8,128)}, f32[2,32,4096]{2,1,0:T(8,128)}, u32[]{:S(2)}, u32[]{:S(2)}) %collective-permute-start.5) | collective-permute-done | bytes 1048608 | tf_op jit(solution)/shard_map/ppermute | solution.py:108
  94.9 1.6 %bitcast_add_fusion.1 = f32[2,32,4096]{2,1,0:T(8,128)S(1)} fusion(f32[2,32,4096]{2,1,0:T(8,128)} %collective-permute-done.5, f32[2,2,32,4096]{3,2,1,0:T(8,128)} %copy-done.5, s32[]{:T(128)S(6)} %select_n.196), kind=kLoop, calls=%fused_computation.12 | loop fusion | flops 262144 | bytes 3145732 | tf_op jit(solution)/shard_map/add | solution.py:108
  96.6 0.8 dynamic-slice_bitcast_fusion.2
  97.4 2.5 %collective-permute-start.6 = (f32[32,4096]{1,0:T(8,128)}, f32[32,4096]{1,0:T(8,128)}, u32[]{:S(2)}, u32[]{:S(2)}) collective-permute-start(f32[32,4096]{1,0:T(8,128)} %dynamic-slice_bitcast_fusion.2), channel_id=1, source_target_pairs={{0,4},{1,5},{2,6},{3,7},{4,0},{5,1},{6,2},{7,3},{8,12},{9,13},{10,... | collective-permute-start | bytes 1572872 | tf_op jit(solution)/shard_map/ppermute | solution.py:108
  100.0 2.5 %convolution_bitcast_fusion.3 = f32[1,288,256]{2,1,0:T(8,128)S(1)} fusion(bf16[4,288,1024]{2,1,0:T(8,128)(2,1)S(1)} %bitcast.196, bf16[4,256,1024]{2,1,0:T(8,128)(2,1)} %all-gather.2.cloned.1.call-done), kind=kOutput, calls=%fused_computation.9 | convolution fusion | flops 603979776 | bytes 4751360 | tf_op jit(solution)/shard_map/zkn,zin->ki/dot_general | solution.py:160
  102.9 0.8 convolution_bitcast_fusion.4
  104.3 0.8 convolution_bitcast_fusion.5
  105.3 1.5 %collective-permute-start.7 = (f32[448,256]{1,0:T(8,128)S(1)}, f32[448,256]{1,0:T(8,128)S(1)}, u32[]{:S(2)}, u32[]{:S(2)}) collective-permute-start(f32[448,256]{1,0:T(8,128)S(1)} %constant_dynamic-slice_fusion.1), channel_id=1, source_target_pairs={{0,8},{8,0},{16,24},{24,16},{1,9},{9,1},{17,25},{25,17},{2,10},{10... | collective-permute-start | bytes 1376264 | tf_op jit(solution)/shard_map/ppermute | solution.py:66
  106.9 0.8 convolution_bitcast_fusion
  107.6 0.8 convolution_bitcast_fusion.1
  108.4 0.8 convolution_bitcast_fusion.2
  109.2 2.3 %pad_add_fusion = f32[6,288,1024]{2,1,0:T(8,128)S(1)} fusion(f32[4,288,1024]{2,1,0:T(8,128)S(1)} %convolution_bitcast_fusion, f32[4,288,1024]{2,1,0:T(8,128)S(1)} %convolution_bitcast_fusion.1, f32[4,288,1024]{2,1,0:T(8,128)S(1)} %convolution_bitcast_fusion.2), kind=kLoop, calls=%fused_computation | loop fusion | flops 3538944 | bytes 21233664 | tf_op jit(solution)/shard_map/add | solution.py:135
  111.5 1.0 slice_bitcast_fusion
  112.5 5.0 %collective-permute-done.7 = f32[448,256]{1,0:T(8,128)S(1)} collective-permute-done((f32[448,256]{1,0:T(8,128)S(1)}, f32[448,256]{1,0:T(8,128)S(1)}, u32[]{:S(2)}, u32[]{:S(2)}) %collective-permute-start.7) | collective-permute-done | bytes 458784 | tf_op jit(solution)/shard_map/ppermute | solution.py:66
  117.6 1.4 collective-permute-start.8
  119.1 1.7 %fusion.10 = f32[6,32,1024]{2,1,0:T(8,128)S(1)} fusion(f32[6,32,1024]{2,1,0:T(8,128)S(1)} %get-tuple-element.29, f32[6,32,1024]{2,1,0:T(8,128)S(1)} %get-tuple-element.28, f32[6,32,1024]{2,1,0:T(8,128)S(1)} %get-tuple-element.27, f32[6,32,1024]{2,1,0:T(8,128)S(1)} %get-tuple-element.26, f32[6,32,1024]{2,1,0:T(8,128)S(1)} %get-tuple-element.25, ...), kind=kLoop, calls=%fused_computation.35 | loop fusion | flops 3342336 | bytes 7867392 | tf_op jit(solution)/shard_map/add | solution.py:140
  120.8 3.4 %collective-permute-done.8 = f32[224,256]{1,0:T(8,128)S(1)} collective-permute-done((f32[224,256]{1,0:T(8,128)S(1)}, f32[224,256]{1,0:T(8,128)S(1)}, u32[]{:S(2)}, u32[]{:S(2)}) %collective-permute-start.8) | collective-permute-done | bytes 229408 | tf_op jit(solution)/shard_map/ppermute | solution.py:66
  124.2 1.3 collective-permute-start.9
  125.6 2.4 %collective-permute-start = (f32[1,32,1024]{2,1,0:T(8,128)S(1)}, f32[1,32,1024]{2,1,0:T(8,128)S(1)}, u32[]{:S(2)}, u32[]{:S(2)}) collective-permute-start(f32[1,32,1024]{2,1,0:T(8,128)S(1)} %get-tuple-element.33), channel_id=1, source_target_pairs={{0,8},{8,16},{16,24},{1,9},{9,17},{17,25},{2,10},{10,18},{18,26},{... | collective-permute-start | bytes 393224 | tf_op jit(solution)/shard_map/ppermute | solution.py:144
  128.0 1.3 collective-permute-start.1
  129.3 1.3 collective-permute-done.9
  130.6 1.4 collective-permute-start.10
  132.0 1.1 fusion.24
  133.1 0.9 reshape.116
  134.0 2.9 %collective-permute-done.1 = f32[1,32,1024]{2,1,0:T(8,128)S(1)} collective-permute-done((f32[1,32,1024]{2,1,0:T(8,128)S(1)}, f32[1,32,1024]{2,1,0:T(8,128)S(1)}, u32[]{:S(2)}, u32[]{:S(2)}) %collective-permute-start.1) | collective-permute-done | bytes 131104 | tf_op jit(solution)/shard_map/ppermute | solution.py:145
  137.0 0.9 copy.47
  138.0 6.0 %collective-permute-done.10 = f32[448,256]{1,0:T(8,128)S(1)} collective-permute-done((f32[448,256]{1,0:T(8,128)S(1)}, f32[448,256]{1,0:T(8,128)S(1)}, u32[]{:S(2)}, u32[]{:S(2)}) %collective-permute-start.10) | collective-permute-done | bytes 458784 | tf_op jit(solution)/shard_map/ppermute | solution.py:71
  144.1 1.0 slice.234
  (84 shorter events, 7.4 us)
Async XLA Ops:
  7.2 92.8 %all-gather.2.cloned.1.call-start = ((), (), s32[]{:S(2)}) async-start(), calls=%async_computation | async-start | bytes 2359296 | tf_op jit(solution)/shard_map/all_gather | solution.py:122
  8.3 9.3 %collective-permute-start.2 = (bf16[1,32,1024]{2,1,0:T(8,128)(2,1)S(1)}, bf16[1,32,1024]{2,1,0:T(8,128)(2,1)S(1)}, u32[]{:S(2)}, u32[]{:S(2)}) collective-permute-start(bf16[1,32,1024]{2,1,0:T(8,128)(2,1)S(1)} %get-tuple-element.43), channel_id=1, source_target_pairs={{0,8},{8,16},{16,24},{1,9},{9,17},{17,25},{2,10},{10,18},{18,26},{... | collective-permute-start | bytes 196616 | tf_op jit(solution)/shard_map/ppermute | solution.py:28
  13.1 6.2 %collective-permute-start.3 = (bf16[1,32,1024]{2,1,0:T(8,128)(2,1)S(1)}, bf16[1,32,1024]{2,1,0:T(8,128)(2,1)S(1)}, u32[]{:S(2)}, u32[]{:S(2)}) collective-permute-start(bf16[1,32,1024]{2,1,0:T(8,128)(2,1)S(1)} %get-tuple-element.44), channel_id=1, source_target_pairs={{8,0},{16,8},{24,16},{9,1},{17,9},{25,17},{10,2},{18,10},{26,18},{... | collective-permute-start | bytes 196616 | tf_op jit(solution)/shard_map/ppermute | solution.py:29
  14.4 6.0 %copy-start.11 = (pred[1024]{0:T(1024)(128)(4,1)}, pred[1024]{0:T(1024)(128)(4,1)S(1)}, u32[]{:S(2)}) copy-start(pred[1024]{0:T(1024)(128)(4,1)S(1)} %get-tuple-element.45) | copy-start | bytes 3076
  14.4 6.3 %copy-start.13 = (pred[1024]{0:T(1024)(128)(4,1)}, pred[1024]{0:T(1024)(128)(4,1)S(1)}, u32[]{:S(2)}) copy-start(pred[1024]{0:T(1024)(128)(4,1)S(1)} %get-tuple-element.46) | copy-start | bytes 3076
  17.5 3.3 %copy-start.15 = (pred[1024]{0:T(1024)(128)(4,1)}, pred[1024]{0:T(1024)(128)(4,1)S(1)}, u32[]{:S(2)}) copy-start(pred[1024]{0:T(1024)(128)(4,1)S(1)} %fusion.62) | copy-start | bytes 3076
  22.5 2.1 %copy-start.1 = (bf16[4,9,32,1024]{3,2,1,0:T(8,128)(2,1)}, bf16[4,9,32,1024]{3,2,1,0:T(8,128)(2,1)S(1)}, u32[]{:S(2)}) copy-start(bf16[4,9,32,1024]{3,2,1,0:T(8,128)(2,1)S(1)} %copy.42) | copy-start | bytes 7077892
  22.8 2.1 %copy-start.3 = (bf16[4,9,32,1024]{3,2,1,0:T(8,128)(2,1)}, bf16[4,9,32,1024]{3,2,1,0:T(8,128)(2,1)S(1)}, u32[]{:S(2)}) copy-start(bf16[4,9,32,1024]{3,2,1,0:T(8,128)(2,1)S(1)} %copy.40) | copy-start | bytes 7077892
  40.0 3.2 %copy-start.10 = (bf16[32,4,1024]{2,1,0:T(4,128)(2,1)S(1)}, bf16[32,4,1024]{2,1,0:T(4,128)(2,1)}, u32[]{:S(2)}) copy-start(bf16[32,4,1024]{2,1,0:T(4,128)(2,1)} %param.6) | copy-start | bytes 786436
  43.1 4.5 %collective-permute-start.4 = (f32[2,2,32,4096]{3,2,1,0:T(8,128)}, f32[2,2,32,4096]{3,2,1,0:T(8,128)}, u32[]{:S(2)}, u32[]{:S(2)}) collective-permute-start(f32[2,2,32,4096]{3,2,1,0:T(8,128)} %dynamic-slice_bitcast_fusion), channel_id=1, source_target_pairs={{0,1},{1,0},{2,3},{3,2},{4,5},{5,4},{6,7},{7,6},{8,9},{9,8},{10,11... | collective-permute-start | bytes 6291464 | tf_op jit(solution)/shard_map/ppermute | solution.py:108
  44.0 10.7 %copy-start.7 = (bf16[32,4,1024]{2,1,0:T(4,128)(2,1)S(1)}, bf16[32,4,1024]{2,1,0:T(4,128)(2,1)}, u32[]{:S(2)}) copy-start(bf16[32,4,1024]{2,1,0:T(4,128)(2,1)} %param.9) | copy-start | bytes 786436
  44.0 11.5 %copy-start.6 = (bf16[27,256,32]{1,2,0:T(8,128)(2,1)S(1)}, bf16[27,256,32]{1,2,0:T(8,128)(2,1)}, u32[]{:S(2)}) copy-start(bf16[27,256,32]{1,2,0:T(8,128)(2,1)} %param.7) | copy-start | bytes 1327108
  50.1 1.4 copy-start.5
  52.6 42.4 %collective-permute-start.5 = (f32[2,32,4096]{2,1,0:T(8,128)}, f32[2,32,4096]{2,1,0:T(8,128)}, u32[]{:S(2)}, u32[]{:S(2)}) collective-permute-start(f32[2,32,4096]{2,1,0:T(8,128)} %dynamic-slice_bitcast_fusion.1), channel_id=1, source_target_pairs={{0,2},{1,3},{2,0},{3,1},{4,6},{5,7},{6,4},{7,5},{8,10},{9,11},{10,... | collective-permute-start | bytes 3145736 | tf_op jit(solution)/shard_map/ppermute | solution.py:108
  97.4 34.6 %collective-permute-start.6 = (f32[32,4096]{1,0:T(8,128)}, f32[32,4096]{1,0:T(8,128)}, u32[]{:S(2)}, u32[]{:S(2)}) collective-permute-start(f32[32,4096]{1,0:T(8,128)} %dynamic-slice_bitcast_fusion.2), channel_id=1, source_target_pairs={{0,4},{1,5},{2,6},{3,7},{4,0},{5,1},{6,2},{7,3},{8,12},{9,13},{10,... | collective-permute-start | bytes 1572872 | tf_op jit(solution)/shard_map/ppermute | solution.py:108
  100.0 2.6 %copy-start = (bf16[4,256,1024]{2,1,0:T(8,128)(2,1)S(1)}, bf16[4,256,1024]{2,1,0:T(8,128)(2,1)}, u32[]{:S(2)}) copy-start(bf16[4,256,1024]{2,1,0:T(8,128)(2,1)} %all-gather.2.cloned.1.call-done) | copy-start | bytes 6291460
  100.0 2.9 %copy-start.2 = (bf16[4,9,32,1024]{3,2,1,0:T(8,128)(2,1)S(1)}, bf16[4,9,32,1024]{3,2,1,0:T(8,128)(2,1)}, u32[]{:S(2)}) copy-start(bf16[4,9,32,1024]{3,2,1,0:T(8,128)(2,1)} %copy-done.1) | copy-start | bytes 7077892
  102.5 1.8 %copy-start.4 = (bf16[4,9,32,1024]{3,2,1,0:T(8,128)(2,1)S(1)}, bf16[4,9,32,1024]{3,2,1,0:T(8,128)(2,1)}, u32[]{:S(2)}) copy-start(bf16[4,9,32,1024]{3,2,1,0:T(8,128)(2,1)} %copy-done.3) | copy-start | bytes 7077892
  104.3 0.9 copy-start.17
  105.1 1.8 %copy-start.9 = (bf16[1,9,32,256]{3,2,1,0:T(8,128)(2,1)S(1)}, bf16[1,9,32,256]{3,2,1,0:T(8,128)(2,1)}, u32[]{:S(2)}) copy-start(bf16[1,9,32,256]{3,2,1,0:T(8,128)(2,1)} %get-tuple-element.39) | copy-start | bytes 442372
  105.3 2.3 %copy-start.8 = (bf16[1,9,32,256]{3,2,1,0:T(8,128)(2,1)S(1)}, bf16[1,9,32,256]{3,2,1,0:T(8,128)(2,1)}, u32[]{:S(2)}) copy-start(bf16[1,9,32,256]{3,2,1,0:T(8,128)(2,1)} %get-tuple-element.40) | copy-start | bytes 442372
  105.3 12.2 %collective-permute-start.7 = (f32[448,256]{1,0:T(8,128)S(1)}, f32[448,256]{1,0:T(8,128)S(1)}, u32[]{:S(2)}, u32[]{:S(2)}) collective-permute-start(f32[448,256]{1,0:T(8,128)S(1)} %constant_dynamic-slice_fusion.1), channel_id=1, source_target_pairs={{0,8},{8,0},{16,24},{24,16},{1,9},{9,1},{17,25},{25,17},{2,10},{10... | collective-permute-start | bytes 1376264 | tf_op jit(solution)/shard_map/ppermute | solution.py:66
  111.5 7.5 %copy-start.12 = (pred[1024]{0:T(1024)(128)(4,1)S(1)}, pred[1024]{0:T(1024)(128)(4,1)}, u32[]{:S(2)}) copy-start(pred[1024]{0:T(1024)(128)(4,1)} %copy-done.11) | copy-start | bytes 3076
  111.5 7.5 %copy-start.14 = (pred[1024]{0:T(1024)(128)(4,1)S(1)}, pred[1024]{0:T(1024)(128)(4,1)}, u32[]{:S(2)}) copy-start(pred[1024]{0:T(1024)(128)(4,1)} %copy-done.13) | copy-start | bytes 3076
  111.5 7.5 %copy-start.16 = (pred[1024]{0:T(1024)(128)(4,1)S(1)}, pred[1024]{0:T(1024)(128)(4,1)}, u32[]{:S(2)}) copy-start(pred[1024]{0:T(1024)(128)(4,1)} %copy-done.15) | copy-start | bytes 3076
  117.6 6.5 %collective-permute-start.8 = (f32[224,256]{1,0:T(8,128)S(1)}, f32[224,256]{1,0:T(8,128)S(1)}, u32[]{:S(2)}, u32[]{:S(2)}) collective-permute-start(f32[224,256]{1,0:T(8,128)S(1)} %constant_dynamic-slice_fusion), channel_id=1, source_target_pairs={{0,16},{8,24},{16,0},{24,8},{1,17},{9,25},{17,1},{25,9},{2,18},{10... | collective-permute-start | bytes 688136 | tf_op jit(solution)/shard_map/ppermute | solution.py:66
  120.8 16.1 %copy-start.18 = (f32[32]{0:T(128)S(1)}, f32[32]{0:T(128)}, u32[]{:S(2)}) copy-start(f32[32]{0:T(128)} %param.8) | copy-start | bytes 388
  120.8 16.1 %copy-start.19 = (f32[4]{0:T(128)S(1)}, f32[4]{0:T(128)}, u32[]{:S(2)}) copy-start(f32[4]{0:T(128)} %pad.79.clone) | copy-start | bytes 52
  124.2 6.4 %collective-permute-start.9 = (f32[224,256]{1,0:T(8,128)S(1)}, f32[224,256]{1,0:T(8,128)S(1)}, u32[]{:S(2)}, u32[]{:S(2)}) collective-permute-start(f32[224,256]{1,0:T(8,128)S(1)} %get-tuple-element.21), channel_id=1, source_target_pairs={{0,16},{8,24},{16,0},{24,8},{1,17},{9,25},{17,1},{25,9},{2,18},{10... | collective-permute-start | bytes 688136 | tf_op jit(solution)/shard_map/ppermute | solution.py:71
  125.6 8.5 %collective-permute-start = (f32[1,32,1024]{2,1,0:T(8,128)S(1)}, f32[1,32,1024]{2,1,0:T(8,128)S(1)}, u32[]{:S(2)}, u32[]{:S(2)}) collective-permute-start(f32[1,32,1024]{2,1,0:T(8,128)S(1)} %get-tuple-element.33), channel_id=1, source_target_pairs={{0,8},{8,16},{16,24},{1,9},{9,17},{17,25},{2,10},{10,18},{18,26},{... | collective-permute-start | bytes 393224 | tf_op jit(solution)/shard_map/ppermute | solution.py:144
  128.0 8.9 %collective-permute-start.1 = (f32[1,32,1024]{2,1,0:T(8,128)S(1)}, f32[1,32,1024]{2,1,0:T(8,128)S(1)}, u32[]{:S(2)}, u32[]{:S(2)}) collective-permute-start(f32[1,32,1024]{2,1,0:T(8,128)S(1)} %get-tuple-element.34), channel_id=1, source_target_pairs={{8,0},{16,8},{24,16},{9,1},{17,9},{25,17},{10,2},{18,10},{26,18},{... | collective-permute-start | bytes 393224 | tf_op jit(solution)/shard_map/ppermute | solution.py:145
  130.6 13.5 %collective-permute-start.10 = (f32[448,256]{1,0:T(8,128)S(1)}, f32[448,256]{1,0:T(8,128)S(1)}, u32[]{:S(2)}, u32[]{:S(2)}) collective-permute-start(f32[448,256]{1,0:T(8,128)S(1)} %constant_dynamic-update-slice_fusion.2), channel_id=1, source_target_pairs={{0,8},{8,0},{16,24},{24,16},{1,9},{9,1},{17,25},{25,17},{2,10},{10... | collective-permute-start | bytes 1376264 | tf_op jit(solution)/shard_map/ppermute | solution.py:71
Sparse Core Ops, SparseCore 0:
  44.1 42.0 all-gather.1

commit v3 on v1

--- a/solution.py
+++ b/solution.py
@@ -3,7 +3,7 @@
 import jax
 import jax.numpy as jnp
 from jax import lax
-from jax.sharding import PartitionSpec as P
+from jax.sharding import Mesh, PartitionSpec as P
 
 W = 64
 
@@ -93,6 +93,31 @@
 plane_offsets = tuple((row_step, column_step) for row_step in (-1, 0, 1) for column_step in (-1, 0, 1))
 
 
+def other_core(value):
+    return lax.ppermute(value, "core", [(0, 1), (1, 0)])
+
+
+def gather_channels(planes):
+    chip_blocks = lax.all_gather(planes, "chips", axis=1, tiled=False)
+    partner = other_core(chip_blocks)
+    first = lax.axis_index("core") == 0
+    low = jnp.where(first, chip_blocks, partner)
+    high = jnp.where(first, partner, chip_blocks)
+    both = jnp.stack([low, high], axis=2)
+    return both.reshape(planes.shape[0], -1, planes.shape[2])
+
+
+def scatter_channels(blocks):
+    by_core = blocks.reshape(-1, 2, blocks.shape[1], blocks.shape[2])
+    core = lax.axis_index("core")
+    keep = lax.dynamic_index_in_dim(by_core, core, axis=1, keepdims=False)
+    send = lax.dynamic_index_in_dim(by_core, 1 - core, axis=1, keepdims=False)
+    partial = keep + other_core(send)
+    return lax.psum_scatter(
+        partial.reshape(-1, blocks.shape[2]), "chips", scatter_dimension=0, tiled=True
+    )
+
+
 def body(inputs, weight, bias_term, output_grad):
     taps_total = weight.shape[0]
     channels_in = weight.shape[1]
@@ -103,7 +128,7 @@
     grad_scale = 1.0 / math.sqrt(lax.axis_size("space") * depth_cells * plane_cells)
     inputs_planes = jnp.transpose(inputs, (1, 0, 2))
     grad_planes = jnp.transpose(output_grad, (1, 0, 2))
-    gathered = lax.all_gather(inputs_planes, "chan", axis=1, tiled=True)
+    gathered = gather_channels(inputs_planes)
 
     weight_grid = weight.reshape(3, 9, channels_in, block_out)
     forward_weight = jnp.transpose(weight_grid, (0, 1, 3, 2)).reshape(3, 9 * block_out, channels_in)
@@ -163,7 +188,7 @@
     )
     bias_grad = reduced[taps_total * block_out, :block_out]
 
-    chan_devices = lax.axis_size("chan")
+    chan_devices = lax.axis_size("chips") * lax.axis_size("core")
     backward_weight = jnp.transpose(weight_grid, (0, 2, 1, 3)).reshape(
         3, chan_devices, channels_in // chan_devices, 9 * block_out
     )
@@ -176,24 +201,25 @@
             preferred_element_type=jnp.float32,
         )
         spread = part if spread is None else spread + part
-    summed = lax.psum_scatter(
-        spread.reshape(channels_in, depth_cells * plane_cells), "chan", scatter_dimension=0, tiled=True
-    )
+    summed = scatter_channels(spread.reshape(chan_devices, channels_in // chan_devices, depth_cells * plane_cells))
     input_grad = summed.astype(jnp.bfloat16).reshape(block_in, depth_cells, plane_cells)
     return (outputs, input_grad, weight_grad, bias_grad)
 
 
 def solution(mesh):
-    placed = (P("chan", "space", None), P(None, None, "chan"), P("chan"), P("chan", "space", None))
+    space_devices, chan_devices = mesh.shape["space"], mesh.shape["chan"]
+    split = Mesh(mesh.devices.reshape(space_devices, chan_devices // 2, 2), ("space", "chips", "core"))
+    chan = ("chips", "core")
+    placed = (P(chan, "space", None), P(None, None, chan), P(chan), P(chan, "space", None))
     return jax.shard_map(
         body,
-        mesh=mesh,
+        mesh=split,
         in_specs=placed,
         out_specs=(
-            P("chan", "space", None),
-            P("chan", "space", None),
-            P(None, None, "chan"),
-            P("chan"),
+            P(chan, "space", None),
+            P(chan, "space", None),
+            P(None, None, chan),
+            P(chan),
         ),
         check_vma=False,
     )

time: 109 us -> 138 us (1.27)
  waiting for transfers between devices: 34.2 us -> 53.2 us
  local copies, waits for them, and re-layouts: 23.2 us -> 29.5 us
  other arithmetic: 7.47 us -> 13.7 us
  matrix products: 12.4 us -> 10.6 us
    all_gather x1, waiting for transfers between devices: 8.86 us -> 28.6 us  [gather_channels(): chip_blocks = lax.all_gather(planes, 'chips', axis=1, tiled=False)]
    unnamed x20 -> x36, local copies, waits for them, and re-layouts: 11.6 us -> 3.3 us
    another operation x0 -> x1, local copies, waits for them, and re-layouts: none -> 6.05 us  [scatter_channels(): by_core = blocks.reshape(-1, 2, blocks.shape[1], blocks.shape[2])]
    add x0 -> x1, other arithmetic: none -> 3.96 us  [scatter_channels(): partial = keep + other_core(send)]
    reduce_scatter x1, waiting for transfers between devices: 3.95 us -> 0.01 us  [scatter_channels(): lax.psum_scatter(partial.reshape(-1, blocks.shape[2]), 'chips', scatter_d...]
    squeeze x0 -> x1, local copies, waits for them, and re-layouts: none -> 3.25 us  [scatter_channels(): send = lax.dynamic_index_in_dim(by_core, 1 - core, axis=1, keepdims=False)]
    all_gather x0 -> x1, local copies, waits for them, and re-layouts: none -> 2.52 us  [gather_channels(): chip_blocks = lax.all_gather(planes, 'chips', axis=1, tiled=False)]
    another operation x0 -> x2, other arithmetic: none -> 2.04 us  [gather_channels(): both = jnp.stack([low, high], axis=2)]
  transfers between devices with their start and end apart: 10 -> 12, of which waited for: 7 -> 7; matrix products, arithmetic and copies ran while one was open for 35% -> 19% of each run, Pallas kernels for 0% -> 0%
where the time goes in v3:
time: 138 us
  waiting for transfers between devices  53.2 us (39%)
  local copies, waits for them, and re-layouts  29.5 us (21%)
  starting transfers between devices  16 us (12%)
  between operations  14.6 us (11%)
  other arithmetic  13.7 us (10%)
  matrix products  10.6 us (8%)
    all_gather x1, waiting for transfers between devices, gather_channels(): chip_blocks = lax.all_gather(planes, 'chips', axis=1, tiled=False)  28.6 us
    ppermute x2, waiting for transfers between devices, all_reduce_rows(): current = keep + lax.ppermute(send, axis, pairs)  9.8 us
    ppermute x2, waiting for transfers between devices, all_reduce_rows(): other = lax.ppermute(current, axis, pairs)  8.85 us
    another operation x1, local copies, waits for them, and re-layouts, scatter_channels(): by_core = blocks.reshape(-1, 2, blocks.shape[1], blocks.shape[2])  6.05 us
    dot_general x3, matrix products, body(): jnp.einsum('bjk,zkn->bjzn', backward_weight[depth_index], grad_shifted[2...  5.86 us
    add x1, local copies, waits for them, and re-layouts, body(): spread = part if spread is None else spread + part  4.93 us
    ppermute x1, starting transfers between devices, padded_2(): before = lax.ppermute(last, axis, up)  4.85 us
    ppermute x1, waiting for transfers between devices, body(): from_above = lax.ppermute(forward[:1], 'space', down)  4.2 us
  transfers between devices with their start and end apart: 12, of which 7 were waited for; matrix products, arithmetic and copies ran while one was open for 19% of the time, Pallas kernels for 0%

profile of v3, /device:TPU:0, one launch (start us, length us, event | category | flops | bytes accessed | tf_op | source)
XLA Modules:
  0.0 137.7 jit_solution(7129855398322682480)
XLA Ops:
  7.2 1.0 copy.94
  8.3 4.8 %collective-permute-start.3 = (bf16[1,32,1024]{2,1,0:T(8,128)(2,1)S(1)}, bf16[1,32,1024]{2,1,0:T(8,128)(2,1)S(1)}, u32[]{:S(2)}, u32[]{:S(2)}) collective-permute-start(bf16[1,32,1024]{2,1,0:T(8,128)(2,1)S(1)} %get-tuple-element.49), channel_id=1, source_target_pairs={{0,8},{8,16},{16,24},{1,9},{9,17},{17,25},{2,10},{10,18},{18,26},{... | collective-permute-start | bytes 196616 | tf_op jit(solution)/shard_map/ppermute | solution.py:28
  13.1 1.3 collective-permute-start.4
  14.5 1.1 fusion.65
  15.8 0.4 copy.73
  16.5 0.4 copy.71
  17.1 0.4 copy.75
  17.5 1.8 %collective-permute-done.4 = bf16[1,32,1024]{2,1,0:T(8,128)(2,1)S(1)} collective-permute-done((bf16[1,32,1024]{2,1,0:T(8,128)(2,1)S(1)}, bf16[1,32,1024]{2,1,0:T(8,128)(2,1)S(1)}, u32[]{:S(2)}, u32[]{:S(2)}) %collective-permute-start.4) | collective-permute-done | bytes 65568 | tf_op jit(solution)/shard_map/ppermute | solution.py:29
  20.9 1.0 fusion.63
  22.1 0.3 copy.72
  22.8 1.8 %fusion.45 = f32[4,1024,8,32]{1,3,2,0:T(8,128)S(1)} fusion(bf16[4,288,1024,1]{2,1,3,0:T(8,128)(2,1)S(1)} %bitcast.200, bf16[8,32,288]{2,1,0:T(8,128)(2,1)S(1)} %copy.73), kind=kOutput, calls=%fused_computation.95 | convolution fusion | flops 603979776 | bytes 6701056 | tf_op jit(solution)/shard_map/bjk,zkn->bjzn/dot_general | solution.py:197
  24.9 1.8 %fusion.47 = f32[4,1024,8,32]{1,3,2,0:T(8,128)S(1)} fusion(bf16[4,288,1024,1]{2,1,3,0:T(8,128)(2,1)S(1)} %bitcast.202, bf16[8,32,288]{2,1,0:T(8,128)(2,1)S(1)} %copy.71), kind=kOutput, calls=%fused_computation.97 | convolution fusion | flops 603979776 | bytes 6701056 | tf_op jit(solution)/shard_map/bjk,zkn->bjzn/dot_general | solution.py:197
  26.7 2.3 %add_bitcast_fusion = f32[8,32,4,1024]{3,1,0,2:T(8,128)S(1)} fusion(f32[4,1024,8,32]{1,3,2,0:T(8,128)S(1)} %fusion.47, f32[4,1024,8,32]{1,3,2,0:T(8,128)S(1)} %fusion.45, bf16[4,288,1024,1]{2,1,3,0:T(8,128)(2,1)S(1)} %bitcast.198, bf16[8,32,288]{2,1,0:T(8,128)(2,1)S(1)} %copy.75), kind=kOutput, calls=%fused_computation.1 | convolution fusion | flops 606076928 | bytes 15089664 | tf_op jit(solution)/shard_map/bjk,zkn->bjzn/dot_general | solution.py:197
  29.0 4.9 %copy.76 = f32[8,32,4,1024]{3,2,1,0:T(4,128)} copy(f32[8,32,4,1024]{3,1,0,2:T(8,128)S(1)} %add_bitcast_fusion) | data formatting | bytes 8388608 | tf_op jit(solution)/shard_map/add | solution.py:203
  33.9 6.0 %reshape_reshape.3 = f32[4,2,32,4096]{3,2,1,0:T(8,128)} reshape(f32[8,32,4,1024]{3,2,1,0:T(4,128)} %copy.76) | data formatting | bytes 8388608 | tf_op jit(solution)/shard_map/reshape;reshape | solution.py:111
  40.0 3.2 %dynamic-slice_bitcast_fusion = f32[4,32,4096]{2,1,0:T(8,128)} fusion(f32[4,2,32,4096]{3,2,1,0:T(8,128)} %reshape_reshape.3, s32[]{:T(128)S(6)} %select_n.196), kind=kLoop, calls=%fused_computation.7 | loop fusion | bytes 4194308 | tf_op jit(solution)/shard_map/jit(dynamic_index_in_dim)/squeeze | solution.py:114
  43.3 0.7 fusion.66
  44.1 28.6 %all-gather.3.cloned.1.call-done = bf16[4,128,1024]{2,0,1:T(4,128)(2,1)} async-done(((bf16[4,32,1024]{2,0,1:T(4,128)(2,1)}), bf16[4,128,1024]{2,0,1:T(4,128)(2,1)}) %all-gather.3.cloned.1.call-update) | async-done | bytes 1048592 | tf_op jit(solution)/shard_map/all_gather | solution.py:101
  72.6 2.5 %copy.55 = bf16[4,4,32,1024]{3,2,1,0:T(8,128)(2,1)} copy(bf16[4,4,32,1024]{3,0,2,1:T(4,128)(2,1)} %bitcast.205) | data formatting | bytes 2097152 | tf_op jit(solution)/shard_map/all_gather | solution.py:101
  75.2 0.8 convert_reduce_fusion
  76.0 4.0 %bitcast_add_fusion = f32[4,32,4096]{2,1,0:T(8,128)} fusion(f32[4,32,4096]{2,1,0:T(8,128)} %collective-permute-done.5, f32[4,2,32,4096]{3,2,1,0:T(8,128)} %reshape_reshape.3, s32[]{:T(128)S(6)} %select_n.195), kind=kLoop, calls=%fused_computation.6 | loop fusion | flops 524288 | bytes 6291460 | tf_op jit(solution)/shard_map/add | solution.py:115
  80.0 1.8 %select_bitcast_fusion.1 = (bf16[4,4,1,32,1024]{4,3,2,1,0:T(8,128)(2,1)S(1)}, bf16[4,4,1,32,1024]{4,3,2,1,0:T(8,128)(2,1)S(1)}) fusion(bf16[4,4,32,1024]{3,2,1,0:T(8,128)(2,1)} %collective-permute-done, pred[]{:T(512)S(6)} %eq.22, bf16[4,4,32,1024]{3,0,2,1:T(4,128)(2,1)S(1)} %bitcast.206), kind=kLoop, calls=%fused_computation.14 | loop fusion | flops 1048576 | bytes 4194305 | tf_op jit(solution)/shard_map/stack | solution.py:106
  82.1 0.8 convolution_bitcast_fusion.3
  82.9 0.8 copy-done.1
  83.7 0.8 convolution_bitcast_fusion.4
  84.7 0.8 convolution_bitcast_fusion.5
  85.8 1.5 %collective-permute-start.6 = (f32[448,256]{1,0:T(8,128)S(1)}, f32[448,256]{1,0:T(8,128)S(1)}, u32[]{:S(2)}, u32[]{:S(2)}) collective-permute-start(f32[448,256]{1,0:T(8,128)S(1)} %constant_dynamic-slice_fusion.1), channel_id=1, source_target_pairs={{0,8},{8,0},{16,24},{24,16},{1,9},{9,1},{17,25},{25,17},{2,10},{10... | collective-permute-start | bytes 1376264 | tf_op jit(solution)/shard_map/ppermute | solution.py:66
  87.3 0.8 convolution_bitcast_fusion.1
  88.1 0.8 convolution_bitcast_fusion.2
  88.9 0.8 convolution_bitcast_fusion
  89.7 2.3 %pad_add_fusion = f32[6,288,1024]{2,1,0:T(8,128)S(1)} fusion(f32[4,288,1024]{2,1,0:T(8,128)S(1)} %convolution_bitcast_fusion, f32[4,288,1024]{2,1,0:T(8,128)S(1)} %convolution_bitcast_fusion.1, f32[4,288,1024]{2,1,0:T(8,128)S(1)} %convolution_bitcast_fusion.2), kind=kLoop, calls=%fused_computation | loop fusion | flops 3538944 | bytes 21233664 | tf_op jit(solution)/shard_map/add | solution.py:144
  92.0 1.1 slice_bitcast_fusion
  93.1 5.6 %collective-permute-done.6 = f32[448,256]{1,0:T(8,128)S(1)} collective-permute-done((f32[448,256]{1,0:T(8,128)S(1)}, f32[448,256]{1,0:T(8,128)S(1)}, u32[]{:S(2)}, u32[]{:S(2)}) %collective-permute-start.6) | collective-permute-done | bytes 458784 | tf_op jit(solution)/shard_map/ppermute | solution.py:66
  98.9 1.5 %collective-permute-start.7 = (f32[224,256]{1,0:T(8,128)S(1)}, f32[224,256]{1,0:T(8,128)S(1)}, u32[]{:S(2)}, u32[]{:S(2)}) collective-permute-start(f32[224,256]{1,0:T(8,128)S(1)} %constant_dynamic-slice_fusion), channel_id=1, source_target_pairs={{0,16},{8,24},{16,0},{24,8},{1,17},{9,25},{17,1},{25,9},{2,18},{10... | collective-permute-start | bytes 688136 | tf_op jit(solution)/shard_map/ppermute | solution.py:66
  100.4 1.7 %fusion.10 = f32[6,32,1024]{2,1,0:T(8,128)S(1)} fusion(f32[6,32,1024]{2,1,0:T(8,128)S(1)} %get-tuple-element.33, f32[6,32,1024]{2,1,0:T(8,128)S(1)} %get-tuple-element.32, f32[6,32,1024]{2,1,0:T(8,128)S(1)} %get-tuple-element.31, f32[6,32,1024]{2,1,0:T(8,128)S(1)} %get-tuple-element.30, f32[6,32,1024]{2,1,0:T(8,128)S(1)} %get-tuple-element.29, ...), kind=kLoop, calls=%fused_computation.36 | loop fusion | flops 3342336 | bytes 7867392 | tf_op jit(solution)/shard_map/add | solution.py:149
  102.1 4.2 %collective-permute-done.7 = f32[224,256]{1,0:T(8,128)S(1)} collective-permute-done((f32[224,256]{1,0:T(8,128)S(1)}, f32[224,256]{1,0:T(8,128)S(1)}, u32[]{:S(2)}, u32[]{:S(2)}) %collective-permute-start.7) | collective-permute-done | bytes 229408 | tf_op jit(solution)/shard_map/ppermute | solution.py:66
  106.4 1.5 %collective-permute-start.8 = (f32[224,256]{1,0:T(8,128)S(1)}, f32[224,256]{1,0:T(8,128)S(1)}, u32[]{:S(2)}, u32[]{:S(2)}) collective-permute-start(f32[224,256]{1,0:T(8,128)S(1)} %get-tuple-element.25), channel_id=1, source_target_pairs={{0,16},{8,24},{16,0},{24,8},{1,17},{9,25},{17,1},{25,9},{2,18},{10... | collective-permute-start | bytes 688136 | tf_op jit(solution)/shard_map/ppermute | solution.py:71
  107.9 3.4 %collective-permute-start.1 = (f32[1,32,1024]{2,1,0:T(8,128)S(1)}, f32[1,32,1024]{2,1,0:T(8,128)S(1)}, u32[]{:S(2)}, u32[]{:S(2)}) collective-permute-start(f32[1,32,1024]{2,1,0:T(8,128)S(1)} %get-tuple-element.39), channel_id=1, source_target_pairs={{0,8},{8,16},{16,24},{1,9},{9,17},{17,25},{2,10},{10,18},{18,26},{... | collective-permute-start | bytes 393224 | tf_op jit(solution)/shard_map/ppermute | solution.py:153
  111.3 1.3 collective-permute-start.2
  112.6 2.2 %collective-permute-done.8 = f32[224,256]{1,0:T(8,128)S(1)} collective-permute-done((f32[224,256]{1,0:T(8,128)S(1)}, f32[224,256]{1,0:T(8,128)S(1)}, u32[]{:S(2)}, u32[]{:S(2)}) %collective-permute-start.8) | collective-permute-done | bytes 229408 | tf_op jit(solution)/shard_map/ppermute | solution.py:71
  114.9 0.5 collective-permute-start.9
  115.4 4.2 %collective-permute-done.2 = f32[1,32,1024]{2,1,0:T(8,128)S(1)} collective-permute-done((f32[1,32,1024]{2,1,0:T(8,128)S(1)}, f32[1,32,1024]{2,1,0:T(8,128)S(1)}, u32[]{:S(2)}, u32[]{:S(2)}) %collective-permute-start.2) | collective-permute-done | bytes 131104 | tf_op jit(solution)/shard_map/ppermute | solution.py:154
  119.8 0.9 copy.77
  120.8 6.6 %collective-permute-done.9 = f32[448,256]{1,0:T(8,128)S(1)} collective-permute-done((f32[448,256]{1,0:T(8,128)S(1)}, f32[448,256]{1,0:T(8,128)S(1)}, u32[]{:S(2)}, u32[]{:S(2)}) %collective-permute-start.9) | collective-permute-done | bytes 458784 | tf_op jit(solution)/shard_map/ppermute | solution.py:71
  127.5 1.0 slice.234
  128.4 0.5 slice_bitcast_fusion.9
  128.9 1.1 convert_element_type.36
  130.0 0.9 reshape.124
  (78 shorter events, 4.4 us)
Async XLA Ops:
  7.2 65.5 %all-gather.3.cloned.1.call-start = ((), (), s32[]{:S(2)}) async-start(), calls=%async_computation.2 | async-start | bytes 1310720 | tf_op jit(solution)/shard_map/all_gather | solution.py:101
  8.3 9.3 %collective-permute-start.3 = (bf16[1,32,1024]{2,1,0:T(8,128)(2,1)S(1)}, bf16[1,32,1024]{2,1,0:T(8,128)(2,1)S(1)}, u32[]{:S(2)}, u32[]{:S(2)}) collective-permute-start(bf16[1,32,1024]{2,1,0:T(8,128)(2,1)S(1)} %get-tuple-element.49), channel_id=1, source_target_pairs={{0,8},{8,16},{16,24},{1,9},{9,17},{17,25},{2,10},{10,18},{18,26},{... | collective-permute-start | bytes 196616 | tf_op jit(solution)/shard_map/ppermute | solution.py:28
  13.1 6.2 %collective-permute-start.4 = (bf16[1,32,1024]{2,1,0:T(8,128)(2,1)S(1)}, bf16[1,32,1024]{2,1,0:T(8,128)(2,1)S(1)}, u32[]{:S(2)}, u32[]{:S(2)}) collective-permute-start(bf16[1,32,1024]{2,1,0:T(8,128)(2,1)S(1)} %get-tuple-element.50), channel_id=1, source_target_pairs={{8,0},{16,8},{24,16},{9,1},{17,9},{25,17},{10,2},{18,10},{26,18},{... | collective-permute-start | bytes 196616 | tf_op jit(solution)/shard_map/ppermute | solution.py:29
  14.4 6.0 %copy-start.9 = (pred[1024]{0:T(1024)(128)(4,1)}, pred[1024]{0:T(1024)(128)(4,1)S(1)}, u32[]{:S(2)}) copy-start(pred[1024]{0:T(1024)(128)(4,1)S(1)} %get-tuple-element.51) | copy-start | bytes 3076
  14.4 6.3 %copy-start.11 = (pred[1024]{0:T(1024)(128)(4,1)}, pred[1024]{0:T(1024)(128)(4,1)S(1)}, u32[]{:S(2)}) copy-start(pred[1024]{0:T(1024)(128)(4,1)S(1)} %get-tuple-element.52) | copy-start | bytes 3076
  17.5 3.3 %copy-start.13 = (pred[1024]{0:T(1024)(128)(4,1)}, pred[1024]{0:T(1024)(128)(4,1)S(1)}, u32[]{:S(2)}) copy-start(pred[1024]{0:T(1024)(128)(4,1)S(1)} %fusion.61) | copy-start | bytes 3076
  22.5 2.1 %copy-start = (bf16[4,9,32,1024]{3,2,1,0:T(8,128)(2,1)}, bf16[4,9,32,1024]{3,2,1,0:T(8,128)(2,1)S(1)}, u32[]{:S(2)}) copy-start(bf16[4,9,32,1024]{3,2,1,0:T(8,128)(2,1)S(1)} %copy.72) | copy-start | bytes 7077892
  22.8 2.1 %copy-start.2 = (bf16[4,9,32,1024]{3,2,1,0:T(8,128)(2,1)}, bf16[4,9,32,1024]{3,2,1,0:T(8,128)(2,1)S(1)}, u32[]{:S(2)}) copy-start(bf16[4,9,32,1024]{3,2,1,0:T(8,128)(2,1)S(1)} %copy.70) | copy-start | bytes 7077892
  40.0 3.3 %copy-start.5 = (bf16[27,256,32]{1,2,0:T(8,128)(2,1)S(1)}, bf16[27,256,32]{1,2,0:T(8,128)(2,1)}, u32[]{:S(2)}) copy-start(bf16[27,256,32]{1,2,0:T(8,128)(2,1)} %param.7) | copy-start | bytes 1327108
  40.0 35.2 %copy-start.6 = (bf16[32,4,1024]{2,1,0:T(4,128)(2,1)S(1)}, bf16[32,4,1024]{2,1,0:T(4,128)(2,1)}, u32[]{:S(2)}) copy-start(bf16[32,4,1024]{2,1,0:T(4,128)(2,1)} %param.9) | copy-start | bytes 786436
  43.2 32.8 %collective-permute-start.5 = (f32[4,32,4096]{2,1,0:T(8,128)}, f32[4,32,4096]{2,1,0:T(8,128)}, u32[]{:S(2)}, u32[]{:S(2)}) collective-permute-start(f32[4,32,4096]{2,1,0:T(8,128)} %dynamic-slice_bitcast_fusion), channel_id=1, source_target_pairs={{0,1},{1,0},{2,3},{3,2},{4,5},{5,4},{6,7},{7,6},{8,9},{9,8},{10,11... | collective-permute-start | bytes 6291464 | tf_op jit(solution)/shard_map/ppermute | solution.py:97
  43.3 85.7 %reduce-scatter.2.cloned.1.call-start = ((), (), s32[]{:S(2)}) async-start(), calls=%async_computation.1 | async-start | bytes 2621440 | tf_op jit(solution)/shard_map/reduce_scatter | solution.py:116
  75.2 4.8 %collective-permute-start = (bf16[4,4,32,1024]{3,2,1,0:T(8,128)(2,1)}, bf16[4,4,32,1024]{3,2,1,0:T(8,128)(2,1)}, u32[]{:S(2)}, u32[]{:S(2)}) collective-permute-start(bf16[4,4,32,1024]{3,2,1,0:T(8,128)(2,1)} %copy.55), channel_id=1, source_target_pairs={{0,1},{1,0},{2,3},{3,2},{4,5},{5,4},{6,7},{7,6},{8,9},{9,8},{10,11... | collective-permute-start | bytes 3145736 | tf_op jit(solution)/shard_map/ppermute | solution.py:97
  76.0 4.0 %copy-start.4 = (bf16[4,128,1024]{2,0,1:T(4,128)(2,1)S(1)}, bf16[4,128,1024]{2,0,1:T(4,128)(2,1)}, u32[]{:S(2)}) copy-start(bf16[4,128,1024]{2,0,1:T(4,128)(2,1)} %all-gather.3.cloned.1.call-done) | copy-start | bytes 3145732
  82.1 1.7 %copy-start.1 = (bf16[4,9,32,1024]{3,2,1,0:T(8,128)(2,1)S(1)}, bf16[4,9,32,1024]{3,2,1,0:T(8,128)(2,1)}, u32[]{:S(2)}) copy-start(bf16[4,9,32,1024]{3,2,1,0:T(8,128)(2,1)} %copy-done) | copy-start | bytes 7077892
  82.9 1.8 %copy-start.3 = (bf16[4,9,32,1024]{3,2,1,0:T(8,128)(2,1)S(1)}, bf16[4,9,32,1024]{3,2,1,0:T(8,128)(2,1)}, u32[]{:S(2)}) copy-start(bf16[4,9,32,1024]{3,2,1,0:T(8,128)(2,1)} %copy-done.2) | copy-start | bytes 7077892
  84.7 0.9 copy-start.15
  85.6 1.8 %copy-start.8 = (bf16[1,9,32,256]{3,2,1,0:T(8,128)(2,1)S(1)}, bf16[1,9,32,256]{3,2,1,0:T(8,128)(2,1)}, u32[]{:S(2)}) copy-start(bf16[1,9,32,256]{3,2,1,0:T(8,128)(2,1)} %get-tuple-element.46) | copy-start | bytes 442372
  85.8 2.3 %copy-start.7 = (bf16[1,9,32,256]{3,2,1,0:T(8,128)(2,1)S(1)}, bf16[1,9,32,256]{3,2,1,0:T(8,128)(2,1)}, u32[]{:S(2)}) copy-start(bf16[1,9,32,256]{3,2,1,0:T(8,128)(2,1)} %get-tuple-element.44) | copy-start | bytes 442372
  85.8 13.0 %collective-permute-start.6 = (f32[448,256]{1,0:T(8,128)S(1)}, f32[448,256]{1,0:T(8,128)S(1)}, u32[]{:S(2)}, u32[]{:S(2)}) collective-permute-start(f32[448,256]{1,0:T(8,128)S(1)} %constant_dynamic-slice_fusion.1), channel_id=1, source_target_pairs={{0,8},{8,0},{16,24},{24,16},{1,9},{9,1},{17,25},{25,17},{2,10},{10... | collective-permute-start | bytes 1376264 | tf_op jit(solution)/shard_map/ppermute | solution.py:66
  92.0 8.4 %copy-start.10 = (pred[1024]{0:T(1024)(128)(4,1)S(1)}, pred[1024]{0:T(1024)(128)(4,1)}, u32[]{:S(2)}) copy-start(pred[1024]{0:T(1024)(128)(4,1)} %copy-done.9) | copy-start | bytes 3076
  92.0 8.4 %copy-start.12 = (pred[1024]{0:T(1024)(128)(4,1)S(1)}, pred[1024]{0:T(1024)(128)(4,1)}, u32[]{:S(2)}) copy-start(pred[1024]{0:T(1024)(128)(4,1)} %copy-done.11) | copy-start | bytes 3076
  92.0 8.4 %copy-start.14 = (pred[1024]{0:T(1024)(128)(4,1)S(1)}, pred[1024]{0:T(1024)(128)(4,1)}, u32[]{:S(2)}) copy-start(pred[1024]{0:T(1024)(128)(4,1)} %copy-done.13) | copy-start | bytes 3076
  98.9 7.4 %collective-permute-start.7 = (f32[224,256]{1,0:T(8,128)S(1)}, f32[224,256]{1,0:T(8,128)S(1)}, u32[]{:S(2)}, u32[]{:S(2)}) collective-permute-start(f32[224,256]{1,0:T(8,128)S(1)} %constant_dynamic-slice_fusion), channel_id=1, source_target_pairs={{0,16},{8,24},{16,0},{24,8},{1,17},{9,25},{17,1},{25,9},{2,18},{10... | collective-permute-start | bytes 688136 | tf_op jit(solution)/shard_map/ppermute | solution.py:66
  100.4 19.2 %copy-start.16 = (f32[32]{0:T(128)S(1)}, f32[32]{0:T(128)}, u32[]{:S(2)}) copy-start(f32[32]{0:T(128)} %param.8) | copy-start | bytes 388
  106.4 8.5 %collective-permute-start.8 = (f32[224,256]{1,0:T(8,128)S(1)}, f32[224,256]{1,0:T(8,128)S(1)}, u32[]{:S(2)}, u32[]{:S(2)}) collective-permute-start(f32[224,256]{1,0:T(8,128)S(1)} %get-tuple-element.25), channel_id=1, source_target_pairs={{0,16},{8,24},{16,0},{24,8},{1,17},{9,25},{17,1},{25,9},{2,18},{10... | collective-permute-start | bytes 688136 | tf_op jit(solution)/shard_map/ppermute | solution.py:71
  107.9 7.5 %collective-permute-start.1 = (f32[1,32,1024]{2,1,0:T(8,128)S(1)}, f32[1,32,1024]{2,1,0:T(8,128)S(1)}, u32[]{:S(2)}, u32[]{:S(2)}) collective-permute-start(f32[1,32,1024]{2,1,0:T(8,128)S(1)} %get-tuple-element.39), channel_id=1, source_target_pairs={{0,8},{8,16},{16,24},{1,9},{9,17},{17,25},{2,10},{10,18},{18,26},{... | collective-permute-start | bytes 393224 | tf_op jit(solution)/shard_map/ppermute | solution.py:153
  111.3 8.3 %collective-permute-start.2 = (f32[1,32,1024]{2,1,0:T(8,128)S(1)}, f32[1,32,1024]{2,1,0:T(8,128)S(1)}, u32[]{:S(2)}, u32[]{:S(2)}) collective-permute-start(f32[1,32,1024]{2,1,0:T(8,128)S(1)} %get-tuple-element.40), channel_id=1, source_target_pairs={{8,0},{16,8},{24,16},{9,1},{17,9},{25,17},{10,2},{18,10},{26,18},{... | collective-permute-start | bytes 393224 | tf_op jit(solution)/shard_map/ppermute | solution.py:154
  114.9 12.6 %collective-permute-start.9 = (f32[448,256]{1,0:T(8,128)S(1)}, f32[448,256]{1,0:T(8,128)S(1)}, u32[]{:S(2)}, u32[]{:S(2)}) collective-permute-start(f32[448,256]{1,0:T(8,128)S(1)} %constant_dynamic-update-slice_fusion.2), channel_id=1, source_target_pairs={{0,8},{8,0},{16,24},{24,16},{1,9},{9,1},{17,25},{25,17},{2,10},{10... | collective-permute-start | bytes 1376264 | tf_op jit(solution)/shard_map/ppermute | solution.py:71
Sparse Core Ops, SparseCore 0:
  43.4 29.2 all-gather.2
  80.1 43.5 reduce-scatter.1

commit v4 on v1

--- a/solution.py
+++ b/solution.py
@@ -91,6 +91,25 @@
 
 
 plane_offsets = tuple((row_step, column_step) for row_step in (-1, 0, 1) for column_step in (-1, 0, 1))
+
+
+def all_reduce_direct(block, axis):
+    devices = lax.axis_size(axis)
+    index = lax.axis_index(axis)
+    chunks = block.reshape((devices, block.shape[0] // devices) + block.shape[1:])
+    reduced = lax.dynamic_index_in_dim(chunks, index, 0, keepdims=False)
+    for distance in range(1, devices):
+        pairs = [(i, i ^ distance) for i in range(devices)]
+        send = lax.dynamic_index_in_dim(chunks, index ^ distance, 0, keepdims=False)
+        reduced = reduced + lax.ppermute(send, axis, pairs)
+    pieces = [reduced] + [
+        lax.ppermute(reduced, axis, [(i, i ^ distance) for i in range(devices)])
+        for distance in range(1, devices)
+    ]
+    stacked = jnp.stack(pieces)
+    return jnp.concatenate(
+        [lax.dynamic_index_in_dim(stacked, index ^ chunk, 0, keepdims=False) for chunk in range(devices)]
+    )
 
 
 def body(inputs, weight, bias_term, output_grad):
@@ -155,9 +174,8 @@
     total_rows = -(-(taps_total * block_out + 1) // unit) * unit
     bias_rows = jnp.zeros((total_rows - taps_total * block_out, channels_in), jnp.float32)
     bias_rows = bias_rows.at[0, :block_out].set(bias_part)
-    reduced = all_reduce_rows(
-        jnp.concatenate([weight_part, bias_rows]) * grad_scale, "space"
-    )
+    space_reduce = all_reduce_direct if space_devices <= 4 else all_reduce_rows
+    reduced = space_reduce(jnp.concatenate([weight_part, bias_rows]) * grad_scale, "space")
     weight_grad = jnp.transpose(
         reduced[: taps_total * block_out].reshape(taps_total, block_out, channels_in), (0, 2, 1)
     )

time: 109 us -> 109 us (level)
  starting transfers between devices: 16.7 us -> 19.5 us
  waiting for transfers between devices: 34.2 us -> 31.6 us
  local copies, waits for them, and re-layouts: 23.2 us -> 22 us
    ppermute x4 -> x6, waiting for transfers between devices: 17.1 us -> 7.78 us  [the longest x3 7.77 us: all_reduce_direct(): lax.ppermute(reduced, axis, [(i, i ^ distance) for i in range(devices)])]
    reduce_scatter x1, waiting for transfers between devices: 3.95 us -> 13 us  [body(): lax.psum_scatter(spread.reshape(channels_in, depth_cells * plane_cells),...]
    ppermute x4 -> x6, starting transfers between devices: 5.85 us -> 8.63 us  [the longest x3 5.08 us: all_reduce_direct(): lax.ppermute(reduced, axis, [(i, i ^ distance) for i in range(devices)])]
    ppermute x1, waiting for transfers between devices: 4.19 us -> 1.84 us  [body(): from_above = lax.ppermute(forward[:1], 'space', down)]
  transfers between devices with their start and end apart: 10 -> 12, of which waited for: 7 -> 5; matrix products, arithmetic and copies ran while one was open for 35% -> 35% of each run, Pallas kernels for 0% -> 0%
where the time goes in v4:
time: 109 us; the launch traced here: 108 us
  waiting for transfers between devices  31.6 us (29%)
  local copies, waits for them, and re-layouts  22 us (20%)
  starting transfers between devices  19.5 us (18%)
  between operations  14.5 us (13%)
  matrix products  12.4 us (11%)
  other arithmetic  8.46 us (8%)
    reduce_scatter x1, waiting for transfers between devices, body(): lax.psum_scatter(spread.reshape(channels_in, depth_cells * plane_cells),...  13 us
    unnamed x20, local copies, waits for them, and re-layouts  11.5 us
    all_gather x1, waiting for transfers between devices, body(): gathered = lax.all_gather(inputs_planes, 'chan', axis=1, tiled=True)  8.88 us
    ppermute x3, waiting for transfers between devices, all_reduce_direct(): lax.ppermute(reduced, axis, [(i, i ^ distance) for i in range(devices)])  7.77 us
    dot_general x3, matrix products, body(): jnp.einsum('bjk,zkn->bjzn', backward_weight[depth_index], grad_shifted[2...  5.85 us
    ppermute x3, starting transfers between devices, all_reduce_direct(): lax.ppermute(reduced, axis, [(i, i ^ distance) for i in range(devices)])  5.08 us
    ppermute x1, starting transfers between devices, padded_2(): before = lax.ppermute(last, axis, up)  4.85 us
    dot_general x3, matrix products, body(): jnp.einsum('zkn,zin->ki', grad_shifted[2 - depth_index:2 - depth_index +...  4.15 us
  transfers between devices with their start and end apart: 12, of which 5 were waited for; matrix products, arithmetic and copies ran while one was open for 35% of the time, Pallas kernels for 0%

profile of v4, /device:TPU:0, one launch (start us, length us, event | category | flops | bytes accessed | tf_op | source)
XLA Modules:
  0.0 108.5 jit_solution(10144933183446684154)
XLA Ops:
  7.2 1.0 copy.65
  8.3 4.8 %collective-permute-start.2 = (bf16[1,32,1024]{2,1,0:T(8,128)(2,1)S(1)}, bf16[1,32,1024]{2,1,0:T(8,128)(2,1)S(1)}, u32[]{:S(2)}, u32[]{:S(2)}) collective-permute-start(bf16[1,32,1024]{2,1,0:T(8,128)(2,1)S(1)} %get-tuple-element.48), channel_id=1, source_target_pairs={{0,8},{8,16},{16,24},{1,9},{9,17},{17,25},{2,10},{10,18},{18,26},{... | collective-permute-start | bytes 196616 | tf_op jit(solution)/shard_map/ppermute | solution.py:28
  13.1 1.3 %collective-permute-start.3 = (bf16[1,32,1024]{2,1,0:T(8,128)(2,1)S(1)}, bf16[1,32,1024]{2,1,0:T(8,128)(2,1)S(1)}, u32[]{:S(2)}, u32[]{:S(2)}) collective-permute-start(bf16[1,32,1024]{2,1,0:T(8,128)(2,1)S(1)} %get-tuple-element.49), channel_id=1, source_target_pairs={{8,0},{16,8},{24,16},{9,1},{17,9},{25,17},{10,2},{18,10},{26,18},{... | collective-permute-start | bytes 196616 | tf_op jit(solution)/shard_map/ppermute | solution.py:29
  14.4 1.7 %copy.64 = bf16[32,4,1024]{2,0,1:T(8,128)(2,1)} copy(bf16[32,4,1024]{2,1,0:T(4,128)(2,1)} %param.6) | data formatting | bytes 524288 | tf_op args[0]
  16.2 1.1 %fusion.67 = (bf16[1,256,9,32]{1,3,2,0:T(8,128)(2,1)S(1)}, bf16[1,256,9,32]{1,3,2,0:T(8,128)(2,1)S(1)}, bf16[1,256,9,32]{1,3,2,0:T(8,128)(2,1)S(1)}) fusion(bf16[3,256,9,32]{1,3,2,0:T(8,128)(2,1)} %bitcast.223), kind=kLoop, calls=%fused_computation.126 | loop fusion | bytes 884736 | tf_op jit(solution)/shard_map/slice | solution.py:192
  17.6 0.4 copy.43
  18.0 0.2 squeeze.85
  18.2 0.4 copy.41
  18.9 0.4 copy.45
  20.9 1.0 fusion.65
  22.1 0.3 copy.42
  22.5 0.3 copy.40
  22.8 1.8 %fusion.47 = f32[4,1024,8,32]{1,3,2,0:T(8,128)S(1)} fusion(bf16[4,288,1024,1]{2,1,3,0:T(8,128)(2,1)S(1)} %bitcast.213, bf16[8,32,288]{2,1,0:T(8,128)(2,1)S(1)} %copy.43), kind=kOutput, calls=%fused_computation.103 | convolution fusion | flops 603979776 | bytes 6701056 | tf_op jit(solution)/shard_map/bjk,zkn->bjzn/dot_general | solution.py:190
  24.9 1.8 %fusion.49 = f32[4,1024,8,32]{1,3,2,0:T(8,128)S(1)} fusion(bf16[4,288,1024,1]{2,1,3,0:T(8,128)(2,1)S(1)} %bitcast.215, bf16[8,32,288]{2,1,0:T(8,128)(2,1)S(1)} %copy.41), kind=kOutput, calls=%fused_computation.105 | convolution fusion | flops 603979776 | bytes 6701056 | tf_op jit(solution)/shard_map/bjk,zkn->bjzn/dot_general | solution.py:190
  26.6 2.3 %add_bitcast_fusion = f32[8,32,4,1024]{3,1,0,2:T(8,128)S(1)} fusion(f32[4,1024,8,32]{1,3,2,0:T(8,128)S(1)} %fusion.49, f32[4,1024,8,32]{1,3,2,0:T(8,128)S(1)} %fusion.47, bf16[4,288,1024,1]{2,1,3,0:T(8,128)(2,1)S(1)} %bitcast.209, bf16[8,32,288]{2,1,0:T(8,128)(2,1)S(1)} %copy.45), kind=kOutput, calls=%fused_computation.1 | convolution fusion | flops 606076928 | bytes 15089664 | tf_op jit(solution)/shard_map/bjk,zkn->bjzn/dot_general | solution.py:190
  29.0 2.9 %copy.46 = f32[8,32,4,1024]{3,2,1,0:T(4,128)S(1)} copy(f32[8,32,4,1024]{3,1,0,2:T(8,128)S(1)} %add_bitcast_fusion) | data formatting | bytes 8388608 | tf_op jit(solution)/shard_map/add | solution.py:196
  31.9 5.7 %copy.60 = f32[32,8,4,1024]{3,1,2,0:T(8,128)} copy(f32[32,8,4,1024]{3,2,1,0:T(4,128)S(1)} %bitcast.212) | data formatting | bytes 8388608
  37.8 0.8 copy-done.6
  38.6 0.3 convert_reduce_fusion
  39.0 8.9 %all-gather.2.cloned.1.call-done = bf16[4,256,1024]{2,1,0:T(8,128)(2,1)} async-done(((bf16[4,32,1024]{2,1,0:T(8,128)(2,1)}), bf16[4,256,1024]{2,1,0:T(8,128)(2,1)}) %all-gather.2.cloned.1.call-update) | async-done | bytes 2097168 | tf_op jit(solution)/shard_map/all_gather | solution.py:125
  47.8 2.5 %convolution_bitcast_fusion.3 = f32[1,288,256]{2,1,0:T(8,128)S(1)} fusion(bf16[4,288,1024]{2,1,0:T(8,128)(2,1)S(1)} %bitcast.210, bf16[4,256,1024]{2,1,0:T(8,128)(2,1)} %all-gather.2.cloned.1.call-done), kind=kOutput, calls=%fused_computation.7 | convolution fusion | flops 603979776 | bytes 4751360 | tf_op jit(solution)/shard_map/zkn,zin->ki/dot_general | solution.py:163
  50.4 0.3 copy-done.2
  50.8 0.8 convolution_bitcast_fusion.4
  51.6 0.6 copy-done.4
  52.2 0.8 convolution_bitcast_fusion.5
  53.2 1.5 %collective-permute-start.4 = (f32[224,256]{1,0:T(8,128)S(1)}, f32[224,256]{1,0:T(8,128)S(1)}, u32[]{:S(2)}, u32[]{:S(2)}) collective-permute-start(f32[224,256]{1,0:T(8,128)S(1)} %get-tuple-element.35), channel_id=1, source_target_pairs={{0,8},{8,0},{16,24},{24,16},{1,9},{9,1},{17,25},{25,17},{2,10},{10... | collective-permute-start | bytes 688136 | tf_op jit(solution)/shard_map/ppermute | solution.py:104
  54.7 1.5 %collective-permute-start.5 = (f32[224,256]{1,0:T(8,128)S(1)}, f32[224,256]{1,0:T(8,128)S(1)}, u32[]{:S(2)}, u32[]{:S(2)}) collective-permute-start(f32[224,256]{1,0:T(8,128)S(1)} %get-tuple-element.37), channel_id=1, source_target_pairs={{0,16},{8,24},{16,0},{24,8},{1,17},{9,25},{17,1},{25,9},{2,18},{10... | collective-permute-start | bytes 688136 | tf_op jit(solution)/shard_map/ppermute | solution.py:104
  56.2 0.5 collective-permute-start.6
  56.7 0.8 convolution_bitcast_fusion
  57.5 0.8 convolution_bitcast_fusion.1
  58.3 0.8 convolution_bitcast_fusion.2
  59.1 2.5 %pad_add_fusion = f32[6,288,1024]{2,1,0:T(8,128)S(1)} fusion(f32[4,288,1024]{2,1,0:T(8,128)S(1)} %convolution_bitcast_fusion, f32[4,288,1024]{2,1,0:T(8,128)S(1)} %convolution_bitcast_fusion.1, f32[4,288,1024]{2,1,0:T(8,128)S(1)} %convolution_bitcast_fusion.2), kind=kLoop, calls=%fused_computation | loop fusion | flops 3538944 | bytes 21233664 | tf_op jit(solution)/shard_map/add | solution.py:138
  61.6 1.1 %slice_bitcast_fusion = (f32[6,32,1024]{2,1,0:T(8,128)S(1)}, f32[6,32,1024]{2,1,0:T(8,128)S(1)}, f32[6,32,1024]{2,1,0:T(8,128)S(1)}, f32[6,32,1024]{2,1,0:T(8,12...) fusion(f32[6,9,32,1024]{3,2,1,0:T(8,128)S(1)} %bitcast.207), kind=kLoop, calls=%fused_computation.43 | loop fusion | bytes 12582912 | tf_op jit(solution)/shard_map/squeeze | solution.py:142
  62.8 1.7 %fusion.10 = f32[6,32,1024]{2,1,0:T(8,128)S(1)} fusion(f32[6,32,1024]{2,1,0:T(8,128)S(1)} %get-tuple-element.27, f32[6,32,1024]{2,1,0:T(8,128)S(1)} %get-tuple-element.26, f32[6,32,1024]{2,1,0:T(8,128)S(1)} %get-tuple-element.25, f32[6,32,1024]{2,1,0:T(8,128)S(1)} %get-tuple-element.24, f32[6,32,1024]{2,1,0:T(8,128)S(1)} %get-tuple-element.23, ...), kind=kLoop, calls=%fused_computation.35 | loop fusion | flops 3342336 | bytes 7867392 | tf_op jit(solution)/shard_map/add | solution.py:143
  64.5 3.4 %collective-permute-start = (f32[1,32,1024]{2,1,0:T(8,128)S(1)}, f32[1,32,1024]{2,1,0:T(8,128)S(1)}, u32[]{:S(2)}, u32[]{:S(2)}) collective-permute-start(f32[1,32,1024]{2,1,0:T(8,128)S(1)} %get-tuple-element.38), channel_id=1, source_target_pairs={{0,8},{8,16},{16,24},{1,9},{9,17},{17,25},{2,10},{10,18},{18,26},{... | collective-permute-start | bytes 393224 | tf_op jit(solution)/shard_map/ppermute | solution.py:147
  67.9 1.3 %collective-permute-start.1 = (f32[1,32,1024]{2,1,0:T(8,128)S(1)}, f32[1,32,1024]{2,1,0:T(8,128)S(1)}, u32[]{:S(2)}, u32[]{:S(2)}) collective-permute-start(f32[1,32,1024]{2,1,0:T(8,128)S(1)} %get-tuple-element.39), channel_id=1, source_target_pairs={{8,0},{16,8},{24,16},{9,1},{17,9},{25,17},{10,2},{18,10},{26,18},{... | collective-permute-start | bytes 393224 | tf_op jit(solution)/shard_map/ppermute | solution.py:148
  69.3 2.7 %collective-permute-start.7 = (f32[224,256]{1,0:T(8,128)S(1)}, f32[224,256]{1,0:T(8,128)S(1)}, u32[]{:S(2)}, u32[]{:S(2)}) collective-permute-start(f32[224,256]{1,0:T(8,128)S(1)} %fusion.45), channel_id=1, source_target_pairs={{0,8},{8,0},{16,24},{24,16},{1,9},{9,1},{17,25},{25,17},{2,10},{10... | collective-permute-start | bytes 688136 | tf_op jit(solution)/shard_map/ppermute | solution.py:106
  72.0 1.5 %collective-permute-start.8 = (f32[224,256]{1,0:T(8,128)S(1)}, f32[224,256]{1,0:T(8,128)S(1)}, u32[]{:S(2)}, u32[]{:S(2)}) collective-permute-start(f32[224,256]{1,0:T(8,128)S(1)} %fusion.45), channel_id=1, source_target_pairs={{0,16},{8,24},{16,0},{24,8},{1,17},{9,25},{17,1},{25,9},{2,18},{10... | collective-permute-start | bytes 688136 | tf_op jit(solution)/shard_map/ppermute | solution.py:106
  73.5 0.9 collective-permute-start.9
  74.4 1.8 %collective-permute-done.1 = f32[1,32,1024]{2,1,0:T(8,128)S(1)} collective-permute-done((f32[1,32,1024]{2,1,0:T(8,128)S(1)}, f32[1,32,1024]{2,1,0:T(8,128)S(1)}, u32[]{:S(2)}, u32[]{:S(2)}) %collective-permute-start.1) | collective-permute-done | bytes 131104 | tf_op jit(solution)/shard_map/ppermute | solution.py:148
  76.3 0.9 copy.47
  77.2 3.9 %collective-permute-done.7 = f32[224,256]{1,0:T(8,128)S(1)} collective-permute-done((f32[224,256]{1,0:T(8,128)S(1)}, f32[224,256]{1,0:T(8,128)S(1)}, u32[]{:S(2)}, u32[]{:S(2)}) %collective-permute-start.7) | collective-permute-done | bytes 229408 | tf_op jit(solution)/shard_map/ppermute | solution.py:106
  81.1 3.9 %collective-permute-done.9 = f32[224,256]{1,0:T(8,128)S(1)} collective-permute-done((f32[224,256]{1,0:T(8,128)S(1)}, f32[224,256]{1,0:T(8,128)S(1)}, u32[]{:S(2)}, u32[]{:S(2)}) %collective-permute-start.9) | collective-permute-done | bytes 229408 | tf_op jit(solution)/shard_map/ppermute | solution.py:106
  85.2 1.0 pad_maximum_fusion.1
  86.1 0.5 slice_bitcast_fusion.9
  86.7 13.0 %reduce-scatter.2.cloned.1.call-done = f32[32,4096]{1,0:T(8,128)} async-done(((f32[256,4096]{1,0:T(8,128)}), f32[32,4096]{1,0:T(8,128)}) %reduce-scatter.2.cloned.1.call-update) | async-done | bytes 524304 | tf_op jit(solution)/shard_map/reduce_scatter | solution.py:197
  99.7 1.1 convert_element_type.36
  100.7 0.9 reshape.124
  (51 shorter events, 3.3 us)
Async XLA Ops:
  7.2 40.7 %all-gather.2.cloned.1.call-start = ((), (), s32[]{:S(2)}) async-start(), calls=%async_computation.1 | async-start | bytes 2359296 | tf_op jit(solution)/shard_map/all_gather | solution.py:125
  8.3 11.0 %collective-permute-start.2 = (bf16[1,32,1024]{2,1,0:T(8,128)(2,1)S(1)}, bf16[1,32,1024]{2,1,0:T(8,128)(2,1)S(1)}, u32[]{:S(2)}, u32[]{:S(2)}) collective-permute-start(bf16[1,32,1024]{2,1,0:T(8,128)(2,1)S(1)} %get-tuple-element.48), channel_id=1, source_target_pairs={{0,8},{8,16},{16,24},{1,9},{9,17},{17,25},{2,10},{10,18},{18,26},{... | collective-permute-start | bytes 196616 | tf_op jit(solution)/shard_map/ppermute | solution.py:28
  13.1 6.2 %collective-permute-start.3 = (bf16[1,32,1024]{2,1,0:T(8,128)(2,1)S(1)}, bf16[1,32,1024]{2,1,0:T(8,128)(2,1)S(1)}, u32[]{:S(2)}, u32[]{:S(2)}) collective-permute-start(bf16[1,32,1024]{2,1,0:T(8,128)(2,1)S(1)} %get-tuple-element.49), channel_id=1, source_target_pairs={{8,0},{16,8},{24,16},{9,1},{17,9},{25,17},{10,2},{18,10},{26,18},{... | collective-permute-start | bytes 196616 | tf_op jit(solution)/shard_map/ppermute | solution.py:29
  16.2 83.5 %reduce-scatter.2.cloned.1.call-start = ((), (), s32[]{:S(2)}) async-start(), calls=%async_computation.2 | async-start | bytes 4718592 | tf_op jit(solution)/shard_map/reduce_scatter | solution.py:197
  22.5 2.1 %copy-start.1 = (bf16[4,9,32,1024]{3,2,1,0:T(8,128)(2,1)}, bf16[4,9,32,1024]{3,2,1,0:T(8,128)(2,1)S(1)}, u32[]{:S(2)}) copy-start(bf16[4,9,32,1024]{3,2,1,0:T(8,128)(2,1)S(1)} %copy.42) | copy-start | bytes 7077892
  22.8 2.0 %copy-start.3 = (bf16[4,9,32,1024]{3,2,1,0:T(8,128)(2,1)}, bf16[4,9,32,1024]{3,2,1,0:T(8,128)(2,1)S(1)}, u32[]{:S(2)}) copy-start(bf16[4,9,32,1024]{3,2,1,0:T(8,128)(2,1)S(1)} %copy.40) | copy-start | bytes 7077892
  37.6 1.0 copy-start.6
  37.6 1.3 %copy-start.5 = (bf16[27,256,32]{1,2,0:T(8,128)(2,1)S(1)}, bf16[27,256,32]{1,2,0:T(8,128)(2,1)}, u32[]{:S(2)}) copy-start(bf16[27,256,32]{1,2,0:T(8,128)(2,1)} %param.7) | copy-start | bytes 1327108
  47.8 2.6 %copy-start = (bf16[4,256,1024]{2,1,0:T(8,128)(2,1)S(1)}, bf16[4,256,1024]{2,1,0:T(8,128)(2,1)}, u32[]{:S(2)}) copy-start(bf16[4,256,1024]{2,1,0:T(8,128)(2,1)} %all-gather.2.cloned.1.call-done) | copy-start | bytes 6291460
  47.8 2.9 %copy-start.2 = (bf16[4,9,32,1024]{3,2,1,0:T(8,128)(2,1)S(1)}, bf16[4,9,32,1024]{3,2,1,0:T(8,128)(2,1)}, u32[]{:S(2)}) copy-start(bf16[4,9,32,1024]{3,2,1,0:T(8,128)(2,1)} %copy-done.1) | copy-start | bytes 7077892
  50.4 1.8 %copy-start.4 = (bf16[4,9,32,1024]{3,2,1,0:T(8,128)(2,1)S(1)}, bf16[4,9,32,1024]{3,2,1,0:T(8,128)(2,1)}, u32[]{:S(2)}) copy-start(bf16[4,9,32,1024]{3,2,1,0:T(8,128)(2,1)} %copy-done.3) | copy-start | bytes 7077892
  53.2 16.0 %collective-permute-start.4 = (f32[224,256]{1,0:T(8,128)S(1)}, f32[224,256]{1,0:T(8,128)S(1)}, u32[]{:S(2)}, u32[]{:S(2)}) collective-permute-start(f32[224,256]{1,0:T(8,128)S(1)} %get-tuple-element.35), channel_id=1, source_target_pairs={{0,8},{8,0},{16,24},{24,16},{1,9},{9,1},{17,25},{25,17},{2,10},{10... | collective-permute-start | bytes 688136 | tf_op jit(solution)/shard_map/ppermute | solution.py:104
  54.7 14.5 %collective-permute-start.5 = (f32[224,256]{1,0:T(8,128)S(1)}, f32[224,256]{1,0:T(8,128)S(1)}, u32[]{:S(2)}, u32[]{:S(2)}) collective-permute-start(f32[224,256]{1,0:T(8,128)S(1)} %get-tuple-element.37), channel_id=1, source_target_pairs={{0,16},{8,24},{16,0},{24,8},{1,17},{9,25},{17,1},{25,9},{2,18},{10... | collective-permute-start | bytes 688136 | tf_op jit(solution)/shard_map/ppermute | solution.py:104
  56.2 13.0 %collective-permute-start.6 = (f32[224,256]{1,0:T(8,128)S(1)}, f32[224,256]{1,0:T(8,128)S(1)}, u32[]{:S(2)}, u32[]{:S(2)}) collective-permute-start(f32[224,256]{1,0:T(8,128)S(1)} %get-tuple-element.36), channel_id=1, source_target_pairs={{0,24},{8,16},{16,8},{24,0},{1,25},{9,17},{17,9},{25,1},{2,26},{10... | collective-permute-start | bytes 688136 | tf_op jit(solution)/shard_map/ppermute | solution.py:104
  62.7 13.5 %copy-start.7 = (f32[32]{0:T(128)S(1)}, f32[32]{0:T(128)}, u32[]{:S(2)}) copy-start(f32[32]{0:T(128)} %param.8) | copy-start | bytes 388
  64.5 9.9 %collective-permute-start = (f32[1,32,1024]{2,1,0:T(8,128)S(1)}, f32[1,32,1024]{2,1,0:T(8,128)S(1)}, u32[]{:S(2)}, u32[]{:S(2)}) collective-permute-start(f32[1,32,1024]{2,1,0:T(8,128)S(1)} %get-tuple-element.38), channel_id=1, source_target_pairs={{0,8},{8,16},{16,24},{1,9},{9,17},{17,25},{2,10},{10,18},{18,26},{... | collective-permute-start | bytes 393224 | tf_op jit(solution)/shard_map/ppermute | solution.py:147
  67.9 8.3 %collective-permute-start.1 = (f32[1,32,1024]{2,1,0:T(8,128)S(1)}, f32[1,32,1024]{2,1,0:T(8,128)S(1)}, u32[]{:S(2)}, u32[]{:S(2)}) collective-permute-start(f32[1,32,1024]{2,1,0:T(8,128)S(1)} %get-tuple-element.39), channel_id=1, source_target_pairs={{8,0},{16,8},{24,16},{9,1},{17,9},{25,17},{10,2},{18,10},{26,18},{... | collective-permute-start | bytes 393224 | tf_op jit(solution)/shard_map/ppermute | solution.py:148
  69.3 11.8 %collective-permute-start.7 = (f32[224,256]{1,0:T(8,128)S(1)}, f32[224,256]{1,0:T(8,128)S(1)}, u32[]{:S(2)}, u32[]{:S(2)}) collective-permute-start(f32[224,256]{1,0:T(8,128)S(1)} %fusion.45), channel_id=1, source_target_pairs={{0,8},{8,0},{16,24},{24,16},{1,9},{9,1},{17,25},{25,17},{2,10},{10... | collective-permute-start | bytes 688136 | tf_op jit(solution)/shard_map/ppermute | solution.py:106
  72.0 9.1 %collective-permute-start.8 = (f32[224,256]{1,0:T(8,128)S(1)}, f32[224,256]{1,0:T(8,128)S(1)}, u32[]{:S(2)}, u32[]{:S(2)}) collective-permute-start(f32[224,256]{1,0:T(8,128)S(1)} %fusion.45), channel_id=1, source_target_pairs={{0,16},{8,24},{16,0},{24,8},{1,17},{9,25},{17,1},{25,9},{2,18},{10... | collective-permute-start | bytes 688136 | tf_op jit(solution)/shard_map/ppermute | solution.py:106
  73.5 11.6 %collective-permute-start.9 = (f32[224,256]{1,0:T(8,128)S(1)}, f32[224,256]{1,0:T(8,128)S(1)}, u32[]{:S(2)}, u32[]{:S(2)}) collective-permute-start(f32[224,256]{1,0:T(8,128)S(1)} %fusion.45), channel_id=1, source_target_pairs={{0,24},{8,16},{16,8},{24,0},{1,25},{9,17},{17,9},{25,1},{2,26},{10... | collective-permute-start | bytes 688136 | tf_op jit(solution)/shard_map/ppermute | solution.py:106
Sparse Core Ops, SparseCore 0:
  16.3 31.4 all-gather.1
  50.1 49.4 reduce-scatter.1

commit v5 on v4

--- a/solution.py
+++ b/solution.py
@@ -112,6 +112,36 @@
     )
 
 
+def shift_sum(stacked, steps_sign):
+    total = None
+    for shift_index, (row_step, column_step) in enumerate(plane_offsets):
+        term = shift_cells(stacked[:, shift_index], steps_sign * row_step, steps_sign * column_step)
+        total = term if total is None else total + term
+    return total
+
+
+def depth_products(weights, planes, toward_output):
+    total = None
+    for depth_index in range(3):
+        part = jnp.einsum("ki,zin->zkn", weights[depth_index], planes, preferred_element_type=jnp.float32)
+        front = 2 - depth_index if toward_output else depth_index
+        part = jnp.pad(part, ((front, 2 - front), (0, 0), (0, 0)))
+        total = part if total is None else total + part
+    return total
+
+
+def settle_rims(field):
+    depth = field.shape[0] - 2
+    space_devices = lax.axis_size("space")
+    up = [(i, i + 1) for i in range(space_devices - 1)]
+    down = [(i + 1, i) for i in range(space_devices - 1)]
+    from_below = lax.ppermute(field[depth + 1 :], "space", up)
+    from_above = lax.ppermute(field[:1], "space", down)
+    return field[1 : depth + 1] + jnp.concatenate(
+        [from_below, jnp.zeros((depth - 2,) + field.shape[1:], field.dtype), from_above]
+    )
+
+
 def body(inputs, weight, bias_term, output_grad):
     taps_total = weight.shape[0]
     channels_in = weight.shape[1]
@@ -122,33 +152,17 @@
     grad_scale = 1.0 / math.sqrt(lax.axis_size("space") * depth_cells * plane_cells)
     inputs_planes = jnp.transpose(inputs, (1, 0, 2))
     grad_planes = jnp.transpose(output_grad, (1, 0, 2))
-    gathered = lax.all_gather(inputs_planes, "chan", axis=1, tiled=True)
+    both = lax.all_gather(jnp.concatenate([inputs_planes, grad_planes]), "chan", axis=1, tiled=True)
+    gathered = both[:depth_cells]
+    grad_gathered = both[depth_cells:]
+    weight_rows = lax.all_to_all(weight, "chan", 1, 2, tiled=True)
 
     weight_grid = weight.reshape(3, 9, channels_in, block_out)
     forward_weight = jnp.transpose(weight_grid, (0, 1, 3, 2)).reshape(3, 9 * block_out, channels_in)
-    in_plane = None
-    for depth_index in range(3):
-        part = jnp.einsum(
-            "ki,zin->zkn",
-            forward_weight[depth_index],
-            gathered,
-            preferred_element_type=jnp.float32,
-        )
-        part = jnp.pad(part, ((2 - depth_index, depth_index), (0, 0), (0, 0)))
-        in_plane = part if in_plane is None else in_plane + part
-    in_plane = in_plane.reshape(depth_cells + 2, 9, block_out, plane_cells)
-    forward = None
-    for shift_index, (row_step, column_step) in enumerate(plane_offsets):
-        term = shift_cells(in_plane[:, shift_index], row_step, column_step)
-        forward = term if forward is None else forward + term
-    space_devices = lax.axis_size("space")
-    up = [(i, i + 1) for i in range(space_devices - 1)]
-    down = [(i + 1, i) for i in range(space_devices - 1)]
-    from_below = lax.ppermute(forward[depth_cells + 1 :], "space", up)
-    from_above = lax.ppermute(forward[:1], "space", down)
-    forward = forward[1 : depth_cells + 1] + jnp.concatenate(
-        [from_below, jnp.zeros((depth_cells - 2, block_out, plane_cells), jnp.float32), from_above]
-    )
+    forward = shift_sum(
+        depth_products(forward_weight, gathered, True).reshape(depth_cells + 2, 9, block_out, plane_cells), 1
+    )
+    forward = settle_rims(forward)
     outputs = jnp.transpose(
         (forward + bias_term[None, :, None]).astype(jnp.bfloat16), (1, 0, 2)
     )
@@ -170,6 +184,7 @@
         ]
     ).reshape(taps_total * block_out, channels_in)
     bias_part = jnp.sum(output_grad.astype(jnp.float32), axis=(1, 2))
+    space_devices = lax.axis_size("space")
     unit = 8 * space_devices
     total_rows = -(-(taps_total * block_out + 1) // unit) * unit
     bias_rows = jnp.zeros((total_rows - taps_total * block_out, channels_in), jnp.float32)
@@ -181,23 +196,13 @@
     )
     bias_grad = reduced[taps_total * block_out, :block_out]
 
-    chan_devices = lax.axis_size("chan")
-    backward_weight = jnp.transpose(weight_grid, (0, 2, 1, 3)).reshape(
-        3, chan_devices, channels_in // chan_devices, 9 * block_out
-    )
-    spread = None
-    for depth_index in range(3):
-        part = jnp.einsum(
-            "bjk,zkn->bjzn",
-            backward_weight[depth_index],
-            grad_shifted[2 - depth_index : 2 - depth_index + depth_cells],
-            preferred_element_type=jnp.float32,
-        )
-        spread = part if spread is None else spread + part
-    summed = lax.psum_scatter(
-        spread.reshape(channels_in, depth_cells * plane_cells), "chan", scatter_dimension=0, tiled=True
-    )
-    input_grad = summed.astype(jnp.bfloat16).reshape(block_in, depth_cells, plane_cells)
+    channels_out = weight_rows.shape[2]
+    backward_weight = weight_rows.reshape(3, 9 * block_in, channels_out)
+    spread = shift_sum(
+        depth_products(backward_weight, grad_gathered, False).reshape(depth_cells + 2, 9, block_in, plane_cells), -1
+    )
+    spread = settle_rims(spread)
+    input_grad = jnp.transpose(spread.astype(jnp.bfloat16), (1, 0, 2))
     return (outputs, input_grad, weight_grad, bias_grad)
 
 

time: 109 us -> 131 us (1.20)
  starting transfers between devices: 19.5 us -> 31.8 us
  other arithmetic: 8.46 us -> 14 us
  local copies, waits for them, and re-layouts: 22 us -> 25.6 us
  waiting for transfers between devices: 31.6 us -> 35 us
  matrix products: 12.4 us -> 9.62 us
    all_to_all x0 -> x1, waiting for transfers between devices: none -> 15.8 us  [body(): weight_rows = lax.all_to_all(weight, 'chan', 1, 2, tiled=True)]
    reduce_scatter x1 -> x0, waiting for transfers between devices: 13 us -> none  [body(): lax.psum_scatter(spread.reshape(channels_in, depth_cells * plane_cells),...]
    ppermute x2 -> x4, starting transfers between devices: 4.68 us -> 10.5 us  [the longest x2 7.94 us: settle_rims(): from_below = lax.ppermute(field[depth + 1:], 'space', up)]
    all_to_all x0 -> x1, starting transfers between devices: none -> 4.88 us  [body(): weight_rows = lax.all_to_all(weight, 'chan', 1, 2, tiled=True)]
    slice x4, local copies, waits for them, and re-layouts: 1.89 us -> 6.22 us  [body(): grad_shifted[2 - depth_index:2 - depth_index + depth_cells]]
    add x2 -> x4, other arithmetic: 4.19 us -> 8.15 us  [the longest x2 4.77 us: depth_products(): total = part if total is None else total + part]
    dot_general x6, matrix products: 8.22 us -> 4.75 us  [depth_products(): jnp.einsum('ki,zin->zkn', weights[depth_index], planes, preferred_element...]
    add x1 -> x0, local copies, waits for them, and re-layouts: 2.9 us -> none  [body(): spread = part if spread is None else spread + part]
  transfers between devices with their start and end apart: 12 -> 14, of which waited for: 5 -> 5; matrix products, arithmetic and copies ran while one was open for 35% -> 29% of each run, Pallas kernels for 0% -> 0%
where the time goes in v5:
time: 131 us
  waiting for transfers between devices  35 us (27%)
  starting transfers between devices  31.8 us (24%)
  local copies, waits for them, and re-layouts  25.6 us (20%)
  between operations  14.4 us (11%)
  other arithmetic  14 us (11%)
  matrix products  9.62 us (7%)
    all_to_all x1, waiting for transfers between devices, body(): weight_rows = lax.all_to_all(weight, 'chan', 1, 2, tiled=True)  15.8 us
    unnamed x19, local copies, waits for them, and re-layouts  13.3 us
    all_gather x1, waiting for transfers between devices, body(): lax.all_gather(jnp.concatenate([inputs_planes, grad_planes]), 'chan', axi...  11.2 us
    ppermute x2, starting transfers between devices, settle_rims(): from_below = lax.ppermute(field[depth + 1:], 'space', up)  7.94 us
    slice x4, local copies, waits for them, and re-layouts, body(): grad_shifted[2 - depth_index:2 - depth_index + depth_cells]  6.22 us
    ppermute x3, starting transfers between devices, all_reduce_direct(): lax.ppermute(reduced, axis, [(i, i ^ distance) for i in range(devices)])  6.03 us
    ppermute x3, waiting for transfers between devices, all_reduce_direct(): lax.ppermute(reduced, axis, [(i, i ^ distance) for i in range(devices)])  5.93 us
    ppermute x1, starting transfers between devices, padded_2(): before = lax.ppermute(last, axis, up)  5.47 us
  transfers between devices with their start and end apart: 14, of which 5 were waited for; matrix products, arithmetic and copies ran while one was open for 29% of the time, Pallas kernels for 0%

profile of v5, /device:TPU:0, one launch (start us, length us, event | category | flops | bytes accessed | tf_op | source)
XLA Modules:
  0.0 130.5 jit_solution(6209768241215491830)
XLA Ops:
  7.2 1.0 copy.96
  8.2 1.0 copy.95
  9.3 0.8 pad_maximum_fusion.5
  10.8 5.5 %collective-permute-start.4 = (bf16[1,32,1024]{2,1,0:T(8,128)(2,1)}, bf16[1,32,1024]{2,1,0:T(8,128)(2,1)}, u32[]{:S(2)}, u32[]{:S(2)}) collective-permute-start(bf16[1,32,1024]{2,1,0:T(8,128)(2,1)} %get-tuple-element.66), channel_id=1, source_target_pairs={{0,8},{8,16},{16,24},{1,9},{9,17},{17,25},{2,10},{10,18},{18,26},{... | collective-permute-start | bytes 196616 | tf_op jit(solution)/shard_map/ppermute | solution.py:28
  16.3 1.3 collective-permute-start.5
  17.6 3.8 %copy.54 = bf16[27,256,32]{2,0,1:T(8,128)(2,1)S(1)} copy(bf16[27,256,32]{1,2,0:T(8,128)(2,1)} %param.7) | data formatting | bytes 884736 | tf_op args[1]
  21.4 2.1 %reshape.137 = bf16[8,2,13824]{2,1,0:T(2,128)(2,1)} reshape(bf16[256,27,32]{2,1,0:T(8,128)(2,1)S(1)} %bitcast.226) | data formatting | bytes 884736
  23.5 4.9 %all-to-all-start = ((bf16[8,2,13824]{2,1,0:T(2,128)(2,1)}), bf16[8,2,13824]{2,1,0:T(2,128)(2,1)S(1)}, u32[]{:S(2)}, u32[]{:S(2)}) async-start(bf16[8,2,13824]{2,1,0:T(2,128)(2,1)} %reshape.137), calls=%async_computation | async-start | bytes 884736 | tf_op jit(solution)/shard_map/all_to_all | solution.py:158
  28.9 1.1 fusion.52
  30.6 0.9 fusion.69
  32.2 1.0 fusion.88
  33.2 1.7 %copy.69 = bf16[4,9,32,1024]{3,2,1,0:T(8,128)(2,1)} copy(bf16[4,9,32,1024]{3,2,0,1:T(8,128)(2,1)S(1)} %get-tuple-element.45) | data formatting | bytes 4718592 | tf_op jit(solution)/shard_map/slice | solution.py:179
  34.9 1.7 %copy.68 = bf16[4,9,32,1024]{3,2,1,0:T(8,128)(2,1)} copy(bf16[4,9,32,1024]{3,2,0,1:T(8,128)(2,1)S(1)} %get-tuple-element.46) | data formatting | bytes 4718592 | tf_op jit(solution)/shard_map/slice | solution.py:179
  36.7 1.8 %copy.67 = bf16[4,9,32,1024]{3,2,1,0:T(8,128)(2,1)} copy(bf16[4,9,32,1024]{3,2,0,1:T(8,128)(2,1)S(1)} %get-tuple-element.44) | data formatting | bytes 4718592 | tf_op jit(solution)/shard_map/slice | solution.py:179
  38.4 15.8 %all-to-all-done = bf16[8,2,13824]{2,1,0:T(2,128)(2,1)S(1)} async-done(((bf16[8,2,13824]{2,1,0:T(2,128)(2,1)}), bf16[8,2,13824]{2,1,0:T(2,128)(2,1)S(1)}, u32[]{:S(2)}, u32[]{:S(2)}) %all-to-all-start) | async-done | bytes 442400 | tf_op jit(solution)/shard_map/all_to_all | solution.py:158
  54.2 1.6 %reshape.138 = bf16[256,27,32]{2,1,0:T(8,128)(2,1)S(1)} reshape(bf16[8,2,13824]{2,1,0:T(2,128)(2,1)S(1)} %all-to-all-done) | data formatting | bytes 884736
  55.8 1.2 copy.94
  58.3 11.2 %all-gather.2.cloned.1.call-done = bf16[8,256,1024]{2,1,0:T(8,128)(2,1)} async-done(((bf16[8,32,1024]{2,1,0:T(8,128)(2,1)}), bf16[8,256,1024]{2,1,0:T(8,128)(2,1)}) %all-gather.2.cloned.1.call-update) | async-done | bytes 4194320 | tf_op jit(solution)/shard_map/all_gather | solution.py:155
  69.5 3.3 %convolution_bitcast_fusion.6 = f32[1,288,256]{2,1,0:T(8,128)S(1)} fusion(bf16[4,288,1024]{2,1,0:T(8,128)(2,1)} %bitcast.236, bf16[8,256,1024]{2,1,0:T(8,128)(2,1)} %all-gather.2.cloned.1.call-done), kind=kOutput, calls=%fused_computation.14 | convolution fusion | flops 603979776 | bytes 4751360 | tf_op jit(solution)/shard_map/zkn,zin->ki/dot_general | solution.py:177
  73.8 0.8 convolution_bitcast_fusion.7
  74.6 0.8 copy-done.2
  75.5 0.8 convolution_bitcast_fusion.8
  76.5 1.5 %collective-permute-start.6 = (f32[224,256]{1,0:T(8,128)S(1)}, f32[224,256]{1,0:T(8,128)S(1)}, u32[]{:S(2)}, u32[]{:S(2)}) collective-permute-start(f32[224,256]{1,0:T(8,128)S(1)} %get-tuple-element.54), channel_id=1, source_target_pairs={{0,8},{8,0},{16,24},{24,16},{1,9},{9,1},{17,25},{25,17},{2,10},{10... | collective-permute-start | bytes 688136 | tf_op jit(solution)/shard_map/ppermute | solution.py:104
  78.0 1.5 %collective-permute-start.7 = (f32[224,256]{1,0:T(8,128)S(1)}, f32[224,256]{1,0:T(8,128)S(1)}, u32[]{:S(2)}, u32[]{:S(2)}) collective-permute-start(f32[224,256]{1,0:T(8,128)S(1)} %get-tuple-element.56), channel_id=1, source_target_pairs={{0,16},{8,24},{16,0},{24,8},{1,17},{9,25},{17,1},{25,9},{2,18},{10... | collective-permute-start | bytes 688136 | tf_op jit(solution)/shard_map/ppermute | solution.py:104
  80.8 0.8 convolution_bitcast_fusion.4
  81.6 0.8 convolution_bitcast_fusion.5
  82.4 2.5 %pad_add_fusion.1 = f32[6,288,1024]{2,1,0:T(8,128)S(1)} fusion(f32[4,288,1024]{2,1,0:T(8,128)S(1)} %convolution_bitcast_fusion.3, f32[4,288,1024]{2,1,0:T(8,128)S(1)} %convolution_bitcast_fusion.4, f32[4,288,1024]{2,1,0:T(8,128)S(1)} %convolution_bitcast_fusion.5), kind=kLoop, calls=%fused_computation.1 | loop fusion | flops 3538944 | bytes 21233664 | tf_op jit(solution)/shard_map/add | solution.py:129
  84.9 1.1 slice_bitcast_fusion.9
  86.1 1.7 %fusion.19 = f32[6,32,1024]{2,1,0:T(8,128)S(1)} fusion(f32[6,32,1024]{2,1,0:T(8,128)S(1)} %get-tuple-element.43, f32[6,32,1024]{2,1,0:T(8,128)S(1)} %get-tuple-element.42, f32[6,32,1024]{2,1,0:T(8,128)S(1)} %get-tuple-element.41, f32[6,32,1024]{2,1,0:T(8,128)S(1)} %get-tuple-element.40, f32[6,32,1024]{2,1,0:T(8,128)S(1)} %get-tuple-element.39, ...), kind=kLoop, calls=%fused_computation.56 | loop fusion | flops 3342336 | bytes 7867392 | tf_op jit(solution)/shard_map/add | solution.py:119
  87.8 3.4 %collective-permute-start = (f32[1,32,1024]{2,1,0:T(8,128)S(1)}, f32[1,32,1024]{2,1,0:T(8,128)S(1)}, u32[]{:S(2)}, u32[]{:S(2)}) collective-permute-start(f32[1,32,1024]{2,1,0:T(8,128)S(1)} %get-tuple-element.59), channel_id=1, source_target_pairs={{0,8},{8,16},{16,24},{1,9},{9,17},{17,25},{2,10},{10,18},{18,26},{... | collective-permute-start | bytes 393224 | tf_op jit(solution)/shard_map/ppermute | solution.py:138
  91.2 1.3 collective-permute-start.1
  92.5 0.8 convolution_bitcast_fusion
  93.3 0.8 convolution_bitcast_fusion.1
  94.1 0.8 convolution_bitcast_fusion.2
  94.9 2.3 %pad_add_fusion = f32[6,288,1024]{2,1,0:T(8,128)S(1)} fusion(f32[4,288,1024]{2,1,0:T(8,128)S(1)} %convolution_bitcast_fusion, f32[4,288,1024]{2,1,0:T(8,128)S(1)} %convolution_bitcast_fusion.1, f32[4,288,1024]{2,1,0:T(8,128)S(1)} %convolution_bitcast_fusion.2), kind=kLoop, calls=%fused_computation | loop fusion | flops 3538944 | bytes 21233664 | tf_op jit(solution)/shard_map/add | solution.py:129
  97.2 1.1 slice_bitcast_fusion
  98.3 1.7 %fusion.35 = f32[6,32,1024]{2,1,0:T(8,128)S(1)} fusion(f32[6,32,1024]{2,1,0:T(8,128)S(1)} %get-tuple-element.35, f32[6,32,1024]{2,1,0:T(8,128)S(1)} %get-tuple-element.34, f32[6,32,1024]{2,1,0:T(8,128)S(1)} %get-tuple-element.33, f32[6,32,1024]{2,1,0:T(8,128)S(1)} %get-tuple-element.32, f32[6,32,1024]{2,1,0:T(8,128)S(1)} %get-tuple-element.31, ...), kind=kLoop, calls=%fused_computation.72 | loop fusion | flops 3342336 | bytes 7867392 | tf_op jit(solution)/shard_map/add | solution.py:119
  100.0 4.6 %collective-permute-start.2 = (f32[1,32,1024]{2,1,0:T(8,128)S(1)}, f32[1,32,1024]{2,1,0:T(8,128)S(1)}, u32[]{:S(2)}, u32[]{:S(2)}) collective-permute-start(f32[1,32,1024]{2,1,0:T(8,128)S(1)} %get-tuple-element.57), channel_id=1, source_target_pairs={{0,8},{8,16},{16,24},{1,9},{9,17},{17,25},{2,10},{10,18},{18,26},{... | collective-permute-start | bytes 393224 | tf_op jit(solution)/shard_map/ppermute | solution.py:138
  104.6 1.3 collective-permute-start.3
  106.0 3.1 %collective-permute-start.9 = (f32[224,256]{1,0:T(8,128)S(1)}, f32[224,256]{1,0:T(8,128)S(1)}, u32[]{:S(2)}, u32[]{:S(2)}) collective-permute-start(f32[224,256]{1,0:T(8,128)S(1)} %fusion.73), channel_id=1, source_target_pairs={{0,8},{8,0},{16,24},{24,16},{1,9},{9,1},{17,25},{25,17},{2,10},{10... | collective-permute-start | bytes 688136 | tf_op jit(solution)/shard_map/ppermute | solution.py:106
  109.0 1.5 %collective-permute-start.10 = (f32[224,256]{1,0:T(8,128)S(1)}, f32[224,256]{1,0:T(8,128)S(1)}, u32[]{:S(2)}, u32[]{:S(2)}) collective-permute-start(f32[224,256]{1,0:T(8,128)S(1)} %fusion.73), channel_id=1, source_target_pairs={{0,16},{8,24},{16,0},{24,8},{1,17},{9,25},{17,1},{25,9},{2,18},{10... | collective-permute-start | bytes 688136 | tf_op jit(solution)/shard_map/ppermute | solution.py:106
  110.6 1.4 %collective-permute-start.11 = (f32[224,256]{1,0:T(8,128)S(1)}, f32[224,256]{1,0:T(8,128)S(1)}, u32[]{:S(2)}, u32[]{:S(2)}) collective-permute-start(f32[224,256]{1,0:T(8,128)S(1)} %fusion.73), channel_id=1, source_target_pairs={{0,24},{8,16},{16,8},{24,0},{1,25},{9,17},{17,9},{25,1},{2,26},{10... | collective-permute-start | bytes 688136 | tf_op jit(solution)/shard_map/ppermute | solution.py:106
  112.0 2.0 %collective-permute-done.3 = f32[1,32,1024]{2,1,0:T(8,128)S(1)} collective-permute-done((f32[1,32,1024]{2,1,0:T(8,128)S(1)}, f32[1,32,1024]{2,1,0:T(8,128)S(1)}, u32[]{:S(2)}, u32[]{:S(2)}) %collective-permute-start.3) | collective-permute-done | bytes 131104 | tf_op jit(solution)/shard_map/ppermute | solution.py:139
  114.3 0.9 copy.70
  115.2 0.9 copy.71
  116.1 2.9 %collective-permute-done.9 = f32[224,256]{1,0:T(8,128)S(1)} collective-permute-done((f32[224,256]{1,0:T(8,128)S(1)}, f32[224,256]{1,0:T(8,128)S(1)}, u32[]{:S(2)}, u32[]{:S(2)}) %collective-permute-start.9) | collective-permute-done | bytes 229408 | tf_op jit(solution)/shard_map/ppermute | solution.py:106
  119.0 3.0 %collective-permute-done.11 = f32[224,256]{1,0:T(8,128)S(1)} collective-permute-done((f32[224,256]{1,0:T(8,128)S(1)}, f32[224,256]{1,0:T(8,128)S(1)}, u32[]{:S(2)}, u32[]{:S(2)}) %collective-permute-start.11) | collective-permute-done | bytes 229408 | tf_op jit(solution)/shard_map/ppermute | solution.py:106
  122.7 1.0 pad_maximum_fusion.1
  (53 shorter events, 7.2 us)
Async XLA Ops:
  7.2 62.4 %all-gather.2.cloned.1.call-start = ((), (), s32[]{:S(2)}) async-start(), calls=%async_computation.1 | async-start | bytes 4718592 | tf_op jit(solution)/shard_map/all_gather | solution.py:155
  10.1 18.3 %copy-start.4 = (bf16[32,4,1024]{2,1,0:T(4,128)(2,1)S(1)}, bf16[32,4,1024]{2,1,0:T(4,128)(2,1)}, u32[]{:S(2)}) copy-start(bf16[32,4,1024]{2,1,0:T(4,128)(2,1)} %param.9) | copy-start | bytes 786436
  10.1 18.7 %copy-start.3 = (bf16[27,256,32]{1,2,0:T(8,128)(2,1)S(1)}, bf16[27,256,32]{1,2,0:T(8,128)(2,1)}, u32[]{:S(2)}) copy-start(bf16[27,256,32]{1,2,0:T(8,128)(2,1)} %param.7) | copy-start | bytes 1327108
  10.8 18.0 %collective-permute-start.4 = (bf16[1,32,1024]{2,1,0:T(8,128)(2,1)}, bf16[1,32,1024]{2,1,0:T(8,128)(2,1)}, u32[]{:S(2)}, u32[]{:S(2)}) collective-permute-start(bf16[1,32,1024]{2,1,0:T(8,128)(2,1)} %get-tuple-element.66), channel_id=1, source_target_pairs={{0,8},{8,16},{16,24},{1,9},{9,17},{17,25},{2,10},{10,18},{18,26},{... | collective-permute-start | bytes 196616 | tf_op jit(solution)/shard_map/ppermute | solution.py:28
  16.3 12.6 %collective-permute-start.5 = (bf16[1,32,1024]{2,1,0:T(8,128)(2,1)}, bf16[1,32,1024]{2,1,0:T(8,128)(2,1)}, u32[]{:S(2)}, u32[]{:S(2)}) collective-permute-start(bf16[1,32,1024]{2,1,0:T(8,128)(2,1)} %get-tuple-element.67), channel_id=1, source_target_pairs={{8,0},{16,8},{24,16},{9,1},{17,9},{25,17},{10,2},{18,10},{26,18},{... | collective-permute-start | bytes 196616 | tf_op jit(solution)/shard_map/ppermute | solution.py:29
  23.5 30.7 %all-to-all-start = ((bf16[8,2,13824]{2,1,0:T(2,128)(2,1)}), bf16[8,2,13824]{2,1,0:T(2,128)(2,1)S(1)}, u32[]{:S(2)}, u32[]{:S(2)}) async-start(bf16[8,2,13824]{2,1,0:T(2,128)(2,1)} %reshape.137), calls=%async_computation | async-start | bytes 884736 | tf_op jit(solution)/shard_map/all_to_all | solution.py:158
  69.5 3.5 %copy-start = (bf16[8,256,1024]{2,1,0:T(8,128)(2,1)S(1)}, bf16[8,256,1024]{2,1,0:T(8,128)(2,1)}, u32[]{:S(2)}) copy-start(bf16[8,256,1024]{2,1,0:T(8,128)(2,1)} %all-gather.2.cloned.1.call-done) | copy-start | bytes 12582916
  69.5 4.3 %copy-start.1 = (bf16[4,9,32,1024]{3,2,1,0:T(8,128)(2,1)S(1)}, bf16[4,9,32,1024]{3,2,1,0:T(8,128)(2,1)}, u32[]{:S(2)}) copy-start(bf16[4,9,32,1024]{3,2,1,0:T(8,128)(2,1)} %copy.68) | copy-start | bytes 7077892
  73.8 1.7 %copy-start.2 = (bf16[4,9,32,1024]{3,2,1,0:T(8,128)(2,1)S(1)}, bf16[4,9,32,1024]{3,2,1,0:T(8,128)(2,1)}, u32[]{:S(2)}) copy-start(bf16[4,9,32,1024]{3,2,1,0:T(8,128)(2,1)} %copy.67) | copy-start | bytes 7077892
  76.5 23.5 %collective-permute-start.6 = (f32[224,256]{1,0:T(8,128)S(1)}, f32[224,256]{1,0:T(8,128)S(1)}, u32[]{:S(2)}, u32[]{:S(2)}) collective-permute-start(f32[224,256]{1,0:T(8,128)S(1)} %get-tuple-element.54), channel_id=1, source_target_pairs={{0,8},{8,0},{16,24},{24,16},{1,9},{9,1},{17,25},{25,17},{2,10},{10... | collective-permute-start | bytes 688136 | tf_op jit(solution)/shard_map/ppermute | solution.py:104
  78.0 26.6 %collective-permute-start.7 = (f32[224,256]{1,0:T(8,128)S(1)}, f32[224,256]{1,0:T(8,128)S(1)}, u32[]{:S(2)}, u32[]{:S(2)}) collective-permute-start(f32[224,256]{1,0:T(8,128)S(1)} %get-tuple-element.56), channel_id=1, source_target_pairs={{0,16},{8,24},{16,0},{24,8},{1,17},{9,25},{17,1},{25,9},{2,18},{10... | collective-permute-start | bytes 688136 | tf_op jit(solution)/shard_map/ppermute | solution.py:104
  79.5 26.4 %collective-permute-start.8 = (f32[224,256]{1,0:T(8,128)S(1)}, f32[224,256]{1,0:T(8,128)S(1)}, u32[]{:S(2)}, u32[]{:S(2)}) collective-permute-start(f32[224,256]{1,0:T(8,128)S(1)} %get-tuple-element.55), channel_id=1, source_target_pairs={{0,24},{8,16},{16,8},{24,0},{1,25},{9,17},{17,9},{25,1},{2,26},{10... | collective-permute-start | bytes 688136 | tf_op jit(solution)/shard_map/ppermute | solution.py:104
  87.8 21.3 %collective-permute-start = (f32[1,32,1024]{2,1,0:T(8,128)S(1)}, f32[1,32,1024]{2,1,0:T(8,128)S(1)}, u32[]{:S(2)}, u32[]{:S(2)}) collective-permute-start(f32[1,32,1024]{2,1,0:T(8,128)S(1)} %get-tuple-element.59), channel_id=1, source_target_pairs={{0,8},{8,16},{16,24},{1,9},{9,17},{17,25},{2,10},{10,18},{18,26},{... | collective-permute-start | bytes 393224 | tf_op jit(solution)/shard_map/ppermute | solution.py:138
  91.2 19.4 %collective-permute-start.1 = (f32[1,32,1024]{2,1,0:T(8,128)S(1)}, f32[1,32,1024]{2,1,0:T(8,128)S(1)}, u32[]{:S(2)}, u32[]{:S(2)}) collective-permute-start(f32[1,32,1024]{2,1,0:T(8,128)S(1)} %get-tuple-element.60), channel_id=1, source_target_pairs={{8,0},{16,8},{24,16},{9,1},{17,9},{25,17},{10,2},{18,10},{26,18},{... | collective-permute-start | bytes 393224 | tf_op jit(solution)/shard_map/ppermute | solution.py:139
  98.3 15.8 %copy-start.5 = (f32[32]{0:T(128)S(1)}, f32[32]{0:T(128)}, u32[]{:S(2)}) copy-start(f32[32]{0:T(128)} %param.8) | copy-start | bytes 388
  100.0 12.0 %collective-permute-start.2 = (f32[1,32,1024]{2,1,0:T(8,128)S(1)}, f32[1,32,1024]{2,1,0:T(8,128)S(1)}, u32[]{:S(2)}, u32[]{:S(2)}) collective-permute-start(f32[1,32,1024]{2,1,0:T(8,128)S(1)} %get-tuple-element.57), channel_id=1, source_target_pairs={{0,8},{8,16},{16,24},{1,9},{9,17},{17,25},{2,10},{10,18},{18,26},{... | collective-permute-start | bytes 393224 | tf_op jit(solution)/shard_map/ppermute | solution.py:138
  104.6 9.5 %collective-permute-start.3 = (f32[1,32,1024]{2,1,0:T(8,128)S(1)}, f32[1,32,1024]{2,1,0:T(8,128)S(1)}, u32[]{:S(2)}, u32[]{:S(2)}) collective-permute-start(f32[1,32,1024]{2,1,0:T(8,128)S(1)} %get-tuple-element.58), channel_id=1, source_target_pairs={{8,0},{16,8},{24,16},{9,1},{17,9},{25,17},{10,2},{18,10},{26,18},{... | collective-permute-start | bytes 393224 | tf_op jit(solution)/shard_map/ppermute | solution.py:139
  106.0 13.0 %collective-permute-start.9 = (f32[224,256]{1,0:T(8,128)S(1)}, f32[224,256]{1,0:T(8,128)S(1)}, u32[]{:S(2)}, u32[]{:S(2)}) collective-permute-start(f32[224,256]{1,0:T(8,128)S(1)} %fusion.73), channel_id=1, source_target_pairs={{0,8},{8,0},{16,24},{24,16},{1,9},{9,1},{17,25},{25,17},{2,10},{10... | collective-permute-start | bytes 688136 | tf_op jit(solution)/shard_map/ppermute | solution.py:106
  109.0 10.0 %collective-permute-start.10 = (f32[224,256]{1,0:T(8,128)S(1)}, f32[224,256]{1,0:T(8,128)S(1)}, u32[]{:S(2)}, u32[]{:S(2)}) collective-permute-start(f32[224,256]{1,0:T(8,128)S(1)} %fusion.73), channel_id=1, source_target_pairs={{0,16},{8,24},{16,0},{24,8},{1,17},{9,25},{17,1},{25,9},{2,18},{10... | collective-permute-start | bytes 688136 | tf_op jit(solution)/shard_map/ppermute | solution.py:106
  110.6 11.5 %collective-permute-start.11 = (f32[224,256]{1,0:T(8,128)S(1)}, f32[224,256]{1,0:T(8,128)S(1)}, u32[]{:S(2)}, u32[]{:S(2)}) collective-permute-start(f32[224,256]{1,0:T(8,128)S(1)} %fusion.73), channel_id=1, source_target_pairs={{0,24},{8,16},{16,8},{24,0},{1,25},{9,17},{17,9},{25,1},{2,26},{10... | collective-permute-start | bytes 688136 | tf_op jit(solution)/shard_map/ppermute | solution.py:106
Sparse Core Ops, SparseCore 0:
  10.3 59.2 all-gather.1

commit v6 on v5

--- a/solution.py
+++ b/solution.py
@@ -152,9 +152,8 @@
     grad_scale = 1.0 / math.sqrt(lax.axis_size("space") * depth_cells * plane_cells)
     inputs_planes = jnp.transpose(inputs, (1, 0, 2))
     grad_planes = jnp.transpose(output_grad, (1, 0, 2))
-    both = lax.all_gather(jnp.concatenate([inputs_planes, grad_planes]), "chan", axis=1, tiled=True)
-    gathered = both[:depth_cells]
-    grad_gathered = both[depth_cells:]
+    gathered = lax.all_gather(inputs_planes, "chan", axis=1, tiled=True)
+    grad_gathered = lax.all_gather(grad_planes, "chan", axis=1, tiled=True)
     weight_rows = lax.all_to_all(weight, "chan", 1, 2, tiled=True)
 
     weight_grid = weight.reshape(3, 9, channels_in, block_out)

time: 131 us -> 121 us (0.924)
  waiting for transfers between devices: 35 us -> 23.2 us
  local copies, waits for them, and re-layouts: 25.6 us -> 28.4 us
  starting transfers between devices: 31.8 us -> 29.8 us
  matrix products: 9.62 us -> 11.3 us
    all_gather x1 -> x2, waiting for transfers between devices: 11.2 us -> 2.25 us  [the longest x1 2.25 us: body(): grad_gathered = lax.all_gather(grad_planes, 'chan', axis=1, tiled=True)]
    all_to_all x1, waiting for transfers between devices: 15.8 us -> 11.5 us  [body(): weight_rows = lax.all_to_all(weight, 'chan', 1, 2, tiled=True)]
    dot_general x6, matrix products: 4.75 us -> 6.46 us  [depth_products(): jnp.einsum('ki,zin->zkn', weights[depth_index], planes, preferred_element...]
    ppermute x3, waiting for transfers between devices: 5.93 us -> 7.58 us  [all_reduce_direct(): lax.ppermute(reduced, axis, [(i, i ^ distance) for i in range(devices)])]
    squeeze x3, local copies, waits for them, and re-layouts: 1.15 us -> 2.51 us  [depth_products(): weights[depth_index]]
    unnamed x19 -> x31, local copies, waits for them, and re-layouts: 13.3 us -> 13.3 us
  transfers between devices with their start and end apart: 14 -> 15, of which waited for: 5 -> 5; matrix products, arithmetic and copies ran while one was open for 29% -> 40% of each run, Pallas kernels for 0% -> 0%
where the time goes in v6:
time: 121 us; the launch traced here: 120 us
  starting transfers between devices  29.8 us (25%)
  local copies, waits for them, and re-layouts  28.4 us (23%)
  waiting for transfers between devices  23.2 us (19%)
  between operations  14.6 us (12%)
  other arithmetic  13.2 us (11%)
  matrix products  11.3 us (9%)
    unnamed x31, local copies, waits for them, and re-layouts  13.3 us
    all_to_all x1, waiting for transfers between devices, body(): weight_rows = lax.all_to_all(weight, 'chan', 1, 2, tiled=True)  11.5 us
    ppermute x3, waiting for transfers between devices, all_reduce_direct(): lax.ppermute(reduced, axis, [(i, i ^ distance) for i in range(devices)])  7.58 us
    ppermute x2, starting transfers between devices, settle_rims(): from_below = lax.ppermute(field[depth + 1:], 'space', up)  6.87 us
    dot_general x6, matrix products, depth_products(): jnp.einsum('ki,zin->zkn', weights[depth_index], planes, preferred_element...  6.46 us
    slice x4, local copies, waits for them, and re-layouts, body(): grad_shifted[2 - depth_index:2 - depth_index + depth_cells]  6.21 us
    ppermute x1, starting transfers between devices, padded_2(): before = lax.ppermute(last, axis, up)  5.46 us
    ppermute x3, starting transfers between devices, all_reduce_direct(): lax.ppermute(reduced, axis, [(i, i ^ distance) for i in range(devices)])  5.14 us
  transfers between devices with their start and end apart: 15, of which 5 were waited for; matrix products, arithmetic and copies ran while one was open for 40% of the time, Pallas kernels for 0%

profile of v6, /device:TPU:0, one launch (start us, length us, event | category | flops | bytes accessed | tf_op | source)
XLA Modules:
  0.0 120.4 jit_solution(10582914548342873684)
XLA Ops:
  7.2 1.7 %copy.104 = bf16[32,4,1024]{2,0,1:T(8,128)(2,1)} copy(bf16[32,4,1024]{2,1,0:T(4,128)(2,1)} %param.6) | data formatting | bytes 524288 | tf_op args[0]
  9.0 1.1 copy.105
  10.8 5.5 %collective-permute-start.4 = (bf16[1,32,1024]{2,1,0:T(8,128)(2,1)}, bf16[1,32,1024]{2,1,0:T(8,128)(2,1)}, u32[]{:S(2)}, u32[]{:S(2)}) collective-permute-start(bf16[1,32,1024]{2,1,0:T(8,128)(2,1)} %get-tuple-element.66), channel_id=1, source_target_pairs={{0,8},{8,16},{16,24},{1,9},{9,17},{17,25},{2,10},{10,18},{18,26},{... | collective-permute-start | bytes 196616 | tf_op jit(solution)/shard_map/ppermute | solution.py:28
  16.3 1.3 %collective-permute-start.5 = (bf16[1,32,1024]{2,1,0:T(8,128)(2,1)}, bf16[1,32,1024]{2,1,0:T(8,128)(2,1)}, u32[]{:S(2)}, u32[]{:S(2)}) collective-permute-start(bf16[1,32,1024]{2,1,0:T(8,128)(2,1)} %get-tuple-element.67), channel_id=1, source_target_pairs={{8,0},{16,8},{24,16},{9,1},{17,9},{25,17},{10,2},{18,10},{26,18},{... | collective-permute-start | bytes 196616 | tf_op jit(solution)/shard_map/ppermute | solution.py:29
  17.6 3.9 %copy.63 = bf16[27,256,32]{2,0,1:T(8,128)(2,1)S(1)} copy(bf16[27,256,32]{1,2,0:T(8,128)(2,1)} %param.7) | data formatting | bytes 884736 | tf_op args[1]
  21.5 2.1 %reshape.137 = bf16[8,2,13824]{2,1,0:T(2,128)(2,1)} reshape(bf16[256,27,32]{2,1,0:T(8,128)(2,1)S(1)} %bitcast.235) | data formatting | bytes 884736
  23.6 4.9 %all-to-all-start = ((bf16[8,2,13824]{2,1,0:T(2,128)(2,1)}), bf16[8,2,13824]{2,1,0:T(2,128)(2,1)S(1)}, u32[]{:S(2)}, u32[]{:S(2)}) async-start(bf16[8,2,13824]{2,1,0:T(2,128)(2,1)} %reshape.137), calls=%async_computation | async-start | bytes 884736 | tf_op jit(solution)/shard_map/all_to_all | solution.py:157
  29.5 1.1 fusion.43
  31.2 0.9 fusion.60
  32.8 1.0 fusion.79
  33.9 1.7 %copy.78 = bf16[4,9,32,1024]{3,2,1,0:T(8,128)(2,1)} copy(bf16[4,9,32,1024]{3,2,0,1:T(8,128)(2,1)S(1)} %get-tuple-element.45) | data formatting | bytes 4718592 | tf_op jit(solution)/shard_map/slice | solution.py:178
  35.6 1.7 %copy.77 = bf16[4,9,32,1024]{3,2,1,0:T(8,128)(2,1)} copy(bf16[4,9,32,1024]{3,2,0,1:T(8,128)(2,1)S(1)} %get-tuple-element.46) | data formatting | bytes 4718592 | tf_op jit(solution)/shard_map/slice | solution.py:178
  37.3 1.7 %copy.76 = bf16[4,9,32,1024]{3,2,1,0:T(8,128)(2,1)} copy(bf16[4,9,32,1024]{3,2,0,1:T(8,128)(2,1)S(1)} %get-tuple-element.44) | data formatting | bytes 4718592 | tf_op jit(solution)/shard_map/slice | solution.py:178
  39.0 11.5 %all-to-all-done = bf16[8,2,13824]{2,1,0:T(2,128)(2,1)S(1)} async-done(((bf16[8,2,13824]{2,1,0:T(2,128)(2,1)}), bf16[8,2,13824]{2,1,0:T(2,128)(2,1)S(1)}, u32[]{:S(2)}, u32[]{:S(2)}) %all-to-all-start) | async-done | bytes 442400 | tf_op jit(solution)/shard_map/all_to_all | solution.py:157
  50.5 1.6 %reshape.138 = bf16[256,27,32]{2,1,0:T(8,128)(2,1)S(1)} reshape(bf16[8,2,13824]{2,1,0:T(2,128)(2,1)S(1)} %all-to-all-done) | data formatting | bytes 884736
  52.1 1.2 copy.103
  53.8 1.1 reshape.129
  54.9 1.1 reshape.128
  56.0 3.3 %convolution_bitcast_fusion.6 = f32[1,288,256]{2,1,0:T(8,128)S(1)} fusion(bf16[4,288,1024]{2,1,0:T(8,128)(2,1)} %bitcast.245, bf16[4,256,1024]{2,1,0:T(8,128)(2,1)} %all-gather.3.cloned.1.call-done), kind=kOutput, calls=%fused_computation.11 | convolution fusion | flops 603979776 | bytes 4751360 | tf_op jit(solution)/shard_map/zkn,zin->ki/dot_general | solution.py:176
  59.3 0.8 convolution_bitcast_fusion.7
  60.1 1.0 copy-done.5
  61.1 0.8 convolution_bitcast_fusion.8
  62.0 0.8 dynamic-slice_bitcast_fusion.6
  62.9 1.4 %collective-permute-start.6 = (f32[224,256]{1,0:T(8,128)}, f32[224,256]{1,0:T(8,128)S(1)}, u32[]{:S(2)}, u32[]{:S(2)}) collective-permute-start(f32[224,256]{1,0:T(8,128)} %get-tuple-element.54), channel_id=1, source_target_pairs={{0,8},{8,0},{16,24},{24,16},{1,9},{9,1},{17,25},{25,17},{2,10},{10... | collective-permute-start | bytes 688136 | tf_op jit(solution)/shard_map/ppermute | solution.py:104
  64.3 1.5 %collective-permute-start.7 = (f32[224,256]{1,0:T(8,128)}, f32[224,256]{1,0:T(8,128)S(1)}, u32[]{:S(2)}, u32[]{:S(2)}) collective-permute-start(f32[224,256]{1,0:T(8,128)} %get-tuple-element.56), channel_id=1, source_target_pairs={{0,16},{8,24},{16,0},{24,8},{1,17},{9,25},{17,1},{25,9},{2,18},{10... | collective-permute-start | bytes 688136 | tf_op jit(solution)/shard_map/ppermute | solution.py:104
  67.9 0.8 convolution_bitcast_fusion.5
  68.7 2.5 %pad_add_fusion.1 = f32[6,288,1024]{2,1,0:T(8,128)S(1)} fusion(f32[4,288,1024]{2,1,0:T(8,128)S(1)} %convolution_bitcast_fusion.3, f32[4,288,1024]{2,1,0:T(8,128)S(1)} %convolution_bitcast_fusion.4, f32[4,288,1024]{2,1,0:T(8,128)S(1)} %convolution_bitcast_fusion.5), kind=kLoop, calls=%fused_computation.1 | loop fusion | flops 3538944 | bytes 21233664 | tf_op jit(solution)/shard_map/add | solution.py:129
  71.2 1.1 slice_bitcast_fusion.9
  72.4 1.7 %fusion.10 = f32[6,32,1024]{2,1,0:T(8,128)S(1)} fusion(f32[6,32,1024]{2,1,0:T(8,128)S(1)} %get-tuple-element.43, f32[6,32,1024]{2,1,0:T(8,128)S(1)} %get-tuple-element.42, f32[6,32,1024]{2,1,0:T(8,128)S(1)} %get-tuple-element.41, f32[6,32,1024]{2,1,0:T(8,128)S(1)} %get-tuple-element.40, f32[6,32,1024]{2,1,0:T(8,128)S(1)} %get-tuple-element.39, ...), kind=kLoop, calls=%fused_computation.47 | loop fusion | flops 3342336 | bytes 7867392 | tf_op jit(solution)/shard_map/add | solution.py:119
  74.1 3.5 %collective-permute-start = (f32[1,32,1024]{2,1,0:T(8,128)S(1)}, f32[1,32,1024]{2,1,0:T(8,128)S(1)}, u32[]{:S(2)}, u32[]{:S(2)}) collective-permute-start(f32[1,32,1024]{2,1,0:T(8,128)S(1)} %get-tuple-element.59), channel_id=1, source_target_pairs={{0,8},{8,16},{16,24},{1,9},{9,17},{17,25},{2,10},{10,18},{18,26},{... | collective-permute-start | bytes 393224 | tf_op jit(solution)/shard_map/ppermute | solution.py:138
  77.6 1.3 %collective-permute-start.1 = (f32[1,32,1024]{2,1,0:T(8,128)S(1)}, f32[1,32,1024]{2,1,0:T(8,128)S(1)}, u32[]{:S(2)}, u32[]{:S(2)}) collective-permute-start(f32[1,32,1024]{2,1,0:T(8,128)S(1)} %get-tuple-element.60), channel_id=1, source_target_pairs={{8,0},{16,8},{24,16},{9,1},{17,9},{25,17},{10,2},{18,10},{26,18},{... | collective-permute-start | bytes 393224 | tf_op jit(solution)/shard_map/ppermute | solution.py:139
  78.9 2.3 %all-gather.5.cloned.1.call-done = bf16[4,256,1024]{2,1,0:T(8,128)(2,1)} async-done(((bf16[4,32,1024]{2,1,0:T(8,128)(2,1)}), bf16[4,256,1024]{2,1,0:T(8,128)(2,1)}) %all-gather.5.cloned.1.call-update) | async-done | bytes 2097168 | tf_op jit(solution)/shard_map/all_gather | solution.py:156
  81.1 2.5 %convolution_bitcast_fusion = f32[4,288,1024]{2,1,0:T(8,128)S(1)} fusion(bf16[288,256,1]{1,0,2:T(8,128)(2,1)S(1)} %reshape.130, bf16[4,256,1024]{2,1,0:T(8,128)(2,1)} %all-gather.5.cloned.1.call-done), kind=kOutput, calls=%fused_computation.2 | convolution fusion | flops 603979776 | bytes 6963200 | tf_op jit(solution)/shard_map/ki,zin->zkn/dot_general | solution.py:126
  83.7 0.8 convolution_bitcast_fusion.1
  85.4 2.3 %pad_add_fusion = f32[6,288,1024]{2,1,0:T(8,128)S(1)} fusion(f32[4,288,1024]{2,1,0:T(8,128)S(1)} %convolution_bitcast_fusion, f32[4,288,1024]{2,1,0:T(8,128)S(1)} %convolution_bitcast_fusion.1, f32[4,288,1024]{2,1,0:T(8,128)S(1)} %convolution_bitcast_fusion.2), kind=kLoop, calls=%fused_computation | loop fusion | flops 3538944 | bytes 21233664 | tf_op jit(solution)/shard_map/add | solution.py:129
  87.7 1.1 slice_bitcast_fusion
  88.8 1.7 %fusion.26 = f32[6,32,1024]{2,1,0:T(8,128)S(1)} fusion(f32[6,32,1024]{2,1,0:T(8,128)S(1)} %get-tuple-element.35, f32[6,32,1024]{2,1,0:T(8,128)S(1)} %get-tuple-element.34, f32[6,32,1024]{2,1,0:T(8,128)S(1)} %get-tuple-element.33, f32[6,32,1024]{2,1,0:T(8,128)S(1)} %get-tuple-element.32, f32[6,32,1024]{2,1,0:T(8,128)S(1)} %get-tuple-element.31, ...), kind=kLoop, calls=%fused_computation.63 | loop fusion | flops 3342336 | bytes 7867392 | tf_op jit(solution)/shard_map/add | solution.py:119
  90.5 3.4 %collective-permute-start.2 = (f32[1,32,1024]{2,1,0:T(8,128)S(1)}, f32[1,32,1024]{2,1,0:T(8,128)S(1)}, u32[]{:S(2)}, u32[]{:S(2)}) collective-permute-start(f32[1,32,1024]{2,1,0:T(8,128)S(1)} %get-tuple-element.57), channel_id=1, source_target_pairs={{0,8},{8,16},{16,24},{1,9},{9,17},{17,25},{2,10},{10,18},{18,26},{... | collective-permute-start | bytes 393224 | tf_op jit(solution)/shard_map/ppermute | solution.py:138
  93.9 1.3 %collective-permute-start.3 = (f32[1,32,1024]{2,1,0:T(8,128)S(1)}, f32[1,32,1024]{2,1,0:T(8,128)S(1)}, u32[]{:S(2)}, u32[]{:S(2)}) collective-permute-start(f32[1,32,1024]{2,1,0:T(8,128)S(1)} %get-tuple-element.58), channel_id=1, source_target_pairs={{8,0},{16,8},{24,16},{9,1},{17,9},{25,17},{10,2},{18,10},{26,18},{... | collective-permute-start | bytes 393224 | tf_op jit(solution)/shard_map/ppermute | solution.py:139
  95.3 2.7 %collective-permute-start.9 = (f32[224,256]{1,0:T(8,128)S(1)}, f32[224,256]{1,0:T(8,128)S(1)}, u32[]{:S(2)}, u32[]{:S(2)}) collective-permute-start(f32[224,256]{1,0:T(8,128)S(1)} %fusion.64), channel_id=1, source_target_pairs={{0,8},{8,0},{16,24},{24,16},{1,9},{9,1},{17,25},{25,17},{2,10},{10... | collective-permute-start | bytes 688136 | tf_op jit(solution)/shard_map/ppermute | solution.py:106
  98.0 1.5 %collective-permute-start.10 = (f32[224,256]{1,0:T(8,128)S(1)}, f32[224,256]{1,0:T(8,128)S(1)}, u32[]{:S(2)}, u32[]{:S(2)}) collective-permute-start(f32[224,256]{1,0:T(8,128)S(1)} %fusion.64), channel_id=1, source_target_pairs={{0,16},{8,24},{16,0},{24,8},{1,17},{9,25},{17,1},{25,9},{2,18},{10... | collective-permute-start | bytes 688136 | tf_op jit(solution)/shard_map/ppermute | solution.py:106
  99.5 1.0 collective-permute-start.11
  100.5 1.8 %collective-permute-done.3 = f32[1,32,1024]{2,1,0:T(8,128)S(1)} collective-permute-done((f32[1,32,1024]{2,1,0:T(8,128)S(1)}, f32[1,32,1024]{2,1,0:T(8,128)S(1)}, u32[]{:S(2)}, u32[]{:S(2)}) %collective-permute-start.3) | collective-permute-done | bytes 131104 | tf_op jit(solution)/shard_map/ppermute | solution.py:139
  102.5 0.9 copy.79
  103.4 0.9 copy.80
  104.4 2.9 %collective-permute-done.9 = f32[224,256]{1,0:T(8,128)S(1)} collective-permute-done((f32[224,256]{1,0:T(8,128)S(1)}, f32[224,256]{1,0:T(8,128)S(1)}, u32[]{:S(2)}, u32[]{:S(2)}) %collective-permute-start.9) | collective-permute-done | bytes 229408 | tf_op jit(solution)/shard_map/ppermute | solution.py:106
  107.2 4.7 %collective-permute-done.11 = f32[224,256]{1,0:T(8,128)S(1)} collective-permute-done((f32[224,256]{1,0:T(8,128)S(1)}, f32[224,256]{1,0:T(8,128)S(1)}, u32[]{:S(2)}, u32[]{:S(2)}) %collective-permute-start.11) | collective-permute-done | bytes 229408 | tf_op jit(solution)/shard_map/ppermute | solution.py:106
  112.6 1.0 pad_maximum_fusion.1
  (67 shorter events, 7.7 us)
Async XLA Ops:
  7.2 48.8 %all-gather.3.cloned.1.call-start = ((), (), s32[]{:S(2)}) async-start(), calls=%async_computation.1 | async-start | bytes 2359296 | tf_op jit(solution)/shard_map/all_gather | solution.py:155
  9.0 19.5 %copy-start.7 = (bf16[32,4,1024]{2,1,0:T(4,128)(2,1)S(1)}, bf16[32,4,1024]{2,1,0:T(4,128)(2,1)}, u32[]{:S(2)}) copy-start(bf16[32,4,1024]{2,1,0:T(4,128)(2,1)} %param.9) | copy-start | bytes 786436
  9.0 19.8 %copy-start.6 = (bf16[27,256,32]{1,2,0:T(8,128)(2,1)S(1)}, bf16[27,256,32]{1,2,0:T(8,128)(2,1)}, u32[]{:S(2)}) copy-start(bf16[27,256,32]{1,2,0:T(8,128)(2,1)} %param.7) | copy-start | bytes 1327108
  9.0 72.1 %all-gather.5.cloned.1.call-start = ((), (), s32[]{:S(2)}) async-start(), calls=%async_computation.2 | async-start | bytes 2359296 | tf_op jit(solution)/shard_map/all_gather | solution.py:156
  10.1 7.5 %copy-start.2 = (bf16[32,4,1024]{2,0,1:T(8,128)(2,1)}, bf16[32,4,1024]{2,0,1:T(8,128)(2,1)S(1)}, u32[]{:S(2)}) copy-start(bf16[32,4,1024]{2,0,1:T(8,128)(2,1)S(1)} %copy.105) | copy-start | bytes 786436
  10.8 18.6 %collective-permute-start.4 = (bf16[1,32,1024]{2,1,0:T(8,128)(2,1)}, bf16[1,32,1024]{2,1,0:T(8,128)(2,1)}, u32[]{:S(2)}, u32[]{:S(2)}) collective-permute-start(bf16[1,32,1024]{2,1,0:T(8,128)(2,1)} %get-tuple-element.66), channel_id=1, source_target_pairs={{0,8},{8,16},{16,24},{1,9},{9,17},{17,25},{2,10},{10,18},{18,26},{... | collective-permute-start | bytes 196616 | tf_op jit(solution)/shard_map/ppermute | solution.py:28
  16.3 13.2 %collective-permute-start.5 = (bf16[1,32,1024]{2,1,0:T(8,128)(2,1)}, bf16[1,32,1024]{2,1,0:T(8,128)(2,1)}, u32[]{:S(2)}, u32[]{:S(2)}) collective-permute-start(bf16[1,32,1024]{2,1,0:T(8,128)(2,1)} %get-tuple-element.67), channel_id=1, source_target_pairs={{8,0},{16,8},{24,16},{9,1},{17,9},{25,17},{10,2},{18,10},{26,18},{... | collective-permute-start | bytes 196616 | tf_op jit(solution)/shard_map/ppermute | solution.py:29
  17.6 11.9 %copy-start.3 = (bf16[32,4,1024]{2,0,1:T(8,128)(2,1)S(1)}, bf16[32,4,1024]{2,0,1:T(8,128)(2,1)}, u32[]{:S(2)}) copy-start(bf16[32,4,1024]{2,0,1:T(8,128)(2,1)} %copy-done.2) | copy-start | bytes 786436
  23.6 26.9 %all-to-all-start = ((bf16[8,2,13824]{2,1,0:T(2,128)(2,1)}), bf16[8,2,13824]{2,1,0:T(2,128)(2,1)S(1)}, u32[]{:S(2)}, u32[]{:S(2)}) async-start(bf16[8,2,13824]{2,1,0:T(2,128)(2,1)} %reshape.137), calls=%async_computation | async-start | bytes 884736 | tf_op jit(solution)/shard_map/all_to_all | solution.py:157
  54.9 4.3 %copy-start.4 = (bf16[4,9,32,1024]{3,2,1,0:T(8,128)(2,1)S(1)}, bf16[4,9,32,1024]{3,2,1,0:T(8,128)(2,1)}, u32[]{:S(2)}) copy-start(bf16[4,9,32,1024]{3,2,1,0:T(8,128)(2,1)} %copy.77) | copy-start | bytes 7077892
  56.0 3.3 %copy-start.1 = (bf16[4,256,1024]{2,1,0:T(8,128)(2,1)S(1)}, bf16[4,256,1024]{2,1,0:T(8,128)(2,1)}, u32[]{:S(2)}) copy-start(bf16[4,256,1024]{2,1,0:T(8,128)(2,1)} %all-gather.3.cloned.1.call-done) | copy-start | bytes 6291460
  59.2 1.8 %copy-start.5 = (bf16[4,9,32,1024]{3,2,1,0:T(8,128)(2,1)S(1)}, bf16[4,9,32,1024]{3,2,1,0:T(8,128)(2,1)}, u32[]{:S(2)}) copy-start(bf16[4,9,32,1024]{3,2,1,0:T(8,128)(2,1)} %copy.76) | copy-start | bytes 7077892
  62.9 27.7 %collective-permute-start.6 = (f32[224,256]{1,0:T(8,128)}, f32[224,256]{1,0:T(8,128)S(1)}, u32[]{:S(2)}, u32[]{:S(2)}) collective-permute-start(f32[224,256]{1,0:T(8,128)} %get-tuple-element.54), channel_id=1, source_target_pairs={{0,8},{8,0},{16,24},{24,16},{1,9},{9,1},{17,25},{25,17},{2,10},{10... | collective-permute-start | bytes 688136 | tf_op jit(solution)/shard_map/ppermute | solution.py:104
  64.3 29.6 %collective-permute-start.7 = (f32[224,256]{1,0:T(8,128)}, f32[224,256]{1,0:T(8,128)S(1)}, u32[]{:S(2)}, u32[]{:S(2)}) collective-permute-start(f32[224,256]{1,0:T(8,128)} %get-tuple-element.56), channel_id=1, source_target_pairs={{0,16},{8,24},{16,0},{24,8},{1,17},{9,25},{17,1},{25,9},{2,18},{10... | collective-permute-start | bytes 688136 | tf_op jit(solution)/shard_map/ppermute | solution.py:104
  65.8 29.5 %collective-permute-start.8 = (f32[224,256]{1,0:T(8,128)S(1)}, f32[224,256]{1,0:T(8,128)S(1)}, u32[]{:S(2)}, u32[]{:S(2)}) collective-permute-start(f32[224,256]{1,0:T(8,128)S(1)} %get-tuple-element.55), channel_id=1, source_target_pairs={{0,24},{8,16},{16,8},{24,0},{1,25},{9,17},{17,9},{25,1},{2,26},{10... | collective-permute-start | bytes 688136 | tf_op jit(solution)/shard_map/ppermute | solution.py:104
  74.1 9.6 %copy-start.8 = (bf16[288,256,1]{1,0,2:T(8,128)(2,1)S(1)}, bf16[288,256,1]{1,0,2:T(8,128)(2,1)}, u32[]{:S(2)}) copy-start(bf16[288,256,1]{1,0,2:T(8,128)(2,1)} %reshape.129) | copy-start | bytes 442372
  74.1 23.9 %collective-permute-start = (f32[1,32,1024]{2,1,0:T(8,128)S(1)}, f32[1,32,1024]{2,1,0:T(8,128)S(1)}, u32[]{:S(2)}, u32[]{:S(2)}) collective-permute-start(f32[1,32,1024]{2,1,0:T(8,128)S(1)} %get-tuple-element.59), channel_id=1, source_target_pairs={{0,8},{8,16},{16,24},{1,9},{9,17},{17,25},{2,10},{10,18},{18,26},{... | collective-permute-start | bytes 393224 | tf_op jit(solution)/shard_map/ppermute | solution.py:138
  77.6 21.9 %collective-permute-start.1 = (f32[1,32,1024]{2,1,0:T(8,128)S(1)}, f32[1,32,1024]{2,1,0:T(8,128)S(1)}, u32[]{:S(2)}, u32[]{:S(2)}) collective-permute-start(f32[1,32,1024]{2,1,0:T(8,128)S(1)} %get-tuple-element.60), channel_id=1, source_target_pairs={{8,0},{16,8},{24,16},{9,1},{17,9},{25,17},{10,2},{18,10},{26,18},{... | collective-permute-start | bytes 393224 | tf_op jit(solution)/shard_map/ppermute | solution.py:139
  81.1 2.5 %copy-start = (bf16[4,256,1024]{2,1,0:T(8,128)(2,1)S(1)}, bf16[4,256,1024]{2,1,0:T(8,128)(2,1)}, u32[]{:S(2)}) copy-start(bf16[4,256,1024]{2,1,0:T(8,128)(2,1)} %all-gather.5.cloned.1.call-done) | copy-start | bytes 6291460
  83.7 0.9 copy-start.9
  88.8 13.5 %copy-start.10 = (f32[32]{0:T(128)S(1)}, f32[32]{0:T(128)}, u32[]{:S(2)}) copy-start(f32[32]{0:T(128)} %param.8) | copy-start | bytes 388
  88.8 13.5 %copy-start.11 = (f32[4]{0:T(128)S(1)}, f32[4]{0:T(128)}, u32[]{:S(2)}) copy-start(f32[4]{0:T(128)} %pad.135.clone) | copy-start | bytes 52
  90.5 9.9 %collective-permute-start.2 = (f32[1,32,1024]{2,1,0:T(8,128)S(1)}, f32[1,32,1024]{2,1,0:T(8,128)S(1)}, u32[]{:S(2)}, u32[]{:S(2)}) collective-permute-start(f32[1,32,1024]{2,1,0:T(8,128)S(1)} %get-tuple-element.57), channel_id=1, source_target_pairs={{0,8},{8,16},{16,24},{1,9},{9,17},{17,25},{2,10},{10,18},{18,26},{... | collective-permute-start | bytes 393224 | tf_op jit(solution)/shard_map/ppermute | solution.py:138
  93.9 8.4 %collective-permute-start.3 = (f32[1,32,1024]{2,1,0:T(8,128)S(1)}, f32[1,32,1024]{2,1,0:T(8,128)S(1)}, u32[]{:S(2)}, u32[]{:S(2)}) collective-permute-start(f32[1,32,1024]{2,1,0:T(8,128)S(1)} %get-tuple-element.58), channel_id=1, source_target_pairs={{8,0},{16,8},{24,16},{9,1},{17,9},{25,17},{10,2},{18,10},{26,18},{... | collective-permute-start | bytes 393224 | tf_op jit(solution)/shard_map/ppermute | solution.py:139
  95.3 11.9 %collective-permute-start.9 = (f32[224,256]{1,0:T(8,128)S(1)}, f32[224,256]{1,0:T(8,128)S(1)}, u32[]{:S(2)}, u32[]{:S(2)}) collective-permute-start(f32[224,256]{1,0:T(8,128)S(1)} %fusion.64), channel_id=1, source_target_pairs={{0,8},{8,0},{16,24},{24,16},{1,9},{9,1},{17,25},{25,17},{2,10},{10... | collective-permute-start | bytes 688136 | tf_op jit(solution)/shard_map/ppermute | solution.py:106
  98.0 9.2 %collective-permute-start.10 = (f32[224,256]{1,0:T(8,128)S(1)}, f32[224,256]{1,0:T(8,128)S(1)}, u32[]{:S(2)}, u32[]{:S(2)}) collective-permute-start(f32[224,256]{1,0:T(8,128)S(1)} %fusion.64), channel_id=1, source_target_pairs={{0,16},{8,24},{16,0},{24,8},{1,17},{9,25},{17,1},{25,9},{2,18},{10... | collective-permute-start | bytes 688136 | tf_op jit(solution)/shard_map/ppermute | solution.py:106
  99.5 12.4 %collective-permute-start.11 = (f32[224,256]{1,0:T(8,128)S(1)}, f32[224,256]{1,0:T(8,128)S(1)}, u32[]{:S(2)}, u32[]{:S(2)}) collective-permute-start(f32[224,256]{1,0:T(8,128)S(1)} %fusion.64), channel_id=1, source_target_pairs={{0,24},{8,16},{16,8},{24,0},{1,25},{9,17},{17,9},{25,1},{2,26},{10... | collective-permute-start | bytes 688136 | tf_op jit(solution)/shard_map/ppermute | solution.py:106
Sparse Core Ops, SparseCore 0:
  10.2 41.2 all-gather.2
  53.6 27.4 all-gather.4

commit v7 on v4

--- a/solution.py
+++ b/solution.py
@@ -3,7 +3,7 @@
 import jax
 import jax.numpy as jnp
 from jax import lax
-from jax.sharding import PartitionSpec as P
+from jax.sharding import Mesh, PartitionSpec as P
 
 W = 64
 
@@ -112,6 +112,17 @@
     )
 
 
+def scatter_channels(blocks):
+    by_core = blocks.reshape(-1, 2, blocks.shape[1], blocks.shape[2])
+    core = lax.axis_index("core")
+    keep = lax.dynamic_index_in_dim(by_core, core, axis=1, keepdims=False)
+    send = lax.dynamic_index_in_dim(by_core, 1 - core, axis=1, keepdims=False)
+    partial = keep + lax.ppermute(send, "core", [(0, 1), (1, 0)])
+    return lax.psum_scatter(
+        partial.reshape(-1, blocks.shape[2]), "chips", scatter_dimension=0, tiled=True
+    )
+
+
 def body(inputs, weight, bias_term, output_grad):
     taps_total = weight.shape[0]
     channels_in = weight.shape[1]
@@ -122,7 +133,7 @@
     grad_scale = 1.0 / math.sqrt(lax.axis_size("space") * depth_cells * plane_cells)
     inputs_planes = jnp.transpose(inputs, (1, 0, 2))
     grad_planes = jnp.transpose(output_grad, (1, 0, 2))
-    gathered = lax.all_gather(inputs_planes, "chan", axis=1, tiled=True)
+    gathered = lax.all_gather(inputs_planes, ("chips", "core"), axis=1, tiled=True)
 
     weight_grid = weight.reshape(3, 9, channels_in, block_out)
     forward_weight = jnp.transpose(weight_grid, (0, 1, 3, 2)).reshape(3, 9 * block_out, channels_in)
@@ -181,7 +192,7 @@
     )
     bias_grad = reduced[taps_total * block_out, :block_out]
 
-    chan_devices = lax.axis_size("chan")
+    chan_devices = lax.axis_size("chips") * lax.axis_size("core")
     backward_weight = jnp.transpose(weight_grid, (0, 2, 1, 3)).reshape(
         3, chan_devices, channels_in // chan_devices, 9 * block_out
     )
@@ -194,24 +205,25 @@
             preferred_element_type=jnp.float32,
         )
         spread = part if spread is None else spread + part
-    summed = lax.psum_scatter(
-        spread.reshape(channels_in, depth_cells * plane_cells), "chan", scatter_dimension=0, tiled=True
-    )
+    summed = scatter_channels(spread.reshape(chan_devices, channels_in // chan_devices, depth_cells * plane_cells))
     input_grad = summed.astype(jnp.bfloat16).reshape(block_in, depth_cells, plane_cells)
     return (outputs, input_grad, weight_grad, bias_grad)
 
 
 def solution(mesh):
-    placed = (P("chan", "space", None), P(None, None, "chan"), P("chan"), P("chan", "space", None))
+    space_devices, chan_devices = mesh.shape["space"], mesh.shape["chan"]
+    split = Mesh(mesh.devices.reshape(space_devices, chan_devices // 2, 2), ("space", "chips", "core"))
+    chan = ("chips", "core")
+    placed = (P(chan, "space", None), P(None, None, chan), P(chan), P(chan, "space", None))
     return jax.shard_map(
         body,
-        mesh=mesh,
+        mesh=split,
         in_specs=placed,
         out_specs=(
-            P("chan", "space", None),
-            P("chan", "space", None),
-            P(None, None, "chan"),
-            P("chan"),
+            P(chan, "space", None),
+            P(chan, "space", None),
+            P(None, None, chan),
+            P(chan),
         ),
         check_vma=False,
     )

time: 109 us -> 108 us (level)
  waiting for transfers between devices: 31.6 us -> 19.2 us
  local copies, waits for them, and re-layouts: 22 us -> 26.8 us
  other arithmetic: 8.46 us -> 12.1 us
  starting transfers between devices: 19.5 us -> 21.5 us
  between operations: 14.5 us -> 15.9 us
    all_gather x1, waiting for transfers between devices: 8.88 us -> 0.02 us  [body(): lax.all_gather(inputs_planes, ('chips', 'core'), axis=1, tiled=True)]
    reduce_scatter x1, waiting for transfers between devices: 13 us -> 5.64 us  [scatter_channels(): lax.psum_scatter(partial.reshape(-1, blocks.shape[2]), 'chips', scatter_d...]
    unnamed x20 -> x19, local copies, waits for them, and re-layouts: 11.5 us -> 4.87 us
    another operation x0 -> x1, local copies, waits for them, and re-layouts: none -> 6.03 us  [scatter_channels(): by_core = blocks.reshape(-1, 2, blocks.shape[1], blocks.shape[2])]
    ppermute x0 -> x1, waiting for transfers between devices: none -> 4.19 us  [scatter_channels(): partial = keep + lax.ppermute(send, 'core', [(0, 1), (1, 0)])]
    add x0 -> x1, other arithmetic: none -> 3.83 us  [scatter_channels(): partial = keep + lax.ppermute(send, 'core', [(0, 1), (1, 0)])]
    squeeze x0 -> x1, local copies, waits for them, and re-layouts: none -> 3.25 us  [scatter_channels(): send = lax.dynamic_index_in_dim(by_core, 1 - core, axis=1, keepdims=False)]
    add x1, local copies, waits for them, and re-layouts: 2.9 us -> 4.93 us  [body(): spread = part if spread is None else spread + part]
  transfers between devices with their start and end apart: 12 -> 13, of which waited for: 5 -> 5; matrix products, arithmetic and copies ran while one was open for 35% -> 44% of each run, Pallas kernels for 0% -> 0%
where the time goes in v7:
time: 108 us
  local copies, waits for them, and re-layouts  26.8 us (25%)
  starting transfers between devices  21.5 us (20%)
  waiting for transfers between devices  19.2 us (18%)
  between operations  15.9 us (15%)
  matrix products  12.4 us (11%)
  other arithmetic  12.1 us (11%)
    ppermute x3, waiting for transfers between devices, all_reduce_direct(): lax.ppermute(reduced, axis, [(i, i ^ distance) for i in range(devices)])  7.44 us
    another operation x1, local copies, waits for them, and re-layouts, scatter_channels(): by_core = blocks.reshape(-1, 2, blocks.shape[1], blocks.shape[2])  6.03 us
    ppermute x3, starting transfers between devices, all_reduce_direct(): lax.ppermute(reduced, axis, [(i, i ^ distance) for i in range(devices)])  5.9 us
    dot_general x3, matrix products, body(): jnp.einsum('bjk,zkn->bjzn', backward_weight[depth_index], grad_shifted[2...  5.85 us
    reduce_scatter x1, waiting for transfers between devices, scatter_channels(): lax.psum_scatter(partial.reshape(-1, blocks.shape[2]), 'chips', scatter_d...  5.64 us
    ppermute x3, starting transfers between devices, all_reduce_direct(): reduced = reduced + lax.ppermute(send, axis, pairs)  4.99 us
    add x1, local copies, waits for them, and re-layouts, body(): spread = part if spread is None else spread + part  4.93 us
    unnamed x19, local copies, waits for them, and re-layouts  4.87 us
  transfers between devices with their start and end apart: 13, of which 5 were waited for; matrix products, arithmetic and copies ran while one was open for 44% of the time, Pallas kernels for 0%

profile of v7, /device:TPU:0, one launch (start us, length us, event | category | flops | bytes accessed | tf_op | source)
XLA Modules:
  0.0 107.9 jit_solution(14225902750862098537)
XLA Ops:
  8.0 1.0 copy.64
  9.1 4.8 %collective-permute-start.2 = (bf16[1,32,1024]{2,1,0:T(8,128)(2,1)S(1)}, bf16[1,32,1024]{2,1,0:T(8,128)(2,1)S(1)}, u32[]{:S(2)}, u32[]{:S(2)}) collective-permute-start(bf16[1,32,1024]{2,1,0:T(8,128)(2,1)S(1)} %get-tuple-element.48), channel_id=1, source_target_pairs={{0,8},{8,16},{16,24},{1,9},{9,17},{17,25},{2,10},{10,18},{18,26},{... | collective-permute-start | bytes 196616 | tf_op jit(solution)/shard_map/ppermute | solution.py:28
  14.0 1.3 %collective-permute-start.3 = (bf16[1,32,1024]{2,1,0:T(8,128)(2,1)S(1)}, bf16[1,32,1024]{2,1,0:T(8,128)(2,1)S(1)}, u32[]{:S(2)}, u32[]{:S(2)}) collective-permute-start(bf16[1,32,1024]{2,1,0:T(8,128)(2,1)S(1)} %get-tuple-element.49), channel_id=1, source_target_pairs={{8,0},{16,8},{24,16},{9,1},{17,9},{25,17},{10,2},{18,10},{26,18},{... | collective-permute-start | bytes 196616 | tf_op jit(solution)/shard_map/ppermute | solution.py:29
  15.3 1.7 %copy.63 = bf16[32,4,1024]{2,0,1:T(8,128)(2,1)} copy(bf16[32,4,1024]{2,1,0:T(4,128)(2,1)} %param.6) | data formatting | bytes 524288 | tf_op args[0]
  17.1 1.1 %fusion.67 = (bf16[1,256,9,32]{1,3,2,0:T(8,128)(2,1)S(1)}, bf16[1,256,9,32]{1,3,2,0:T(8,128)(2,1)S(1)}, bf16[1,256,9,32]{1,3,2,0:T(8,128)(2,1)S(1)}) fusion(bf16[3,256,9,32]{1,3,2,0:T(8,128)(2,1)} %bitcast.224), kind=kLoop, calls=%fused_computation.128 | loop fusion | bytes 884736 | tf_op jit(solution)/shard_map/slice | solution.py:203
  18.4 0.4 copy.43
  19.1 0.4 copy.41
  19.7 0.4 copy.45
  21.7 1.0 fusion.65
  23.0 0.3 copy.42
  23.3 0.3 copy.40
  23.7 1.8 %fusion.47 = f32[4,1024,8,32]{1,3,2,0:T(8,128)S(1)} fusion(bf16[4,288,1024,1]{2,1,3,0:T(8,128)(2,1)S(1)} %bitcast.213, bf16[8,32,288]{2,1,0:T(8,128)(2,1)S(1)} %copy.43), kind=kOutput, calls=%fused_computation.105 | convolution fusion | flops 603979776 | bytes 6701056 | tf_op jit(solution)/shard_map/bjk,zkn->bjzn/dot_general | solution.py:201
  25.7 1.7 %fusion.49 = f32[4,1024,8,32]{1,3,2,0:T(8,128)S(1)} fusion(bf16[4,288,1024,1]{2,1,3,0:T(8,128)(2,1)S(1)} %bitcast.215, bf16[8,32,288]{2,1,0:T(8,128)(2,1)S(1)} %copy.41), kind=kOutput, calls=%fused_computation.107 | convolution fusion | flops 603979776 | bytes 6701056 | tf_op jit(solution)/shard_map/bjk,zkn->bjzn/dot_general | solution.py:201
  27.5 2.3 %add_bitcast_fusion = f32[8,32,4,1024]{3,1,0,2:T(8,128)S(1)} fusion(f32[4,1024,8,32]{1,3,2,0:T(8,128)S(1)} %fusion.49, f32[4,1024,8,32]{1,3,2,0:T(8,128)S(1)} %fusion.47, bf16[4,288,1024,1]{2,1,3,0:T(8,128)(2,1)S(1)} %bitcast.211, bf16[8,32,288]{2,1,0:T(8,128)(2,1)S(1)} %copy.45), kind=kOutput, calls=%fused_computation.1 | convolution fusion | flops 606076928 | bytes 15089664 | tf_op jit(solution)/shard_map/bjk,zkn->bjzn/dot_general | solution.py:201
  29.8 4.9 %copy.46 = f32[8,32,4,1024]{3,2,1,0:T(4,128)} copy(f32[8,32,4,1024]{3,1,0,2:T(8,128)S(1)} %add_bitcast_fusion) | data formatting | bytes 8388608 | tf_op jit(solution)/shard_map/add | solution.py:207
  34.7 6.0 %reshape_reshape.3 = f32[4,2,32,4096]{3,2,1,0:T(8,128)} reshape(f32[8,32,4,1024]{3,2,1,0:T(4,128)} %copy.46) | data formatting | bytes 8388608 | tf_op jit(solution)/shard_map/reshape;reshape | solution.py:116
  40.8 3.3 %dynamic-slice_bitcast_fusion = f32[4,32,4096]{2,1,0:T(8,128)} fusion(f32[4,2,32,4096]{3,2,1,0:T(8,128)} %reshape_reshape.3, s32[]{:T(128)S(6)} %select_n.182), kind=kLoop, calls=%fused_computation.6 | loop fusion | bytes 4194308 | tf_op jit(solution)/shard_map/jit(dynamic_index_in_dim)/squeeze | solution.py:119
  44.1 0.3 convert_reduce_fusion
  44.5 4.2 %collective-permute-done.4 = f32[4,32,4096]{2,1,0:T(8,128)} collective-permute-done((f32[4,32,4096]{2,1,0:T(8,128)}, f32[4,32,4096]{2,1,0:T(8,128)}, u32[]{:S(2)}, u32[]{:S(2)}) %collective-permute-start.4) | collective-permute-done | bytes 2097184 | tf_op jit(solution)/shard_map/ppermute | solution.py:120
  48.7 3.8 %bitcast_add_fusion = f32[4,32,4096]{2,1,0:T(8,128)} fusion(f32[4,32,4096]{2,1,0:T(8,128)} %collective-permute-done.4, f32[4,2,32,4096]{3,2,1,0:T(8,128)} %reshape_reshape.3, s32[]{:T(128)S(6)} %select_n.181), kind=kLoop, calls=%fused_computation.5 | loop fusion | flops 524288 | bytes 6291460 | tf_op jit(solution)/shard_map/add | solution.py:120
  52.6 2.5 %convolution_bitcast_fusion.3 = f32[1,288,256]{2,1,0:T(8,128)S(1)} fusion(bf16[4,288,1024]{2,1,0:T(8,128)(2,1)S(1)} %bitcast.212, bf16[4,256,1024]{2,1,0:T(8,128)(2,1)} %all-gather.2.cloned.1.call-done), kind=kOutput, calls=%fused_computation.9 | convolution fusion | flops 603979776 | bytes 4751360 | tf_op jit(solution)/shard_map/zkn,zin->ki/dot_general | solution.py:174
  55.2 0.3 copy-done.2
  55.5 0.8 convolution_bitcast_fusion.4
  56.3 0.6 copy-done.4
  56.9 0.8 convolution_bitcast_fusion.5
  57.9 2.7 %collective-permute-start.5 = (f32[224,256]{1,0:T(8,128)S(1)}, f32[224,256]{1,0:T(8,128)S(1)}, u32[]{:S(2)}, u32[]{:S(2)}) collective-permute-start(f32[224,256]{1,0:T(8,128)S(1)} %get-tuple-element.35), channel_id=1, source_target_pairs={{0,8},{8,0},{16,24},{24,16},{1,9},{9,1},{17,25},{25,17},{2,10},{10... | collective-permute-start | bytes 688136 | tf_op jit(solution)/shard_map/ppermute | solution.py:104
  60.6 1.5 %collective-permute-start.6 = (f32[224,256]{1,0:T(8,128)S(1)}, f32[224,256]{1,0:T(8,128)S(1)}, u32[]{:S(2)}, u32[]{:S(2)}) collective-permute-start(f32[224,256]{1,0:T(8,128)S(1)} %get-tuple-element.37), channel_id=1, source_target_pairs={{0,16},{8,24},{16,0},{24,8},{1,17},{9,25},{17,1},{25,9},{2,18},{10... | collective-permute-start | bytes 688136 | tf_op jit(solution)/shard_map/ppermute | solution.py:104
  62.1 0.8 collective-permute-start.7
  62.9 0.8 convolution_bitcast_fusion
  63.7 0.8 convolution_bitcast_fusion.1
  64.5 0.8 convolution_bitcast_fusion.2
  65.3 2.3 %pad_add_fusion = f32[6,288,1024]{2,1,0:T(8,128)S(1)} fusion(f32[4,288,1024]{2,1,0:T(8,128)S(1)} %convolution_bitcast_fusion, f32[4,288,1024]{2,1,0:T(8,128)S(1)} %convolution_bitcast_fusion.1, f32[4,288,1024]{2,1,0:T(8,128)S(1)} %convolution_bitcast_fusion.2), kind=kLoop, calls=%fused_computation | loop fusion | flops 3538944 | bytes 21233664 | tf_op jit(solution)/shard_map/add | solution.py:149
  67.6 1.1 %slice_bitcast_fusion = (f32[6,32,1024]{2,1,0:T(8,128)S(1)}, f32[6,32,1024]{2,1,0:T(8,128)S(1)}, f32[6,32,1024]{2,1,0:T(8,128)S(1)}, f32[6,32,1024]{2,1,0:T(8,12...) fusion(f32[6,9,32,1024]{3,2,1,0:T(8,128)S(1)} %bitcast.209), kind=kLoop, calls=%fused_computation.45 | loop fusion | bytes 12582912 | tf_op jit(solution)/shard_map/squeeze | solution.py:153
  68.7 1.7 %fusion.10 = f32[6,32,1024]{2,1,0:T(8,128)S(1)} fusion(f32[6,32,1024]{2,1,0:T(8,128)S(1)} %get-tuple-element.27, f32[6,32,1024]{2,1,0:T(8,128)S(1)} %get-tuple-element.26, f32[6,32,1024]{2,1,0:T(8,128)S(1)} %get-tuple-element.25, f32[6,32,1024]{2,1,0:T(8,128)S(1)} %get-tuple-element.24, f32[6,32,1024]{2,1,0:T(8,128)S(1)} %get-tuple-element.23, ...), kind=kLoop, calls=%fused_computation.37 | loop fusion | flops 3342336 | bytes 7867392 | tf_op jit(solution)/shard_map/add | solution.py:154
  70.4 3.1 %collective-permute-start = (f32[1,32,1024]{2,1,0:T(8,128)S(1)}, f32[1,32,1024]{2,1,0:T(8,128)S(1)}, u32[]{:S(2)}, u32[]{:S(2)}) collective-permute-start(f32[1,32,1024]{2,1,0:T(8,128)S(1)} %get-tuple-element.38), channel_id=1, source_target_pairs={{0,8},{8,16},{16,24},{1,9},{9,17},{17,25},{2,10},{10,18},{18,26},{... | collective-permute-start | bytes 393224 | tf_op jit(solution)/shard_map/ppermute | solution.py:158
  73.5 1.3 %collective-permute-start.1 = (f32[1,32,1024]{2,1,0:T(8,128)S(1)}, f32[1,32,1024]{2,1,0:T(8,128)S(1)}, u32[]{:S(2)}, u32[]{:S(2)}) collective-permute-start(f32[1,32,1024]{2,1,0:T(8,128)S(1)} %get-tuple-element.39), channel_id=1, source_target_pairs={{8,0},{16,8},{24,16},{9,1},{17,9},{25,17},{10,2},{18,10},{26,18},{... | collective-permute-start | bytes 393224 | tf_op jit(solution)/shard_map/ppermute | solution.py:159
  74.9 3.0 %collective-permute-start.8 = (f32[224,256]{1,0:T(8,128)S(1)}, f32[224,256]{1,0:T(8,128)S(1)}, u32[]{:S(2)}, u32[]{:S(2)}) collective-permute-start(f32[224,256]{1,0:T(8,128)S(1)} %fusion.45), channel_id=1, source_target_pairs={{0,8},{8,0},{16,24},{24,16},{1,9},{9,1},{17,25},{25,17},{2,10},{10... | collective-permute-start | bytes 688136 | tf_op jit(solution)/shard_map/ppermute | solution.py:106
  77.9 1.5 %collective-permute-start.9 = (f32[224,256]{1,0:T(8,128)S(1)}, f32[224,256]{1,0:T(8,128)S(1)}, u32[]{:S(2)}, u32[]{:S(2)}) collective-permute-start(f32[224,256]{1,0:T(8,128)S(1)} %fusion.45), channel_id=1, source_target_pairs={{0,16},{8,24},{16,0},{24,8},{1,17},{9,25},{17,1},{25,9},{2,18},{10... | collective-permute-start | bytes 688136 | tf_op jit(solution)/shard_map/ppermute | solution.py:106
  79.4 1.4 %collective-permute-start.10 = (f32[224,256]{1,0:T(8,128)S(1)}, f32[224,256]{1,0:T(8,128)S(1)}, u32[]{:S(2)}, u32[]{:S(2)}) collective-permute-start(f32[224,256]{1,0:T(8,128)S(1)} %fusion.45), channel_id=1, source_target_pairs={{0,24},{8,16},{16,8},{24,0},{1,25},{9,17},{17,9},{25,1},{2,26},{10... | collective-permute-start | bytes 688136 | tf_op jit(solution)/shard_map/ppermute | solution.py:106
  80.8 1.9 %collective-permute-done.1 = f32[1,32,1024]{2,1,0:T(8,128)S(1)} collective-permute-done((f32[1,32,1024]{2,1,0:T(8,128)S(1)}, f32[1,32,1024]{2,1,0:T(8,128)S(1)}, u32[]{:S(2)}, u32[]{:S(2)}) %collective-permute-start.1) | collective-permute-done | bytes 131104 | tf_op jit(solution)/shard_map/ppermute | solution.py:159
  82.8 0.9 copy.47
  83.8 3.9 %collective-permute-done.8 = f32[224,256]{1,0:T(8,128)S(1)} collective-permute-done((f32[224,256]{1,0:T(8,128)S(1)}, f32[224,256]{1,0:T(8,128)S(1)}, u32[]{:S(2)}, u32[]{:S(2)}) %collective-permute-start.8) | collective-permute-done | bytes 229408 | tf_op jit(solution)/shard_map/ppermute | solution.py:106
  87.6 3.6 %collective-permute-done.10 = f32[224,256]{1,0:T(8,128)S(1)} collective-permute-done((f32[224,256]{1,0:T(8,128)S(1)}, f32[224,256]{1,0:T(8,128)S(1)}, u32[]{:S(2)}, u32[]{:S(2)}) %collective-permute-start.10) | collective-permute-done | bytes 229408 | tf_op jit(solution)/shard_map/ppermute | solution.py:106
  91.3 1.0 pad_maximum_fusion.1
  92.3 0.5 slice_bitcast_fusion.9
  92.8 5.6 %reduce-scatter.2.cloned.1.call-done = f32[32,4096]{1,0:T(8,128)} async-done(((f32[128,4096]{1,0:T(8,128)}), f32[32,4096]{1,0:T(8,128)}) %reduce-scatter.2.cloned.1.call-update) | async-done | bytes 524304 | tf_op jit(solution)/shard_map/reduce_scatter | solution.py:121
  98.5 1.1 convert_element_type.36
  99.5 0.9 reshape.124
  (55 shorter events, 3.6 us)
Async XLA Ops:
  8.0 44.6 %all-gather.2.cloned.1.call-start = ((), (), s32[]{:S(2)}) async-start(), calls=%async_computation.1 | async-start | bytes 2359296 | tf_op jit(solution)/shard_map/all_gather | solution.py:136
  9.1 11.0 %collective-permute-start.2 = (bf16[1,32,1024]{2,1,0:T(8,128)(2,1)S(1)}, bf16[1,32,1024]{2,1,0:T(8,128)(2,1)S(1)}, u32[]{:S(2)}, u32[]{:S(2)}) collective-permute-start(bf16[1,32,1024]{2,1,0:T(8,128)(2,1)S(1)} %get-tuple-element.48), channel_id=1, source_target_pairs={{0,8},{8,16},{16,24},{1,9},{9,17},{17,25},{2,10},{10,18},{18,26},{... | collective-permute-start | bytes 196616 | tf_op jit(solution)/shard_map/ppermute | solution.py:28
  14.0 6.2 %collective-permute-start.3 = (bf16[1,32,1024]{2,1,0:T(8,128)(2,1)S(1)}, bf16[1,32,1024]{2,1,0:T(8,128)(2,1)S(1)}, u32[]{:S(2)}, u32[]{:S(2)}) collective-permute-start(bf16[1,32,1024]{2,1,0:T(8,128)(2,1)S(1)} %get-tuple-element.49), channel_id=1, source_target_pairs={{8,0},{16,8},{24,16},{9,1},{17,9},{25,17},{10,2},{18,10},{26,18},{... | collective-permute-start | bytes 196616 | tf_op jit(solution)/shard_map/ppermute | solution.py:29
  17.0 81.5 %reduce-scatter.2.cloned.1.call-start = ((), (), s32[]{:S(2)}) async-start(), calls=%async_computation.2 | async-start | bytes 2621440 | tf_op jit(solution)/shard_map/reduce_scatter | solution.py:121
  23.3 2.1 %copy-start.1 = (bf16[4,9,32,1024]{3,2,1,0:T(8,128)(2,1)}, bf16[4,9,32,1024]{3,2,1,0:T(8,128)(2,1)S(1)}, u32[]{:S(2)}) copy-start(bf16[4,9,32,1024]{3,2,1,0:T(8,128)(2,1)S(1)} %copy.42) | copy-start | bytes 7077892
  23.7 2.0 %copy-start.3 = (bf16[4,9,32,1024]{3,2,1,0:T(8,128)(2,1)}, bf16[4,9,32,1024]{3,2,1,0:T(8,128)(2,1)S(1)}, u32[]{:S(2)}) copy-start(bf16[4,9,32,1024]{3,2,1,0:T(8,128)(2,1)S(1)} %copy.40) | copy-start | bytes 7077892
  40.8 3.3 %copy-start.6 = (bf16[32,4,1024]{2,1,0:T(4,128)(2,1)S(1)}, bf16[32,4,1024]{2,1,0:T(4,128)(2,1)}, u32[]{:S(2)}) copy-start(bf16[32,4,1024]{2,1,0:T(4,128)(2,1)} %param.9) | copy-start | bytes 786436
  40.8 3.7 %copy-start.5 = (bf16[27,256,32]{1,2,0:T(8,128)(2,1)S(1)}, bf16[27,256,32]{1,2,0:T(8,128)(2,1)}, u32[]{:S(2)}) copy-start(bf16[27,256,32]{1,2,0:T(8,128)(2,1)} %param.7) | copy-start | bytes 1327108
  44.0 4.6 %collective-permute-start.4 = (f32[4,32,4096]{2,1,0:T(8,128)}, f32[4,32,4096]{2,1,0:T(8,128)}, u32[]{:S(2)}, u32[]{:S(2)}) collective-permute-start(f32[4,32,4096]{2,1,0:T(8,128)} %dynamic-slice_bitcast_fusion), channel_id=1, source_target_pairs={{0,1},{1,0},{2,3},{3,2},{4,5},{5,4},{6,7},{7,6},{8,9},{9,8},{10,11... | collective-permute-start | bytes 6291464 | tf_op jit(solution)/shard_map/ppermute | solution.py:120
  52.6 2.6 %copy-start = (bf16[4,256,1024]{2,1,0:T(8,128)(2,1)S(1)}, bf16[4,256,1024]{2,1,0:T(8,128)(2,1)}, u32[]{:S(2)}) copy-start(bf16[4,256,1024]{2,1,0:T(8,128)(2,1)} %all-gather.2.cloned.1.call-done) | copy-start | bytes 6291460
  52.6 2.9 %copy-start.2 = (bf16[4,9,32,1024]{3,2,1,0:T(8,128)(2,1)S(1)}, bf16[4,9,32,1024]{3,2,1,0:T(8,128)(2,1)}, u32[]{:S(2)}) copy-start(bf16[4,9,32,1024]{3,2,1,0:T(8,128)(2,1)} %copy-done.1) | copy-start | bytes 7077892
  55.1 1.8 %copy-start.4 = (bf16[4,9,32,1024]{3,2,1,0:T(8,128)(2,1)S(1)}, bf16[4,9,32,1024]{3,2,1,0:T(8,128)(2,1)}, u32[]{:S(2)}) copy-start(bf16[4,9,32,1024]{3,2,1,0:T(8,128)(2,1)} %copy-done.3) | copy-start | bytes 7077892
  57.9 16.9 %collective-permute-start.5 = (f32[224,256]{1,0:T(8,128)S(1)}, f32[224,256]{1,0:T(8,128)S(1)}, u32[]{:S(2)}, u32[]{:S(2)}) collective-permute-start(f32[224,256]{1,0:T(8,128)S(1)} %get-tuple-element.35), channel_id=1, source_target_pairs={{0,8},{8,0},{16,24},{24,16},{1,9},{9,1},{17,25},{25,17},{2,10},{10... | collective-permute-start | bytes 688136 | tf_op jit(solution)/shard_map/ppermute | solution.py:104
  60.6 14.2 %collective-permute-start.6 = (f32[224,256]{1,0:T(8,128)S(1)}, f32[224,256]{1,0:T(8,128)S(1)}, u32[]{:S(2)}, u32[]{:S(2)}) collective-permute-start(f32[224,256]{1,0:T(8,128)S(1)} %get-tuple-element.37), channel_id=1, source_target_pairs={{0,16},{8,24},{16,0},{24,8},{1,17},{9,25},{17,1},{25,9},{2,18},{10... | collective-permute-start | bytes 688136 | tf_op jit(solution)/shard_map/ppermute | solution.py:104
  62.1 12.7 %collective-permute-start.7 = (f32[224,256]{1,0:T(8,128)S(1)}, f32[224,256]{1,0:T(8,128)S(1)}, u32[]{:S(2)}, u32[]{:S(2)}) collective-permute-start(f32[224,256]{1,0:T(8,128)S(1)} %get-tuple-element.36), channel_id=1, source_target_pairs={{0,24},{8,16},{16,8},{24,0},{1,25},{9,17},{17,9},{25,1},{2,26},{10... | collective-permute-start | bytes 688136 | tf_op jit(solution)/shard_map/ppermute | solution.py:104
  68.7 14.0 %copy-start.7 = (f32[32]{0:T(128)S(1)}, f32[32]{0:T(128)}, u32[]{:S(2)}) copy-start(f32[32]{0:T(128)} %param.8) | copy-start | bytes 388
  70.4 10.4 %collective-permute-start = (f32[1,32,1024]{2,1,0:T(8,128)S(1)}, f32[1,32,1024]{2,1,0:T(8,128)S(1)}, u32[]{:S(2)}, u32[]{:S(2)}) collective-permute-start(f32[1,32,1024]{2,1,0:T(8,128)S(1)} %get-tuple-element.38), channel_id=1, source_target_pairs={{0,8},{8,16},{16,24},{1,9},{9,17},{17,25},{2,10},{10,18},{18,26},{... | collective-permute-start | bytes 393224 | tf_op jit(solution)/shard_map/ppermute | solution.py:158
  73.5 9.2 %collective-permute-start.1 = (f32[1,32,1024]{2,1,0:T(8,128)S(1)}, f32[1,32,1024]{2,1,0:T(8,128)S(1)}, u32[]{:S(2)}, u32[]{:S(2)}) collective-permute-start(f32[1,32,1024]{2,1,0:T(8,128)S(1)} %get-tuple-element.39), channel_id=1, source_target_pairs={{8,0},{16,8},{24,16},{9,1},{17,9},{25,17},{10,2},{18,10},{26,18},{... | collective-permute-start | bytes 393224 | tf_op jit(solution)/shard_map/ppermute | solution.py:159
  74.9 12.7 %collective-permute-start.8 = (f32[224,256]{1,0:T(8,128)S(1)}, f32[224,256]{1,0:T(8,128)S(1)}, u32[]{:S(2)}, u32[]{:S(2)}) collective-permute-start(f32[224,256]{1,0:T(8,128)S(1)} %fusion.45), channel_id=1, source_target_pairs={{0,8},{8,0},{16,24},{24,16},{1,9},{9,1},{17,25},{25,17},{2,10},{10... | collective-permute-start | bytes 688136 | tf_op jit(solution)/shard_map/ppermute | solution.py:106
  77.9 9.7 %collective-permute-start.9 = (f32[224,256]{1,0:T(8,128)S(1)}, f32[224,256]{1,0:T(8,128)S(1)}, u32[]{:S(2)}, u32[]{:S(2)}) collective-permute-start(f32[224,256]{1,0:T(8,128)S(1)} %fusion.45), channel_id=1, source_target_pairs={{0,16},{8,24},{16,0},{24,8},{1,17},{9,25},{17,1},{25,9},{2,18},{10... | collective-permute-start | bytes 688136 | tf_op jit(solution)/shard_map/ppermute | solution.py:106
  79.4 11.7 %collective-permute-start.10 = (f32[224,256]{1,0:T(8,128)S(1)}, f32[224,256]{1,0:T(8,128)S(1)}, u32[]{:S(2)}, u32[]{:S(2)}) collective-permute-start(f32[224,256]{1,0:T(8,128)S(1)} %fusion.45), channel_id=1, source_target_pairs={{0,24},{8,16},{16,8},{24,0},{1,25},{9,17},{17,9},{25,1},{2,26},{10... | collective-permute-start | bytes 688136 | tf_op jit(solution)/shard_map/ppermute | solution.py:106
Sparse Core Ops, SparseCore 0:
  17.1 31.4 all-gather.1
Sparse Core Ops, SparseCore 1:
  52.6 45.8 reduce-scatter.1

commit v8 on v7

--- a/solution.py
+++ b/solution.py
@@ -113,13 +113,13 @@
 
 
 def scatter_channels(blocks):
-    by_core = blocks.reshape(-1, 2, blocks.shape[1], blocks.shape[2])
+    by_core = blocks.reshape((-1, 2) + blocks.shape[1:])
     core = lax.axis_index("core")
     keep = lax.dynamic_index_in_dim(by_core, core, axis=1, keepdims=False)
     send = lax.dynamic_index_in_dim(by_core, 1 - core, axis=1, keepdims=False)
     partial = keep + lax.ppermute(send, "core", [(0, 1), (1, 0)])
     return lax.psum_scatter(
-        partial.reshape(-1, blocks.shape[2]), "chips", scatter_dimension=0, tiled=True
+        partial.reshape(-1, blocks.shape[-1]), "chips", scatter_dimension=0, tiled=True
     )
 
 
@@ -199,14 +199,14 @@
     spread = None
     for depth_index in range(3):
         part = jnp.einsum(
-            "bjk,zkn->bjzn",
+            "bjk,zkn->bzjn",
             backward_weight[depth_index],
             grad_shifted[2 - depth_index : 2 - depth_index + depth_cells],
             preferred_element_type=jnp.float32,
         )
         spread = part if spread is None else spread + part
-    summed = scatter_channels(spread.reshape(chan_devices, channels_in // chan_devices, depth_cells * plane_cells))
-    input_grad = summed.astype(jnp.bfloat16).reshape(block_in, depth_cells, plane_cells)
+    summed = scatter_channels(spread).reshape(depth_cells, block_in, plane_cells)
+    input_grad = jnp.transpose(summed.astype(jnp.bfloat16), (1, 0, 2))
     return (outputs, input_grad, weight_grad, bias_grad)
 
 

time: 108 us -> 98.5 us (0.912)
  local copies, waits for them, and re-layouts: 26.8 us -> 17.1 us
  starting transfers between devices: 21.5 us -> 19.3 us
  waiting for transfers between devices: 19.2 us -> 20.8 us
    another operation x1 -> x0, local copies, waits for them, and re-layouts: 6.03 us -> none  [scatter_channels(): by_core = blocks.reshape(-1, 2, blocks.shape[1], blocks.shape[2])]
    all_gather x1, waiting for transfers between devices: 0.02 us -> 5.85 us  [body(): lax.all_gather(inputs_planes, ('chips', 'core'), axis=1, tiled=True)]
    add x1 -> x0, local copies, waits for them, and re-layouts: 4.93 us -> none  [body(): spread = part if spread is None else spread + part]
    reduce_scatter x1, waiting for transfers between devices: 5.64 us -> 1.12 us  [scatter_channels(): lax.psum_scatter(partial.reshape(-1, blocks.shape[-1]), 'chips', scatter_...]
    dynamic_slice x0 -> x2, local copies, waits for them, and re-layouts: none -> 3.49 us  [the longest x1 1.86 us: scatter_channels(): keep = lax.dynamic_index_in_dim(by_core, core, axis=1, keepdims=False)]
    squeeze x1 -> x0, local copies, waits for them, and re-layouts: 3.25 us -> none  [scatter_channels(): send = lax.dynamic_index_in_dim(by_core, 1 - core, axis=1, keepdims=False)]
    unnamed x19 -> x20, local copies, waits for them, and re-layouts: 4.87 us -> 6.95 us
    ppermute x3, starting transfers between devices: 4.99 us -> 3.55 us  [all_reduce_direct(): reduced = reduced + lax.ppermute(send, axis, pairs)]
  transfers between devices with their start and end apart: 13 -> 13, of which waited for: 5 -> 6; matrix products, arithmetic and copies ran while one was open for 44% -> 37% of each run, Pallas kernels for 0% -> 0%
where the time goes in v8:
time: 98.5 us; the launch traced here: 98.2 us
  waiting for transfers between devices  20.8 us (21%)
  starting transfers between devices  19.3 us (20%)
  local copies, waits for them, and re-layouts  17.1 us (17%)
  between operations  15.9 us (16%)
  matrix products  12.6 us (13%)
  other arithmetic  12.4 us (13%)
    ppermute x3, waiting for transfers between devices, all_reduce_direct(): lax.ppermute(reduced, axis, [(i, i ^ distance) for i in range(devices)])  7.78 us
    unnamed x20, local copies, waits for them, and re-layouts  6.95 us
    dot_general x3, matrix products, body(): jnp.einsum('bjk,zkn->bzjn', backward_weight[depth_index], grad_shifted[2...  5.85 us
    all_gather x1, waiting for transfers between devices, body(): lax.all_gather(inputs_planes, ('chips', 'core'), axis=1, tiled=True)  5.85 us
    ppermute x3, starting transfers between devices, all_reduce_direct(): lax.ppermute(reduced, axis, [(i, i ^ distance) for i in range(devices)])  5.07 us
    ppermute x1, starting transfers between devices, padded_2(): before = lax.ppermute(last, axis, up)  4.85 us
    dot_general x3, matrix products, body(): jnp.einsum('zkn,zin->ki', grad_shifted[2 - depth_index:2 - depth_index +...  4.36 us
    add x1, other arithmetic, scatter_channels(): partial = keep + lax.ppermute(send, 'core', [(0, 1), (1, 0)])  4.19 us
  transfers between devices with their start and end apart: 13, of which 6 were waited for; matrix products, arithmetic and copies ran while one was open for 37% of the time, Pallas kernels for 0%

profile of v8, /device:TPU:0, one launch (start us, length us, event | category | flops | bytes accessed | tf_op | source)
XLA Modules:
  0.0 98.2 jit_solution(3218763710035897945)
XLA Ops:
  8.0 1.0 %copy.69 = bf16[32,4,1024]{2,0,1:T(8,128)(2,1)S(1)} copy(bf16[32,4,1024]{2,1,0:T(4,128)(2,1)} %param.9) | data formatting | bytes 524288 | tf_op args[3]
  9.1 4.8 %collective-permute-start.2 = (bf16[1,32,1024]{2,1,0:T(8,128)(2,1)S(1)}, bf16[1,32,1024]{2,1,0:T(8,128)(2,1)S(1)}, u32[]{:S(2)}, u32[]{:S(2)}) collective-permute-start(bf16[1,32,1024]{2,1,0:T(8,128)(2,1)S(1)} %get-tuple-element.50), channel_id=1, source_target_pairs={{0,8},{8,16},{16,24},{1,9},{9,17},{17,25},{2,10},{10,18},{18,26},{... | collective-permute-start | bytes 196616 | tf_op jit(solution)/shard_map/ppermute | solution.py:28
  14.0 1.3 %collective-permute-start.3 = (bf16[1,32,1024]{2,1,0:T(8,128)(2,1)S(1)}, bf16[1,32,1024]{2,1,0:T(8,128)(2,1)S(1)}, u32[]{:S(2)}, u32[]{:S(2)}) collective-permute-start(bf16[1,32,1024]{2,1,0:T(8,128)(2,1)S(1)} %get-tuple-element.51), channel_id=1, source_target_pairs={{8,0},{16,8},{24,16},{9,1},{17,9},{25,17},{10,2},{18,10},{26,18},{... | collective-permute-start | bytes 196616 | tf_op jit(solution)/shard_map/ppermute | solution.py:29
  15.3 1.7 %copy.68 = bf16[32,4,1024]{2,0,1:T(8,128)(2,1)} copy(bf16[32,4,1024]{2,1,0:T(4,128)(2,1)} %param.6) | data formatting | bytes 524288 | tf_op args[0]
  17.1 1.1 %fusion.67 = (bf16[1,256,9,32]{1,3,2,0:T(8,128)(2,1)S(1)}, bf16[1,256,9,32]{1,3,2,0:T(8,128)(2,1)S(1)}, bf16[1,256,9,32]{1,3,2,0:T(8,128)(2,1)S(1)}) fusion(bf16[3,256,9,32]{1,3,2,0:T(8,128)(2,1)} %bitcast.230), kind=kLoop, calls=%fused_computation.130 | loop fusion | bytes 884736 | tf_op jit(solution)/shard_map/slice | solution.py:203
  18.4 0.4 copy.43
  19.1 0.4 copy.41
  19.7 0.4 copy.45
  21.7 1.0 %fusion.65 = (bf16[4,9,32,1024]{3,2,0,1:T(8,128)(2,1)S(1)}, bf16[4,9,32,1024]{3,2,0,1:T(8,128)(2,1)S(1)}, bf16[4,9,32,1024]{3,2,0,1:T(8,128)(2,1)S(1)}) fusion(bf16[6,9,32,1024]{3,2,0,1:T(8,128)(2,1)S(1)} %fusion.27), kind=kLoop, calls=%fused_computation.128 | loop fusion | bytes 14155776 | tf_op jit(solution)/shard_map/slice | solution.py:204
  23.2 0.3 copy.40
  23.6 1.1 %copy-done.1 = bf16[4,9,32,1024]{3,2,1,0:T(8,128)(2,1)} copy-done((bf16[4,9,32,1024]{3,2,1,0:T(8,128)(2,1)}, bf16[4,9,32,1024]{3,2,1,0:T(8,128)(2,1)S(1)}, u32[]{:S(2)}) %copy-start.1) | copy-done | bytes 2359320
  24.6 1.8 %fusion.47 = f32[4,1024,8,32]{1,3,2,0:T(8,128)S(1)} fusion(bf16[4,288,1024,1]{2,1,3,0:T(8,128)(2,1)S(1)} %bitcast.219, bf16[8,32,288]{2,1,0:T(8,128)(2,1)S(1)} %copy.43), kind=kOutput, calls=%fused_computation.105 | convolution fusion | flops 603979776 | bytes 6701056 | tf_op jit(solution)/shard_map/bjk,zkn->bzjn/dot_general | solution.py:201
  26.4 1.8 %fusion.49 = f32[4,1024,8,32]{1,3,2,0:T(8,128)S(1)} fusion(bf16[4,288,1024,1]{2,1,3,0:T(8,128)(2,1)S(1)} %bitcast.221, bf16[8,32,288]{2,1,0:T(8,128)(2,1)S(1)} %copy.41), kind=kOutput, calls=%fused_computation.107 | convolution fusion | flops 603979776 | bytes 6701056 | tf_op jit(solution)/shard_map/bjk,zkn->bzjn/dot_general | solution.py:201
  28.2 2.3 %add_add_fusion = f32[4,1024,8,32]{1,3,2,0:T(8,128)S(1)} fusion(f32[4,1024,8,32]{1,3,2,0:T(8,128)S(1)} %fusion.49, f32[4,1024,8,32]{1,3,2,0:T(8,128)S(1)} %fusion.47, bf16[4,288,1024,1]{2,1,3,0:T(8,128)(2,1)S(1)} %bitcast.217, bf16[8,32,288]{2,1,0:T(8,128)(2,1)S(1)} %copy.45), kind=kOutput, calls=%fused_computation.1 | convolution fusion | flops 606076928 | bytes 15089664 | tf_op jit(solution)/shard_map/bjk,zkn->bzjn/dot_general | solution.py:201
  30.5 1.9 %constant_dynamic-slice_fusion.1 = (f32[4,1,4,32,1024]{4,3,1,0,2:T(8,128)}, f32[4,1,4,32,1024]{4,3,1,0,2:T(8,128)S(1)}) fusion(f32[4,2,4,32,1024]{4,3,1,0,2:T(8,128)S(1)} %bitcast.214, s32[]{:T(128)S(6)} %select_n.181, s32[]{:T(128)S(6)} %select_n.182), kind=kLoop, calls=%fused_computation.126 | loop fusion | bytes 8388616 | tf_op jit(solution)/shard_map/jit(dynamic_index_in_dim)/dynamic_slice | solution.py:118
  32.4 1.6 %copy.67 = f32[4,1,4,32,1024]{4,3,2,0,1:T(8,128)} copy(f32[4,1,4,32,1024]{4,3,1,0,2:T(8,128)S(1)} %get-tuple-element.29) | data formatting | bytes 4194304 | tf_op jit(solution)/shard_map/jit(dynamic_index_in_dim)/dynamic_slice | solution.py:119
  34.1 0.3 convert_reduce_fusion
  34.5 4.1 %collective-permute-done.4 = f32[4,4,32,1024]{3,2,1,0:T(8,128)} collective-permute-done((f32[4,4,32,1024]{3,2,1,0:T(8,128)}, f32[4,4,32,1024]{3,2,1,0:T(8,128)}, u32[]{:S(2)}, u32[]{:S(2)}) %collective-permute-start.4) | collective-permute-done | bytes 2097184 | tf_op jit(solution)/shard_map/ppermute | solution.py:120
  38.6 4.2 %bitcast_add_fusion = f32[4,4,32,1024]{3,2,1,0:T(8,128)} fusion(f32[4,4,32,1024]{3,2,1,0:T(8,128)} %collective-permute-done.4, f32[4,1,4,32,1024]{4,3,1,0,2:T(8,128)} %get-tuple-element.28), kind=kLoop, calls=%fused_computation.5 | loop fusion | flops 524288 | bytes 6291456 | tf_op jit(solution)/shard_map/add | solution.py:120
  42.8 5.8 %all-gather.2.cloned.1.call-done = bf16[4,256,1024]{2,1,0:T(8,128)(2,1)} async-done(((bf16[4,32,1024]{2,1,0:T(8,128)(2,1)}), bf16[4,256,1024]{2,1,0:T(8,128)(2,1)}) %all-gather.2.cloned.1.call-update) | async-done | bytes 2097168 | tf_op jit(solution)/shard_map/all_gather | solution.py:136
  48.7 2.5 %convolution_bitcast_fusion.3 = f32[1,288,256]{2,1,0:T(8,128)S(1)} fusion(bf16[4,288,1024]{2,1,0:T(8,128)(2,1)S(1)} %bitcast.218, bf16[4,256,1024]{2,1,0:T(8,128)(2,1)} %all-gather.2.cloned.1.call-done), kind=kOutput, calls=%fused_computation.9 | convolution fusion | flops 603979776 | bytes 4751360 | tf_op jit(solution)/shard_map/zkn,zin->ki/dot_general | solution.py:174
  51.2 0.6 copy-done.2
  51.9 1.0 %convolution_bitcast_fusion.4 = f32[1,288,256]{2,1,0:T(8,128)S(1)} fusion(bf16[4,288,1024]{2,1,0:T(8,128)(2,1)S(1)} %bitcast.220, bf16[4,256,1024]{2,1,0:T(8,128)(2,1)S(1)} %copy-done), kind=kOutput, calls=%fused_computation.10 | convolution fusion | flops 603979776 | bytes 4751360 | tf_op jit(solution)/shard_map/zkn,zin->ki/dot_general | solution.py:174
  52.9 0.6 copy-done.4
  53.5 0.8 convolution_bitcast_fusion.5
  54.5 1.3 %collective-permute-start.5 = (f32[224,256]{1,0:T(8,128)S(1)}, f32[224,256]{1,0:T(8,128)S(1)}, u32[]{:S(2)}, u32[]{:S(2)}) collective-permute-start(f32[224,256]{1,0:T(8,128)S(1)} %get-tuple-element.37), channel_id=1, source_target_pairs={{0,8},{8,0},{16,24},{24,16},{1,9},{9,1},{17,25},{25,17},{2,10},{10... | collective-permute-start | bytes 688136 | tf_op jit(solution)/shard_map/ppermute | solution.py:104
  55.9 1.5 %collective-permute-start.6 = (f32[224,256]{1,0:T(8,128)S(1)}, f32[224,256]{1,0:T(8,128)S(1)}, u32[]{:S(2)}, u32[]{:S(2)}) collective-permute-start(f32[224,256]{1,0:T(8,128)S(1)} %get-tuple-element.39), channel_id=1, source_target_pairs={{0,16},{8,24},{16,0},{24,8},{1,17},{9,25},{17,1},{25,9},{2,18},{10... | collective-permute-start | bytes 688136 | tf_op jit(solution)/shard_map/ppermute | solution.py:104
  57.4 0.7 collective-permute-start.7
  58.1 0.8 convolution_bitcast_fusion
  58.9 0.8 convolution_bitcast_fusion.1
  59.7 0.8 convolution_bitcast_fusion.2
  60.5 2.3 %pad_add_fusion = f32[6,288,1024]{2,1,0:T(8,128)S(1)} fusion(f32[4,288,1024]{2,1,0:T(8,128)S(1)} %convolution_bitcast_fusion, f32[4,288,1024]{2,1,0:T(8,128)S(1)} %convolution_bitcast_fusion.1, f32[4,288,1024]{2,1,0:T(8,128)S(1)} %convolution_bitcast_fusion.2), kind=kLoop, calls=%fused_computation | loop fusion | flops 3538944 | bytes 21233664 | tf_op jit(solution)/shard_map/add | solution.py:149
  62.8 1.1 %slice_bitcast_fusion = (f32[6,32,1024]{2,1,0:T(8,128)S(1)}, f32[6,32,1024]{2,1,0:T(8,128)S(1)}, f32[6,32,1024]{2,1,0:T(8,128)S(1)}, f32[6,32,1024]{2,1,0:T(8,12...) fusion(f32[6,9,32,1024]{3,2,1,0:T(8,128)S(1)} %bitcast.215), kind=kLoop, calls=%fused_computation.45 | loop fusion | bytes 12582912 | tf_op jit(solution)/shard_map/squeeze | solution.py:153
  63.9 1.7 %fusion.10 = f32[6,32,1024]{2,1,0:T(8,128)S(1)} fusion(f32[6,32,1024]{2,1,0:T(8,128)S(1)} %get-tuple-element.27, f32[6,32,1024]{2,1,0:T(8,128)S(1)} %get-tuple-element.26, f32[6,32,1024]{2,1,0:T(8,128)S(1)} %get-tuple-element.25, f32[6,32,1024]{2,1,0:T(8,128)S(1)} %get-tuple-element.24, f32[6,32,1024]{2,1,0:T(8,128)S(1)} %get-tuple-element.23, ...), kind=kLoop, calls=%fused_computation.37 | loop fusion | flops 3342336 | bytes 7867392 | tf_op jit(solution)/shard_map/add | solution.py:154
  65.6 3.2 %collective-permute-start = (f32[1,32,1024]{2,1,0:T(8,128)S(1)}, f32[1,32,1024]{2,1,0:T(8,128)S(1)}, u32[]{:S(2)}, u32[]{:S(2)}) collective-permute-start(f32[1,32,1024]{2,1,0:T(8,128)S(1)} %get-tuple-element.40), channel_id=1, source_target_pairs={{0,8},{8,16},{16,24},{1,9},{9,17},{17,25},{2,10},{10,18},{18,26},{... | collective-permute-start | bytes 393224 | tf_op jit(solution)/shard_map/ppermute | solution.py:158
  68.8 1.3 %collective-permute-start.1 = (f32[1,32,1024]{2,1,0:T(8,128)S(1)}, f32[1,32,1024]{2,1,0:T(8,128)S(1)}, u32[]{:S(2)}, u32[]{:S(2)}) collective-permute-start(f32[1,32,1024]{2,1,0:T(8,128)S(1)} %get-tuple-element.41), channel_id=1, source_target_pairs={{8,0},{16,8},{24,16},{9,1},{17,9},{25,17},{10,2},{18,10},{26,18},{... | collective-permute-start | bytes 393224 | tf_op jit(solution)/shard_map/ppermute | solution.py:159
  70.2 2.7 %collective-permute-start.8 = (f32[224,256]{1,0:T(8,128)S(1)}, f32[224,256]{1,0:T(8,128)S(1)}, u32[]{:S(2)}, u32[]{:S(2)}) collective-permute-start(f32[224,256]{1,0:T(8,128)S(1)} %fusion.45), channel_id=1, source_target_pairs={{0,8},{8,0},{16,24},{24,16},{1,9},{9,1},{17,25},{25,17},{2,10},{10... | collective-permute-start | bytes 688136 | tf_op jit(solution)/shard_map/ppermute | solution.py:106
  72.9 1.5 %collective-permute-start.9 = (f32[224,256]{1,0:T(8,128)S(1)}, f32[224,256]{1,0:T(8,128)S(1)}, u32[]{:S(2)}, u32[]{:S(2)}) collective-permute-start(f32[224,256]{1,0:T(8,128)S(1)} %fusion.45), channel_id=1, source_target_pairs={{0,16},{8,24},{16,0},{24,8},{1,17},{9,25},{17,1},{25,9},{2,18},{10... | collective-permute-start | bytes 688136 | tf_op jit(solution)/shard_map/ppermute | solution.py:106
  74.4 0.9 collective-permute-start.10
  75.3 1.9 %collective-permute-done.1 = f32[1,32,1024]{2,1,0:T(8,128)S(1)} collective-permute-done((f32[1,32,1024]{2,1,0:T(8,128)S(1)}, f32[1,32,1024]{2,1,0:T(8,128)S(1)}, u32[]{:S(2)}, u32[]{:S(2)}) %collective-permute-start.1) | collective-permute-done | bytes 131104 | tf_op jit(solution)/shard_map/ppermute | solution.py:159
  77.3 0.9 copy.48
  78.2 3.9 %collective-permute-done.8 = f32[224,256]{1,0:T(8,128)S(1)} collective-permute-done((f32[224,256]{1,0:T(8,128)S(1)}, f32[224,256]{1,0:T(8,128)S(1)}, u32[]{:S(2)}, u32[]{:S(2)}) %collective-permute-start.8) | collective-permute-done | bytes 229408 | tf_op jit(solution)/shard_map/ppermute | solution.py:106
  82.1 3.9 %collective-permute-done.10 = f32[224,256]{1,0:T(8,128)S(1)} collective-permute-done((f32[224,256]{1,0:T(8,128)S(1)}, f32[224,256]{1,0:T(8,128)S(1)}, u32[]{:S(2)}, u32[]{:S(2)}) %collective-permute-start.10) | collective-permute-done | bytes 229408 | tf_op jit(solution)/shard_map/ppermute | solution.py:106
  86.1 1.0 pad_maximum_fusion.1
  87.1 0.5 slice_bitcast_fusion.9
  87.6 1.1 %reduce-scatter.2.cloned.1.call-done = f32[128,1024]{1,0:T(8,128)} async-done(((f32[512,1024]{1,0:T(8,128)}), f32[128,1024]{1,0:T(8,128)}) %reduce-scatter.2.cloned.1.call-update) | async-done | bytes 524304 | tf_op jit(solution)/shard_map/reduce_scatter | solution.py:121
  88.7 1.1 %convert_element_type.39 = bf16[128,1024]{1,0:T(8,128)(2,1)S(1)} convert(f32[128,1024]{1,0:T(8,128)} %reduce-scatter.2.cloned.1.call-done) | non-fusion elementwise | flops 131072 | bytes 786432 | tf_op jit(solution)/shard_map/convert_element_type | solution.py:209
  89.8 0.9 copy.49
  (54 shorter events, 3.5 us)
Async XLA Ops:
  8.0 40.7 %all-gather.2.cloned.1.call-start = ((), (), s32[]{:S(2)}) async-start(), calls=%async_computation.1 | async-start | bytes 2359296 | tf_op jit(solution)/shard_map/all_gather | solution.py:136
  9.1 11.0 %collective-permute-start.2 = (bf16[1,32,1024]{2,1,0:T(8,128)(2,1)S(1)}, bf16[1,32,1024]{2,1,0:T(8,128)(2,1)S(1)}, u32[]{:S(2)}, u32[]{:S(2)}) collective-permute-start(bf16[1,32,1024]{2,1,0:T(8,128)(2,1)S(1)} %get-tuple-element.50), channel_id=1, source_target_pairs={{0,8},{8,16},{16,24},{1,9},{9,17},{17,25},{2,10},{10,18},{18,26},{... | collective-permute-start | bytes 196616 | tf_op jit(solution)/shard_map/ppermute | solution.py:28
  14.0 6.2 %collective-permute-start.3 = (bf16[1,32,1024]{2,1,0:T(8,128)(2,1)S(1)}, bf16[1,32,1024]{2,1,0:T(8,128)(2,1)S(1)}, u32[]{:S(2)}, u32[]{:S(2)}) collective-permute-start(bf16[1,32,1024]{2,1,0:T(8,128)(2,1)S(1)} %get-tuple-element.51), channel_id=1, source_target_pairs={{8,0},{16,8},{24,16},{9,1},{17,9},{25,17},{10,2},{18,10},{26,18},{... | collective-permute-start | bytes 196616 | tf_op jit(solution)/shard_map/ppermute | solution.py:29
  17.0 71.7 %reduce-scatter.2.cloned.1.call-start = ((), (), s32[]{:S(2)}) async-start(), calls=%async_computation.2 | async-start | bytes 2621440 | tf_op jit(solution)/shard_map/reduce_scatter | solution.py:121
  23.2 1.4 %copy-start.1 = (bf16[4,9,32,1024]{3,2,1,0:T(8,128)(2,1)}, bf16[4,9,32,1024]{3,2,1,0:T(8,128)(2,1)S(1)}, u32[]{:S(2)}) copy-start(bf16[4,9,32,1024]{3,2,1,0:T(8,128)(2,1)S(1)} %copy.42) | copy-start | bytes 7077892
  23.6 2.8 %copy-start.3 = (bf16[4,9,32,1024]{3,2,1,0:T(8,128)(2,1)}, bf16[4,9,32,1024]{3,2,1,0:T(8,128)(2,1)S(1)}, u32[]{:S(2)}) copy-start(bf16[4,9,32,1024]{3,2,1,0:T(8,128)(2,1)S(1)} %copy.40) | copy-start | bytes 7077892
  32.4 1.7 %copy-start.6 = (bf16[32,4,1024]{2,1,0:T(4,128)(2,1)S(1)}, bf16[32,4,1024]{2,1,0:T(4,128)(2,1)}, u32[]{:S(2)}) copy-start(bf16[32,4,1024]{2,1,0:T(4,128)(2,1)} %param.9) | copy-start | bytes 786436
  32.4 2.0 %copy-start.5 = (bf16[27,256,32]{1,2,0:T(8,128)(2,1)S(1)}, bf16[27,256,32]{1,2,0:T(8,128)(2,1)}, u32[]{:S(2)}) copy-start(bf16[27,256,32]{1,2,0:T(8,128)(2,1)} %param.7) | copy-start | bytes 1327108
  34.0 4.6 %collective-permute-start.4 = (f32[4,4,32,1024]{3,2,1,0:T(8,128)}, f32[4,4,32,1024]{3,2,1,0:T(8,128)}, u32[]{:S(2)}, u32[]{:S(2)}) collective-permute-start(f32[4,4,32,1024]{3,2,1,0:T(8,128)} %bitcast.211), channel_id=1, source_target_pairs={{0,1},{1,0},{2,3},{3,2},{4,5},{5,4},{6,7},{7,6},{8,9},{9,8},{10,11... | collective-permute-start | bytes 6291464 | tf_op jit(solution)/shard_map/ppermute | solution.py:120
  48.7 2.6 %copy-start = (bf16[4,256,1024]{2,1,0:T(8,128)(2,1)S(1)}, bf16[4,256,1024]{2,1,0:T(8,128)(2,1)}, u32[]{:S(2)}) copy-start(bf16[4,256,1024]{2,1,0:T(8,128)(2,1)} %all-gather.2.cloned.1.call-done) | copy-start | bytes 6291460
  48.7 3.2 %copy-start.2 = (bf16[4,9,32,1024]{3,2,1,0:T(8,128)(2,1)S(1)}, bf16[4,9,32,1024]{3,2,1,0:T(8,128)(2,1)}, u32[]{:S(2)}) copy-start(bf16[4,9,32,1024]{3,2,1,0:T(8,128)(2,1)} %copy-done.1) | copy-start | bytes 7077892
  51.9 1.7 %copy-start.4 = (bf16[4,9,32,1024]{3,2,1,0:T(8,128)(2,1)S(1)}, bf16[4,9,32,1024]{3,2,1,0:T(8,128)(2,1)}, u32[]{:S(2)}) copy-start(bf16[4,9,32,1024]{3,2,1,0:T(8,128)(2,1)} %copy-done.3) | copy-start | bytes 7077892
  54.5 15.6 %collective-permute-start.5 = (f32[224,256]{1,0:T(8,128)S(1)}, f32[224,256]{1,0:T(8,128)S(1)}, u32[]{:S(2)}, u32[]{:S(2)}) collective-permute-start(f32[224,256]{1,0:T(8,128)S(1)} %get-tuple-element.37), channel_id=1, source_target_pairs={{0,8},{8,0},{16,24},{24,16},{1,9},{9,1},{17,25},{25,17},{2,10},{10... | collective-permute-start | bytes 688136 | tf_op jit(solution)/shard_map/ppermute | solution.py:104
  55.9 14.3 %collective-permute-start.6 = (f32[224,256]{1,0:T(8,128)S(1)}, f32[224,256]{1,0:T(8,128)S(1)}, u32[]{:S(2)}, u32[]{:S(2)}) collective-permute-start(f32[224,256]{1,0:T(8,128)S(1)} %get-tuple-element.39), channel_id=1, source_target_pairs={{0,16},{8,24},{16,0},{24,8},{1,17},{9,25},{17,1},{25,9},{2,18},{10... | collective-permute-start | bytes 688136 | tf_op jit(solution)/shard_map/ppermute | solution.py:104
  57.4 12.8 %collective-permute-start.7 = (f32[224,256]{1,0:T(8,128)S(1)}, f32[224,256]{1,0:T(8,128)S(1)}, u32[]{:S(2)}, u32[]{:S(2)}) collective-permute-start(f32[224,256]{1,0:T(8,128)S(1)} %get-tuple-element.38), channel_id=1, source_target_pairs={{0,24},{8,16},{16,8},{24,0},{1,25},{9,17},{17,9},{25,1},{2,26},{10... | collective-permute-start | bytes 688136 | tf_op jit(solution)/shard_map/ppermute | solution.py:104
  63.9 13.3 %copy-start.7 = (f32[32]{0:T(128)S(1)}, f32[32]{0:T(128)}, u32[]{:S(2)}) copy-start(f32[32]{0:T(128)} %param.8) | copy-start | bytes 388
  65.6 9.7 %collective-permute-start = (f32[1,32,1024]{2,1,0:T(8,128)S(1)}, f32[1,32,1024]{2,1,0:T(8,128)S(1)}, u32[]{:S(2)}, u32[]{:S(2)}) collective-permute-start(f32[1,32,1024]{2,1,0:T(8,128)S(1)} %get-tuple-element.40), channel_id=1, source_target_pairs={{0,8},{8,16},{16,24},{1,9},{9,17},{17,25},{2,10},{10,18},{18,26},{... | collective-permute-start | bytes 393224 | tf_op jit(solution)/shard_map/ppermute | solution.py:158
  68.8 8.3 %collective-permute-start.1 = (f32[1,32,1024]{2,1,0:T(8,128)S(1)}, f32[1,32,1024]{2,1,0:T(8,128)S(1)}, u32[]{:S(2)}, u32[]{:S(2)}) collective-permute-start(f32[1,32,1024]{2,1,0:T(8,128)S(1)} %get-tuple-element.41), channel_id=1, source_target_pairs={{8,0},{16,8},{24,16},{9,1},{17,9},{25,17},{10,2},{18,10},{26,18},{... | collective-permute-start | bytes 393224 | tf_op jit(solution)/shard_map/ppermute | solution.py:159
  70.2 11.8 %collective-permute-start.8 = (f32[224,256]{1,0:T(8,128)S(1)}, f32[224,256]{1,0:T(8,128)S(1)}, u32[]{:S(2)}, u32[]{:S(2)}) collective-permute-start(f32[224,256]{1,0:T(8,128)S(1)} %fusion.45), channel_id=1, source_target_pairs={{0,8},{8,0},{16,24},{24,16},{1,9},{9,1},{17,25},{25,17},{2,10},{10... | collective-permute-start | bytes 688136 | tf_op jit(solution)/shard_map/ppermute | solution.py:106
  72.9 9.1 %collective-permute-start.9 = (f32[224,256]{1,0:T(8,128)S(1)}, f32[224,256]{1,0:T(8,128)S(1)}, u32[]{:S(2)}, u32[]{:S(2)}) collective-permute-start(f32[224,256]{1,0:T(8,128)S(1)} %fusion.45), channel_id=1, source_target_pairs={{0,16},{8,24},{16,0},{24,8},{1,17},{9,25},{17,1},{25,9},{2,18},{10... | collective-permute-start | bytes 688136 | tf_op jit(solution)/shard_map/ppermute | solution.py:106
  74.4 11.6 %collective-permute-start.10 = (f32[224,256]{1,0:T(8,128)S(1)}, f32[224,256]{1,0:T(8,128)S(1)}, u32[]{:S(2)}, u32[]{:S(2)}) collective-permute-start(f32[224,256]{1,0:T(8,128)S(1)} %fusion.45), channel_id=1, source_target_pairs={{0,24},{8,16},{16,8},{24,0},{1,25},{9,17},{17,9},{25,1},{2,26},{10... | collective-permute-start | bytes 688136 | tf_op jit(solution)/shard_map/ppermute | solution.py:106
Sparse Core Ops, SparseCore 0:
  17.1 31.4 all-gather.1
Sparse Core Ops, SparseCore 1:
  42.9 45.8 reduce-scatter.1

commit v9 on v6

--- a/solution.py
+++ b/solution.py
@@ -142,6 +142,23 @@
     )
 
 
+def exchange_rows(weight, axis):
+    devices = lax.axis_size(axis)
+    if devices > 8:
+        return lax.all_to_all(weight, axis, 1, 2, tiled=True)
+    index = lax.axis_index(axis)
+    rows = weight.reshape(weight.shape[0], devices, weight.shape[1] // devices, weight.shape[2])
+    pieces = [lax.dynamic_index_in_dim(rows, index, 1, keepdims=False)]
+    for distance in range(1, devices):
+        send = lax.dynamic_index_in_dim(rows, index ^ distance, 1, keepdims=False)
+        pieces.append(lax.ppermute(send, axis, [(i, i ^ distance) for i in range(devices)]))
+    stacked = jnp.stack(pieces)
+    return jnp.concatenate(
+        [lax.dynamic_index_in_dim(stacked, index ^ block, 0, keepdims=False) for block in range(devices)],
+        axis=2,
+    )
+
+
 def body(inputs, weight, bias_term, output_grad):
     taps_total = weight.shape[0]
     channels_in = weight.shape[1]
@@ -154,7 +171,7 @@
     grad_planes = jnp.transpose(output_grad, (1, 0, 2))
     gathered = lax.all_gather(inputs_planes, "chan", axis=1, tiled=True)
     grad_gathered = lax.all_gather(grad_planes, "chan", axis=1, tiled=True)
-    weight_rows = lax.all_to_all(weight, "chan", 1, 2, tiled=True)
+    weight_rows = exchange_rows(weight, "chan")
 
     weight_grid = weight.reshape(3, 9, channels_in, block_out)
     forward_weight = jnp.transpose(weight_grid, (0, 1, 3, 2)).reshape(3, 9 * block_out, channels_in)

time: 121 us -> 176 us (1.45)
  the two profiles are of different devices: /device:TPU:0 before, /device:TPU:19 now
where the time goes in v9:
time: 176 us; the launch traced here: 175 us
  starting transfers between devices  54 us (31%)
  local copies, waits for them, and re-layouts  43.6 us (25%)
  waiting for transfers between devices  37.4 us (21%)
  between operations  14.7 us (8%)
  other arithmetic  14.1 us (8%)
  matrix products  11.4 us (6%)
    ppermute x7, starting transfers between devices, exchange_rows(): lax.ppermute(send, axis, [(i, i ^ distance) for i in range(devices)])  31.1 us
    ppermute x7, waiting for transfers between devices, exchange_rows(): lax.ppermute(send, axis, [(i, i ^ distance) for i in range(devices)])  27.3 us
    dynamic_slice x8, local copies, waits for them, and re-layouts, exchange_rows(): send = lax.dynamic_index_in_dim(rows, index ^ distance, 1, keepdims=False)  16.6 us
    ppermute x3, waiting for transfers between devices, all_reduce_direct(): lax.ppermute(reduced, axis, [(i, i ^ distance) for i in range(devices)])  10 us
    unnamed x37, local copies, waits for them, and re-layouts  9.05 us
    ppermute x2, starting transfers between devices, settle_rims(): from_below = lax.ppermute(field[depth + 1:], 'space', up)  6.69 us
    dot_general x6, matrix products, depth_products(): jnp.einsum('ki,zin->zkn', weights[depth_index], planes, preferred_element...  6.47 us
    slice x4, local copies, waits for them, and re-layouts, body(): grad_shifted[2 - depth_index:2 - depth_index + depth_cells]  6.21 us
  transfers between devices with their start and end apart: 21, of which 8 were waited for; matrix products, arithmetic and copies ran while one was open for 37% of the time, Pallas kernels for 0%

profile of v9, /device:TPU:19, one launch (start us, length us, event | category | flops | bytes accessed | tf_op | source)
XLA Modules:
  0.0 175.2 jit_solution(9685156346974337023)
XLA Ops:
  7.2 1.7 copy.106
  9.0 1.0 copy.107
  10.8 3.1 %collective-permute-start.11 = (bf16[1,32,1024]{2,1,0:T(8,128)(2,1)}, bf16[1,32,1024]{2,1,0:T(8,128)(2,1)}, u32[]{:S(2)}, u32[]{:S(2)}) collective-permute-start(bf16[1,32,1024]{2,1,0:T(8,128)(2,1)} %get-tuple-element.82), channel_id=1, source_target_pairs={{0,8},{8,16},{16,24},{1,9},{9,17},{17,25},{2,10},{10,18},{18,26},{... | collective-permute-start | bytes 196616 | tf_op jit(solution)/shard_map/ppermute | solution.py:28
  13.9 2.8 %collective-permute-start.12 = (bf16[1,32,1024]{2,1,0:T(8,128)(2,1)}, bf16[1,32,1024]{2,1,0:T(8,128)(2,1)}, u32[]{:S(2)}, u32[]{:S(2)}) collective-permute-start(bf16[1,32,1024]{2,1,0:T(8,128)(2,1)} %get-tuple-element.83), channel_id=1, source_target_pairs={{8,0},{16,8},{24,16},{9,1},{17,9},{25,17},{10,2},{18,10},{26,18},{... | collective-permute-start | bytes 196616 | tf_op jit(solution)/shard_map/ppermute | solution.py:29
  16.7 2.3 %reshape.124 = bf16[27,8,32,32]{2,1,3,0:T(8,128)(2,1)S(1)} reshape(bf16[27,256,32]{1,2,0:T(8,128)(2,1)} %param.7) | data formatting | bytes 884736 | tf_op jit(solution)/shard_map/reshape | solution.py:150
  19.0 5.2 %constant_dynamic-slice_fusion = (bf16[27,1,32,32]{2,1,3,0:T(2,128)(2,1)S(1)}, bf16[27,1,32,32]{2,1,3,0:T(2,128)(2,1)S(1)}, bf16[27,1,32,32]{2,1,3,0:T(2,128)(2,...) fusion(bf16[27,8,32,32]{2,1,3,0:T(8,128)(2,1)S(1)} %reshape.124, ...), kind=kLoop, calls=%fused_computation.159 | loop fusion | bytes 884768 | tf_op jit(solution)/shard_map/jit(dynamic_index_in_dim)/dynamic_slice | solution.py:153
  24.2 1.9 %copy.61 = bf16[27,1,32,32]{3,2,0,1:T(8,128)(2,1)} copy(bf16[27,1,32,32]{2,1,3,0:T(2,128)(2,1)} %get-tuple-element.61) | data formatting | bytes 110592 | tf_op jit(solution)/shard_map/jit(dynamic_index_in_dim)/dynamic_slice | solution.py:153
  26.1 1.3 collective-permute-start.2
  27.4 1.9 %copy.62 = bf16[27,1,32,32]{3,2,0,1:T(8,128)(2,1)} copy(bf16[27,1,32,32]{2,1,3,0:T(2,128)(2,1)} %get-tuple-element.60) | data formatting | bytes 110592 | tf_op jit(solution)/shard_map/jit(dynamic_index_in_dim)/dynamic_slice | solution.py:153
  29.3 1.3 collective-permute-start.3
  30.5 1.8 %copy.63 = bf16[27,1,32,32]{3,2,0,1:T(8,128)(2,1)} copy(bf16[27,1,32,32]{2,1,3,0:T(2,128)(2,1)} %get-tuple-element.59) | data formatting | bytes 110592 | tf_op jit(solution)/shard_map/jit(dynamic_index_in_dim)/dynamic_slice | solution.py:153
  33.1 1.2 copy.60
  34.4 1.8 %fusion.83 = (bf16[1,9,32,256]{3,2,1,0:T(8,128)(2,1)}, bf16[1,9,32,256]{3,2,1,0:T(8,128)(2,1)}, bf16[1,9,32,256]{3,2,1,0:T(8,128)(2,1)}) fusion(bf16[3,9,32,256]{3,2,1,0:T(8,128)(2,1)} %bitcast.283), kind=kLoop, calls=%fused_computation.187 | loop fusion | bytes 884736 | tf_op jit(solution)/shard_map/slice | solution.py:126
  36.2 1.9 %copy.64 = bf16[27,1,32,32]{3,2,0,1:T(8,128)(2,1)} copy(bf16[27,1,32,32]{2,1,3,0:T(2,128)(2,1)} %get-tuple-element.58) | data formatting | bytes 110592 | tf_op jit(solution)/shard_map/jit(dynamic_index_in_dim)/dynamic_slice | solution.py:153
  38.1 1.5 copy.65
  39.6 1.2 copy.66
  40.8 1.2 copy.67
  43.6 2.8 %collective-permute-start.6 = (bf16[27,32,32]{2,1,0:T(8,128)(2,1)}, bf16[27,32,32]{2,1,0:T(8,128)(2,1)S(1)}, u32[]{:S(2)}, u32[]{:S(2)}) collective-permute-start(bf16[27,32,32]{2,1,0:T(8,128)(2,1)} %bitcast.298), channel_id=1, source_target_pairs={{0,5},{1,4},{2,7},{3,6},{4,1},{5,0},{6,3},{7,2},{8,13},{9,12},{10,... | collective-permute-start | bytes 165896 | tf_op jit(solution)/shard_map/ppermute | solution.py:154
  48.2 1.9 %collective-permute-start.7 = (bf16[27,32,32]{2,1,0:T(8,128)(2,1)S(1)}, bf16[27,32,32]{2,1,0:T(8,128)(2,1)S(1)}, u32[]{:S(2)}, u32[]{:S(2)}) collective-permute-start(bf16[27,32,32]{2,1,0:T(8,128)(2,1)S(1)} %bitcast.297), channel_id=1, source_target_pairs={{0,6},{1,7},{2,4},{3,5},{4,2},{5,3},{6,0},{7,1},{8,14},{9,15},{10,... | collective-permute-start | bytes 165896 | tf_op jit(solution)/shard_map/ppermute | solution.py:154
  51.7 23.4 %collective-permute-start.8 = (bf16[27,32,32]{2,1,0:T(8,128)(2,1)S(1)}, bf16[27,32,32]{2,1,0:T(8,128)(2,1)S(1)}, u32[]{:S(2)}, u32[]{:S(2)}) collective-permute-start(bf16[27,32,32]{2,1,0:T(8,128)(2,1)S(1)} %bitcast.296), channel_id=1, source_target_pairs={{0,7},{1,6},{2,5},{3,4},{4,3},{5,2},{6,1},{7,0},{8,15},{9,14},{10,... | collective-permute-start | bytes 165896 | tf_op jit(solution)/shard_map/ppermute | solution.py:154
  75.2 8.2 %collective-permute-done.6 = bf16[27,32,32]{2,1,0:T(8,128)(2,1)S(1)} collective-permute-done((bf16[27,32,32]{2,1,0:T(8,128)(2,1)}, bf16[27,32,32]{2,1,0:T(8,128)(2,1)S(1)}, u32[]{:S(2)}, u32[]{:S(2)}) %collective-permute-start.6) | collective-permute-done | bytes 55328 | tf_op jit(solution)/shard_map/ppermute | solution.py:154
  83.4 12.7 %collective-permute-done.7 = bf16[27,32,32]{2,1,0:T(8,128)(2,1)S(1)} collective-permute-done((bf16[27,32,32]{2,1,0:T(8,128)(2,1)S(1)}, bf16[27,32,32]{2,1,0:T(8,128)(2,1)S(1)}, u32[]{:S(2)}, u32[]{:S(2)}) %collective-permute-start.7) | collective-permute-done | bytes 55328 | tf_op jit(solution)/shard_map/ppermute | solution.py:154
  96.2 4.9 %collective-permute-done.8 = bf16[27,32,32]{2,1,0:T(8,128)(2,1)S(1)} collective-permute-done((bf16[27,32,32]{2,1,0:T(8,128)(2,1)S(1)}, bf16[27,32,32]{2,1,0:T(8,128)(2,1)S(1)}, u32[]{:S(2)}, u32[]{:S(2)}) %collective-permute-start.8) | collective-permute-done | bytes 55328 | tf_op jit(solution)/shard_map/ppermute | solution.py:154
  101.5 1.0 concatenate.36
  102.6 1.1 fusion.43
  105.9 1.0 fusion.79
  106.9 1.7 copy.82
  108.7 1.7 copy.81
  110.4 1.7 copy.80
  112.1 3.3 %convolution_bitcast_fusion.6 = f32[1,288,256]{2,1,0:T(8,128)S(1)} fusion(bf16[4,288,1024]{2,1,0:T(8,128)(2,1)} %bitcast.280, bf16[4,256,1024]{2,1,0:T(8,128)(2,1)} %all-gather.3.cloned.1.call-done), kind=kOutput, calls=%fused_computation.10 | convolution fusion | flops 603979776 | bytes 4751360 | tf_op jit(solution)/shard_map/zkn,zin->ki/dot_general | solution.py:193
  119.3 1.8 %collective-permute-start.14 = (f32[224,256]{1,0:T(8,128)}, f32[224,256]{1,0:T(8,128)}, u32[]{:S(2)}, u32[]{:S(2)}) collective-permute-start(f32[224,256]{1,0:T(8,128)} %get-tuple-element.69), channel_id=1, source_target_pairs={{0,16},{8,24},{16,0},{24,8},{1,17},{9,25},{17,1},{25,9},{2,18},{10... | collective-permute-start | bytes 688136 | tf_op jit(solution)/shard_map/ppermute | solution.py:104
  121.9 2.5 %convolution_bitcast_fusion.3 = f32[4,288,1024]{2,1,0:T(8,128)S(1)} fusion(bf16[288,256,1]{1,0,2:T(8,128)(2,1)S(1)} %bitcast.292, bf16[4,256,1024]{2,1,0:T(8,128)(2,1)} %all-gather.5.cloned.1.call-done), kind=kOutput, calls=%fused_computation.5 | convolution fusion | flops 603979776 | bytes 6963200 | tf_op jit(solution)/shard_map/ki,zin->zkn/dot_general | solution.py:126
  126.0 2.3 %pad_add_fusion = f32[6,288,1024]{2,1,0:T(8,128)S(1)} fusion(f32[4,288,1024]{2,1,0:T(8,128)S(1)} %convolution_bitcast_fusion.3, f32[4,288,1024]{2,1,0:T(8,128)S(1)} %convolution_bitcast_fusion.4, f32[4,288,1024]{2,1,0:T(8,128)S(1)} %convolution_bitcast_fusion.5), kind=kLoop, calls=%fused_computation | loop fusion | flops 3538944 | bytes 21233664 | tf_op jit(solution)/shard_map/add | solution.py:129
  128.3 1.1 slice_bitcast_fusion
  129.5 1.7 fusion.26
  131.2 2.3 %collective-permute-start.10 = (f32[1,32,1024]{2,1,0:T(8,128)S(1)}, f32[1,32,1024]{2,1,0:T(8,128)S(1)}, u32[]{:S(2)}, u32[]{:S(2)}) collective-permute-start(f32[1,32,1024]{2,1,0:T(8,128)S(1)} %get-tuple-element.71), channel_id=1, source_target_pairs={{8,0},{16,8},{24,16},{9,1},{17,9},{25,17},{10,2},{18,10},{26,18},{... | collective-permute-start | bytes 393224 | tf_op jit(solution)/shard_map/ppermute | solution.py:139
  133.5 4.1 %collective-permute-start.9 = (f32[1,32,1024]{2,1,0:T(8,128)S(1)}, f32[1,32,1024]{2,1,0:T(8,128)S(1)}, u32[]{:S(2)}, u32[]{:S(2)}) collective-permute-start(f32[1,32,1024]{2,1,0:T(8,128)S(1)} %get-tuple-element.70), channel_id=1, source_target_pairs={{0,8},{8,16},{16,24},{1,9},{9,17},{17,25},{2,10},{10,18},{18,26},{... | collective-permute-start | bytes 393224 | tf_op jit(solution)/shard_map/ppermute | solution.py:138
  140.2 2.3 %pad_add_fusion.1 = f32[6,288,1024]{2,1,0:T(8,128)S(1)} fusion(f32[4,288,1024]{2,1,0:T(8,128)S(1)} %convolution_bitcast_fusion, f32[4,288,1024]{2,1,0:T(8,128)S(1)} %convolution_bitcast_fusion.1, f32[4,288,1024]{2,1,0:T(8,128)S(1)} %convolution_bitcast_fusion.2), kind=kLoop, calls=%fused_computation.1 | loop fusion | flops 3538944 | bytes 21233664 | tf_op jit(solution)/shard_map/add | solution.py:129
  142.5 1.1 slice_bitcast_fusion.9
  143.7 1.7 fusion.10
  145.4 2.6 %collective-permute-start = (f32[1,32,1024]{2,1,0:T(8,128)S(1)}, f32[1,32,1024]{2,1,0:T(8,128)S(1)}, u32[]{:S(2)}, u32[]{:S(2)}) collective-permute-start(f32[1,32,1024]{2,1,0:T(8,128)S(1)} %get-tuple-element.72), channel_id=1, source_target_pairs={{0,8},{8,16},{16,24},{1,9},{9,17},{17,25},{2,10},{10,18},{18,26},{... | collective-permute-start | bytes 393224 | tf_op jit(solution)/shard_map/ppermute | solution.py:138
  148.0 2.7 %collective-permute-start.1 = (f32[1,32,1024]{2,1,0:T(8,128)S(1)}, f32[1,32,1024]{2,1,0:T(8,128)S(1)}, u32[]{:S(2)}, u32[]{:S(2)}) collective-permute-start(f32[1,32,1024]{2,1,0:T(8,128)S(1)} %get-tuple-element.73), channel_id=1, source_target_pairs={{8,0},{16,8},{24,16},{9,1},{17,9},{25,17},{10,2},{18,10},{26,18},{... | collective-permute-start | bytes 393224 | tf_op jit(solution)/shard_map/ppermute | solution.py:139
  150.7 1.2 fusion.64
  151.9 1.6 collective-permute-start.18
  153.6 1.1 collective-permute-start.17
  156.7 3.5 %collective-permute-done.18 = f32[224,256]{1,0:T(8,128)S(1)} collective-permute-done((f32[224,256]{1,0:T(8,128)S(1)}, f32[224,256]{1,0:T(8,128)S(1)}, u32[]{:S(2)}, u32[]{:S(2)}) %collective-permute-start.18) | collective-permute-done | bytes 229408 | tf_op jit(solution)/shard_map/ppermute | solution.py:106
  160.2 2.6 %collective-permute-done.16 = f32[224,256]{1,0:T(8,128)S(1)} collective-permute-done((f32[224,256]{1,0:T(8,128)S(1)}, f32[224,256]{1,0:T(8,128)S(1)}, u32[]{:S(2)}, u32[]{:S(2)}) %collective-permute-start.16) | collective-permute-done | bytes 229408 | tf_op jit(solution)/shard_map/ppermute | solution.py:106
  162.8 3.9 %collective-permute-done.17 = f32[224,256]{1,0:T(8,128)S(1)} collective-permute-done((f32[224,256]{1,0:T(8,128)S(1)}, f32[224,256]{1,0:T(8,128)S(1)}, u32[]{:S(2)}, u32[]{:S(2)}) %collective-permute-start.17) | collective-permute-done | bytes 229408 | tf_op jit(solution)/shard_map/ppermute | solution.py:106
  (94 shorter events, 21.8 us)
Async XLA Ops:
  7.2 105.0 %all-gather.3.cloned.1.call-start = ((), (), s32[]{:S(2)}) async-start(), calls=%async_computation | async-start | bytes 2359296 | tf_op jit(solution)/shard_map/all_gather | solution.py:172
  9.0 112.9 %all-gather.5.cloned.1.call-start = ((), (), s32[]{:S(2)}) async-start(), calls=%async_computation.1 | async-start | bytes 2359296 | tf_op jit(solution)/shard_map/all_gather | solution.py:173
  10.1 14.2 %copy-start.2 = (bf16[32,4,1024]{2,0,1:T(8,128)(2,1)}, bf16[32,4,1024]{2,0,1:T(8,128)(2,1)S(1)}, u32[]{:S(2)}) copy-start(bf16[32,4,1024]{2,0,1:T(8,128)(2,1)S(1)} %copy.107) | copy-start | bytes 786436
  10.8 91.8 %collective-permute-start.11 = (bf16[1,32,1024]{2,1,0:T(8,128)(2,1)}, bf16[1,32,1024]{2,1,0:T(8,128)(2,1)}, u32[]{:S(2)}, u32[]{:S(2)}) collective-permute-start(bf16[1,32,1024]{2,1,0:T(8,128)(2,1)} %get-tuple-element.82), channel_id=1, source_target_pairs={{0,8},{8,16},{16,24},{1,9},{9,17},{17,25},{2,10},{10,18},{18,26},{... | collective-permute-start | bytes 196616 | tf_op jit(solution)/shard_map/ppermute | solution.py:28
  13.9 88.7 %collective-permute-start.12 = (bf16[1,32,1024]{2,1,0:T(8,128)(2,1)}, bf16[1,32,1024]{2,1,0:T(8,128)(2,1)}, u32[]{:S(2)}, u32[]{:S(2)}) collective-permute-start(bf16[1,32,1024]{2,1,0:T(8,128)(2,1)} %get-tuple-element.83), channel_id=1, source_target_pairs={{8,0},{16,8},{24,16},{9,1},{17,9},{25,17},{10,2},{18,10},{26,18},{... | collective-permute-start | bytes 196616 | tf_op jit(solution)/shard_map/ppermute | solution.py:29
  24.2 8.6 %copy-start.7 = (bf16[32,4,1024]{2,1,0:T(4,128)(2,1)S(1)}, bf16[32,4,1024]{2,1,0:T(4,128)(2,1)}, u32[]{:S(2)}) copy-start(bf16[32,4,1024]{2,1,0:T(4,128)(2,1)} %param.9) | copy-start | bytes 786436
  24.2 8.9 %copy-start.6 = (bf16[27,1,32,32]{2,1,3,0:T(2,128)(2,1)S(1)}, bf16[27,1,32,32]{2,1,3,0:T(2,128)(2,1)}, u32[]{:S(2)}) copy-start(bf16[27,1,32,32]{2,1,3,0:T(2,128)(2,1)} %get-tuple-element.62) | copy-start | bytes 165892
  26.1 16.5 %collective-permute-start.2 = (bf16[27,32,32]{2,1,0:T(8,128)(2,1)}, bf16[27,32,32]{2,1,0:T(8,128)(2,1)}, u32[]{:S(2)}, u32[]{:S(2)}) collective-permute-start(bf16[27,32,32]{2,1,0:T(8,128)(2,1)} %bitcast.25), channel_id=1, source_target_pairs={{0,1},{1,0},{2,3},{3,2},{4,5},{5,4},{6,7},{7,6},{8,9},{9,8},{10,11... | collective-permute-start | bytes 165896 | tf_op jit(solution)/shard_map/ppermute | solution.py:154
  29.3 14.4 %collective-permute-start.3 = (bf16[27,32,32]{2,1,0:T(8,128)(2,1)}, bf16[27,32,32]{2,1,0:T(8,128)(2,1)}, u32[]{:S(2)}, u32[]{:S(2)}) collective-permute-start(bf16[27,32,32]{2,1,0:T(8,128)(2,1)} %bitcast.27), channel_id=1, source_target_pairs={{0,2},{1,3},{2,0},{3,1},{4,6},{5,7},{6,4},{7,5},{8,10},{9,11},{10,... | collective-permute-start | bytes 165896 | tf_op jit(solution)/shard_map/ppermute | solution.py:154
  32.4 15.8 %collective-permute-start.4 = (bf16[27,32,32]{2,1,0:T(8,128)(2,1)}, bf16[27,32,32]{2,1,0:T(8,128)(2,1)}, u32[]{:S(2)}, u32[]{:S(2)}) collective-permute-start(bf16[27,32,32]{2,1,0:T(8,128)(2,1)} %bitcast.29), channel_id=1, source_target_pairs={{0,3},{1,2},{2,1},{3,0},{4,7},{5,6},{6,5},{7,4},{8,11},{9,10},{10,... | collective-permute-start | bytes 165896 | tf_op jit(solution)/shard_map/ppermute | solution.py:154
  42.6 9.1 %collective-permute-start.5 = (bf16[27,32,32]{2,1,0:T(8,128)(2,1)}, bf16[27,32,32]{2,1,0:T(8,128)(2,1)S(1)}, u32[]{:S(2)}, u32[]{:S(2)}) collective-permute-start(bf16[27,32,32]{2,1,0:T(8,128)(2,1)} %bitcast.299), channel_id=1, source_target_pairs={{0,4},{1,5},{2,6},{3,7},{4,0},{5,1},{6,2},{7,3},{8,12},{9,13},{10,... | collective-permute-start | bytes 165896 | tf_op jit(solution)/shard_map/ppermute | solution.py:154
  43.6 39.8 %collective-permute-start.6 = (bf16[27,32,32]{2,1,0:T(8,128)(2,1)}, bf16[27,32,32]{2,1,0:T(8,128)(2,1)S(1)}, u32[]{:S(2)}, u32[]{:S(2)}) collective-permute-start(bf16[27,32,32]{2,1,0:T(8,128)(2,1)} %bitcast.298), channel_id=1, source_target_pairs={{0,5},{1,4},{2,7},{3,6},{4,1},{5,0},{6,3},{7,2},{8,13},{9,12},{10,... | collective-permute-start | bytes 165896 | tf_op jit(solution)/shard_map/ppermute | solution.py:154
  48.2 47.9 %collective-permute-start.7 = (bf16[27,32,32]{2,1,0:T(8,128)(2,1)S(1)}, bf16[27,32,32]{2,1,0:T(8,128)(2,1)S(1)}, u32[]{:S(2)}, u32[]{:S(2)}) collective-permute-start(bf16[27,32,32]{2,1,0:T(8,128)(2,1)S(1)} %bitcast.297), channel_id=1, source_target_pairs={{0,6},{1,7},{2,4},{3,5},{4,2},{5,3},{6,0},{7,1},{8,14},{9,15},{10,... | collective-permute-start | bytes 165896 | tf_op jit(solution)/shard_map/ppermute | solution.py:154
  51.7 49.3 %collective-permute-start.8 = (bf16[27,32,32]{2,1,0:T(8,128)(2,1)S(1)}, bf16[27,32,32]{2,1,0:T(8,128)(2,1)S(1)}, u32[]{:S(2)}, u32[]{:S(2)}) collective-permute-start(bf16[27,32,32]{2,1,0:T(8,128)(2,1)S(1)} %bitcast.296), channel_id=1, source_target_pairs={{0,7},{1,6},{2,5},{3,4},{4,3},{5,2},{6,1},{7,0},{8,15},{9,14},{10,... | collective-permute-start | bytes 165896 | tf_op jit(solution)/shard_map/ppermute | solution.py:154
  101.5 1.1 copy-start.3
  112.1 3.3 %copy-start = (bf16[4,256,1024]{2,1,0:T(8,128)(2,1)S(1)}, bf16[4,256,1024]{2,1,0:T(8,128)(2,1)}, u32[]{:S(2)}) copy-start(bf16[4,256,1024]{2,1,0:T(8,128)(2,1)} %all-gather.3.cloned.1.call-done) | copy-start | bytes 6291460
  112.1 3.6 %copy-start.4 = (bf16[4,9,32,1024]{3,2,1,0:T(8,128)(2,1)S(1)}, bf16[4,9,32,1024]{3,2,1,0:T(8,128)(2,1)}, u32[]{:S(2)}) copy-start(bf16[4,9,32,1024]{3,2,1,0:T(8,128)(2,1)} %copy.81) | copy-start | bytes 7077892
  115.8 1.7 copy-start.5
  119.3 26.1 %collective-permute-start.13 = (f32[224,256]{1,0:T(8,128)}, f32[224,256]{1,0:T(8,128)}, u32[]{:S(2)}, u32[]{:S(2)}) collective-permute-start(f32[224,256]{1,0:T(8,128)} %get-tuple-element.67), channel_id=1, source_target_pairs={{0,8},{8,0},{16,24},{24,16},{1,9},{9,1},{17,25},{25,17},{2,10},{10... | collective-permute-start | bytes 688136 | tf_op jit(solution)/shard_map/ppermute | solution.py:104
  119.3 28.7 %collective-permute-start.14 = (f32[224,256]{1,0:T(8,128)}, f32[224,256]{1,0:T(8,128)}, u32[]{:S(2)}, u32[]{:S(2)}) collective-permute-start(f32[224,256]{1,0:T(8,128)} %get-tuple-element.69), channel_id=1, source_target_pairs={{0,16},{8,24},{16,0},{24,8},{1,17},{9,25},{17,1},{25,9},{2,18},{10... | collective-permute-start | bytes 688136 | tf_op jit(solution)/shard_map/ppermute | solution.py:104
  121.1 29.6 %collective-permute-start.15 = (f32[224,256]{1,0:T(8,128)}, f32[224,256]{1,0:T(8,128)}, u32[]{:S(2)}, u32[]{:S(2)}) collective-permute-start(f32[224,256]{1,0:T(8,128)} %get-tuple-element.68), channel_id=1, source_target_pairs={{0,24},{8,16},{16,8},{24,0},{1,25},{9,17},{17,9},{25,1},{2,26},{10... | collective-permute-start | bytes 688136 | tf_op jit(solution)/shard_map/ppermute | solution.py:104
  121.9 2.5 %copy-start.1 = (bf16[4,256,1024]{2,1,0:T(8,128)(2,1)S(1)}, bf16[4,256,1024]{2,1,0:T(8,128)(2,1)}, u32[]{:S(2)}) copy-start(bf16[4,256,1024]{2,1,0:T(8,128)(2,1)} %all-gather.5.cloned.1.call-done) | copy-start | bytes 6291460
  129.4 8.2 %copy-start.10 = (bf16[1,9,32,256]{3,2,1,0:T(8,128)(2,1)S(1)}, bf16[1,9,32,256]{3,2,1,0:T(8,128)(2,1)}, u32[]{:S(2)}) copy-start(bf16[1,9,32,256]{3,2,1,0:T(8,128)(2,1)} %get-tuple-element.78) | copy-start | bytes 442372
  131.2 22.4 %collective-permute-start.10 = (f32[1,32,1024]{2,1,0:T(8,128)S(1)}, f32[1,32,1024]{2,1,0:T(8,128)S(1)}, u32[]{:S(2)}, u32[]{:S(2)}) collective-permute-start(f32[1,32,1024]{2,1,0:T(8,128)S(1)} %get-tuple-element.71), channel_id=1, source_target_pairs={{8,0},{16,8},{24,16},{9,1},{17,9},{25,17},{10,2},{18,10},{26,18},{... | collective-permute-start | bytes 393224 | tf_op jit(solution)/shard_map/ppermute | solution.py:139
  133.5 20.1 %collective-permute-start.9 = (f32[1,32,1024]{2,1,0:T(8,128)S(1)}, f32[1,32,1024]{2,1,0:T(8,128)S(1)}, u32[]{:S(2)}, u32[]{:S(2)}) collective-permute-start(f32[1,32,1024]{2,1,0:T(8,128)S(1)} %get-tuple-element.70), channel_id=1, source_target_pairs={{0,8},{8,16},{16,24},{1,9},{9,17},{17,25},{2,10},{10,18},{18,26},{... | collective-permute-start | bytes 393224 | tf_op jit(solution)/shard_map/ppermute | solution.py:138
  137.6 0.9 copy-start.9
  138.5 0.9 copy-start.8
  143.6 11.0 %copy-start.11 = (f32[32]{0:T(128)S(1)}, f32[32]{0:T(128)}, u32[]{:S(2)}) copy-start(f32[32]{0:T(128)} %param.8) | copy-start | bytes 388
  143.6 11.0 %copy-start.12 = (f32[4]{0:T(128)S(1)}, f32[4]{0:T(128)}, u32[]{:S(2)}) copy-start(f32[4]{0:T(128)} %pad.135.clone) | copy-start | bytes 52
  145.4 9.3 %collective-permute-start = (f32[1,32,1024]{2,1,0:T(8,128)S(1)}, f32[1,32,1024]{2,1,0:T(8,128)S(1)}, u32[]{:S(2)}, u32[]{:S(2)}) collective-permute-start(f32[1,32,1024]{2,1,0:T(8,128)S(1)} %get-tuple-element.72), channel_id=1, source_target_pairs={{0,8},{8,16},{16,24},{1,9},{9,17},{17,25},{2,10},{10,18},{18,26},{... | collective-permute-start | bytes 393224 | tf_op jit(solution)/shard_map/ppermute | solution.py:138
  148.0 6.7 %collective-permute-start.1 = (f32[1,32,1024]{2,1,0:T(8,128)S(1)}, f32[1,32,1024]{2,1,0:T(8,128)S(1)}, u32[]{:S(2)}, u32[]{:S(2)}) collective-permute-start(f32[1,32,1024]{2,1,0:T(8,128)S(1)} %get-tuple-element.73), channel_id=1, source_target_pairs={{8,0},{16,8},{24,16},{9,1},{17,9},{25,17},{10,2},{18,10},{26,18},{... | collective-permute-start | bytes 393224 | tf_op jit(solution)/shard_map/ppermute | solution.py:139
  151.9 8.3 %collective-permute-start.18 = (f32[224,256]{1,0:T(8,128)S(1)}, f32[224,256]{1,0:T(8,128)S(1)}, u32[]{:S(2)}, u32[]{:S(2)}) collective-permute-start(f32[224,256]{1,0:T(8,128)S(1)} %fusion.64), channel_id=1, source_target_pairs={{0,24},{8,16},{16,8},{24,0},{1,25},{9,17},{17,9},{25,1},{2,26},{10... | collective-permute-start | bytes 688136 | tf_op jit(solution)/shard_map/ppermute | solution.py:106
  153.6 9.2 %collective-permute-start.16 = (f32[224,256]{1,0:T(8,128)S(1)}, f32[224,256]{1,0:T(8,128)S(1)}, u32[]{:S(2)}, u32[]{:S(2)}) collective-permute-start(f32[224,256]{1,0:T(8,128)S(1)} %fusion.64), channel_id=1, source_target_pairs={{0,8},{8,0},{16,24},{24,16},{1,9},{9,1},{17,25},{25,17},{2,10},{10... | collective-permute-start | bytes 688136 | tf_op jit(solution)/shard_map/ppermute | solution.py:106
  153.6 13.2 %collective-permute-start.17 = (f32[224,256]{1,0:T(8,128)S(1)}, f32[224,256]{1,0:T(8,128)S(1)}, u32[]{:S(2)}, u32[]{:S(2)}) collective-permute-start(f32[224,256]{1,0:T(8,128)S(1)} %fusion.64), channel_id=1, source_target_pairs={{0,16},{8,24},{16,0},{24,8},{1,17},{9,25},{17,1},{25,9},{2,18},{10... | collective-permute-start | bytes 688136 | tf_op jit(solution)/shard_map/ppermute | solution.py:106
Sparse Core Ops, SparseCore 0:
  10.2 36.5 all-gather.2
  49.0 43.3 all-gather.4

commit v10 on v8

--- a/solution.py
+++ b/solution.py
@@ -112,6 +112,15 @@
     )
 
 
+def gather_channels(planes):
+    chip_blocks = lax.all_gather(planes, "chips", axis=1, tiled=False)
+    partner = lax.ppermute(chip_blocks, "core", [(0, 1), (1, 0)])
+    first = lax.axis_index("core") == 0
+    low = jnp.where(first, chip_blocks, partner)
+    high = jnp.where(first, partner, chip_blocks)
+    return jnp.stack([low, high], axis=2).reshape(planes.shape[0], -1, planes.shape[2])
+
+
 def scatter_channels(blocks):
     by_core = blocks.reshape((-1, 2) + blocks.shape[1:])
     core = lax.axis_index("core")
@@ -133,7 +142,7 @@
     grad_scale = 1.0 / math.sqrt(lax.axis_size("space") * depth_cells * plane_cells)
     inputs_planes = jnp.transpose(inputs, (1, 0, 2))
     grad_planes = jnp.transpose(output_grad, (1, 0, 2))
-    gathered = lax.all_gather(inputs_planes, ("chips", "core"), axis=1, tiled=True)
+    gathered = gather_channels(inputs_planes)
 
     weight_grid = weight.reshape(3, 9, channels_in, block_out)
     forward_weight = jnp.transpose(weight_grid, (0, 1, 3, 2)).reshape(3, 9 * block_out, channels_in)

time: 98.5 us -> 107 us (1.086)
  waiting for transfers between devices: 20.8 us -> 25.1 us
  local copies, waits for them, and re-layouts: 17.1 us -> 21.2 us
  other arithmetic: 12.4 us -> 15.2 us
  matrix products: 12.6 us -> 10.6 us
  between operations: 15.9 us -> 14.6 us
    all_gather x1, waiting for transfers between devices: 5.85 us -> 11.7 us  [gather_channels(): chip_blocks = lax.all_gather(planes, 'chips', axis=1, tiled=False)]
    ppermute x1, waiting for transfers between devices: 4.14 us -> 0.01 us  [scatter_channels(): partial = keep + lax.ppermute(send, 'core', [(0, 1), (1, 0)])]
    all_gather x0 -> x1, local copies, waits for them, and re-layouts: none -> 2.52 us  [gather_channels(): chip_blocks = lax.all_gather(planes, 'chips', axis=1, tiled=False)]
    another operation x0 -> x2, other arithmetic: none -> 2.22 us  [gather_channels(): jnp.stack([low, high], axis=2).reshape(planes.shape[0], -1, planes.shape[2])]
    dot_general x3, matrix products: 4.36 us -> 2.42 us  [body(): jnp.einsum('zkn,zin->ki', grad_shifted[2 - depth_index:2 - depth_index +...]
    ppermute x1, waiting for transfers between devices: 0.01 us -> 1.68 us  [padded_2(): after = lax.ppermute(first, axis, down)]
    unnamed x20 -> x39, local copies, waits for them, and re-layouts: 6.95 us -> 7.25 us
  transfers between devices with their start and end apart: 13 -> 14, of which waited for: 6 -> 6; matrix products, arithmetic and copies ran while one was open for 37% -> 37% of each run, Pallas kernels for 0% -> 0%
where the time goes in v10:
time: 107 us; the launch traced here: 106 us
  waiting for transfers between devices  25.1 us (23%)
  local copies, waits for them, and re-layouts  21.2 us (20%)
  starting transfers between devices  19.6 us (18%)
  other arithmetic  15.2 us (14%)
  between operations  14.6 us (14%)
  matrix products  10.6 us (10%)
    all_gather x1, waiting for transfers between devices, gather_channels(): chip_blocks = lax.all_gather(planes, 'chips', axis=1, tiled=False)  11.7 us
    ppermute x3, waiting for transfers between devices, all_reduce_direct(): lax.ppermute(reduced, axis, [(i, i ^ distance) for i in range(devices)])  7.98 us
    unnamed x39, local copies, waits for them, and re-layouts  7.25 us
    dot_general x3, matrix products, body(): jnp.einsum('bjk,zkn->bzjn', backward_weight[depth_index], grad_shifted[2...  5.85 us
    ppermute x3, starting transfers between devices, all_reduce_direct(): lax.ppermute(reduced, axis, [(i, i ^ distance) for i in range(devices)])  5.08 us
    ppermute x1, starting transfers between devices, padded_2(): before = lax.ppermute(last, axis, up)  4.85 us
    add x1, other arithmetic, scatter_channels(): partial = keep + lax.ppermute(send, 'core', [(0, 1), (1, 0)])  4.13 us
    ppermute x3, starting transfers between devices, all_reduce_direct(): reduced = reduced + lax.ppermute(send, axis, pairs)  3.55 us
  transfers between devices with their start and end apart: 14, of which 6 were waited for; matrix products, arithmetic and copies ran while one was open for 37% of the time, Pallas kernels for 0%

profile of v10, /device:TPU:0, one launch (start us, length us, event | category | flops | bytes accessed | tf_op | source)
XLA Modules:
  0.0 106.3 jit_solution(12599787409148802749)
XLA Ops:
  7.2 1.0 copy.101
  8.3 4.8 %collective-permute-start.3 = (bf16[1,32,1024]{2,1,0:T(8,128)(2,1)S(1)}, bf16[1,32,1024]{2,1,0:T(8,128)(2,1)S(1)}, u32[]{:S(2)}, u32[]{:S(2)}) collective-permute-start(bf16[1,32,1024]{2,1,0:T(8,128)(2,1)S(1)} %get-tuple-element.56), channel_id=1, source_target_pairs={{0,8},{8,16},{16,24},{1,9},{9,17},{17,25},{2,10},{10,18},{18,26},{... | collective-permute-start | bytes 196616 | tf_op jit(solution)/shard_map/ppermute | solution.py:28
  13.1 1.3 %collective-permute-start.4 = (bf16[1,32,1024]{2,1,0:T(8,128)(2,1)S(1)}, bf16[1,32,1024]{2,1,0:T(8,128)(2,1)S(1)}, u32[]{:S(2)}, u32[]{:S(2)}) collective-permute-start(bf16[1,32,1024]{2,1,0:T(8,128)(2,1)S(1)} %get-tuple-element.57), channel_id=1, source_target_pairs={{8,0},{16,8},{24,16},{9,1},{17,9},{25,17},{10,2},{18,10},{26,18},{... | collective-permute-start | bytes 196616 | tf_op jit(solution)/shard_map/ppermute | solution.py:29
  14.5 1.1 %fusion.67 = (bf16[1,256,9,32]{1,3,2,0:T(8,128)(2,1)S(1)}, bf16[1,256,9,32]{1,3,2,0:T(8,128)(2,1)S(1)}, bf16[1,256,9,32]{1,3,2,0:T(8,128)(2,1)S(1)}) fusion(bf16[3,256,9,32]{1,3,2,0:T(8,128)(2,1)} %bitcast.244), kind=kLoop, calls=%fused_computation.132 | loop fusion | bytes 884736 | tf_op jit(solution)/shard_map/slice | solution.py:212
  17.6 1.7 %collective-permute-done.4 = bf16[1,32,1024]{2,1,0:T(8,128)(2,1)S(1)} collective-permute-done((bf16[1,32,1024]{2,1,0:T(8,128)(2,1)S(1)}, bf16[1,32,1024]{2,1,0:T(8,128)(2,1)S(1)}, u32[]{:S(2)}, u32[]{:S(2)}) %collective-permute-start.4) | collective-permute-done | bytes 65568 | tf_op jit(solution)/shard_map/ppermute | solution.py:29
  20.9 1.0 fusion.65
  22.7 1.1 %copy-done = bf16[4,9,32,1024]{3,2,1,0:T(8,128)(2,1)} copy-done((bf16[4,9,32,1024]{3,2,1,0:T(8,128)(2,1)}, bf16[4,9,32,1024]{3,2,1,0:T(8,128)(2,1)S(1)}, u32[]{:S(2)}) %copy-start) | copy-done | bytes 2359320
  23.8 1.8 %fusion.47 = f32[4,1024,8,32]{1,3,2,0:T(8,128)S(1)} fusion(bf16[4,288,1024,1]{2,1,3,0:T(8,128)(2,1)S(1)} %bitcast.231, bf16[8,32,288]{2,1,0:T(8,128)(2,1)S(1)} %copy.75), kind=kOutput, calls=%fused_computation.107 | convolution fusion | flops 603979776 | bytes 6701056 | tf_op jit(solution)/shard_map/bjk,zkn->bzjn/dot_general | solution.py:210
  25.6 1.8 %fusion.49 = f32[4,1024,8,32]{1,3,2,0:T(8,128)S(1)} fusion(bf16[4,288,1024,1]{2,1,3,0:T(8,128)(2,1)S(1)} %bitcast.233, bf16[8,32,288]{2,1,0:T(8,128)(2,1)S(1)} %copy.73), kind=kOutput, calls=%fused_computation.109 | convolution fusion | flops 603979776 | bytes 6701056 | tf_op jit(solution)/shard_map/bjk,zkn->bzjn/dot_general | solution.py:210
  27.3 2.3 %add_add_fusion = f32[4,1024,8,32]{1,3,2,0:T(8,128)S(1)} fusion(f32[4,1024,8,32]{1,3,2,0:T(8,128)S(1)} %fusion.49, f32[4,1024,8,32]{1,3,2,0:T(8,128)S(1)} %fusion.47, bf16[4,288,1024,1]{2,1,3,0:T(8,128)(2,1)S(1)} %bitcast.229, bf16[8,32,288]{2,1,0:T(8,128)(2,1)S(1)} %copy.77), kind=kOutput, calls=%fused_computation.1 | convolution fusion | flops 606076928 | bytes 15089664 | tf_op jit(solution)/shard_map/bjk,zkn->bzjn/dot_general | solution.py:210
  29.7 1.9 %constant_dynamic-slice_fusion.1 = (f32[4,1,4,32,1024]{4,3,1,0,2:T(8,128)}, f32[4,1,4,32,1024]{4,3,1,0,2:T(8,128)S(1)}) fusion(f32[4,2,4,32,1024]{4,3,1,0,2:T(8,128)S(1)} %bitcast.220, s32[]{:T(128)S(6)} %select_n.196, s32[]{:T(128)S(6)} %select_n.197), kind=kLoop, calls=%fused_computation.128 | loop fusion | bytes 8388616 | tf_op jit(solution)/shard_map/jit(dynamic_index_in_dim)/dynamic_slice | solution.py:127
  31.6 1.6 %copy.100 = f32[4,1,4,32,1024]{4,3,2,0,1:T(8,128)} copy(f32[4,1,4,32,1024]{4,3,1,0,2:T(8,128)S(1)} %get-tuple-element.33) | data formatting | bytes 4194304 | tf_op jit(solution)/shard_map/jit(dynamic_index_in_dim)/dynamic_slice | solution.py:128
  33.2 11.7 %all-gather.3.cloned.1.call-done = bf16[4,128,1024]{2,0,1:T(4,128)(2,1)} async-done(((bf16[4,32,1024]{2,0,1:T(4,128)(2,1)}), bf16[4,128,1024]{2,0,1:T(4,128)(2,1)}) %all-gather.3.cloned.1.call-update) | async-done | bytes 1048592 | tf_op jit(solution)/shard_map/all_gather | solution.py:116
  44.9 2.5 %copy.57 = bf16[4,4,32,1024]{3,2,1,0:T(8,128)(2,1)} copy(bf16[4,4,32,1024]{3,0,2,1:T(4,128)(2,1)} %bitcast.236) | data formatting | bytes 2097152 | tf_op jit(solution)/shard_map/all_gather | solution.py:116
  47.5 0.6 pad.87.clone
  48.0 0.9 convert_reduce_fusion
  49.0 0.7 fusion.68
  49.7 4.1 %bitcast_add_fusion = f32[4,4,32,1024]{3,2,1,0:T(8,128)} fusion(f32[4,4,32,1024]{3,2,1,0:T(8,128)} %collective-permute-done.5, f32[4,1,4,32,1024]{4,3,1,0,2:T(8,128)} %get-tuple-element.32), kind=kLoop, calls=%fused_computation.6 | loop fusion | flops 524288 | bytes 6291456 | tf_op jit(solution)/shard_map/add | solution.py:129
  53.9 1.2 %copy-done.4 = bf16[4,128,1024]{2,0,1:T(4,128)(2,1)S(1)} copy-done((bf16[4,128,1024]{2,0,1:T(4,128)(2,1)S(1)}, bf16[4,128,1024]{2,0,1:T(4,128)(2,1)}, u32[]{:S(2)}) %copy-start.4) | copy-done | bytes 1048600
  55.0 1.8 %select_bitcast_fusion.1 = (bf16[4,4,1,32,1024]{4,3,2,1,0:T(8,128)(2,1)S(1)}, bf16[4,4,1,32,1024]{4,3,2,1,0:T(8,128)(2,1)S(1)}) fusion(bf16[4,4,32,1024]{3,2,1,0:T(8,128)(2,1)} %collective-permute-done, pred[]{:T(512)S(6)} %eq.22, bf16[4,4,32,1024]{3,0,2,1:T(4,128)(2,1)S(1)} %bitcast.237), kind=kLoop, calls=%fused_computation.14 | loop fusion | flops 1048576 | bytes 4194305 | tf_op jit(solution)/shard_map/stack | solution.py:121
  57.3 0.8 convolution_bitcast_fusion.3
  58.1 0.8 copy-done.1
  58.9 0.8 convolution_bitcast_fusion.4
  59.8 1.1 %copy-done.3 = bf16[4,9,32,1024]{3,2,1,0:T(8,128)(2,1)S(1)} copy-done((bf16[4,9,32,1024]{3,2,1,0:T(8,128)(2,1)S(1)}, bf16[4,9,32,1024]{3,2,1,0:T(8,128)(2,1)}, u32[]{:S(2)}) %copy-start.3) | copy-done | bytes 2359320
  60.9 0.8 convolution_bitcast_fusion.5
  61.9 1.6 %collective-permute-start.6 = (f32[224,256]{1,0:T(8,128)S(1)}, f32[224,256]{1,0:T(8,128)S(1)}, u32[]{:S(2)}, u32[]{:S(2)}) collective-permute-start(f32[224,256]{1,0:T(8,128)S(1)} %get-tuple-element.43), channel_id=1, source_target_pairs={{0,8},{8,0},{16,24},{24,16},{1,9},{9,1},{17,25},{25,17},{2,10},{10... | collective-permute-start | bytes 688136 | tf_op jit(solution)/shard_map/ppermute | solution.py:104
  63.5 1.5 %collective-permute-start.7 = (f32[224,256]{1,0:T(8,128)S(1)}, f32[224,256]{1,0:T(8,128)S(1)}, u32[]{:S(2)}, u32[]{:S(2)}) collective-permute-start(f32[224,256]{1,0:T(8,128)S(1)} %get-tuple-element.45), channel_id=1, source_target_pairs={{0,16},{8,24},{16,0},{24,8},{1,17},{9,25},{17,1},{25,9},{2,18},{10... | collective-permute-start | bytes 688136 | tf_op jit(solution)/shard_map/ppermute | solution.py:104
  65.0 0.5 collective-permute-start.8
  65.5 0.8 convolution_bitcast_fusion.1
  66.4 0.8 convolution_bitcast_fusion.2
  67.2 0.8 convolution_bitcast_fusion
  68.0 2.3 %pad_add_fusion = f32[6,288,1024]{2,1,0:T(8,128)S(1)} fusion(f32[4,288,1024]{2,1,0:T(8,128)S(1)} %convolution_bitcast_fusion, f32[4,288,1024]{2,1,0:T(8,128)S(1)} %convolution_bitcast_fusion.1, f32[4,288,1024]{2,1,0:T(8,128)S(1)} %convolution_bitcast_fusion.2), kind=kLoop, calls=%fused_computation | loop fusion | flops 3538944 | bytes 21233664 | tf_op jit(solution)/shard_map/add | solution.py:158
  70.3 1.1 %slice_bitcast_fusion = (f32[6,32,1024]{2,1,0:T(8,128)S(1)}, f32[6,32,1024]{2,1,0:T(8,128)S(1)}, f32[6,32,1024]{2,1,0:T(8,128)S(1)}, f32[6,32,1024]{2,1,0:T(8,12...) fusion(f32[6,9,32,1024]{3,2,1,0:T(8,128)S(1)} %bitcast.227), kind=kLoop, calls=%fused_computation.48 | loop fusion | bytes 12582912 | tf_op jit(solution)/shard_map/squeeze | solution.py:162
  71.5 1.7 %fusion.10 = f32[6,32,1024]{2,1,0:T(8,128)S(1)} fusion(f32[6,32,1024]{2,1,0:T(8,128)S(1)} %get-tuple-element.31, f32[6,32,1024]{2,1,0:T(8,128)S(1)} %get-tuple-element.30, f32[6,32,1024]{2,1,0:T(8,128)S(1)} %get-tuple-element.29, f32[6,32,1024]{2,1,0:T(8,128)S(1)} %get-tuple-element.28, f32[6,32,1024]{2,1,0:T(8,128)S(1)} %get-tuple-element.27, ...), kind=kLoop, calls=%fused_computation.40 | loop fusion | flops 3342336 | bytes 7867392 | tf_op jit(solution)/shard_map/add | solution.py:163
  73.2 3.5 %collective-permute-start.1 = (f32[1,32,1024]{2,1,0:T(8,128)S(1)}, f32[1,32,1024]{2,1,0:T(8,128)S(1)}, u32[]{:S(2)}, u32[]{:S(2)}) collective-permute-start(f32[1,32,1024]{2,1,0:T(8,128)S(1)} %get-tuple-element.46), channel_id=1, source_target_pairs={{0,8},{8,16},{16,24},{1,9},{9,17},{17,25},{2,10},{10,18},{18,26},{... | collective-permute-start | bytes 393224 | tf_op jit(solution)/shard_map/ppermute | solution.py:167
  76.6 1.3 %collective-permute-start.2 = (f32[1,32,1024]{2,1,0:T(8,128)S(1)}, f32[1,32,1024]{2,1,0:T(8,128)S(1)}, u32[]{:S(2)}, u32[]{:S(2)}) collective-permute-start(f32[1,32,1024]{2,1,0:T(8,128)S(1)} %get-tuple-element.47), channel_id=1, source_target_pairs={{8,0},{16,8},{24,16},{9,1},{17,9},{25,17},{10,2},{18,10},{26,18},{... | collective-permute-start | bytes 393224 | tf_op jit(solution)/shard_map/ppermute | solution.py:168
  78.0 2.7 %collective-permute-start.9 = (f32[224,256]{1,0:T(8,128)S(1)}, f32[224,256]{1,0:T(8,128)S(1)}, u32[]{:S(2)}, u32[]{:S(2)}) collective-permute-start(f32[224,256]{1,0:T(8,128)S(1)} %fusion.45), channel_id=1, source_target_pairs={{0,8},{8,0},{16,24},{24,16},{1,9},{9,1},{17,25},{25,17},{2,10},{10... | collective-permute-start | bytes 688136 | tf_op jit(solution)/shard_map/ppermute | solution.py:106
  80.8 1.5 %collective-permute-start.10 = (f32[224,256]{1,0:T(8,128)S(1)}, f32[224,256]{1,0:T(8,128)S(1)}, u32[]{:S(2)}, u32[]{:S(2)}) collective-permute-start(f32[224,256]{1,0:T(8,128)S(1)} %fusion.45), channel_id=1, source_target_pairs={{0,16},{8,24},{16,0},{24,8},{1,17},{9,25},{17,1},{25,9},{2,18},{10... | collective-permute-start | bytes 688136 | tf_op jit(solution)/shard_map/ppermute | solution.py:106
  82.2 0.9 collective-permute-start.11
  83.1 1.8 %collective-permute-done.2 = f32[1,32,1024]{2,1,0:T(8,128)S(1)} collective-permute-done((f32[1,32,1024]{2,1,0:T(8,128)S(1)}, f32[1,32,1024]{2,1,0:T(8,128)S(1)}, u32[]{:S(2)}, u32[]{:S(2)}) %collective-permute-start.2) | collective-permute-done | bytes 131104 | tf_op jit(solution)/shard_map/ppermute | solution.py:168
  85.1 0.9 copy.80
  86.0 3.9 %collective-permute-done.9 = f32[224,256]{1,0:T(8,128)S(1)} collective-permute-done((f32[224,256]{1,0:T(8,128)S(1)}, f32[224,256]{1,0:T(8,128)S(1)}, u32[]{:S(2)}, u32[]{:S(2)}) %collective-permute-start.9) | collective-permute-done | bytes 229408 | tf_op jit(solution)/shard_map/ppermute | solution.py:106
  89.9 4.1 %collective-permute-done.11 = f32[224,256]{1,0:T(8,128)S(1)} collective-permute-done((f32[224,256]{1,0:T(8,128)S(1)}, f32[224,256]{1,0:T(8,128)S(1)}, u32[]{:S(2)}, u32[]{:S(2)}) %collective-permute-start.11) | collective-permute-done | bytes 229408 | tf_op jit(solution)/shard_map/ppermute | solution.py:106
  94.2 1.0 pad_maximum_fusion.2
  95.1 0.5 slice_bitcast_fusion.9
  95.6 1.9 %reduce-scatter.2.cloned.1.call-done = f32[128,1024]{1,0:T(8,128)} async-done(((f32[512,1024]{1,0:T(8,128)}), f32[128,1024]{1,0:T(8,128)}) %reduce-scatter.2.cloned.1.call-update) | async-done | bytes 524304 | tf_op jit(solution)/shard_map/reduce_scatter | solution.py:130
  97.5 1.1 %convert_element_type.39 = bf16[128,1024]{1,0:T(8,128)(2,1)S(1)} convert(f32[128,1024]{1,0:T(8,128)} %reduce-scatter.2.cloned.1.call-done) | non-fusion elementwise | flops 131072 | bytes 786432 | tf_op jit(solution)/shard_map/convert_element_type | solution.py:218
  98.6 0.9 copy.81
  (78 shorter events, 5.4 us)
Async XLA Ops:
  7.2 37.8 %all-gather.3.cloned.1.call-start = ((), (), s32[]{:S(2)}) async-start(), calls=%async_computation.2 | async-start | bytes 1310720 | tf_op jit(solution)/shard_map/all_gather | solution.py:116
  8.3 9.3 %collective-permute-start.3 = (bf16[1,32,1024]{2,1,0:T(8,128)(2,1)S(1)}, bf16[1,32,1024]{2,1,0:T(8,128)(2,1)S(1)}, u32[]{:S(2)}, u32[]{:S(2)}) collective-permute-start(bf16[1,32,1024]{2,1,0:T(8,128)(2,1)S(1)} %get-tuple-element.56), channel_id=1, source_target_pairs={{0,8},{8,16},{16,24},{1,9},{9,17},{17,25},{2,10},{10,18},{18,26},{... | collective-permute-start | bytes 196616 | tf_op jit(solution)/shard_map/ppermute | solution.py:28
  13.1 6.2 %collective-permute-start.4 = (bf16[1,32,1024]{2,1,0:T(8,128)(2,1)S(1)}, bf16[1,32,1024]{2,1,0:T(8,128)(2,1)S(1)}, u32[]{:S(2)}, u32[]{:S(2)}) collective-permute-start(bf16[1,32,1024]{2,1,0:T(8,128)(2,1)S(1)} %get-tuple-element.57), channel_id=1, source_target_pairs={{8,0},{16,8},{24,16},{9,1},{17,9},{25,17},{10,2},{18,10},{26,18},{... | collective-permute-start | bytes 196616 | tf_op jit(solution)/shard_map/ppermute | solution.py:29
  14.4 83.1 %reduce-scatter.2.cloned.1.call-start = ((), (), s32[]{:S(2)}) async-start(), calls=%async_computation.1 | async-start | bytes 2621440 | tf_op jit(solution)/shard_map/reduce_scatter | solution.py:130
  14.5 5.9 %copy-start.9 = (pred[1024]{0:T(1024)(128)(4,1)}, pred[1024]{0:T(1024)(128)(4,1)S(1)}, u32[]{:S(2)}) copy-start(pred[1024]{0:T(1024)(128)(4,1)S(1)} %get-tuple-element.58) | copy-start | bytes 3076
  14.5 6.3 %copy-start.11 = (pred[1024]{0:T(1024)(128)(4,1)}, pred[1024]{0:T(1024)(128)(4,1)S(1)}, u32[]{:S(2)}) copy-start(pred[1024]{0:T(1024)(128)(4,1)S(1)} %get-tuple-element.59) | copy-start | bytes 3076
  17.6 3.0 %copy-start.13 = (pred[1024]{0:T(1024)(128)(4,1)}, pred[1024]{0:T(1024)(128)(4,1)S(1)}, u32[]{:S(2)}) copy-start(pred[1024]{0:T(1024)(128)(4,1)S(1)} %fusion.63) | copy-start | bytes 3076
  22.4 1.4 %copy-start = (bf16[4,9,32,1024]{3,2,1,0:T(8,128)(2,1)}, bf16[4,9,32,1024]{3,2,1,0:T(8,128)(2,1)S(1)}, u32[]{:S(2)}) copy-start(bf16[4,9,32,1024]{3,2,1,0:T(8,128)(2,1)S(1)} %copy.74) | copy-start | bytes 7077892
  22.7 2.8 %copy-start.2 = (bf16[4,9,32,1024]{3,2,1,0:T(8,128)(2,1)}, bf16[4,9,32,1024]{3,2,1,0:T(8,128)(2,1)S(1)}, u32[]{:S(2)}) copy-start(bf16[4,9,32,1024]{3,2,1,0:T(8,128)(2,1)S(1)} %copy.72) | copy-start | bytes 7077892
  31.6 16.4 %copy-start.6 = (bf16[32,4,1024]{2,1,0:T(4,128)(2,1)S(1)}, bf16[32,4,1024]{2,1,0:T(4,128)(2,1)}, u32[]{:S(2)}) copy-start(bf16[32,4,1024]{2,1,0:T(4,128)(2,1)} %param.9) | copy-start | bytes 786436
  31.6 17.3 %copy-start.5 = (bf16[27,256,32]{1,2,0:T(8,128)(2,1)S(1)}, bf16[27,256,32]{1,2,0:T(8,128)(2,1)}, u32[]{:S(2)}) copy-start(bf16[27,256,32]{1,2,0:T(8,128)(2,1)} %param.7) | copy-start | bytes 1327108
  33.2 16.5 %collective-permute-start.5 = (f32[4,4,32,1024]{3,2,1,0:T(8,128)}, f32[4,4,32,1024]{3,2,1,0:T(8,128)}, u32[]{:S(2)}, u32[]{:S(2)}) collective-permute-start(f32[4,4,32,1024]{3,2,1,0:T(8,128)} %bitcast.218), channel_id=1, source_target_pairs={{0,1},{1,0},{2,3},{3,2},{4,5},{5,4},{6,7},{7,6},{8,9},{9,8},{10,11... | collective-permute-start | bytes 6291464 | tf_op jit(solution)/shard_map/ppermute | solution.py:129
  47.5 6.4 %collective-permute-start = (bf16[4,4,32,1024]{3,2,1,0:T(8,128)(2,1)}, bf16[4,4,32,1024]{3,2,1,0:T(8,128)(2,1)}, u32[]{:S(2)}, u32[]{:S(2)}) collective-permute-start(bf16[4,4,32,1024]{3,2,1,0:T(8,128)(2,1)} %copy.57), channel_id=1, source_target_pairs={{0,1},{1,0},{2,3},{3,2},{4,5},{5,4},{6,7},{7,6},{8,9},{9,8},{10,11... | collective-permute-start | bytes 3145736 | tf_op jit(solution)/shard_map/ppermute | solution.py:117
  53.8 1.2 %copy-start.4 = (bf16[4,128,1024]{2,0,1:T(4,128)(2,1)S(1)}, bf16[4,128,1024]{2,0,1:T(4,128)(2,1)}, u32[]{:S(2)}) copy-start(bf16[4,128,1024]{2,0,1:T(4,128)(2,1)} %all-gather.3.cloned.1.call-done) | copy-start | bytes 3145732
  57.3 1.7 %copy-start.1 = (bf16[4,9,32,1024]{3,2,1,0:T(8,128)(2,1)S(1)}, bf16[4,9,32,1024]{3,2,1,0:T(8,128)(2,1)}, u32[]{:S(2)}) copy-start(bf16[4,9,32,1024]{3,2,1,0:T(8,128)(2,1)} %copy-done) | copy-start | bytes 7077892
  58.9 1.9 %copy-start.3 = (bf16[4,9,32,1024]{3,2,1,0:T(8,128)(2,1)S(1)}, bf16[4,9,32,1024]{3,2,1,0:T(8,128)(2,1)}, u32[]{:S(2)}) copy-start(bf16[4,9,32,1024]{3,2,1,0:T(8,128)(2,1)} %copy-done.2) | copy-start | bytes 7077892
  60.9 0.9 copy-start.15
  61.7 3.8 %copy-start.8 = (bf16[1,9,32,256]{3,2,1,0:T(8,128)(2,1)S(1)}, bf16[1,9,32,256]{3,2,1,0:T(8,128)(2,1)}, u32[]{:S(2)}) copy-start(bf16[1,9,32,256]{3,2,1,0:T(8,128)(2,1)} %get-tuple-element.53) | copy-start | bytes 442372
  61.9 16.0 %collective-permute-start.6 = (f32[224,256]{1,0:T(8,128)S(1)}, f32[224,256]{1,0:T(8,128)S(1)}, u32[]{:S(2)}, u32[]{:S(2)}) collective-permute-start(f32[224,256]{1,0:T(8,128)S(1)} %get-tuple-element.43), channel_id=1, source_target_pairs={{0,8},{8,0},{16,24},{24,16},{1,9},{9,1},{17,25},{25,17},{2,10},{10... | collective-permute-start | bytes 688136 | tf_op jit(solution)/shard_map/ppermute | solution.py:104
  63.5 14.4 %collective-permute-start.7 = (f32[224,256]{1,0:T(8,128)S(1)}, f32[224,256]{1,0:T(8,128)S(1)}, u32[]{:S(2)}, u32[]{:S(2)}) collective-permute-start(f32[224,256]{1,0:T(8,128)S(1)} %get-tuple-element.45), channel_id=1, source_target_pairs={{0,16},{8,24},{16,0},{24,8},{1,17},{9,25},{17,1},{25,9},{2,18},{10... | collective-permute-start | bytes 688136 | tf_op jit(solution)/shard_map/ppermute | solution.py:104
  65.0 13.0 %collective-permute-start.8 = (f32[224,256]{1,0:T(8,128)S(1)}, f32[224,256]{1,0:T(8,128)S(1)}, u32[]{:S(2)}, u32[]{:S(2)}) collective-permute-start(f32[224,256]{1,0:T(8,128)S(1)} %get-tuple-element.44), channel_id=1, source_target_pairs={{0,24},{8,16},{16,8},{24,0},{1,25},{9,17},{17,9},{25,1},{2,26},{10... | collective-permute-start | bytes 688136 | tf_op jit(solution)/shard_map/ppermute | solution.py:104
  65.5 0.9 copy-start.7
  70.2 1.2 %copy-start.10 = (pred[1024]{0:T(1024)(128)(4,1)S(1)}, pred[1024]{0:T(1024)(128)(4,1)}, u32[]{:S(2)}) copy-start(pred[1024]{0:T(1024)(128)(4,1)} %copy-done.9) | copy-start | bytes 3076
  70.3 1.2 %copy-start.12 = (pred[1024]{0:T(1024)(128)(4,1)S(1)}, pred[1024]{0:T(1024)(128)(4,1)}, u32[]{:S(2)}) copy-start(pred[1024]{0:T(1024)(128)(4,1)} %copy-done.11) | copy-start | bytes 3076
  70.3 1.2 %copy-start.14 = (pred[1024]{0:T(1024)(128)(4,1)S(1)}, pred[1024]{0:T(1024)(128)(4,1)}, u32[]{:S(2)}) copy-start(pred[1024]{0:T(1024)(128)(4,1)} %copy-done.13) | copy-start | bytes 3076
  71.4 13.5 %copy-start.16 = (f32[32]{0:T(128)S(1)}, f32[32]{0:T(128)}, u32[]{:S(2)}) copy-start(f32[32]{0:T(128)} %param.8) | copy-start | bytes 388
  71.4 13.5 %copy-start.17 = (f32[4]{0:T(128)S(1)}, f32[4]{0:T(128)}, u32[]{:S(2)}) copy-start(f32[4]{0:T(128)} %pad.87.clone) | copy-start | bytes 52
  73.2 10.0 %collective-permute-start.1 = (f32[1,32,1024]{2,1,0:T(8,128)S(1)}, f32[1,32,1024]{2,1,0:T(8,128)S(1)}, u32[]{:S(2)}, u32[]{:S(2)}) collective-permute-start(f32[1,32,1024]{2,1,0:T(8,128)S(1)} %get-tuple-element.46), channel_id=1, source_target_pairs={{0,8},{8,16},{16,24},{1,9},{9,17},{17,25},{2,10},{10,18},{18,26},{... | collective-permute-start | bytes 393224 | tf_op jit(solution)/shard_map/ppermute | solution.py:167
  76.6 8.3 %collective-permute-start.2 = (f32[1,32,1024]{2,1,0:T(8,128)S(1)}, f32[1,32,1024]{2,1,0:T(8,128)S(1)}, u32[]{:S(2)}, u32[]{:S(2)}) collective-permute-start(f32[1,32,1024]{2,1,0:T(8,128)S(1)} %get-tuple-element.47), channel_id=1, source_target_pairs={{8,0},{16,8},{24,16},{9,1},{17,9},{25,17},{10,2},{18,10},{26,18},{... | collective-permute-start | bytes 393224 | tf_op jit(solution)/shard_map/ppermute | solution.py:168
  78.0 11.8 %collective-permute-start.9 = (f32[224,256]{1,0:T(8,128)S(1)}, f32[224,256]{1,0:T(8,128)S(1)}, u32[]{:S(2)}, u32[]{:S(2)}) collective-permute-start(f32[224,256]{1,0:T(8,128)S(1)} %fusion.45), channel_id=1, source_target_pairs={{0,8},{8,0},{16,24},{24,16},{1,9},{9,1},{17,25},{25,17},{2,10},{10... | collective-permute-start | bytes 688136 | tf_op jit(solution)/shard_map/ppermute | solution.py:106
  80.8 9.1 %collective-permute-start.10 = (f32[224,256]{1,0:T(8,128)S(1)}, f32[224,256]{1,0:T(8,128)S(1)}, u32[]{:S(2)}, u32[]{:S(2)}) collective-permute-start(f32[224,256]{1,0:T(8,128)S(1)} %fusion.45), channel_id=1, source_target_pairs={{0,16},{8,24},{16,0},{24,8},{1,17},{9,25},{17,1},{25,9},{2,18},{10... | collective-permute-start | bytes 688136 | tf_op jit(solution)/shard_map/ppermute | solution.py:106
  82.2 11.8 %collective-permute-start.11 = (f32[224,256]{1,0:T(8,128)S(1)}, f32[224,256]{1,0:T(8,128)S(1)}, u32[]{:S(2)}, u32[]{:S(2)}) collective-permute-start(f32[224,256]{1,0:T(8,128)S(1)} %fusion.45), channel_id=1, source_target_pairs={{0,24},{8,16},{16,8},{24,0},{1,25},{9,17},{17,9},{25,1},{2,26},{10... | collective-permute-start | bytes 688136 | tf_op jit(solution)/shard_map/ppermute | solution.py:106
Sparse Core Ops, SparseCore 0:
  14.6 30.3 all-gather.2
  54.0 43.5 reduce-scatter.1

commit v11 on v8

--- a/solution.py
+++ b/solution.py
@@ -132,6 +132,7 @@
     plane_cells = inputs.shape[2]
     grad_scale = 1.0 / math.sqrt(lax.axis_size("space") * depth_cells * plane_cells)
     inputs_planes = jnp.transpose(inputs, (1, 0, 2))
+    inputs_planes, output_grad = lax.optimization_barrier((inputs_planes, output_grad))
     grad_planes = jnp.transpose(output_grad, (1, 0, 2))
     gathered = lax.all_gather(inputs_planes, ("chips", "core"), axis=1, tiled=True)
 
@@ -194,18 +195,27 @@
 
     chan_devices = lax.axis_size("chips") * lax.axis_size("core")
     backward_weight = jnp.transpose(weight_grid, (0, 2, 1, 3)).reshape(
-        3, chan_devices, channels_in // chan_devices, 9 * block_out
-    )
-    spread = None
-    for depth_index in range(3):
-        part = jnp.einsum(
-            "bjk,zkn->bzjn",
-            backward_weight[depth_index],
-            grad_shifted[2 - depth_index : 2 - depth_index + depth_cells],
-            preferred_element_type=jnp.float32,
-        )
-        spread = part if spread is None else spread + part
-    summed = scatter_channels(spread).reshape(depth_cells, block_in, plane_cells)
+        3, chan_devices // 2, 2, channels_in // chan_devices, 9 * block_out
+    )
+    core = lax.axis_index("core")
+
+    def partial_sums(core_weight, total):
+        for depth_index in range(3):
+            part = jnp.einsum(
+                "cjk,zkn->czjn",
+                core_weight[depth_index],
+                grad_shifted[2 - depth_index : 2 - depth_index + depth_cells],
+                preferred_element_type=jnp.float32,
+            )
+            total = part if total is None else total + part
+        return total
+
+    sent = partial_sums(lax.dynamic_index_in_dim(backward_weight, 1 - core, axis=2, keepdims=False), None)
+    received = lax.ppermute(sent, "core", [(0, 1), (1, 0)])
+    spread = partial_sums(lax.dynamic_index_in_dim(backward_weight, core, axis=2, keepdims=False), received)
+    summed = lax.psum_scatter(
+        spread.reshape(-1, plane_cells), "chips", scatter_dimension=0, tiled=True
+    ).reshape(depth_cells, block_in, plane_cells)
     input_grad = jnp.transpose(summed.astype(jnp.bfloat16), (1, 0, 2))
     return (outputs, input_grad, weight_grad, bias_grad)
 

time: 98.5 us -> 112 us (1.14)
  local copies, waits for them, and re-layouts: 17.1 us -> 31.6 us
  waiting for transfers between devices: 20.8 us -> 14.8 us
  matrix products: 12.6 us -> 18.1 us
  other arithmetic: 12.4 us -> 9.19 us
  starting transfers between devices: 19.3 us -> 21.6 us
    unnamed x20 -> x31, local copies, waits for them, and re-layouts: 6.95 us -> 15.2 us
    all_gather x1, waiting for transfers between devices: 5.85 us -> 0.02 us  [body(): lax.all_gather(inputs_planes, ('chips', 'core'), axis=1, tiled=True)]
    dot_general x3 -> x6, matrix products: 5.85 us -> 11.5 us  [partial_sums(): jnp.einsum('cjk,zkn->czjn', core_weight[depth_index], grad_shifted[2 - de...]
    reshape x0 -> x1, local copies, waits for them, and re-layouts: none -> 4.42 us  [body(): jnp.transpose(weight_grid, (0, 2, 1, 3))]
    reduce_scatter x1, waiting for transfers between devices: 1.12 us -> 5.46 us  [body(): lax.psum_scatter(spread.reshape(-1, plane_cells), 'chips', scatter_dimens...]
    add x1 -> x0, other arithmetic: 4.19 us -> none  [scatter_channels(): partial = keep + lax.ppermute(send, 'core', [(0, 1), (1, 0)])]
    ppermute x1, waiting for transfers between devices: 4.14 us -> 0.01 us  [body(): received = lax.ppermute(sent, 'core', [(0, 1), (1, 0)])]
    slice x5, local copies, waits for them, and re-layouts: 2.85 us -> 6.5 us  [the longest x1 4.61 us: partial_sums(): core_weight[depth_index]]
  transfers between devices with their start and end apart: 13 -> 13, of which waited for: 6 -> 4; matrix products, arithmetic and copies ran while one was open for 37% -> 47% of each run, Pallas kernels for 0% -> 0%
where the time goes in v11:
time: 112 us; the launch traced here: 111 us
  local copies, waits for them, and re-layouts  31.6 us (28%)
  starting transfers between devices  21.6 us (19%)
  matrix products  18.1 us (16%)
  between operations  16 us (14%)
  waiting for transfers between devices  14.8 us (13%)
  other arithmetic  9.19 us (8%)
    unnamed x31, local copies, waits for them, and re-layouts  15.2 us
    dot_general x6, matrix products, partial_sums(): jnp.einsum('cjk,zkn->czjn', core_weight[depth_index], grad_shifted[2 - de...  11.5 us
    ppermute x3, waiting for transfers between devices, all_reduce_direct(): lax.ppermute(reduced, axis, [(i, i ^ distance) for i in range(devices)])  7.53 us
    ppermute x3, starting transfers between devices, all_reduce_direct(): lax.ppermute(reduced, axis, [(i, i ^ distance) for i in range(devices)])  5.95 us
    reduce_scatter x1, waiting for transfers between devices, body(): lax.psum_scatter(spread.reshape(-1, plane_cells), 'chips', scatter_dimens...  5.46 us
    ppermute x3, starting transfers between devices, all_reduce_direct(): reduced = reduced + lax.ppermute(send, axis, pairs)  5.09 us
    ppermute x1, starting transfers between devices, padded_2(): before = lax.ppermute(last, axis, up)  4.85 us
    slice x1, local copies, waits for them, and re-layouts, partial_sums(): core_weight[depth_index]  4.61 us
  transfers between devices with their start and end apart: 13, of which 4 were waited for; matrix products, arithmetic and copies ran while one was open for 47% of the time, Pallas kernels for 0%

profile of v11, /device:TPU:0, one launch (start us, length us, event | category | flops | bytes accessed | tf_op | source)
XLA Modules:
  0.0 111.3 jit_solution(9677460200184444361)
XLA Ops:
  8.0 1.7 %copy.68 = bf16[32,4,1024]{2,0,1:T(8,128)(2,1)} copy(bf16[32,4,1024]{2,1,0:T(4,128)(2,1)} %param.6) | data formatting | bytes 524288 | tf_op args[0]
  9.8 1.0 copy.69
  10.8 4.8 %collective-permute-start.2 = (bf16[1,32,1024]{2,1,0:T(8,128)(2,1)S(1)}, bf16[1,32,1024]{2,1,0:T(8,128)(2,1)S(1)}, u32[]{:S(2)}, u32[]{:S(2)}) collective-permute-start(bf16[1,32,1024]{2,1,0:T(8,128)(2,1)S(1)} %get-tuple-element.55), channel_id=1, source_target_pairs={{0,8},{8,16},{16,24},{1,9},{9,17},{17,25},{2,10},{10,18},{18,26},{... | collective-permute-start | bytes 196616 | tf_op jit(solution)/shard_map/ppermute | solution.py:28
  15.7 1.3 %collective-permute-start.3 = (bf16[1,32,1024]{2,1,0:T(8,128)(2,1)S(1)}, bf16[1,32,1024]{2,1,0:T(8,128)(2,1)S(1)}, u32[]{:S(2)}, u32[]{:S(2)}) collective-permute-start(bf16[1,32,1024]{2,1,0:T(8,128)(2,1)S(1)} %get-tuple-element.56), channel_id=1, source_target_pairs={{8,0},{16,8},{24,16},{9,1},{17,9},{25,17},{10,2},{18,10},{26,18},{... | collective-permute-start | bytes 196616 | tf_op jit(solution)/shard_map/ppermute | solution.py:29
  17.1 4.4 %reshape.130 = bf16[3,4,2,32,288]{3,2,1,4,0:T(2,128)(2,1)S(1)} reshape(bf16[3,256,9,32]{1,3,2,0:T(8,128)(2,1)} %bitcast.252) | data formatting | bytes 884736 | tf_op jit(solution)/shard_map/reshape | solution.py:197
  21.5 4.6 %constant_dynamic-slice_fusion.4 = (bf16[1,4,1,32,288]{3,2,1,4,0:T(2,128)(2,1)S(1)}, bf16[1,4,1,32,288]{3,2,1,4,0:T(2,128)(2,1)}, bf16[1,4,1,32,288]{3,2,1,4,0:T...) fusion(bf16[3,4,2,32,288]{3,2,1,4,0:T(2,128)(2,1)S(1)} %reshape, ...), kind=kLoop, calls=%fused_computation.135 | loop fusion | bytes 884752 | tf_op jit(solution)/shard_map/slice | solution.py:206
  26.1 1.9 %copy.59 = bf16[1,4,1,32,288]{4,3,1,2,0:T(8,128)(2,1)} copy(bf16[1,4,1,32,288]{3,2,1,4,0:T(2,128)(2,1)} %get-tuple-element.38) | data formatting | bytes 147456
  28.0 1.9 %copy.58 = bf16[1,4,1,32,288]{4,3,1,2,0:T(8,128)(2,1)} copy(bf16[1,4,1,32,288]{3,2,1,4,0:T(2,128)(2,1)} %get-tuple-element.39) | data formatting | bytes 147456
  29.9 1.9 %copy.60 = bf16[1,4,1,32,288]{4,3,1,2,0:T(8,128)(2,1)} copy(bf16[1,4,1,32,288]{3,2,1,4,0:T(2,128)(2,1)} %get-tuple-element.40) | data formatting | bytes 147456
  33.3 1.0 fusion.70
  35.3 1.1 copy-done
  36.4 1.0 fusion.52
  37.4 1.0 fusion.54
  38.4 2.6 %add_bitcast_fusion = f32[4,4,32,1024]{3,2,0,1:T(8,128)} fusion(f32[4,1024,4,32]{1,3,2,0:T(8,128)S(1)} %fusion.54, f32[4,1024,4,32]{1,3,2,0:T(8,128)S(1)} %fusion.52, bf16[4,288,1024,1]{2,1,3,0:T(8,128)(2,1)S(1)} %bitcast.234, bf16[1,4,1,32,288]{4,3,1,2,0:T(8,128)(2,1)S(1)} %copy-done.6), kind=kOutput, calls=%fused_computation.7 | convolution fusion | flops 303038464 | bytes 8724480 | tf_op jit(solution)/shard_map/cjk,zkn->czjn/dot_general | solution.py:204
  41.1 1.9 %copy.63 = bf16[1,4,1,32,288]{4,3,1,2,0:T(8,128)(2,1)} copy(bf16[1,4,1,32,288]{3,2,1,4,0:T(2,128)(2,1)} %get-tuple-element.36) | data formatting | bytes 147456
  42.9 1.1 %copy.62 = bf16[1,4,1,32,288]{4,3,1,2,0:T(8,128)(2,1)} copy(bf16[1,4,1,32,288]{3,2,1,4,0:T(2,128)(2,1)S(1)} %get-tuple-element.37) | data formatting | bytes 147456
  44.9 1.3 %convert_reduce_fusion = f32[32]{0:T(128)S(1)} fusion(bf16[32,4,1024]{2,1,0:T(4,128)(2,1)} %param.9), kind=kLoop, calls=%fused_computation.62 | loop fusion | flops 262112 | bytes 262272 | tf_op jit(solution)/shard_map/reduce_sum | solution.py:184
  46.1 1.1 fusion.72
  47.3 2.8 %fusion.47 = f32[4,1024,4,32]{1,3,2,0:T(8,128)S(1)} fusion(bf16[4,288,1024,1]{2,1,3,0:T(8,128)(2,1)} %bitcast.238, bf16[1,4,1,32,288]{4,3,1,2,0:T(8,128)(2,1)} %copy.63), kind=kOutput, calls=%fused_computation.106 | convolution fusion | flops 301989888 | bytes 4530176 | tf_op jit(solution)/shard_map/cjk,zkn->czjn/dot_general | solution.py:204
  50.1 1.0 fusion.49
  51.1 3.1 %bitcast_add_fusion = f32[4,4,32,1024]{3,2,0,1:T(8,128)S(1)} fusion(f32[4,1024,4,32]{1,3,2,0:T(8,128)S(1)} %fusion.47, f32[4,4,32,1024]{3,2,0,1:T(8,128)} %collective-permute-done.4, f32[4,1024,4,32]{1,3,2,0:T(8,128)S(1)} %fusion.49, bf16[4,288,1024,1]{2,1,3,0:T(8,128)(2,1)S(1)} %bitcast.235, bf16[1,4,1,32,288]{4,3,1,2,0:T(8,128)(2,1)S(1)} %copy.64), kind=kOutput, calls=%fused_computation.4 | convolution fusion | flops 303562752 | bytes 10821632 | tf_op jit(solution)/shard_map/cjk,zkn->czjn/dot_general | solution.py:204
  54.2 1.5 %copy.42 = f32[4,4,32,1024]{3,2,1,0:T(8,128)} copy(f32[4,4,32,1024]{3,2,0,1:T(8,128)S(1)} %bitcast_add_fusion) | data formatting | bytes 4194304 | tf_op jit(solution)/shard_map/add | solution.py:210
  55.8 2.5 %convolution_bitcast_fusion.3 = f32[1,288,256]{2,1,0:T(8,128)S(1)} fusion(bf16[4,288,1024]{2,1,0:T(8,128)(2,1)S(1)} %bitcast.236, bf16[4,256,1024]{2,1,0:T(8,128)(2,1)} %all-gather.2.cloned.1.call-done), kind=kOutput, calls=%fused_computation.10 | convolution fusion | flops 603979776 | bytes 4751360 | tf_op jit(solution)/shard_map/zkn,zin->ki/dot_general | solution.py:175
  58.7 0.8 convolution_bitcast_fusion.4
  59.6 0.8 copy-done.4
  60.4 0.8 convolution_bitcast_fusion.5
  61.4 2.7 %collective-permute-start.5 = (f32[224,256]{1,0:T(8,128)S(1)}, f32[224,256]{1,0:T(8,128)S(1)}, u32[]{:S(2)}, u32[]{:S(2)}) collective-permute-start(f32[224,256]{1,0:T(8,128)S(1)} %get-tuple-element.45), channel_id=1, source_target_pairs={{0,8},{8,0},{16,24},{24,16},{1,9},{9,1},{17,25},{25,17},{2,10},{10... | collective-permute-start | bytes 688136 | tf_op jit(solution)/shard_map/ppermute | solution.py:104
  64.2 1.6 %collective-permute-start.6 = (f32[224,256]{1,0:T(8,128)S(1)}, f32[224,256]{1,0:T(8,128)S(1)}, u32[]{:S(2)}, u32[]{:S(2)}) collective-permute-start(f32[224,256]{1,0:T(8,128)S(1)} %get-tuple-element.47), channel_id=1, source_target_pairs={{0,16},{8,24},{16,0},{24,8},{1,17},{9,25},{17,1},{25,9},{2,18},{10... | collective-permute-start | bytes 688136 | tf_op jit(solution)/shard_map/ppermute | solution.py:104
  65.7 0.8 collective-permute-start.7
  66.5 0.8 convolution_bitcast_fusion
  67.3 0.8 convolution_bitcast_fusion.1
  68.1 0.8 convolution_bitcast_fusion.2
  68.9 2.3 %pad_add_fusion = f32[6,288,1024]{2,1,0:T(8,128)S(1)} fusion(f32[4,288,1024]{2,1,0:T(8,128)S(1)} %convolution_bitcast_fusion, f32[4,288,1024]{2,1,0:T(8,128)S(1)} %convolution_bitcast_fusion.1, f32[4,288,1024]{2,1,0:T(8,128)S(1)} %convolution_bitcast_fusion.2), kind=kLoop, calls=%fused_computation | loop fusion | flops 3538944 | bytes 21233664 | tf_op jit(solution)/shard_map/add | solution.py:150
  71.2 1.1 %slice_bitcast_fusion = (f32[6,32,1024]{2,1,0:T(8,128)S(1)}, f32[6,32,1024]{2,1,0:T(8,128)S(1)}, f32[6,32,1024]{2,1,0:T(8,128)S(1)}, f32[6,32,1024]{2,1,0:T(8,12...) fusion(f32[6,9,32,1024]{3,2,1,0:T(8,128)S(1)} %bitcast.243), kind=kLoop, calls=%fused_computation.46 | loop fusion | bytes 12582912 | tf_op jit(solution)/shard_map/squeeze | solution.py:154
  72.3 1.7 %fusion.10 = f32[6,32,1024]{2,1,0:T(8,128)S(1)} fusion(f32[6,32,1024]{2,1,0:T(8,128)S(1)} %get-tuple-element.31, f32[6,32,1024]{2,1,0:T(8,128)S(1)} %get-tuple-element.30, f32[6,32,1024]{2,1,0:T(8,128)S(1)} %get-tuple-element.29, f32[6,32,1024]{2,1,0:T(8,128)S(1)} %get-tuple-element.28, f32[6,32,1024]{2,1,0:T(8,128)S(1)} %get-tuple-element.27, ...), kind=kLoop, calls=%fused_computation.38 | loop fusion | flops 3342336 | bytes 7867392 | tf_op jit(solution)/shard_map/add | solution.py:155
  74.0 3.1 %collective-permute-start = (f32[1,32,1024]{2,1,0:T(8,128)S(1)}, f32[1,32,1024]{2,1,0:T(8,128)S(1)}, u32[]{:S(2)}, u32[]{:S(2)}) collective-permute-start(f32[1,32,1024]{2,1,0:T(8,128)S(1)} %get-tuple-element.48), channel_id=1, source_target_pairs={{0,8},{8,16},{16,24},{1,9},{9,17},{17,25},{2,10},{10,18},{18,26},{... | collective-permute-start | bytes 393224 | tf_op jit(solution)/shard_map/ppermute | solution.py:159
  77.1 1.3 %collective-permute-start.1 = (f32[1,32,1024]{2,1,0:T(8,128)S(1)}, f32[1,32,1024]{2,1,0:T(8,128)S(1)}, u32[]{:S(2)}, u32[]{:S(2)}) collective-permute-start(f32[1,32,1024]{2,1,0:T(8,128)S(1)} %get-tuple-element.49), channel_id=1, source_target_pairs={{8,0},{16,8},{24,16},{9,1},{17,9},{25,17},{10,2},{18,10},{26,18},{... | collective-permute-start | bytes 393224 | tf_op jit(solution)/shard_map/ppermute | solution.py:160
  78.5 3.0 %collective-permute-start.8 = (f32[224,256]{1,0:T(8,128)S(1)}, f32[224,256]{1,0:T(8,128)S(1)}, u32[]{:S(2)}, u32[]{:S(2)}) collective-permute-start(f32[224,256]{1,0:T(8,128)S(1)} %fusion.45), channel_id=1, source_target_pairs={{0,8},{8,0},{16,24},{24,16},{1,9},{9,1},{17,25},{25,17},{2,10},{10... | collective-permute-start | bytes 688136 | tf_op jit(solution)/shard_map/ppermute | solution.py:106
  81.5 1.5 %collective-permute-start.9 = (f32[224,256]{1,0:T(8,128)S(1)}, f32[224,256]{1,0:T(8,128)S(1)}, u32[]{:S(2)}, u32[]{:S(2)}) collective-permute-start(f32[224,256]{1,0:T(8,128)S(1)} %fusion.45), channel_id=1, source_target_pairs={{0,16},{8,24},{16,0},{24,8},{1,17},{9,25},{17,1},{25,9},{2,18},{10... | collective-permute-start | bytes 688136 | tf_op jit(solution)/shard_map/ppermute | solution.py:106
  83.1 1.4 %collective-permute-start.10 = (f32[224,256]{1,0:T(8,128)S(1)}, f32[224,256]{1,0:T(8,128)S(1)}, u32[]{:S(2)}, u32[]{:S(2)}) collective-permute-start(f32[224,256]{1,0:T(8,128)S(1)} %fusion.45), channel_id=1, source_target_pairs={{0,24},{8,16},{16,8},{24,0},{1,25},{9,17},{17,9},{25,1},{2,26},{10... | collective-permute-start | bytes 688136 | tf_op jit(solution)/shard_map/ppermute | solution.py:106
  84.5 1.7 %collective-permute-done.1 = f32[1,32,1024]{2,1,0:T(8,128)S(1)} collective-permute-done((f32[1,32,1024]{2,1,0:T(8,128)S(1)}, f32[1,32,1024]{2,1,0:T(8,128)S(1)}, u32[]{:S(2)}, u32[]{:S(2)}) %collective-permute-start.1) | collective-permute-done | bytes 131104 | tf_op jit(solution)/shard_map/ppermute | solution.py:160
  86.3 0.9 copy.43
  87.2 3.9 %collective-permute-done.8 = f32[224,256]{1,0:T(8,128)S(1)} collective-permute-done((f32[224,256]{1,0:T(8,128)S(1)}, f32[224,256]{1,0:T(8,128)S(1)}, u32[]{:S(2)}, u32[]{:S(2)}) %collective-permute-start.8) | collective-permute-done | bytes 229408 | tf_op jit(solution)/shard_map/ppermute | solution.py:106
  91.1 3.7 %collective-permute-done.10 = f32[224,256]{1,0:T(8,128)S(1)} collective-permute-done((f32[224,256]{1,0:T(8,128)S(1)}, f32[224,256]{1,0:T(8,128)S(1)}, u32[]{:S(2)}, u32[]{:S(2)}) %collective-permute-start.10) | collective-permute-done | bytes 229408 | tf_op jit(solution)/shard_map/ppermute | solution.py:106
  94.9 1.0 pad_maximum_fusion.1
  96.4 5.5 %reduce-scatter.2.cloned.1.call-done = f32[128,1024]{1,0:T(8,128)} async-done(((f32[512,1024]{1,0:T(8,128)}), f32[128,1024]{1,0:T(8,128)}) %reduce-scatter.2.cloned.1.call-update) | async-done | bytes 524304 | tf_op jit(solution)/shard_map/reduce_scatter | solution.py:216
  101.9 1.1 convert_element_type.39
  102.9 0.9 copy.44
  (62 shorter events, 4.8 us)
Async XLA Ops:
  8.0 47.8 %all-gather.2.cloned.1.call-start = ((), (), s32[]{:S(2)}) async-start(), calls=%async_computation.1 | async-start | bytes 2359296 | tf_op jit(solution)/shard_map/all_gather | solution.py:137
  10.8 20.9 %collective-permute-start.2 = (bf16[1,32,1024]{2,1,0:T(8,128)(2,1)S(1)}, bf16[1,32,1024]{2,1,0:T(8,128)(2,1)S(1)}, u32[]{:S(2)}, u32[]{:S(2)}) collective-permute-start(bf16[1,32,1024]{2,1,0:T(8,128)(2,1)S(1)} %get-tuple-element.55), channel_id=1, source_target_pairs={{0,8},{8,16},{16,24},{1,9},{9,17},{17,25},{2,10},{10,18},{18,26},{... | collective-permute-start | bytes 196616 | tf_op jit(solution)/shard_map/ppermute | solution.py:28
  15.7 16.1 %collective-permute-start.3 = (bf16[1,32,1024]{2,1,0:T(8,128)(2,1)S(1)}, bf16[1,32,1024]{2,1,0:T(8,128)(2,1)S(1)}, u32[]{:S(2)}, u32[]{:S(2)}) collective-permute-start(bf16[1,32,1024]{2,1,0:T(8,128)(2,1)S(1)} %get-tuple-element.56), channel_id=1, source_target_pairs={{8,0},{16,8},{24,16},{9,1},{17,9},{25,17},{10,2},{18,10},{26,18},{... | collective-permute-start | bytes 196616 | tf_op jit(solution)/shard_map/ppermute | solution.py:29
  17.0 84.9 %reduce-scatter.2.cloned.1.call-start = ((), (), s32[]{:S(2)}) async-start(), calls=%async_computation.2 | async-start | bytes 2621440 | tf_op jit(solution)/shard_map/reduce_scatter | solution.py:216
  34.9 1.5 %copy-start = (bf16[4,9,32,1024]{3,2,1,0:T(8,128)(2,1)}, bf16[4,9,32,1024]{3,2,1,0:T(8,128)(2,1)S(1)}, u32[]{:S(2)}) copy-start(bf16[4,9,32,1024]{3,2,1,0:T(8,128)(2,1)S(1)} %copy.39) | copy-start | bytes 7077892
  34.9 1.5 %copy-start.7 = (bf16[1,4,1,32,288]{4,3,1,2,0:T(8,128)(2,1)S(1)}, bf16[1,4,1,32,288]{4,3,1,2,0:T(8,128)(2,1)}, u32[]{:S(2)}) copy-start(bf16[1,4,1,32,288]{4,3,1,2,0:T(8,128)(2,1)} %copy.59) | copy-start | bytes 221188
  35.3 2.1 %copy-start.2 = (bf16[4,9,32,1024]{3,2,1,0:T(8,128)(2,1)}, bf16[4,9,32,1024]{3,2,1,0:T(8,128)(2,1)S(1)}, u32[]{:S(2)}) copy-start(bf16[4,9,32,1024]{3,2,1,0:T(8,128)(2,1)S(1)} %copy.37) | copy-start | bytes 7077892
  36.4 1.0 copy-start.8
  37.4 1.0 copy-start.6
  41.1 10.1 %collective-permute-start.4 = (f32[4,4,32,1024]{3,2,0,1:T(8,128)}, f32[4,4,32,1024]{3,2,0,1:T(8,128)}, u32[]{:S(2)}, u32[]{:S(2)}) collective-permute-start(f32[4,4,32,1024]{3,2,0,1:T(8,128)} %add_bitcast_fusion), channel_id=1, source_target_pairs={{0,1},{1,0},{2,3},{3,2},{4,5},{5,4},{6,7},{7,6},{8,9},{9,8},{10,11... | collective-permute-start | bytes 6291464 | tf_op jit(solution)/shard_map/ppermute | solution.py:214
  47.2 2.9 %copy-start.3 = (bf16[4,9,32,1024]{3,2,1,0:T(8,128)(2,1)S(1)}, bf16[4,9,32,1024]{3,2,1,0:T(8,128)(2,1)}, u32[]{:S(2)}) copy-start(bf16[4,9,32,1024]{3,2,1,0:T(8,128)(2,1)} %copy-done.2) | copy-start | bytes 7077892
  47.2 2.9 %copy-start.9 = (bf16[1,4,1,32,288]{4,3,1,2,0:T(8,128)(2,1)S(1)}, bf16[1,4,1,32,288]{4,3,1,2,0:T(8,128)(2,1)}, u32[]{:S(2)}) copy-start(bf16[1,4,1,32,288]{4,3,1,2,0:T(8,128)(2,1)} %copy.62) | copy-start | bytes 221188
  55.8 2.6 %copy-start.1 = (bf16[4,9,32,1024]{3,2,1,0:T(8,128)(2,1)S(1)}, bf16[4,9,32,1024]{3,2,1,0:T(8,128)(2,1)}, u32[]{:S(2)}) copy-start(bf16[4,9,32,1024]{3,2,1,0:T(8,128)(2,1)} %copy-done) | copy-start | bytes 7077892
  55.8 2.9 %copy-start.5 = (bf16[4,256,1024]{2,1,0:T(8,128)(2,1)S(1)}, bf16[4,256,1024]{2,1,0:T(8,128)(2,1)}, u32[]{:S(2)}) copy-start(bf16[4,256,1024]{2,1,0:T(8,128)(2,1)} %all-gather.2.cloned.1.call-done) | copy-start | bytes 6291460
  58.7 1.7 %copy-start.4 = (bf16[4,9,32,1024]{3,2,1,0:T(8,128)(2,1)S(1)}, bf16[4,9,32,1024]{3,2,1,0:T(8,128)(2,1)}, u32[]{:S(2)}) copy-start(bf16[4,9,32,1024]{3,2,1,0:T(8,128)(2,1)} %copy-done.2) | copy-start | bytes 7077892
  61.4 17.0 %collective-permute-start.5 = (f32[224,256]{1,0:T(8,128)S(1)}, f32[224,256]{1,0:T(8,128)S(1)}, u32[]{:S(2)}, u32[]{:S(2)}) collective-permute-start(f32[224,256]{1,0:T(8,128)S(1)} %get-tuple-element.45), channel_id=1, source_target_pairs={{0,8},{8,0},{16,24},{24,16},{1,9},{9,1},{17,25},{25,17},{2,10},{10... | collective-permute-start | bytes 688136 | tf_op jit(solution)/shard_map/ppermute | solution.py:104
  64.2 14.2 %collective-permute-start.6 = (f32[224,256]{1,0:T(8,128)S(1)}, f32[224,256]{1,0:T(8,128)S(1)}, u32[]{:S(2)}, u32[]{:S(2)}) collective-permute-start(f32[224,256]{1,0:T(8,128)S(1)} %get-tuple-element.47), channel_id=1, source_target_pairs={{0,16},{8,24},{16,0},{24,8},{1,17},{9,25},{17,1},{25,9},{2,18},{10... | collective-permute-start | bytes 688136 | tf_op jit(solution)/shard_map/ppermute | solution.py:104
  65.7 12.7 %collective-permute-start.7 = (f32[224,256]{1,0:T(8,128)S(1)}, f32[224,256]{1,0:T(8,128)S(1)}, u32[]{:S(2)}, u32[]{:S(2)}) collective-permute-start(f32[224,256]{1,0:T(8,128)S(1)} %get-tuple-element.46), channel_id=1, source_target_pairs={{0,24},{8,16},{16,8},{24,0},{1,25},{9,17},{17,9},{25,1},{2,26},{10... | collective-permute-start | bytes 688136 | tf_op jit(solution)/shard_map/ppermute | solution.py:104
  72.3 13.9 %copy-start.10 = (f32[32]{0:T(128)S(1)}, f32[32]{0:T(128)}, u32[]{:S(2)}) copy-start(f32[32]{0:T(128)} %param.8) | copy-start | bytes 388
  74.0 10.4 %collective-permute-start = (f32[1,32,1024]{2,1,0:T(8,128)S(1)}, f32[1,32,1024]{2,1,0:T(8,128)S(1)}, u32[]{:S(2)}, u32[]{:S(2)}) collective-permute-start(f32[1,32,1024]{2,1,0:T(8,128)S(1)} %get-tuple-element.48), channel_id=1, source_target_pairs={{0,8},{8,16},{16,24},{1,9},{9,17},{17,25},{2,10},{10,18},{18,26},{... | collective-permute-start | bytes 393224 | tf_op jit(solution)/shard_map/ppermute | solution.py:159
  77.1 9.1 %collective-permute-start.1 = (f32[1,32,1024]{2,1,0:T(8,128)S(1)}, f32[1,32,1024]{2,1,0:T(8,128)S(1)}, u32[]{:S(2)}, u32[]{:S(2)}) collective-permute-start(f32[1,32,1024]{2,1,0:T(8,128)S(1)} %get-tuple-element.49), channel_id=1, source_target_pairs={{8,0},{16,8},{24,16},{9,1},{17,9},{25,17},{10,2},{18,10},{26,18},{... | collective-permute-start | bytes 393224 | tf_op jit(solution)/shard_map/ppermute | solution.py:160
  78.5 12.6 %collective-permute-start.8 = (f32[224,256]{1,0:T(8,128)S(1)}, f32[224,256]{1,0:T(8,128)S(1)}, u32[]{:S(2)}, u32[]{:S(2)}) collective-permute-start(f32[224,256]{1,0:T(8,128)S(1)} %fusion.45), channel_id=1, source_target_pairs={{0,8},{8,0},{16,24},{24,16},{1,9},{9,1},{17,25},{25,17},{2,10},{10... | collective-permute-start | bytes 688136 | tf_op jit(solution)/shard_map/ppermute | solution.py:106
  81.5 9.6 %collective-permute-start.9 = (f32[224,256]{1,0:T(8,128)S(1)}, f32[224,256]{1,0:T(8,128)S(1)}, u32[]{:S(2)}, u32[]{:S(2)}) collective-permute-start(f32[224,256]{1,0:T(8,128)S(1)} %fusion.45), channel_id=1, source_target_pairs={{0,16},{8,24},{16,0},{24,8},{1,17},{9,25},{17,1},{25,9},{2,18},{10... | collective-permute-start | bytes 688136 | tf_op jit(solution)/shard_map/ppermute | solution.py:106
  83.1 11.7 %collective-permute-start.10 = (f32[224,256]{1,0:T(8,128)S(1)}, f32[224,256]{1,0:T(8,128)S(1)}, u32[]{:S(2)}, u32[]{:S(2)}) collective-permute-start(f32[224,256]{1,0:T(8,128)S(1)} %fusion.45), channel_id=1, source_target_pairs={{0,24},{8,16},{16,8},{24,0},{1,25},{9,17},{17,9},{25,1},{2,26},{10... | collective-permute-start | bytes 688136 | tf_op jit(solution)/shard_map/ppermute | solution.py:106
Sparse Core Ops, SparseCore 0:
  17.1 31.4 all-gather.1
Sparse Core Ops, SparseCore 1:
  55.9 46.0 reduce-scatter.1

commit v12 on v8

--- a/solution.py
+++ b/solution.py
@@ -205,7 +205,9 @@
             preferred_element_type=jnp.float32,
         )
         spread = part if spread is None else spread + part
-    summed = scatter_channels(spread).reshape(depth_cells, block_in, plane_cells)
+    summed = lax.psum_scatter(
+        spread.reshape(-1, plane_cells), ("chips", "core"), scatter_dimension=0, tiled=True
+    ).reshape(depth_cells, block_in, plane_cells)
     input_grad = jnp.transpose(summed.astype(jnp.bfloat16), (1, 0, 2))
     return (outputs, input_grad, weight_grad, bias_grad)
 

time: 98.5 us -> 109 us (1.11)
  waiting for transfers between devices: 20.8 us -> 38 us
  other arithmetic: 12.4 us -> 8.25 us
  local copies, waits for them, and re-layouts: 17.1 us -> 15.6 us
  between operations: 15.9 us -> 14.5 us
    reduce_scatter x1, waiting for transfers between devices: 1.12 us -> 13 us  [body(): lax.psum_scatter(spread.reshape(-1, plane_cells), ('chips', 'core'), scat...]
    all_gather x1, waiting for transfers between devices: 5.85 us -> 15.3 us  [body(): lax.all_gather(inputs_planes, ('chips', 'core'), axis=1, tiled=True)]
    add x1 -> x0, other arithmetic: 4.19 us -> none  [scatter_channels(): partial = keep + lax.ppermute(send, 'core', [(0, 1), (1, 0)])]
    ppermute x1 -> x0, waiting for transfers between devices: 4.14 us -> none  [scatter_channels(): partial = keep + lax.ppermute(send, 'core', [(0, 1), (1, 0)])]
    dynamic_slice x2 -> x0, local copies, waits for them, and re-layouts: 3.49 us -> none  [the longest x1 1.86 us: scatter_channels(): keep = lax.dynamic_index_in_dim(by_core, core, axis=1, keepdims=False)]
    add x0 -> x1, local copies, waits for them, and re-layouts: none -> 2.26 us  [body(): spread = part if spread is None else spread + part]
  transfers between devices with their start and end apart: 13 -> 12, of which waited for: 6 -> 5; matrix products, arithmetic and copies ran while one was open for 37% -> 29% of each run, Pallas kernels for 0% -> 0%
where the time goes in v12:
time: 109 us; the launch traced here: 108 us
  waiting for transfers between devices  38 us (35%)
  starting transfers between devices  19.5 us (18%)
  local copies, waits for them, and re-layouts  15.6 us (14%)
  between operations  14.5 us (13%)
  matrix products  12.6 us (12%)
  other arithmetic  8.25 us (8%)
    all_gather x1, waiting for transfers between devices, body(): lax.all_gather(inputs_planes, ('chips', 'core'), axis=1, tiled=True)  15.3 us
    reduce_scatter x1, waiting for transfers between devices, body(): lax.psum_scatter(spread.reshape(-1, plane_cells), ('chips', 'core'), scat...  13 us
    ppermute x3, waiting for transfers between devices, all_reduce_direct(): lax.ppermute(reduced, axis, [(i, i ^ distance) for i in range(devices)])  7.77 us
    unnamed x20, local copies, waits for them, and re-layouts  6.59 us
    dot_general x3, matrix products, body(): jnp.einsum('bjk,zkn->bzjn', backward_weight[depth_index], grad_shifted[2...  5.86 us
    ppermute x3, starting transfers between devices, all_reduce_direct(): lax.ppermute(reduced, axis, [(i, i ^ distance) for i in range(devices)])  5.08 us
    ppermute x1, starting transfers between devices, padded_2(): before = lax.ppermute(last, axis, up)  4.85 us
    dot_general x3, matrix products, body(): jnp.einsum('zkn,zin->ki', grad_shifted[2 - depth_index:2 - depth_index +...  4.36 us
  transfers between devices with their start and end apart: 12, of which 5 were waited for; matrix products, arithmetic and copies ran while one was open for 29% of the time, Pallas kernels for 0%

profile of v12, /device:TPU:0, one launch (start us, length us, event | category | flops | bytes accessed | tf_op | source)
XLA Modules:
  0.0 108.5 jit_solution(8587672291288388031)
XLA Ops:
  7.2 1.0 copy.65
  8.3 4.8 %collective-permute-start.2 = (bf16[1,32,1024]{2,1,0:T(8,128)(2,1)S(1)}, bf16[1,32,1024]{2,1,0:T(8,128)(2,1)S(1)}, u32[]{:S(2)}, u32[]{:S(2)}) collective-permute-start(bf16[1,32,1024]{2,1,0:T(8,128)(2,1)S(1)} %get-tuple-element.48), channel_id=1, source_target_pairs={{0,8},{8,16},{16,24},{1,9},{9,17},{17,25},{2,10},{10,18},{18,26},{... | collective-permute-start | bytes 196616 | tf_op jit(solution)/shard_map/ppermute | solution.py:28
  13.1 1.3 %collective-permute-start.3 = (bf16[1,32,1024]{2,1,0:T(8,128)(2,1)S(1)}, bf16[1,32,1024]{2,1,0:T(8,128)(2,1)S(1)}, u32[]{:S(2)}, u32[]{:S(2)}) collective-permute-start(bf16[1,32,1024]{2,1,0:T(8,128)(2,1)S(1)} %get-tuple-element.49), channel_id=1, source_target_pairs={{8,0},{16,8},{24,16},{9,1},{17,9},{25,17},{10,2},{18,10},{26,18},{... | collective-permute-start | bytes 196616 | tf_op jit(solution)/shard_map/ppermute | solution.py:29
  14.4 1.7 %copy.64 = bf16[32,4,1024]{2,0,1:T(8,128)(2,1)} copy(bf16[32,4,1024]{2,1,0:T(4,128)(2,1)} %param.6) | data formatting | bytes 524288 | tf_op args[0]
  16.2 1.1 %fusion.67 = (bf16[1,256,9,32]{1,3,2,0:T(8,128)(2,1)S(1)}, bf16[1,256,9,32]{1,3,2,0:T(8,128)(2,1)S(1)}, bf16[1,256,9,32]{1,3,2,0:T(8,128)(2,1)S(1)}) fusion(bf16[3,256,9,32]{1,3,2,0:T(8,128)(2,1)} %bitcast.223), kind=kLoop, calls=%fused_computation.126 | loop fusion | bytes 884736 | tf_op jit(solution)/shard_map/slice | solution.py:203
  17.3 0.2 squeeze.86
  17.6 0.4 copy.43
  18.0 0.2 squeeze.85
  18.2 0.4 copy.41
  18.9 0.4 copy.45
  20.9 1.0 fusion.65
  22.1 0.3 copy.42
  22.5 0.3 copy.40
  22.8 1.8 %fusion.47 = f32[4,1024,8,32]{1,3,2,0:T(8,128)S(1)} fusion(bf16[4,288,1024,1]{2,1,3,0:T(8,128)(2,1)S(1)} %bitcast.213, bf16[8,32,288]{2,1,0:T(8,128)(2,1)S(1)} %copy.43), kind=kOutput, calls=%fused_computation.103 | convolution fusion | flops 603979776 | bytes 6701056 | tf_op jit(solution)/shard_map/bjk,zkn->bzjn/dot_general | solution.py:201
  24.9 1.8 %fusion.49 = f32[4,1024,8,32]{1,3,2,0:T(8,128)S(1)} fusion(bf16[4,288,1024,1]{2,1,3,0:T(8,128)(2,1)S(1)} %bitcast.215, bf16[8,32,288]{2,1,0:T(8,128)(2,1)S(1)} %copy.41), kind=kOutput, calls=%fused_computation.105 | convolution fusion | flops 603979776 | bytes 6701056 | tf_op jit(solution)/shard_map/bjk,zkn->bzjn/dot_general | solution.py:201
  26.6 2.3 %add_bitcast_fusion = f32[8,4,32,1024]{3,2,0,1:T(8,128)S(1)} fusion(f32[4,1024,8,32]{1,3,2,0:T(8,128)S(1)} %fusion.49, f32[4,1024,8,32]{1,3,2,0:T(8,128)S(1)} %fusion.47, bf16[4,288,1024,1]{2,1,3,0:T(8,128)(2,1)S(1)} %bitcast.210, bf16[8,32,288]{2,1,0:T(8,128)(2,1)S(1)} %copy.45), kind=kOutput, calls=%fused_computation.1 | convolution fusion | flops 606076928 | bytes 15089664 | tf_op jit(solution)/shard_map/bjk,zkn->bzjn/dot_general | solution.py:201
  29.0 2.3 %copy.46 = f32[8,4,32,1024]{3,2,1,0:T(8,128)} copy(f32[8,4,32,1024]{3,2,0,1:T(8,128)S(1)} %add_bitcast_fusion) | data formatting | bytes 8388608 | tf_op jit(solution)/shard_map/add | solution.py:207
  31.4 0.8 copy-done.6
  32.2 0.3 convert_reduce_fusion
  32.6 15.3 %all-gather.2.cloned.1.call-done = bf16[4,256,1024]{2,1,0:T(8,128)(2,1)} async-done(((bf16[4,32,1024]{2,1,0:T(8,128)(2,1)}), bf16[4,256,1024]{2,1,0:T(8,128)(2,1)}) %all-gather.2.cloned.1.call-update) | async-done | bytes 2097168 | tf_op jit(solution)/shard_map/all_gather | solution.py:136
  47.8 2.5 %convolution_bitcast_fusion.3 = f32[1,288,256]{2,1,0:T(8,128)S(1)} fusion(bf16[4,288,1024]{2,1,0:T(8,128)(2,1)S(1)} %bitcast.211, bf16[4,256,1024]{2,1,0:T(8,128)(2,1)} %all-gather.2.cloned.1.call-done), kind=kOutput, calls=%fused_computation.7 | convolution fusion | flops 603979776 | bytes 4751360 | tf_op jit(solution)/shard_map/zkn,zin->ki/dot_general | solution.py:174
  50.4 0.3 copy-done.2
  50.8 0.8 convolution_bitcast_fusion.4
  51.6 0.6 copy-done.4
  52.2 1.0 convolution_bitcast_fusion.5
  53.4 1.5 %collective-permute-start.4 = (f32[224,256]{1,0:T(8,128)S(1)}, f32[224,256]{1,0:T(8,128)S(1)}, u32[]{:S(2)}, u32[]{:S(2)}) collective-permute-start(f32[224,256]{1,0:T(8,128)S(1)} %get-tuple-element.35), channel_id=1, source_target_pairs={{0,8},{8,0},{16,24},{24,16},{1,9},{9,1},{17,25},{25,17},{2,10},{10... | collective-permute-start | bytes 688136 | tf_op jit(solution)/shard_map/ppermute | solution.py:104
  54.9 1.5 %collective-permute-start.5 = (f32[224,256]{1,0:T(8,128)S(1)}, f32[224,256]{1,0:T(8,128)S(1)}, u32[]{:S(2)}, u32[]{:S(2)}) collective-permute-start(f32[224,256]{1,0:T(8,128)S(1)} %get-tuple-element.37), channel_id=1, source_target_pairs={{0,16},{8,24},{16,0},{24,8},{1,17},{9,25},{17,1},{25,9},{2,18},{10... | collective-permute-start | bytes 688136 | tf_op jit(solution)/shard_map/ppermute | solution.py:104
  56.4 0.5 collective-permute-start.6
  56.9 0.8 convolution_bitcast_fusion
  57.7 0.8 convolution_bitcast_fusion.1
  58.5 0.8 convolution_bitcast_fusion.2
  59.3 2.3 %pad_add_fusion = f32[6,288,1024]{2,1,0:T(8,128)S(1)} fusion(f32[4,288,1024]{2,1,0:T(8,128)S(1)} %convolution_bitcast_fusion, f32[4,288,1024]{2,1,0:T(8,128)S(1)} %convolution_bitcast_fusion.1, f32[4,288,1024]{2,1,0:T(8,128)S(1)} %convolution_bitcast_fusion.2), kind=kLoop, calls=%fused_computation | loop fusion | flops 3538944 | bytes 21233664 | tf_op jit(solution)/shard_map/add | solution.py:149
  61.6 1.1 %slice_bitcast_fusion = (f32[6,32,1024]{2,1,0:T(8,128)S(1)}, f32[6,32,1024]{2,1,0:T(8,128)S(1)}, f32[6,32,1024]{2,1,0:T(8,128)S(1)}, f32[6,32,1024]{2,1,0:T(8,12...) fusion(f32[6,9,32,1024]{3,2,1,0:T(8,128)S(1)} %bitcast.208), kind=kLoop, calls=%fused_computation.43 | loop fusion | bytes 12582912 | tf_op jit(solution)/shard_map/squeeze | solution.py:153
  62.7 1.7 %fusion.10 = f32[6,32,1024]{2,1,0:T(8,128)S(1)} fusion(f32[6,32,1024]{2,1,0:T(8,128)S(1)} %get-tuple-element.27, f32[6,32,1024]{2,1,0:T(8,128)S(1)} %get-tuple-element.26, f32[6,32,1024]{2,1,0:T(8,128)S(1)} %get-tuple-element.25, f32[6,32,1024]{2,1,0:T(8,128)S(1)} %get-tuple-element.24, f32[6,32,1024]{2,1,0:T(8,128)S(1)} %get-tuple-element.23, ...), kind=kLoop, calls=%fused_computation.35 | loop fusion | flops 3342336 | bytes 7867392 | tf_op jit(solution)/shard_map/add | solution.py:154
  64.5 3.4 %collective-permute-start = (f32[1,32,1024]{2,1,0:T(8,128)S(1)}, f32[1,32,1024]{2,1,0:T(8,128)S(1)}, u32[]{:S(2)}, u32[]{:S(2)}) collective-permute-start(f32[1,32,1024]{2,1,0:T(8,128)S(1)} %get-tuple-element.38), channel_id=1, source_target_pairs={{0,8},{8,16},{16,24},{1,9},{9,17},{17,25},{2,10},{10,18},{18,26},{... | collective-permute-start | bytes 393224 | tf_op jit(solution)/shard_map/ppermute | solution.py:158
  67.8 1.3 %collective-permute-start.1 = (f32[1,32,1024]{2,1,0:T(8,128)S(1)}, f32[1,32,1024]{2,1,0:T(8,128)S(1)}, u32[]{:S(2)}, u32[]{:S(2)}) collective-permute-start(f32[1,32,1024]{2,1,0:T(8,128)S(1)} %get-tuple-element.39), channel_id=1, source_target_pairs={{8,0},{16,8},{24,16},{9,1},{17,9},{25,17},{10,2},{18,10},{26,18},{... | collective-permute-start | bytes 393224 | tf_op jit(solution)/shard_map/ppermute | solution.py:159
  69.2 2.7 %collective-permute-start.7 = (f32[224,256]{1,0:T(8,128)S(1)}, f32[224,256]{1,0:T(8,128)S(1)}, u32[]{:S(2)}, u32[]{:S(2)}) collective-permute-start(f32[224,256]{1,0:T(8,128)S(1)} %fusion.45), channel_id=1, source_target_pairs={{0,8},{8,0},{16,24},{24,16},{1,9},{9,1},{17,25},{25,17},{2,10},{10... | collective-permute-start | bytes 688136 | tf_op jit(solution)/shard_map/ppermute | solution.py:106
  72.0 1.5 %collective-permute-start.8 = (f32[224,256]{1,0:T(8,128)S(1)}, f32[224,256]{1,0:T(8,128)S(1)}, u32[]{:S(2)}, u32[]{:S(2)}) collective-permute-start(f32[224,256]{1,0:T(8,128)S(1)} %fusion.45), channel_id=1, source_target_pairs={{0,16},{8,24},{16,0},{24,8},{1,17},{9,25},{17,1},{25,9},{2,18},{10... | collective-permute-start | bytes 688136 | tf_op jit(solution)/shard_map/ppermute | solution.py:106
  73.4 0.9 collective-permute-start.9
  74.3 1.8 %collective-permute-done.1 = f32[1,32,1024]{2,1,0:T(8,128)S(1)} collective-permute-done((f32[1,32,1024]{2,1,0:T(8,128)S(1)}, f32[1,32,1024]{2,1,0:T(8,128)S(1)}, u32[]{:S(2)}, u32[]{:S(2)}) %collective-permute-start.1) | collective-permute-done | bytes 131104 | tf_op jit(solution)/shard_map/ppermute | solution.py:159
  76.3 0.9 copy.47
  77.2 3.9 %collective-permute-done.7 = f32[224,256]{1,0:T(8,128)S(1)} collective-permute-done((f32[224,256]{1,0:T(8,128)S(1)}, f32[224,256]{1,0:T(8,128)S(1)}, u32[]{:S(2)}, u32[]{:S(2)}) %collective-permute-start.7) | collective-permute-done | bytes 229408 | tf_op jit(solution)/shard_map/ppermute | solution.py:106
  81.1 3.9 %collective-permute-done.9 = f32[224,256]{1,0:T(8,128)S(1)} collective-permute-done((f32[224,256]{1,0:T(8,128)S(1)}, f32[224,256]{1,0:T(8,128)S(1)}, u32[]{:S(2)}, u32[]{:S(2)}) %collective-permute-start.9) | collective-permute-done | bytes 229408 | tf_op jit(solution)/shard_map/ppermute | solution.py:106
  85.1 1.0 pad_maximum_fusion.1
  86.1 0.5 slice_bitcast_fusion.9
  86.6 13.0 %reduce-scatter.2.cloned.1.call-done = f32[128,1024]{1,0:T(8,128)} async-done(((f32[1024,1024]{1,0:T(8,128)}), f32[128,1024]{1,0:T(8,128)}) %reduce-scatter.2.cloned.1.call-update) | async-done | bytes 524304 | tf_op jit(solution)/shard_map/reduce_scatter | solution.py:208
  99.7 1.1 convert_element_type.39
  100.8 0.9 copy.48
  (50 shorter events, 3.0 us)
Async XLA Ops:
  7.2 40.7 %all-gather.2.cloned.1.call-start = ((), (), s32[]{:S(2)}) async-start(), calls=%async_computation.1 | async-start | bytes 2359296 | tf_op jit(solution)/shard_map/all_gather | solution.py:136
  8.3 11.0 %collective-permute-start.2 = (bf16[1,32,1024]{2,1,0:T(8,128)(2,1)S(1)}, bf16[1,32,1024]{2,1,0:T(8,128)(2,1)S(1)}, u32[]{:S(2)}, u32[]{:S(2)}) collective-permute-start(bf16[1,32,1024]{2,1,0:T(8,128)(2,1)S(1)} %get-tuple-element.48), channel_id=1, source_target_pairs={{0,8},{8,16},{16,24},{1,9},{9,17},{17,25},{2,10},{10,18},{18,26},{... | collective-permute-start | bytes 196616 | tf_op jit(solution)/shard_map/ppermute | solution.py:28
  13.1 6.2 %collective-permute-start.3 = (bf16[1,32,1024]{2,1,0:T(8,128)(2,1)S(1)}, bf16[1,32,1024]{2,1,0:T(8,128)(2,1)S(1)}, u32[]{:S(2)}, u32[]{:S(2)}) collective-permute-start(bf16[1,32,1024]{2,1,0:T(8,128)(2,1)S(1)} %get-tuple-element.49), channel_id=1, source_target_pairs={{8,0},{16,8},{24,16},{9,1},{17,9},{25,17},{10,2},{18,10},{26,18},{... | collective-permute-start | bytes 196616 | tf_op jit(solution)/shard_map/ppermute | solution.py:29
  16.2 83.5 %reduce-scatter.2.cloned.1.call-start = ((), (), s32[]{:S(2)}) async-start(), calls=%async_computation.2 | async-start | bytes 4718592 | tf_op jit(solution)/shard_map/reduce_scatter | solution.py:208
  22.5 2.1 %copy-start.1 = (bf16[4,9,32,1024]{3,2,1,0:T(8,128)(2,1)}, bf16[4,9,32,1024]{3,2,1,0:T(8,128)(2,1)S(1)}, u32[]{:S(2)}) copy-start(bf16[4,9,32,1024]{3,2,1,0:T(8,128)(2,1)S(1)} %copy.42) | copy-start | bytes 7077892
  22.8 2.0 %copy-start.3 = (bf16[4,9,32,1024]{3,2,1,0:T(8,128)(2,1)}, bf16[4,9,32,1024]{3,2,1,0:T(8,128)(2,1)S(1)}, u32[]{:S(2)}) copy-start(bf16[4,9,32,1024]{3,2,1,0:T(8,128)(2,1)S(1)} %copy.40) | copy-start | bytes 7077892
  31.2 0.9 copy-start.6
  31.2 1.3 %copy-start.5 = (bf16[27,256,32]{1,2,0:T(8,128)(2,1)S(1)}, bf16[27,256,32]{1,2,0:T(8,128)(2,1)}, u32[]{:S(2)}) copy-start(bf16[27,256,32]{1,2,0:T(8,128)(2,1)} %param.7) | copy-start | bytes 1327108
  47.8 2.6 %copy-start = (bf16[4,256,1024]{2,1,0:T(8,128)(2,1)S(1)}, bf16[4,256,1024]{2,1,0:T(8,128)(2,1)}, u32[]{:S(2)}) copy-start(bf16[4,256,1024]{2,1,0:T(8,128)(2,1)} %all-gather.2.cloned.1.call-done) | copy-start | bytes 6291460
  47.8 2.9 %copy-start.2 = (bf16[4,9,32,1024]{3,2,1,0:T(8,128)(2,1)S(1)}, bf16[4,9,32,1024]{3,2,1,0:T(8,128)(2,1)}, u32[]{:S(2)}) copy-start(bf16[4,9,32,1024]{3,2,1,0:T(8,128)(2,1)} %copy-done.1) | copy-start | bytes 7077892
  50.4 1.8 %copy-start.4 = (bf16[4,9,32,1024]{3,2,1,0:T(8,128)(2,1)S(1)}, bf16[4,9,32,1024]{3,2,1,0:T(8,128)(2,1)}, u32[]{:S(2)}) copy-start(bf16[4,9,32,1024]{3,2,1,0:T(8,128)(2,1)} %copy-done.3) | copy-start | bytes 7077892
  53.4 15.8 %collective-permute-start.4 = (f32[224,256]{1,0:T(8,128)S(1)}, f32[224,256]{1,0:T(8,128)S(1)}, u32[]{:S(2)}, u32[]{:S(2)}) collective-permute-start(f32[224,256]{1,0:T(8,128)S(1)} %get-tuple-element.35), channel_id=1, source_target_pairs={{0,8},{8,0},{16,24},{24,16},{1,9},{9,1},{17,25},{25,17},{2,10},{10... | collective-permute-start | bytes 688136 | tf_op jit(solution)/shard_map/ppermute | solution.py:104
  54.9 14.2 %collective-permute-start.5 = (f32[224,256]{1,0:T(8,128)S(1)}, f32[224,256]{1,0:T(8,128)S(1)}, u32[]{:S(2)}, u32[]{:S(2)}) collective-permute-start(f32[224,256]{1,0:T(8,128)S(1)} %get-tuple-element.37), channel_id=1, source_target_pairs={{0,16},{8,24},{16,0},{24,8},{1,17},{9,25},{17,1},{25,9},{2,18},{10... | collective-permute-start | bytes 688136 | tf_op jit(solution)/shard_map/ppermute | solution.py:104
  56.4 12.8 %collective-permute-start.6 = (f32[224,256]{1,0:T(8,128)S(1)}, f32[224,256]{1,0:T(8,128)S(1)}, u32[]{:S(2)}, u32[]{:S(2)}) collective-permute-start(f32[224,256]{1,0:T(8,128)S(1)} %get-tuple-element.36), channel_id=1, source_target_pairs={{0,24},{8,16},{16,8},{24,0},{1,25},{9,17},{17,9},{25,1},{2,26},{10... | collective-permute-start | bytes 688136 | tf_op jit(solution)/shard_map/ppermute | solution.py:104
  62.7 13.5 %copy-start.7 = (f32[32]{0:T(128)S(1)}, f32[32]{0:T(128)}, u32[]{:S(2)}) copy-start(f32[32]{0:T(128)} %param.8) | copy-start | bytes 388
  64.5 9.9 %collective-permute-start = (f32[1,32,1024]{2,1,0:T(8,128)S(1)}, f32[1,32,1024]{2,1,0:T(8,128)S(1)}, u32[]{:S(2)}, u32[]{:S(2)}) collective-permute-start(f32[1,32,1024]{2,1,0:T(8,128)S(1)} %get-tuple-element.38), channel_id=1, source_target_pairs={{0,8},{8,16},{16,24},{1,9},{9,17},{17,25},{2,10},{10,18},{18,26},{... | collective-permute-start | bytes 393224 | tf_op jit(solution)/shard_map/ppermute | solution.py:158
  67.8 8.3 %collective-permute-start.1 = (f32[1,32,1024]{2,1,0:T(8,128)S(1)}, f32[1,32,1024]{2,1,0:T(8,128)S(1)}, u32[]{:S(2)}, u32[]{:S(2)}) collective-permute-start(f32[1,32,1024]{2,1,0:T(8,128)S(1)} %get-tuple-element.39), channel_id=1, source_target_pairs={{8,0},{16,8},{24,16},{9,1},{17,9},{25,17},{10,2},{18,10},{26,18},{... | collective-permute-start | bytes 393224 | tf_op jit(solution)/shard_map/ppermute | solution.py:159
  69.2 11.8 %collective-permute-start.7 = (f32[224,256]{1,0:T(8,128)S(1)}, f32[224,256]{1,0:T(8,128)S(1)}, u32[]{:S(2)}, u32[]{:S(2)}) collective-permute-start(f32[224,256]{1,0:T(8,128)S(1)} %fusion.45), channel_id=1, source_target_pairs={{0,8},{8,0},{16,24},{24,16},{1,9},{9,1},{17,25},{25,17},{2,10},{10... | collective-permute-start | bytes 688136 | tf_op jit(solution)/shard_map/ppermute | solution.py:106
  72.0 9.1 %collective-permute-start.8 = (f32[224,256]{1,0:T(8,128)S(1)}, f32[224,256]{1,0:T(8,128)S(1)}, u32[]{:S(2)}, u32[]{:S(2)}) collective-permute-start(f32[224,256]{1,0:T(8,128)S(1)} %fusion.45), channel_id=1, source_target_pairs={{0,16},{8,24},{16,0},{24,8},{1,17},{9,25},{17,1},{25,9},{2,18},{10... | collective-permute-start | bytes 688136 | tf_op jit(solution)/shard_map/ppermute | solution.py:106
  73.4 11.6 %collective-permute-start.9 = (f32[224,256]{1,0:T(8,128)S(1)}, f32[224,256]{1,0:T(8,128)S(1)}, u32[]{:S(2)}, u32[]{:S(2)}) collective-permute-start(f32[224,256]{1,0:T(8,128)S(1)} %fusion.45), channel_id=1, source_target_pairs={{0,24},{8,16},{16,8},{24,0},{1,25},{9,17},{17,9},{25,1},{2,26},{10... | collective-permute-start | bytes 688136 | tf_op jit(solution)/shard_map/ppermute | solution.py:106
Sparse Core Ops, SparseCore 0:
  16.3 31.4 all-gather.1
  50.1 49.4 reduce-scatter.1

commit v13 on v12

--- a/solution.py
+++ b/solution.py
@@ -193,9 +193,10 @@
     bias_grad = reduced[taps_total * block_out, :block_out]
 
     chan_devices = lax.axis_size("chips") * lax.axis_size("core")
-    backward_weight = jnp.transpose(weight_grid, (0, 2, 1, 3)).reshape(
-        3, chan_devices, channels_in // chan_devices, 9 * block_out
-    )
+    chips_devices = lax.axis_size("chips")
+    backward_weight = jnp.transpose(
+        weight_grid.reshape(3, 9, chips_devices, 2, channels_in // chan_devices, block_out), (0, 3, 2, 4, 1, 5)
+    ).reshape(3, chan_devices, channels_in // chan_devices, 9 * block_out)
     spread = None
     for depth_index in range(3):
         part = jnp.einsum(
@@ -206,7 +207,7 @@
         )
         spread = part if spread is None else spread + part
     summed = lax.psum_scatter(
-        spread.reshape(-1, plane_cells), ("chips", "core"), scatter_dimension=0, tiled=True
+        spread.reshape(-1, plane_cells), ("core", "chips"), scatter_dimension=0, tiled=True
     ).reshape(depth_cells, block_in, plane_cells)
     input_grad = jnp.transpose(summed.astype(jnp.bfloat16), (1, 0, 2))
     return (outputs, input_grad, weight_grad, bias_grad)

time: 109 us -> 148 us (1.36)
  waiting for transfers between devices: 38 us -> 74.6 us
  local copies, waits for them, and re-layouts: 15.6 us -> 17.6 us
    reduce_scatter x1, waiting for transfers between devices: 13 us -> 52 us  [body(): lax.psum_scatter(spread.reshape(-1, plane_cells), ('core', 'chips'), scat...]
    another operation x0 -> x2, local copies, waits for them, and re-layouts: none -> 4.74 us  [body(): weight_grid.reshape(3, 9, chips_devices, 2, channels_in // chan_devices,...]
    all_gather x1, waiting for transfers between devices: 15.3 us -> 12.9 us  [body(): lax.all_gather(inputs_planes, ('chips', 'core'), axis=1, tiled=True)]
    squeeze x6 -> x0, local copies, waits for them, and re-layouts: 1.91 us -> none  [body(): backward_weight[depth_index]]
  transfers between devices with their start and end apart: 12 -> 12, of which waited for: 5 -> 5; matrix products, arithmetic and copies ran while one was open for 29% -> 23% of each run, Pallas kernels for 0% -> 0%
where the time goes in v13:
time: 148 us; the launch traced here: 147 us
  waiting for transfers between devices  74.6 us (50%)
  starting transfers between devices  19.5 us (13%)
  local copies, waits for them, and re-layouts  17.6 us (12%)
  between operations  14.5 us (10%)
  matrix products  13.1 us (9%)
  other arithmetic  8.24 us (6%)
    reduce_scatter x1, waiting for transfers between devices, body(): lax.psum_scatter(spread.reshape(-1, plane_cells), ('core', 'chips'), scat...  52 us
    all_gather x1, waiting for transfers between devices, body(): lax.all_gather(inputs_planes, ('chips', 'core'), axis=1, tiled=True)  12.9 us
    ppermute x3, waiting for transfers between devices, all_reduce_direct(): lax.ppermute(reduced, axis, [(i, i ^ distance) for i in range(devices)])  7.76 us
    unnamed x20, local copies, waits for them, and re-layouts  6.59 us
    dot_general x3, matrix products, body(): jnp.einsum('bjk,zkn->bzjn', backward_weight[depth_index], grad_shifted[2...  6.31 us
    ppermute x3, starting transfers between devices, all_reduce_direct(): lax.ppermute(reduced, axis, [(i, i ^ distance) for i in range(devices)])  5.07 us
    ppermute x1, starting transfers between devices, padded_2(): before = lax.ppermute(last, axis, up)  4.85 us
    another operation x2, local copies, waits for them, and re-layouts, body(): weight_grid.reshape(3, 9, chips_devices, 2, channels_in // chan_devices,...  4.74 us
  transfers between devices with their start and end apart: 12, of which 5 were waited for; matrix products, arithmetic and copies ran while one was open for 23% of the time, Pallas kernels for 0%

profile of v13, /device:TPU:0, one launch (start us, length us, event | category | flops | bytes accessed | tf_op | source)
XLA Modules:
  0.0 147.5 jit_solution(1473623898036208956)
XLA Ops:
  7.2 1.0 copy.72
  8.3 4.8 %collective-permute-start.2 = (bf16[1,32,1024]{2,1,0:T(8,128)(2,1)S(1)}, bf16[1,32,1024]{2,1,0:T(8,128)(2,1)S(1)}, u32[]{:S(2)}, u32[]{:S(2)}) collective-permute-start(bf16[1,32,1024]{2,1,0:T(8,128)(2,1)S(1)} %get-tuple-element.48), channel_id=1, source_target_pairs={{0,8},{8,16},{16,24},{1,9},{9,17},{17,25},{2,10},{10,18},{18,26},{... | collective-permute-start | bytes 196616 | tf_op jit(solution)/shard_map/ppermute | solution.py:28
  13.1 1.3 collective-permute-start.3
  14.4 1.7 %copy.71 = bf16[32,4,1024]{2,0,1:T(8,128)(2,1)} copy(bf16[32,4,1024]{2,1,0:T(4,128)(2,1)} %param.6) | data formatting | bytes 524288 | tf_op args[0]
  16.2 4.4 %reshape_reshape.3 = bf16[3,9,4,2,32,32]{4,3,2,5,1,0:T(2,128)(2,1)S(1)} reshape(bf16[27,256,32]{1,2,0:T(8,128)(2,1)} %param.7) | data formatting | bytes 884736 | tf_op jit(solution)/shard_map/reshape;reshape | solution.py:198
  20.7 0.3 copy.70
  21.0 0.4 fusion.61
  21.4 0.2 fusion.25
  23.0 1.0 fusion.60
  24.0 0.2 copy.43
  24.2 0.3 copy.41
  24.6 0.2 copy.38
  24.8 1.8 %fusion.65 = f32[4,1024,8,32]{1,3,2,0:T(8,128)S(1)} fusion(bf16[4,288,1024,1]{2,1,3,0:T(8,128)(2,1)S(1)} %bitcast.209, bf16[8,32,288,1]{1,2,0,3:T(8,128)(2,1)S(1)} %bitcast.220), kind=kOutput, calls=%fused_computation.125 | convolution fusion | flops 603979776 | bytes 6701056 | tf_op jit(solution)/shard_map/bjk,zkn->bzjn/dot_general | solution.py:202
  26.6 0.2 copy-done.1
  26.8 1.8 %fusion.66 = f32[4,1024,8,32]{1,3,2,0:T(8,128)S(1)} fusion(bf16[4,288,1024,1]{2,1,3,0:T(8,128)(2,1)S(1)} %bitcast.207, bf16[8,32,288,1]{1,2,0,3:T(8,128)(2,1)S(1)} %bitcast.219), kind=kOutput, calls=%fused_computation.126 | convolution fusion | flops 603979776 | bytes 6701056 | tf_op jit(solution)/shard_map/bjk,zkn->bzjn/dot_general | solution.py:202
  28.6 2.8 %add_bitcast_fusion = f32[8,4,32,1024]{3,2,0,1:T(8,128)S(1)} fusion(f32[4,1024,8,32]{1,3,2,0:T(8,128)S(1)} %fusion.65, f32[4,1024,8,32]{1,3,2,0:T(8,128)S(1)} %fusion.66, bf16[4,288,1024,1]{2,1,3,0:T(8,128)(2,1)S(1)} %bitcast.205, bf16[8,32,288,1]{1,2,0,3:T(8,128)(2,1)S(1)} %bitcast.212), kind=kOutput, calls=%fused_computation.1 | convolution fusion | flops 606076928 | bytes 15089664 | tf_op jit(solution)/shard_map/bjk,zkn->bzjn/dot_general | solution.py:202
  31.4 2.3 %copy.45 = f32[8,4,32,1024]{3,2,1,0:T(8,128)} copy(f32[8,4,32,1024]{3,2,0,1:T(8,128)S(1)} %add_bitcast_fusion) | data formatting | bytes 8388608 | tf_op jit(solution)/shard_map/add | solution.py:208
  33.8 0.8 copy-done.6
  34.6 0.3 convert_reduce_fusion
  35.0 12.9 %all-gather.2.cloned.1.call-done = bf16[4,256,1024]{2,1,0:T(8,128)(2,1)} async-done(((bf16[4,32,1024]{2,1,0:T(8,128)(2,1)}), bf16[4,256,1024]{2,1,0:T(8,128)(2,1)}) %all-gather.2.cloned.1.call-update) | async-done | bytes 2097168 | tf_op jit(solution)/shard_map/all_gather | solution.py:136
  47.8 2.5 %convolution_bitcast_fusion.3 = f32[1,288,256]{2,1,0:T(8,128)S(1)} fusion(bf16[4,288,1024]{2,1,0:T(8,128)(2,1)S(1)} %bitcast.206, bf16[4,256,1024]{2,1,0:T(8,128)(2,1)} %all-gather.2.cloned.1.call-done), kind=kOutput, calls=%fused_computation.8 | convolution fusion | flops 603979776 | bytes 4751360 | tf_op jit(solution)/shard_map/zkn,zin->ki/dot_general | solution.py:174
  50.4 0.3 copy-done.2
  50.8 0.8 convolution_bitcast_fusion.4
  51.6 0.6 copy-done.4
  52.2 0.8 convolution_bitcast_fusion.5
  53.2 1.5 %collective-permute-start.4 = (f32[224,256]{1,0:T(8,128)S(1)}, f32[224,256]{1,0:T(8,128)S(1)}, u32[]{:S(2)}, u32[]{:S(2)}) collective-permute-start(f32[224,256]{1,0:T(8,128)S(1)} %get-tuple-element.38), channel_id=1, source_target_pairs={{0,8},{8,0},{16,24},{24,16},{1,9},{9,1},{17,25},{25,17},{2,10},{10... | collective-permute-start | bytes 688136 | tf_op jit(solution)/shard_map/ppermute | solution.py:104
  54.7 1.5 collective-permute-start.5
  56.2 0.5 collective-permute-start.6
  56.7 1.0 convolution_bitcast_fusion
  57.7 0.8 convolution_bitcast_fusion.1
  58.5 0.8 convolution_bitcast_fusion.2
  59.3 2.3 %pad_add_fusion = f32[6,288,1024]{2,1,0:T(8,128)S(1)} fusion(f32[4,288,1024]{2,1,0:T(8,128)S(1)} %convolution_bitcast_fusion, f32[4,288,1024]{2,1,0:T(8,128)S(1)} %convolution_bitcast_fusion.1, f32[4,288,1024]{2,1,0:T(8,128)S(1)} %convolution_bitcast_fusion.2), kind=kLoop, calls=%fused_computation | loop fusion | flops 3538944 | bytes 21233664 | tf_op jit(solution)/shard_map/add | solution.py:149
  61.6 1.1 slice_bitcast_fusion
  62.7 1.7 %fusion.10 = f32[6,32,1024]{2,1,0:T(8,128)S(1)} fusion(f32[6,32,1024]{2,1,0:T(8,128)S(1)} %get-tuple-element.27, f32[6,32,1024]{2,1,0:T(8,128)S(1)} %get-tuple-element.26, f32[6,32,1024]{2,1,0:T(8,128)S(1)} %get-tuple-element.25, f32[6,32,1024]{2,1,0:T(8,128)S(1)} %get-tuple-element.24, f32[6,32,1024]{2,1,0:T(8,128)S(1)} %get-tuple-element.23, ...), kind=kLoop, calls=%fused_computation.36 | loop fusion | flops 3342336 | bytes 7867392 | tf_op jit(solution)/shard_map/add | solution.py:154
  64.5 3.4 %collective-permute-start = (f32[1,32,1024]{2,1,0:T(8,128)S(1)}, f32[1,32,1024]{2,1,0:T(8,128)S(1)}, u32[]{:S(2)}, u32[]{:S(2)}) collective-permute-start(f32[1,32,1024]{2,1,0:T(8,128)S(1)} %get-tuple-element.41), channel_id=1, source_target_pairs={{0,8},{8,16},{16,24},{1,9},{9,17},{17,25},{2,10},{10,18},{18,26},{... | collective-permute-start | bytes 393224 | tf_op jit(solution)/shard_map/ppermute | solution.py:158
  67.9 1.3 collective-permute-start.1
  69.3 2.7 %collective-permute-start.7 = (f32[224,256]{1,0:T(8,128)S(1)}, f32[224,256]{1,0:T(8,128)S(1)}, u32[]{:S(2)}, u32[]{:S(2)}) collective-permute-start(f32[224,256]{1,0:T(8,128)S(1)} %fusion.45), channel_id=1, source_target_pairs={{0,8},{8,0},{16,24},{24,16},{1,9},{9,1},{17,25},{25,17},{2,10},{10... | collective-permute-start | bytes 688136 | tf_op jit(solution)/shard_map/ppermute | solution.py:106
  72.0 1.5 collective-permute-start.8
  73.4 0.9 collective-permute-start.9
  74.3 1.9 %collective-permute-done.1 = f32[1,32,1024]{2,1,0:T(8,128)S(1)} collective-permute-done((f32[1,32,1024]{2,1,0:T(8,128)S(1)}, f32[1,32,1024]{2,1,0:T(8,128)S(1)}, u32[]{:S(2)}, u32[]{:S(2)}) %collective-permute-start.1) | collective-permute-done | bytes 131104 | tf_op jit(solution)/shard_map/ppermute | solution.py:159
  76.3 0.9 copy.46
  77.2 3.9 %collective-permute-done.7 = f32[224,256]{1,0:T(8,128)S(1)} collective-permute-done((f32[224,256]{1,0:T(8,128)S(1)}, f32[224,256]{1,0:T(8,128)S(1)}, u32[]{:S(2)}, u32[]{:S(2)}) %collective-permute-start.7) | collective-permute-done | bytes 229408 | tf_op jit(solution)/shard_map/ppermute | solution.py:106
  81.1 3.9 %collective-permute-done.9 = f32[224,256]{1,0:T(8,128)S(1)} collective-permute-done((f32[224,256]{1,0:T(8,128)S(1)}, f32[224,256]{1,0:T(8,128)S(1)}, u32[]{:S(2)}, u32[]{:S(2)}) %collective-permute-start.9) | collective-permute-done | bytes 229408 | tf_op jit(solution)/shard_map/ppermute | solution.py:106
  85.1 1.0 pad_maximum_fusion.1
  86.1 0.5 slice_bitcast_fusion.9
  86.6 52.0 %reduce-scatter.2.cloned.1.call-done = f32[128,1024]{1,0:T(8,128)} async-done(((f32[1024,1024]{1,0:T(8,128)}), f32[128,1024]{1,0:T(8,128)}) %reduce-scatter.2.cloned.1.call-update) | async-done | bytes 524304 | tf_op jit(solution)/shard_map/reduce_scatter | solution.py:209
  138.6 1.1 convert_element_type.39
  139.7 0.9 copy.47
  (46 shorter events, 2.2 us)
Async XLA Ops:
  7.2 40.7 %all-gather.2.cloned.1.call-start = ((), (), s32[]{:S(2)}) async-start(), calls=%async_computation.1 | async-start | bytes 2359296 | tf_op jit(solution)/shard_map/all_gather | solution.py:136
  8.3 13.1 %collective-permute-start.2 = (bf16[1,32,1024]{2,1,0:T(8,128)(2,1)S(1)}, bf16[1,32,1024]{2,1,0:T(8,128)(2,1)S(1)}, u32[]{:S(2)}, u32[]{:S(2)}) collective-permute-start(bf16[1,32,1024]{2,1,0:T(8,128)(2,1)S(1)} %get-tuple-element.48), channel_id=1, source_target_pairs={{0,8},{8,16},{16,24},{1,9},{9,17},{17,25},{2,10},{10,18},{18,26},{... | collective-permute-start | bytes 196616 | tf_op jit(solution)/shard_map/ppermute | solution.py:28
  13.1 8.3 %collective-permute-start.3 = (bf16[1,32,1024]{2,1,0:T(8,128)(2,1)S(1)}, bf16[1,32,1024]{2,1,0:T(8,128)(2,1)S(1)}, u32[]{:S(2)}, u32[]{:S(2)}) collective-permute-start(bf16[1,32,1024]{2,1,0:T(8,128)(2,1)S(1)} %get-tuple-element.49), channel_id=1, source_target_pairs={{8,0},{16,8},{24,16},{9,1},{17,9},{25,17},{10,2},{18,10},{26,18},{... | collective-permute-start | bytes 196616 | tf_op jit(solution)/shard_map/ppermute | solution.py:29
  16.2 122.5 %reduce-scatter.2.cloned.1.call-start = ((), (), s32[]{:S(2)}) async-start(), calls=%async_computation.2 | async-start | bytes 4718592 | tf_op jit(solution)/shard_map/reduce_scatter | solution.py:209
  24.6 2.2 %copy-start.1 = (bf16[4,9,32,1024]{3,2,1,0:T(8,128)(2,1)}, bf16[4,9,32,1024]{3,2,1,0:T(8,128)(2,1)S(1)}, u32[]{:S(2)}) copy-start(bf16[4,9,32,1024]{3,2,1,0:T(8,128)(2,1)S(1)} %copy.41) | copy-start | bytes 7077892
  24.8 1.8 %copy-start.3 = (bf16[4,9,32,1024]{3,2,1,0:T(8,128)(2,1)}, bf16[4,9,32,1024]{3,2,1,0:T(8,128)(2,1)S(1)}, u32[]{:S(2)}) copy-start(bf16[4,9,32,1024]{3,2,1,0:T(8,128)(2,1)S(1)} %copy.38) | copy-start | bytes 7077892
  33.6 1.0 copy-start.6
  33.6 1.3 copy-start.5
  47.8 2.6 %copy-start = (bf16[4,256,1024]{2,1,0:T(8,128)(2,1)S(1)}, bf16[4,256,1024]{2,1,0:T(8,128)(2,1)}, u32[]{:S(2)}) copy-start(bf16[4,256,1024]{2,1,0:T(8,128)(2,1)} %all-gather.2.cloned.1.call-done) | copy-start | bytes 6291460
  47.8 2.9 %copy-start.2 = (bf16[4,9,32,1024]{3,2,1,0:T(8,128)(2,1)S(1)}, bf16[4,9,32,1024]{3,2,1,0:T(8,128)(2,1)}, u32[]{:S(2)}) copy-start(bf16[4,9,32,1024]{3,2,1,0:T(8,128)(2,1)} %copy-done.1) | copy-start | bytes 7077892
  50.4 1.8 %copy-start.4 = (bf16[4,9,32,1024]{3,2,1,0:T(8,128)(2,1)S(1)}, bf16[4,9,32,1024]{3,2,1,0:T(8,128)(2,1)}, u32[]{:S(2)}) copy-start(bf16[4,9,32,1024]{3,2,1,0:T(8,128)(2,1)} %copy-done.3) | copy-start | bytes 7077892
  53.2 16.0 %collective-permute-start.4 = (f32[224,256]{1,0:T(8,128)S(1)}, f32[224,256]{1,0:T(8,128)S(1)}, u32[]{:S(2)}, u32[]{:S(2)}) collective-permute-start(f32[224,256]{1,0:T(8,128)S(1)} %get-tuple-element.38), channel_id=1, source_target_pairs={{0,8},{8,0},{16,24},{24,16},{1,9},{9,1},{17,25},{25,17},{2,10},{10... | collective-permute-start | bytes 688136 | tf_op jit(solution)/shard_map/ppermute | solution.py:104
  54.7 14.5 %collective-permute-start.5 = (f32[224,256]{1,0:T(8,128)S(1)}, f32[224,256]{1,0:T(8,128)S(1)}, u32[]{:S(2)}, u32[]{:S(2)}) collective-permute-start(f32[224,256]{1,0:T(8,128)S(1)} %get-tuple-element.40), channel_id=1, source_target_pairs={{0,16},{8,24},{16,0},{24,8},{1,17},{9,25},{17,1},{25,9},{2,18},{10... | collective-permute-start | bytes 688136 | tf_op jit(solution)/shard_map/ppermute | solution.py:104
  56.2 13.0 %collective-permute-start.6 = (f32[224,256]{1,0:T(8,128)S(1)}, f32[224,256]{1,0:T(8,128)S(1)}, u32[]{:S(2)}, u32[]{:S(2)}) collective-permute-start(f32[224,256]{1,0:T(8,128)S(1)} %get-tuple-element.39), channel_id=1, source_target_pairs={{0,24},{8,16},{16,8},{24,0},{1,25},{9,17},{17,9},{25,1},{2,26},{10... | collective-permute-start | bytes 688136 | tf_op jit(solution)/shard_map/ppermute | solution.py:104
  62.7 13.5 %copy-start.7 = (f32[32]{0:T(128)S(1)}, f32[32]{0:T(128)}, u32[]{:S(2)}) copy-start(f32[32]{0:T(128)} %param.8) | copy-start | bytes 388
  64.5 9.9 %collective-permute-start = (f32[1,32,1024]{2,1,0:T(8,128)S(1)}, f32[1,32,1024]{2,1,0:T(8,128)S(1)}, u32[]{:S(2)}, u32[]{:S(2)}) collective-permute-start(f32[1,32,1024]{2,1,0:T(8,128)S(1)} %get-tuple-element.41), channel_id=1, source_target_pairs={{0,8},{8,16},{16,24},{1,9},{9,17},{17,25},{2,10},{10,18},{18,26},{... | collective-permute-start | bytes 393224 | tf_op jit(solution)/shard_map/ppermute | solution.py:158
  67.9 8.3 %collective-permute-start.1 = (f32[1,32,1024]{2,1,0:T(8,128)S(1)}, f32[1,32,1024]{2,1,0:T(8,128)S(1)}, u32[]{:S(2)}, u32[]{:S(2)}) collective-permute-start(f32[1,32,1024]{2,1,0:T(8,128)S(1)} %get-tuple-element.42), channel_id=1, source_target_pairs={{8,0},{16,8},{24,16},{9,1},{17,9},{25,17},{10,2},{18,10},{26,18},{... | collective-permute-start | bytes 393224 | tf_op jit(solution)/shard_map/ppermute | solution.py:159
  69.3 11.8 %collective-permute-start.7 = (f32[224,256]{1,0:T(8,128)S(1)}, f32[224,256]{1,0:T(8,128)S(1)}, u32[]{:S(2)}, u32[]{:S(2)}) collective-permute-start(f32[224,256]{1,0:T(8,128)S(1)} %fusion.45), channel_id=1, source_target_pairs={{0,8},{8,0},{16,24},{24,16},{1,9},{9,1},{17,25},{25,17},{2,10},{10... | collective-permute-start | bytes 688136 | tf_op jit(solution)/shard_map/ppermute | solution.py:106
  72.0 9.1 %collective-permute-start.8 = (f32[224,256]{1,0:T(8,128)S(1)}, f32[224,256]{1,0:T(8,128)S(1)}, u32[]{:S(2)}, u32[]{:S(2)}) collective-permute-start(f32[224,256]{1,0:T(8,128)S(1)} %fusion.45), channel_id=1, source_target_pairs={{0,16},{8,24},{16,0},{24,8},{1,17},{9,25},{17,1},{25,9},{2,18},{10... | collective-permute-start | bytes 688136 | tf_op jit(solution)/shard_map/ppermute | solution.py:106
  73.4 11.6 %collective-permute-start.9 = (f32[224,256]{1,0:T(8,128)S(1)}, f32[224,256]{1,0:T(8,128)S(1)}, u32[]{:S(2)}, u32[]{:S(2)}) collective-permute-start(f32[224,256]{1,0:T(8,128)S(1)} %fusion.45), channel_id=1, source_target_pairs={{0,24},{8,16},{16,8},{24,0},{1,25},{9,17},{17,9},{25,1},{2,26},{10... | collective-permute-start | bytes 688136 | tf_op jit(solution)/shard_map/ppermute | solution.py:106
Sparse Core Ops, SparseCore 0:
  16.3 31.4 all-gather.1
  50.1 88.4 reduce-scatter.1

commit v14 on v8

--- a/solution.py
+++ b/solution.py
@@ -131,9 +131,8 @@
     depth_cells = inputs.shape[1]
     plane_cells = inputs.shape[2]
     grad_scale = 1.0 / math.sqrt(lax.axis_size("space") * depth_cells * plane_cells)
-    inputs_planes = jnp.transpose(inputs, (1, 0, 2))
     grad_planes = jnp.transpose(output_grad, (1, 0, 2))
-    gathered = lax.all_gather(inputs_planes, ("chips", "core"), axis=1, tiled=True)
+    gathered = jnp.transpose(lax.all_gather(inputs, ("chips", "core"), axis=0, tiled=True), (1, 0, 2))
 
     weight_grid = weight.reshape(3, 9, channels_in, block_out)
     forward_weight = jnp.transpose(weight_grid, (0, 1, 3, 2)).reshape(3, 9 * block_out, channels_in)

time: 98.5 us -> 98.4 us (level)
    unnamed x20 -> x18, local copies, waits for them, and re-layouts: 6.95 us -> 6.14 us
  transfers between devices with their start and end apart: 13 -> 13, of which waited for: 6 -> 6; matrix products, arithmetic and copies ran while one was open for 37% -> 38% of each run, Pallas kernels for 0% -> 0%
where the time goes in v14:
time: 98.4 us; the launch traced here: 98.1 us
  waiting for transfers between devices  20.6 us (21%)
  starting transfers between devices  19.5 us (20%)
  local copies, waits for them, and re-layouts  16.3 us (17%)
  between operations  15.9 us (16%)
  matrix products  13.3 us (14%)
  other arithmetic  12.4 us (13%)
    ppermute x3, waiting for transfers between devices, all_reduce_direct(): lax.ppermute(reduced, axis, [(i, i ^ distance) for i in range(devices)])  7.76 us
    all_gather x1, waiting for transfers between devices, body(): lax.all_gather(inputs, ('chips', 'core'), axis=0, tiled=True)  6.14 us
    unnamed x18, local copies, waits for them, and re-layouts  6.14 us
    dot_general x3, matrix products, body(): jnp.einsum('bjk,zkn->bzjn', backward_weight[depth_index], grad_shifted[2...  5.84 us
    dot_general x3, matrix products, body(): jnp.einsum('zkn,zin->ki', grad_shifted[2 - depth_index:2 - depth_index +...  5.1 us
    ppermute x3, starting transfers between devices, all_reduce_direct(): lax.ppermute(reduced, axis, [(i, i ^ distance) for i in range(devices)])  5.07 us
    ppermute x1, starting transfers between devices, padded_2(): before = lax.ppermute(last, axis, up)  4.85 us
    add x1, other arithmetic, scatter_channels(): partial = keep + lax.ppermute(send, 'core', [(0, 1), (1, 0)])  4.19 us
  transfers between devices with their start and end apart: 13, of which 6 were waited for; matrix products, arithmetic and copies ran while one was open for 38% of the time, Pallas kernels for 0%

profile of v14, /device:TPU:0, one launch (start us, length us, event | category | flops | bytes accessed | tf_op | source)
XLA Modules:
  0.0 98.1 jit_solution(1261966343542023361)
XLA Ops:
  8.0 1.0 %copy.67 = bf16[32,4,1024]{2,0,1:T(8,128)(2,1)S(1)} copy(bf16[32,4,1024]{2,1,0:T(4,128)(2,1)} %param.9) | data formatting | bytes 524288 | tf_op args[3]
  9.1 4.8 %collective-permute-start.2 = (bf16[1,32,1024]{2,1,0:T(8,128)(2,1)S(1)}, bf16[1,32,1024]{2,1,0:T(8,128)(2,1)S(1)}, u32[]{:S(2)}, u32[]{:S(2)}) collective-permute-start(bf16[1,32,1024]{2,1,0:T(8,128)(2,1)S(1)} %get-tuple-element.50), channel_id=1, source_target_pairs={{0,8},{8,16},{16,24},{1,9},{9,17},{17,25},{2,10},{10,18},{18,26},{... | collective-permute-start | bytes 196616 | tf_op jit(solution)/shard_map/ppermute | solution.py:28
  14.0 1.3 %collective-permute-start.3 = (bf16[1,32,1024]{2,1,0:T(8,128)(2,1)S(1)}, bf16[1,32,1024]{2,1,0:T(8,128)(2,1)S(1)}, u32[]{:S(2)}, u32[]{:S(2)}) collective-permute-start(bf16[1,32,1024]{2,1,0:T(8,128)(2,1)S(1)} %get-tuple-element.51), channel_id=1, source_target_pairs={{8,0},{16,8},{24,16},{9,1},{17,9},{25,17},{10,2},{18,10},{26,18},{... | collective-permute-start | bytes 196616 | tf_op jit(solution)/shard_map/ppermute | solution.py:29
  15.3 1.7 %copy.27 = bf16[32,4,1024]{2,0,1:T(8,128)(2,1)} copy(bf16[32,4,1024]{2,1,0:T(4,128)(2,1)} %param.6) | data formatting | bytes 524288 | tf_op args[0]
  17.1 1.1 %fusion.85 = (bf16[1,256,9,32]{1,3,2,0:T(8,128)(2,1)S(1)}, bf16[1,256,9,32]{1,3,2,0:T(8,128)(2,1)S(1)}, bf16[1,256,9,32]{1,3,2,0:T(8,128)(2,1)S(1)}) fusion(bf16[3,256,9,32]{1,3,2,0:T(8,128)(2,1)} %bitcast.240), kind=kLoop, calls=%fused_computation.138 | loop fusion | bytes 884736 | tf_op jit(solution)/shard_map/slice | solution.py:202
  18.4 0.4 copy.43
  18.8 0.2 squeeze.92
  19.1 0.4 copy.41
  19.7 0.4 copy.45
  21.7 1.0 %fusion.83 = (bf16[4,9,32,1024]{3,2,0,1:T(8,128)(2,1)S(1)}, bf16[4,9,32,1024]{3,2,0,1:T(8,128)(2,1)S(1)}, bf16[4,9,32,1024]{3,2,0,1:T(8,128)(2,1)S(1)}) fusion(bf16[6,9,32,1024]{3,2,0,1:T(8,128)(2,1)S(1)} %fusion.45), kind=kLoop, calls=%fused_computation.136 | loop fusion | bytes 14155776 | tf_op jit(solution)/shard_map/slice | solution.py:203
  23.2 0.3 copy.40
  23.6 0.9 copy-done.1
  24.4 1.7 %fusion.65 = f32[4,1024,8,32]{1,3,2,0:T(8,128)S(1)} fusion(bf16[4,288,1024,1]{2,1,3,0:T(8,128)(2,1)S(1)} %bitcast.229, bf16[8,32,288]{2,1,0:T(8,128)(2,1)S(1)} %copy.43), kind=kOutput, calls=%fused_computation.113 | convolution fusion | flops 603979776 | bytes 6701056 | tf_op jit(solution)/shard_map/bjk,zkn->bzjn/dot_general | solution.py:200
  26.2 1.8 %fusion.67 = f32[4,1024,8,32]{1,3,2,0:T(8,128)S(1)} fusion(bf16[4,288,1024,1]{2,1,3,0:T(8,128)(2,1)S(1)} %bitcast.231, bf16[8,32,288]{2,1,0:T(8,128)(2,1)S(1)} %copy.41), kind=kOutput, calls=%fused_computation.115 | convolution fusion | flops 603979776 | bytes 6701056 | tf_op jit(solution)/shard_map/bjk,zkn->bzjn/dot_general | solution.py:200
  28.0 2.3 %add_add_fusion = f32[4,1024,8,32]{1,3,2,0:T(8,128)S(1)} fusion(f32[4,1024,8,32]{1,3,2,0:T(8,128)S(1)} %fusion.67, f32[4,1024,8,32]{1,3,2,0:T(8,128)S(1)} %fusion.65, bf16[4,288,1024,1]{2,1,3,0:T(8,128)(2,1)S(1)} %bitcast.227, bf16[8,32,288]{2,1,0:T(8,128)(2,1)S(1)} %copy.45), kind=kOutput, calls=%fused_computation.1 | convolution fusion | flops 606076928 | bytes 15089664 | tf_op jit(solution)/shard_map/bjk,zkn->bzjn/dot_general | solution.py:200
  30.3 1.9 %constant_dynamic-slice_fusion.1 = (f32[4,1,4,32,1024]{4,3,1,0,2:T(8,128)}, f32[4,1,4,32,1024]{4,3,1,0,2:T(8,128)S(1)}) fusion(f32[4,2,4,32,1024]{4,3,1,0,2:T(8,128)S(1)} %bitcast.224, s32[]{:T(128)S(6)} %select_n.181, s32[]{:T(128)S(6)} %select_n.182), kind=kLoop, calls=%fused_computation.134 | loop fusion | bytes 8388616 | tf_op jit(solution)/shard_map/jit(dynamic_index_in_dim)/dynamic_slice | solution.py:118
  32.2 1.6 %copy.66 = f32[4,1,4,32,1024]{4,3,2,0,1:T(8,128)} copy(f32[4,1,4,32,1024]{4,3,1,0,2:T(8,128)S(1)} %get-tuple-element.29) | data formatting | bytes 4194304 | tf_op jit(solution)/shard_map/jit(dynamic_index_in_dim)/dynamic_slice | solution.py:119
  33.9 0.3 convert_reduce_fusion
  34.3 4.1 %collective-permute-done.4 = f32[4,4,32,1024]{3,2,1,0:T(8,128)} collective-permute-done((f32[4,4,32,1024]{3,2,1,0:T(8,128)}, f32[4,4,32,1024]{3,2,1,0:T(8,128)}, u32[]{:S(2)}, u32[]{:S(2)}) %collective-permute-start.4) | collective-permute-done | bytes 2097184 | tf_op jit(solution)/shard_map/ppermute | solution.py:120
  38.3 4.2 %bitcast_add_fusion = f32[4,4,32,1024]{3,2,1,0:T(8,128)} fusion(f32[4,4,32,1024]{3,2,1,0:T(8,128)} %collective-permute-done.4, f32[4,1,4,32,1024]{4,3,1,0,2:T(8,128)} %get-tuple-element.28), kind=kLoop, calls=%fused_computation.5 | loop fusion | flops 524288 | bytes 6291456 | tf_op jit(solution)/shard_map/add | solution.py:120
  42.5 6.1 %all-gather.2.cloned.1.call-done = bf16[256,4,1024]{2,0,1:T(8,128)(2,1)} async-done(((bf16[32,4,1024]{2,0,1:T(8,128)(2,1)}), bf16[256,4,1024]{2,0,1:T(8,128)(2,1)}) %all-gather.2.cloned.1.call-update) | async-done | bytes 2097168 | tf_op jit(solution)/shard_map/all_gather | solution.py:135
  48.7 3.3 %fusion.12 = f32[1,288,256]{2,1,0:T(8,128)S(1)} fusion(bf16[4,288,1024]{2,1,0:T(8,128)(2,1)} %bitcast.230, bf16[256,4,1024]{2,0,1:T(8,128)(2,1)} %all-gather.2.cloned.1.call-done), kind=kOutput, calls=%fused_computation.19 | convolution fusion | flops 603979776 | bytes 4751360 | tf_op jit(solution)/shard_map/zkn,zin->ki/dot_general | solution.py:173
  52.0 1.0 %fusion.15 = f32[1,288,256]{2,1,0:T(8,128)S(1)} fusion(bf16[4,288,1024]{2,1,0:T(8,128)(2,1)S(1)} %bitcast.228, bf16[256,4,1024]{2,0,1:T(8,128)(2,1)S(1)} %copy-done), kind=kOutput, calls=%fused_computation.20 | convolution fusion | flops 603979776 | bytes 4751360 | tf_op jit(solution)/shard_map/zkn,zin->ki/dot_general | solution.py:173
  53.0 0.6 copy-done.3
  53.6 0.8 fusion.9
  54.7 1.5 %collective-permute-start.5 = (f32[224,256]{1,0:T(8,128)S(1)}, f32[224,256]{1,0:T(8,128)S(1)}, u32[]{:S(2)}, u32[]{:S(2)}) collective-permute-start(f32[224,256]{1,0:T(8,128)S(1)} %get-tuple-element.37), channel_id=1, source_target_pairs={{0,8},{8,0},{16,24},{24,16},{1,9},{9,1},{17,25},{25,17},{2,10},{10... | collective-permute-start | bytes 688136 | tf_op jit(solution)/shard_map/ppermute | solution.py:104
  56.2 1.5 %collective-permute-start.6 = (f32[224,256]{1,0:T(8,128)S(1)}, f32[224,256]{1,0:T(8,128)S(1)}, u32[]{:S(2)}, u32[]{:S(2)}) collective-permute-start(f32[224,256]{1,0:T(8,128)S(1)} %get-tuple-element.39), channel_id=1, source_target_pairs={{0,16},{8,24},{16,0},{24,8},{1,17},{9,25},{17,1},{25,9},{2,18},{10... | collective-permute-start | bytes 688136 | tf_op jit(solution)/shard_map/ppermute | solution.py:104
  57.7 0.6 collective-permute-start.7
  58.2 0.8 convolution_bitcast_fusion
  59.0 0.8 convolution_bitcast_fusion.1
  59.8 0.8 convolution_bitcast_fusion.2
  60.6 2.3 %pad_add_fusion = f32[6,288,1024]{2,1,0:T(8,128)S(1)} fusion(f32[4,288,1024]{2,1,0:T(8,128)S(1)} %convolution_bitcast_fusion, f32[4,288,1024]{2,1,0:T(8,128)S(1)} %convolution_bitcast_fusion.1, f32[4,288,1024]{2,1,0:T(8,128)S(1)} %convolution_bitcast_fusion.2), kind=kLoop, calls=%fused_computation | loop fusion | flops 3538944 | bytes 21233664 | tf_op jit(solution)/shard_map/add | solution.py:148
  62.9 1.1 %slice_bitcast_fusion = (f32[6,32,1024]{2,1,0:T(8,128)S(1)}, f32[6,32,1024]{2,1,0:T(8,128)S(1)}, f32[6,32,1024]{2,1,0:T(8,128)S(1)}, f32[6,32,1024]{2,1,0:T(8,12...) fusion(f32[6,9,32,1024]{3,2,1,0:T(8,128)S(1)} %bitcast.225), kind=kLoop, calls=%fused_computation.54 | loop fusion | bytes 12582912 | tf_op jit(solution)/shard_map/squeeze | solution.py:152
  64.0 1.7 %fusion.28 = f32[6,32,1024]{2,1,0:T(8,128)S(1)} fusion(f32[6,32,1024]{2,1,0:T(8,128)S(1)} %get-tuple-element.27, f32[6,32,1024]{2,1,0:T(8,128)S(1)} %get-tuple-element.26, f32[6,32,1024]{2,1,0:T(8,128)S(1)} %get-tuple-element.25, f32[6,32,1024]{2,1,0:T(8,128)S(1)} %get-tuple-element.24, f32[6,32,1024]{2,1,0:T(8,128)S(1)} %get-tuple-element.23, ...), kind=kLoop, calls=%fused_computation.46 | loop fusion | flops 3342336 | bytes 7867392 | tf_op jit(solution)/shard_map/add | solution.py:153
  65.7 3.4 %collective-permute-start = (f32[1,32,1024]{2,1,0:T(8,128)S(1)}, f32[1,32,1024]{2,1,0:T(8,128)S(1)}, u32[]{:S(2)}, u32[]{:S(2)}) collective-permute-start(f32[1,32,1024]{2,1,0:T(8,128)S(1)} %get-tuple-element.40), channel_id=1, source_target_pairs={{0,8},{8,16},{16,24},{1,9},{9,17},{17,25},{2,10},{10,18},{18,26},{... | collective-permute-start | bytes 393224 | tf_op jit(solution)/shard_map/ppermute | solution.py:157
  69.1 1.3 %collective-permute-start.1 = (f32[1,32,1024]{2,1,0:T(8,128)S(1)}, f32[1,32,1024]{2,1,0:T(8,128)S(1)}, u32[]{:S(2)}, u32[]{:S(2)}) collective-permute-start(f32[1,32,1024]{2,1,0:T(8,128)S(1)} %get-tuple-element.41), channel_id=1, source_target_pairs={{8,0},{16,8},{24,16},{9,1},{17,9},{25,17},{10,2},{18,10},{26,18},{... | collective-permute-start | bytes 393224 | tf_op jit(solution)/shard_map/ppermute | solution.py:158
  70.5 2.7 %collective-permute-start.8 = (f32[224,256]{1,0:T(8,128)S(1)}, f32[224,256]{1,0:T(8,128)S(1)}, u32[]{:S(2)}, u32[]{:S(2)}) collective-permute-start(f32[224,256]{1,0:T(8,128)S(1)} %fusion.63), channel_id=1, source_target_pairs={{0,8},{8,0},{16,24},{24,16},{1,9},{9,1},{17,25},{25,17},{2,10},{10... | collective-permute-start | bytes 688136 | tf_op jit(solution)/shard_map/ppermute | solution.py:106
  73.2 1.5 %collective-permute-start.9 = (f32[224,256]{1,0:T(8,128)S(1)}, f32[224,256]{1,0:T(8,128)S(1)}, u32[]{:S(2)}, u32[]{:S(2)}) collective-permute-start(f32[224,256]{1,0:T(8,128)S(1)} %fusion.63), channel_id=1, source_target_pairs={{0,16},{8,24},{16,0},{24,8},{1,17},{9,25},{17,1},{25,9},{2,18},{10... | collective-permute-start | bytes 688136 | tf_op jit(solution)/shard_map/ppermute | solution.py:106
  74.7 0.9 collective-permute-start.10
  75.6 1.8 %collective-permute-done.1 = f32[1,32,1024]{2,1,0:T(8,128)S(1)} collective-permute-done((f32[1,32,1024]{2,1,0:T(8,128)S(1)}, f32[1,32,1024]{2,1,0:T(8,128)S(1)}, u32[]{:S(2)}, u32[]{:S(2)}) %collective-permute-start.1) | collective-permute-done | bytes 131104 | tf_op jit(solution)/shard_map/ppermute | solution.py:158
  77.6 0.9 copy.48
  78.5 3.9 %collective-permute-done.8 = f32[224,256]{1,0:T(8,128)S(1)} collective-permute-done((f32[224,256]{1,0:T(8,128)S(1)}, f32[224,256]{1,0:T(8,128)S(1)}, u32[]{:S(2)}, u32[]{:S(2)}) %collective-permute-start.8) | collective-permute-done | bytes 229408 | tf_op jit(solution)/shard_map/ppermute | solution.py:106
  82.4 3.9 %collective-permute-done.10 = f32[224,256]{1,0:T(8,128)S(1)} collective-permute-done((f32[224,256]{1,0:T(8,128)S(1)}, f32[224,256]{1,0:T(8,128)S(1)}, u32[]{:S(2)}, u32[]{:S(2)}) %collective-permute-start.10) | collective-permute-done | bytes 229408 | tf_op jit(solution)/shard_map/ppermute | solution.py:106
  86.4 1.0 pad_maximum_fusion.1
  87.4 0.5 slice_bitcast_fusion.9
  87.9 0.8 reduce-scatter.2.cloned.1.call-done
  88.7 1.1 %convert_element_type.39 = bf16[128,1024]{1,0:T(8,128)(2,1)S(1)} convert(f32[128,1024]{1,0:T(8,128)} %reduce-scatter.2.cloned.1.call-done) | non-fusion elementwise | flops 131072 | bytes 786432 | tf_op jit(solution)/shard_map/convert_element_type | solution.py:208
  89.7 0.9 copy.49
  (52 shorter events, 3.3 us)
Async XLA Ops:
  8.0 40.7 %all-gather.2.cloned.1.call-start = ((), (), s32[]{:S(2)}) async-start(), calls=%async_computation.1 | async-start | bytes 2359296 | tf_op jit(solution)/shard_map/all_gather | solution.py:135
  9.1 11.0 %collective-permute-start.2 = (bf16[1,32,1024]{2,1,0:T(8,128)(2,1)S(1)}, bf16[1,32,1024]{2,1,0:T(8,128)(2,1)S(1)}, u32[]{:S(2)}, u32[]{:S(2)}) collective-permute-start(bf16[1,32,1024]{2,1,0:T(8,128)(2,1)S(1)} %get-tuple-element.50), channel_id=1, source_target_pairs={{0,8},{8,16},{16,24},{1,9},{9,17},{17,25},{2,10},{10,18},{18,26},{... | collective-permute-start | bytes 196616 | tf_op jit(solution)/shard_map/ppermute | solution.py:28
  14.0 6.2 %collective-permute-start.3 = (bf16[1,32,1024]{2,1,0:T(8,128)(2,1)S(1)}, bf16[1,32,1024]{2,1,0:T(8,128)(2,1)S(1)}, u32[]{:S(2)}, u32[]{:S(2)}) collective-permute-start(bf16[1,32,1024]{2,1,0:T(8,128)(2,1)S(1)} %get-tuple-element.51), channel_id=1, source_target_pairs={{8,0},{16,8},{24,16},{9,1},{17,9},{25,17},{10,2},{18,10},{26,18},{... | collective-permute-start | bytes 196616 | tf_op jit(solution)/shard_map/ppermute | solution.py:29
  17.0 71.6 %reduce-scatter.2.cloned.1.call-start = ((), (), s32[]{:S(2)}) async-start(), calls=%async_computation.2 | async-start | bytes 2621440 | tf_op jit(solution)/shard_map/reduce_scatter | solution.py:121
  23.0 1.5 %copy-start.1 = (bf16[4,9,32,1024]{3,2,1,0:T(8,128)(2,1)}, bf16[4,9,32,1024]{3,2,1,0:T(8,128)(2,1)S(1)}, u32[]{:S(2)}) copy-start(bf16[4,9,32,1024]{3,2,1,0:T(8,128)(2,1)S(1)} %copy.42) | copy-start | bytes 7077892
  23.6 2.7 %copy-start.2 = (bf16[4,9,32,1024]{3,2,1,0:T(8,128)(2,1)}, bf16[4,9,32,1024]{3,2,1,0:T(8,128)(2,1)S(1)}, u32[]{:S(2)}) copy-start(bf16[4,9,32,1024]{3,2,1,0:T(8,128)(2,1)S(1)} %copy.40) | copy-start | bytes 7077892
  32.2 1.7 %copy-start.5 = (bf16[32,4,1024]{2,1,0:T(4,128)(2,1)S(1)}, bf16[32,4,1024]{2,1,0:T(4,128)(2,1)}, u32[]{:S(2)}) copy-start(bf16[32,4,1024]{2,1,0:T(4,128)(2,1)} %param.9) | copy-start | bytes 786436
  32.2 2.0 %copy-start.4 = (bf16[27,256,32]{1,2,0:T(8,128)(2,1)S(1)}, bf16[27,256,32]{1,2,0:T(8,128)(2,1)}, u32[]{:S(2)}) copy-start(bf16[27,256,32]{1,2,0:T(8,128)(2,1)} %param.7) | copy-start | bytes 1327108
  33.8 4.5 %collective-permute-start.4 = (f32[4,4,32,1024]{3,2,1,0:T(8,128)}, f32[4,4,32,1024]{3,2,1,0:T(8,128)}, u32[]{:S(2)}, u32[]{:S(2)}) collective-permute-start(f32[4,4,32,1024]{3,2,1,0:T(8,128)} %bitcast.222), channel_id=1, source_target_pairs={{0,1},{1,0},{2,3},{3,2},{4,5},{5,4},{6,7},{7,6},{8,9},{9,8},{10,11... | collective-permute-start | bytes 6291464 | tf_op jit(solution)/shard_map/ppermute | solution.py:120
  48.7 3.3 %copy-start = (bf16[256,4,1024]{2,0,1:T(8,128)(2,1)S(1)}, bf16[256,4,1024]{2,0,1:T(8,128)(2,1)}, u32[]{:S(2)}) copy-start(bf16[256,4,1024]{2,0,1:T(8,128)(2,1)} %all-gather.2.cloned.1.call-done) | copy-start | bytes 6291460
  52.0 1.7 %copy-start.3 = (bf16[4,9,32,1024]{3,2,1,0:T(8,128)(2,1)S(1)}, bf16[4,9,32,1024]{3,2,1,0:T(8,128)(2,1)}, u32[]{:S(2)}) copy-start(bf16[4,9,32,1024]{3,2,1,0:T(8,128)(2,1)} %copy-done.2) | copy-start | bytes 7077892
  54.7 15.8 %collective-permute-start.5 = (f32[224,256]{1,0:T(8,128)S(1)}, f32[224,256]{1,0:T(8,128)S(1)}, u32[]{:S(2)}, u32[]{:S(2)}) collective-permute-start(f32[224,256]{1,0:T(8,128)S(1)} %get-tuple-element.37), channel_id=1, source_target_pairs={{0,8},{8,0},{16,24},{24,16},{1,9},{9,1},{17,25},{25,17},{2,10},{10... | collective-permute-start | bytes 688136 | tf_op jit(solution)/shard_map/ppermute | solution.py:104
  56.2 14.2 %collective-permute-start.6 = (f32[224,256]{1,0:T(8,128)S(1)}, f32[224,256]{1,0:T(8,128)S(1)}, u32[]{:S(2)}, u32[]{:S(2)}) collective-permute-start(f32[224,256]{1,0:T(8,128)S(1)} %get-tuple-element.39), channel_id=1, source_target_pairs={{0,16},{8,24},{16,0},{24,8},{1,17},{9,25},{17,1},{25,9},{2,18},{10... | collective-permute-start | bytes 688136 | tf_op jit(solution)/shard_map/ppermute | solution.py:104
  57.7 12.8 %collective-permute-start.7 = (f32[224,256]{1,0:T(8,128)S(1)}, f32[224,256]{1,0:T(8,128)S(1)}, u32[]{:S(2)}, u32[]{:S(2)}) collective-permute-start(f32[224,256]{1,0:T(8,128)S(1)} %get-tuple-element.38), channel_id=1, source_target_pairs={{0,24},{8,16},{16,8},{24,0},{1,25},{9,17},{17,9},{25,1},{2,26},{10... | collective-permute-start | bytes 688136 | tf_op jit(solution)/shard_map/ppermute | solution.py:104
  64.0 13.4 %copy-start.6 = (f32[32]{0:T(128)S(1)}, f32[32]{0:T(128)}, u32[]{:S(2)}) copy-start(f32[32]{0:T(128)} %param.8) | copy-start | bytes 388
  65.7 9.8 %collective-permute-start = (f32[1,32,1024]{2,1,0:T(8,128)S(1)}, f32[1,32,1024]{2,1,0:T(8,128)S(1)}, u32[]{:S(2)}, u32[]{:S(2)}) collective-permute-start(f32[1,32,1024]{2,1,0:T(8,128)S(1)} %get-tuple-element.40), channel_id=1, source_target_pairs={{0,8},{8,16},{16,24},{1,9},{9,17},{17,25},{2,10},{10,18},{18,26},{... | collective-permute-start | bytes 393224 | tf_op jit(solution)/shard_map/ppermute | solution.py:157
  69.1 8.3 %collective-permute-start.1 = (f32[1,32,1024]{2,1,0:T(8,128)S(1)}, f32[1,32,1024]{2,1,0:T(8,128)S(1)}, u32[]{:S(2)}, u32[]{:S(2)}) collective-permute-start(f32[1,32,1024]{2,1,0:T(8,128)S(1)} %get-tuple-element.41), channel_id=1, source_target_pairs={{8,0},{16,8},{24,16},{9,1},{17,9},{25,17},{10,2},{18,10},{26,18},{... | collective-permute-start | bytes 393224 | tf_op jit(solution)/shard_map/ppermute | solution.py:158
  70.5 11.8 %collective-permute-start.8 = (f32[224,256]{1,0:T(8,128)S(1)}, f32[224,256]{1,0:T(8,128)S(1)}, u32[]{:S(2)}, u32[]{:S(2)}) collective-permute-start(f32[224,256]{1,0:T(8,128)S(1)} %fusion.63), channel_id=1, source_target_pairs={{0,8},{8,0},{16,24},{24,16},{1,9},{9,1},{17,25},{25,17},{2,10},{10... | collective-permute-start | bytes 688136 | tf_op jit(solution)/shard_map/ppermute | solution.py:106
  73.2 9.1 %collective-permute-start.9 = (f32[224,256]{1,0:T(8,128)S(1)}, f32[224,256]{1,0:T(8,128)S(1)}, u32[]{:S(2)}, u32[]{:S(2)}) collective-permute-start(f32[224,256]{1,0:T(8,128)S(1)} %fusion.63), channel_id=1, source_target_pairs={{0,16},{8,24},{16,0},{24,8},{1,17},{9,25},{17,1},{25,9},{2,18},{10... | collective-permute-start | bytes 688136 | tf_op jit(solution)/shard_map/ppermute | solution.py:106
  74.7 11.6 %collective-permute-start.10 = (f32[224,256]{1,0:T(8,128)S(1)}, f32[224,256]{1,0:T(8,128)S(1)}, u32[]{:S(2)}, u32[]{:S(2)}) collective-permute-start(f32[224,256]{1,0:T(8,128)S(1)} %fusion.63), channel_id=1, source_target_pairs={{0,24},{8,16},{16,8},{24,0},{1,25},{9,17},{17,9},{25,1},{2,26},{10... | collective-permute-start | bytes 688136 | tf_op jit(solution)/shard_map/ppermute | solution.py:106
Sparse Core Ops, SparseCore 0:
  17.1 31.4 all-gather.1
Sparse Core Ops, SparseCore 1:
  42.6 46.0 reduce-scatter.1

commit v15 on v14

--- a/solution.py
+++ b/solution.py
@@ -110,6 +110,17 @@
     return jnp.concatenate(
         [lax.dynamic_index_in_dim(stacked, index ^ chunk, 0, keepdims=False) for chunk in range(devices)]
     )
+
+
+def scatter_chips_first(blocks):
+    by_chip = blocks.reshape((-1, 2) + blocks.shape[1:])
+    pairs = lax.psum_scatter(
+        by_chip.reshape(-1, blocks.shape[-1]), "chips", scatter_dimension=0, tiled=True
+    ).reshape((2,) + blocks.shape[1:])
+    core = lax.axis_index("core")
+    keep = lax.dynamic_index_in_dim(pairs, core, 0, keepdims=False)
+    send = lax.dynamic_index_in_dim(pairs, 1 - core, 0, keepdims=False)
+    return keep + lax.ppermute(send, "core", [(0, 1), (1, 0)])
 
 
 def scatter_channels(blocks):
@@ -204,7 +215,7 @@
             preferred_element_type=jnp.float32,
         )
         spread = part if spread is None else spread + part
-    summed = scatter_channels(spread).reshape(depth_cells, block_in, plane_cells)
+    summed = scatter_chips_first(spread).reshape(depth_cells, block_in, plane_cells)
     input_grad = jnp.transpose(summed.astype(jnp.bfloat16), (1, 0, 2))
     return (outputs, input_grad, weight_grad, bias_grad)
 

time: 98.4 us -> 127 us (1.29)
  waiting for transfers between devices: 20.6 us -> 53.2 us
  other arithmetic: 12.4 us -> 7.25 us
    all_gather x1, waiting for transfers between devices: 6.14 us -> 37.7 us  [body(): lax.all_gather(inputs, ('chips', 'core'), axis=0, tiled=True)]
    reduce_scatter x1, waiting for transfers between devices: 0.77 us -> 13.4 us  [scatter_chips_first(): lax.psum_scatter(by_chip.reshape(-1, blocks.shape[-1]), 'chips', scatter_...]
    ppermute x3, waiting for transfers between devices: 7.76 us -> 0.01 us  [all_reduce_direct(): lax.ppermute(reduced, axis, [(i, i ^ distance) for i in range(devices)])]
    add x1 -> x0, other arithmetic: 4.19 us -> none  [scatter_channels(): partial = keep + lax.ppermute(send, 'core', [(0, 1), (1, 0)])]
    ppermute x1, waiting for transfers between devices: 4.05 us -> 0.23 us  [scatter_chips_first(): return keep + lax.ppermute(send, 'core', [(0, 1), (1, 0)])]
    dynamic_slice x2 -> x0, local copies, waits for them, and re-layouts: 3.48 us -> none  [the longest x1 1.87 us: scatter_channels(): keep = lax.dynamic_index_in_dim(by_core, core, axis=1, keepdims=False)]
    add x0 -> x1, local copies, waits for them, and re-layouts: none -> 2.25 us  [body(): spread = part if spread is None else spread + part]
    unnamed x18 -> x20, local copies, waits for them, and re-layouts: 6.14 us -> 7.25 us
  transfers between devices with their start and end apart: 13 -> 13, of which waited for: 6 -> 4; matrix products, arithmetic and copies ran while one was open for 38% -> 26% of each run, Pallas kernels for 0% -> 0%
where the time goes in v15:
time: 127 us
  waiting for transfers between devices  53.2 us (42%)
  starting transfers between devices  19.5 us (15%)
  local copies, waits for them, and re-layouts  17.2 us (14%)
  between operations  16 us (13%)
  matrix products  13.7 us (11%)
  other arithmetic  7.25 us (6%)
    all_gather x1, waiting for transfers between devices, body(): lax.all_gather(inputs, ('chips', 'core'), axis=0, tiled=True)  37.7 us
    reduce_scatter x1, waiting for transfers between devices, scatter_chips_first(): lax.psum_scatter(by_chip.reshape(-1, blocks.shape[-1]), 'chips', scatter_...  13.4 us
    unnamed x20, local copies, waits for them, and re-layouts  7.25 us
    dot_general x3, matrix products, body(): jnp.einsum('bjk,zkn->bzjn', backward_weight[depth_index], grad_shifted[2...  6.2 us
    dot_general x3, matrix products, body(): jnp.einsum('zkn,zin->ki', grad_shifted[2 - depth_index:2 - depth_index +...  5.15 us
    ppermute x3, starting transfers between devices, all_reduce_direct(): lax.ppermute(reduced, axis, [(i, i ^ distance) for i in range(devices)])  5.08 us
    ppermute x1, starting transfers between devices, padded_2(): before = lax.ppermute(last, axis, up)  4.85 us
    ppermute x3, starting transfers between devices, all_reduce_direct(): reduced = reduced + lax.ppermute(send, axis, pairs)  3.55 us
  transfers between devices with their start and end apart: 13, of which 4 were waited for; matrix products, arithmetic and copies ran while one was open for 26% of the time, Pallas kernels for 0%

profile of v15, /device:TPU:0, one launch (start us, length us, event | category | flops | bytes accessed | tf_op | source)
XLA Modules:
  0.0 126.9 jit_solution(12040518305598714832)
XLA Ops:
  8.0 1.0 copy.84
  9.1 4.8 %collective-permute-start.2 = (bf16[1,32,1024]{2,1,0:T(8,128)(2,1)S(1)}, bf16[1,32,1024]{2,1,0:T(8,128)(2,1)S(1)}, u32[]{:S(2)}, u32[]{:S(2)}) collective-permute-start(bf16[1,32,1024]{2,1,0:T(8,128)(2,1)S(1)} %get-tuple-element.52), channel_id=1, source_target_pairs={{0,8},{8,16},{16,24},{1,9},{9,17},{17,25},{2,10},{10,18},{18,26},{... | collective-permute-start | bytes 196616 | tf_op jit(solution)/shard_map/ppermute | solution.py:28
  14.0 1.3 %collective-permute-start.3 = (bf16[1,32,1024]{2,1,0:T(8,128)(2,1)S(1)}, bf16[1,32,1024]{2,1,0:T(8,128)(2,1)S(1)}, u32[]{:S(2)}, u32[]{:S(2)}) collective-permute-start(bf16[1,32,1024]{2,1,0:T(8,128)(2,1)S(1)} %get-tuple-element.53), channel_id=1, source_target_pairs={{8,0},{16,8},{24,16},{9,1},{17,9},{25,17},{10,2},{18,10},{26,18},{... | collective-permute-start | bytes 196616 | tf_op jit(solution)/shard_map/ppermute | solution.py:29
  15.3 1.7 %copy.48 = bf16[32,4,1024]{2,0,1:T(8,128)(2,1)} copy(bf16[32,4,1024]{2,1,0:T(4,128)(2,1)} %param.6) | data formatting | bytes 524288 | tf_op args[0]
  17.1 1.1 fusion.87
  18.2 0.2 squeeze.93
  18.4 0.4 copy.64
  18.8 0.2 squeeze.92
  19.1 0.4 copy.62
  19.5 0.2 squeeze.94
  19.7 0.4 copy.66
  21.7 1.0 fusion.85
  22.8 0.2 copy.63
  23.2 0.2 copy.61
  23.4 1.0 copy-done.1
  24.4 1.8 %fusion.67 = f32[4,1024,8,32]{1,3,2,0:T(8,128)S(1)} fusion(bf16[4,288,1024,1]{2,1,3,0:T(8,128)(2,1)S(1)} %bitcast.231, bf16[8,32,288]{2,1,0:T(8,128)(2,1)S(1)} %copy.64), kind=kOutput, calls=%fused_computation.115 | convolution fusion | flops 603979776 | bytes 6701056 | tf_op jit(solution)/shard_map/bjk,zkn->bzjn/dot_general | solution.py:211
  26.2 1.7 %fusion.69 = f32[4,1024,8,32]{1,3,2,0:T(8,128)S(1)} fusion(bf16[4,288,1024,1]{2,1,3,0:T(8,128)(2,1)S(1)} %bitcast.233, bf16[8,32,288]{2,1,0:T(8,128)(2,1)S(1)} %copy.62), kind=kOutput, calls=%fused_computation.117 | convolution fusion | flops 603979776 | bytes 6701056 | tf_op jit(solution)/shard_map/bjk,zkn->bzjn/dot_general | solution.py:211
  28.0 2.7 %add_bitcast_fusion = f32[8,4,32,1024]{3,2,0,1:T(8,128)S(1)} fusion(f32[4,1024,8,32]{1,3,2,0:T(8,128)S(1)} %fusion.69, f32[4,1024,8,32]{1,3,2,0:T(8,128)S(1)} %fusion.67, bf16[4,288,1024,1]{2,1,3,0:T(8,128)(2,1)S(1)} %bitcast.228, bf16[8,32,288]{2,1,0:T(8,128)(2,1)S(1)} %copy.66), kind=kOutput, calls=%fused_computation.1 | convolution fusion | flops 606076928 | bytes 15089664 | tf_op jit(solution)/shard_map/bjk,zkn->bzjn/dot_general | solution.py:211
  30.7 2.3 %copy.67 = f32[8,4,32,1024]{3,2,1,0:T(8,128)} copy(f32[8,4,32,1024]{3,2,0,1:T(8,128)S(1)} %add_bitcast_fusion) | data formatting | bytes 8388608 | tf_op jit(solution)/shard_map/add | solution.py:217
  33.1 0.8 copy-done.6
  33.9 0.3 convert_reduce_fusion
  34.2 37.7 %all-gather.2.cloned.1.call-done = bf16[256,4,1024]{2,0,1:T(8,128)(2,1)} async-done(((bf16[32,4,1024]{2,0,1:T(8,128)(2,1)}), bf16[256,4,1024]{2,0,1:T(8,128)(2,1)}) %all-gather.2.cloned.1.call-update) | async-done | bytes 2097168 | tf_op jit(solution)/shard_map/all_gather | solution.py:146
  71.9 3.3 %fusion.12 = f32[1,288,256]{2,1,0:T(8,128)S(1)} fusion(bf16[4,288,1024]{2,1,0:T(8,128)(2,1)} %bitcast.232, bf16[256,4,1024]{2,0,1:T(8,128)(2,1)} %all-gather.2.cloned.1.call-done), kind=kOutput, calls=%fused_computation.17 | convolution fusion | flops 603979776 | bytes 4751360 | tf_op jit(solution)/shard_map/zkn,zin->ki/dot_general | solution.py:184
  75.3 0.8 fusion.15
  76.1 0.8 copy-done.3
  76.9 1.0 fusion.9
  78.2 1.5 %collective-permute-start.5 = (f32[224,256]{1,0:T(8,128)S(1)}, f32[224,256]{1,0:T(8,128)S(1)}, u32[]{:S(2)}, u32[]{:S(2)}) collective-permute-start(f32[224,256]{1,0:T(8,128)S(1)} %get-tuple-element.39), channel_id=1, source_target_pairs={{0,8},{8,0},{16,24},{24,16},{1,9},{9,1},{17,25},{25,17},{2,10},{10... | collective-permute-start | bytes 688136 | tf_op jit(solution)/shard_map/ppermute | solution.py:104
  79.6 1.5 %collective-permute-start.6 = (f32[224,256]{1,0:T(8,128)S(1)}, f32[224,256]{1,0:T(8,128)S(1)}, u32[]{:S(2)}, u32[]{:S(2)}) collective-permute-start(f32[224,256]{1,0:T(8,128)S(1)} %get-tuple-element.41), channel_id=1, source_target_pairs={{0,16},{8,24},{16,0},{24,8},{1,17},{9,25},{17,1},{25,9},{2,18},{10... | collective-permute-start | bytes 688136 | tf_op jit(solution)/shard_map/ppermute | solution.py:104
  81.1 0.6 collective-permute-start.7
  81.7 0.8 convolution_bitcast_fusion
  82.5 0.8 convolution_bitcast_fusion.1
  83.3 0.8 convolution_bitcast_fusion.2
  84.1 2.3 %pad_add_fusion = f32[6,288,1024]{2,1,0:T(8,128)S(1)} fusion(f32[4,288,1024]{2,1,0:T(8,128)S(1)} %convolution_bitcast_fusion, f32[4,288,1024]{2,1,0:T(8,128)S(1)} %convolution_bitcast_fusion.1, f32[4,288,1024]{2,1,0:T(8,128)S(1)} %convolution_bitcast_fusion.2), kind=kLoop, calls=%fused_computation | loop fusion | flops 3538944 | bytes 21233664 | tf_op jit(solution)/shard_map/add | solution.py:159
  86.4 1.1 slice_bitcast_fusion
  87.5 1.7 %fusion.28 = f32[6,32,1024]{2,1,0:T(8,128)S(1)} fusion(f32[6,32,1024]{2,1,0:T(8,128)S(1)} %get-tuple-element.31, f32[6,32,1024]{2,1,0:T(8,128)S(1)} %get-tuple-element.30, f32[6,32,1024]{2,1,0:T(8,128)S(1)} %get-tuple-element.29, f32[6,32,1024]{2,1,0:T(8,128)S(1)} %get-tuple-element.28, f32[6,32,1024]{2,1,0:T(8,128)S(1)} %get-tuple-element.27, ...), kind=kLoop, calls=%fused_computation.44 | loop fusion | flops 3342336 | bytes 7867392 | tf_op jit(solution)/shard_map/add | solution.py:164
  89.2 3.3 %collective-permute-start = (f32[1,32,1024]{2,1,0:T(8,128)S(1)}, f32[1,32,1024]{2,1,0:T(8,128)S(1)}, u32[]{:S(2)}, u32[]{:S(2)}) collective-permute-start(f32[1,32,1024]{2,1,0:T(8,128)S(1)} %get-tuple-element.42), channel_id=1, source_target_pairs={{0,8},{8,16},{16,24},{1,9},{9,17},{17,25},{2,10},{10,18},{18,26},{... | collective-permute-start | bytes 393224 | tf_op jit(solution)/shard_map/ppermute | solution.py:168
  92.6 1.3 %collective-permute-start.1 = (f32[1,32,1024]{2,1,0:T(8,128)S(1)}, f32[1,32,1024]{2,1,0:T(8,128)S(1)}, u32[]{:S(2)}, u32[]{:S(2)}) collective-permute-start(f32[1,32,1024]{2,1,0:T(8,128)S(1)} %get-tuple-element.43), channel_id=1, source_target_pairs={{8,0},{16,8},{24,16},{9,1},{17,9},{25,17},{10,2},{18,10},{26,18},{... | collective-permute-start | bytes 393224 | tf_op jit(solution)/shard_map/ppermute | solution.py:169
  94.0 2.7 %collective-permute-start.8 = (f32[224,256]{1,0:T(8,128)S(1)}, f32[224,256]{1,0:T(8,128)S(1)}, u32[]{:S(2)}, u32[]{:S(2)}) collective-permute-start(f32[224,256]{1,0:T(8,128)S(1)} %fusion.65), channel_id=1, source_target_pairs={{0,8},{8,0},{16,24},{24,16},{1,9},{9,1},{17,25},{25,17},{2,10},{10... | collective-permute-start | bytes 688136 | tf_op jit(solution)/shard_map/ppermute | solution.py:106
  96.7 1.5 %collective-permute-start.9 = (f32[224,256]{1,0:T(8,128)S(1)}, f32[224,256]{1,0:T(8,128)S(1)}, u32[]{:S(2)}, u32[]{:S(2)}) collective-permute-start(f32[224,256]{1,0:T(8,128)S(1)} %fusion.65), channel_id=1, source_target_pairs={{0,16},{8,24},{16,0},{24,8},{1,17},{9,25},{17,1},{25,9},{2,18},{10... | collective-permute-start | bytes 688136 | tf_op jit(solution)/shard_map/ppermute | solution.py:106
  98.2 0.9 collective-permute-start.10
  99.1 1.8 %collective-permute-done.1 = f32[1,32,1024]{2,1,0:T(8,128)S(1)} collective-permute-done((f32[1,32,1024]{2,1,0:T(8,128)S(1)}, f32[1,32,1024]{2,1,0:T(8,128)S(1)}, u32[]{:S(2)}, u32[]{:S(2)}) %collective-permute-start.1) | collective-permute-done | bytes 131104 | tf_op jit(solution)/shard_map/ppermute | solution.py:169
  101.0 0.9 copy.68
  102.0 13.4 %reduce-scatter.2.cloned.1.call-done = f32[256,1024]{1,0:T(8,128)} async-done(((f32[1024,1024]{1,0:T(8,128)}), f32[256,1024]{1,0:T(8,128)}) %reduce-scatter.2.cloned.1.call-update) | async-done | bytes 1048592 | tf_op jit(solution)/shard_map/reduce_scatter | solution.py:117
  115.3 1.2 dynamic-slice_bitcast_fusion
  116.8 1.0 pad_maximum_fusion.1
  117.7 0.5 slice_bitcast_fusion.9
  118.2 0.2 collective-permute-done.4
  118.5 0.9 copy.69
  (53 shorter events, 2.7 us)
Async XLA Ops:
  8.0 63.9 %all-gather.2.cloned.1.call-start = ((), (), s32[]{:S(2)}) async-start(), calls=%async_computation.1 | async-start | bytes 2359296 | tf_op jit(solution)/shard_map/all_gather | solution.py:146
  9.1 11.0 %collective-permute-start.2 = (bf16[1,32,1024]{2,1,0:T(8,128)(2,1)S(1)}, bf16[1,32,1024]{2,1,0:T(8,128)(2,1)S(1)}, u32[]{:S(2)}, u32[]{:S(2)}) collective-permute-start(bf16[1,32,1024]{2,1,0:T(8,128)(2,1)S(1)} %get-tuple-element.52), channel_id=1, source_target_pairs={{0,8},{8,16},{16,24},{1,9},{9,17},{17,25},{2,10},{10,18},{18,26},{... | collective-permute-start | bytes 196616 | tf_op jit(solution)/shard_map/ppermute | solution.py:28
  14.0 6.2 %collective-permute-start.3 = (bf16[1,32,1024]{2,1,0:T(8,128)(2,1)S(1)}, bf16[1,32,1024]{2,1,0:T(8,128)(2,1)S(1)}, u32[]{:S(2)}, u32[]{:S(2)}) collective-permute-start(bf16[1,32,1024]{2,1,0:T(8,128)(2,1)S(1)} %get-tuple-element.53), channel_id=1, source_target_pairs={{8,0},{16,8},{24,16},{9,1},{17,9},{25,17},{10,2},{18,10},{26,18},{... | collective-permute-start | bytes 196616 | tf_op jit(solution)/shard_map/ppermute | solution.py:29
  17.0 98.3 %reduce-scatter.2.cloned.1.call-start = ((), (), s32[]{:S(2)}) async-start(), calls=%async_computation.2 | async-start | bytes 5242880 | tf_op jit(solution)/shard_map/reduce_scatter | solution.py:117
  23.0 1.4 %copy-start.1 = (bf16[4,9,32,1024]{3,2,1,0:T(8,128)(2,1)}, bf16[4,9,32,1024]{3,2,1,0:T(8,128)(2,1)S(1)}, u32[]{:S(2)}) copy-start(bf16[4,9,32,1024]{3,2,1,0:T(8,128)(2,1)S(1)} %copy.63) | copy-start | bytes 7077892
  23.4 2.8 %copy-start.2 = (bf16[4,9,32,1024]{3,2,1,0:T(8,128)(2,1)}, bf16[4,9,32,1024]{3,2,1,0:T(8,128)(2,1)S(1)}, u32[]{:S(2)}) copy-start(bf16[4,9,32,1024]{3,2,1,0:T(8,128)(2,1)S(1)} %copy.61) | copy-start | bytes 7077892
  32.9 1.0 copy-start.6
  32.9 1.3 %copy-start.4 = (bf16[27,256,32]{1,2,0:T(8,128)(2,1)S(1)}, bf16[27,256,32]{1,2,0:T(8,128)(2,1)}, u32[]{:S(2)}) copy-start(bf16[27,256,32]{1,2,0:T(8,128)(2,1)} %param.7) | copy-start | bytes 1327108
  71.9 3.4 %copy-start = (bf16[256,4,1024]{2,0,1:T(8,128)(2,1)S(1)}, bf16[256,4,1024]{2,0,1:T(8,128)(2,1)}, u32[]{:S(2)}) copy-start(bf16[256,4,1024]{2,0,1:T(8,128)(2,1)} %all-gather.2.cloned.1.call-done) | copy-start | bytes 6291460
  75.3 1.7 %copy-start.3 = (bf16[4,9,32,1024]{3,2,1,0:T(8,128)(2,1)S(1)}, bf16[4,9,32,1024]{3,2,1,0:T(8,128)(2,1)}, u32[]{:S(2)}) copy-start(bf16[4,9,32,1024]{3,2,1,0:T(8,128)(2,1)} %copy-done.2) | copy-start | bytes 7077892
  78.2 15.7 %collective-permute-start.5 = (f32[224,256]{1,0:T(8,128)S(1)}, f32[224,256]{1,0:T(8,128)S(1)}, u32[]{:S(2)}, u32[]{:S(2)}) collective-permute-start(f32[224,256]{1,0:T(8,128)S(1)} %get-tuple-element.39), channel_id=1, source_target_pairs={{0,8},{8,0},{16,24},{24,16},{1,9},{9,1},{17,25},{25,17},{2,10},{10... | collective-permute-start | bytes 688136 | tf_op jit(solution)/shard_map/ppermute | solution.py:104
  79.6 14.2 %collective-permute-start.6 = (f32[224,256]{1,0:T(8,128)S(1)}, f32[224,256]{1,0:T(8,128)S(1)}, u32[]{:S(2)}, u32[]{:S(2)}) collective-permute-start(f32[224,256]{1,0:T(8,128)S(1)} %get-tuple-element.41), channel_id=1, source_target_pairs={{0,16},{8,24},{16,0},{24,8},{1,17},{9,25},{17,1},{25,9},{2,18},{10... | collective-permute-start | bytes 688136 | tf_op jit(solution)/shard_map/ppermute | solution.py:104
  81.1 12.8 %collective-permute-start.7 = (f32[224,256]{1,0:T(8,128)S(1)}, f32[224,256]{1,0:T(8,128)S(1)}, u32[]{:S(2)}, u32[]{:S(2)}) collective-permute-start(f32[224,256]{1,0:T(8,128)S(1)} %get-tuple-element.40), channel_id=1, source_target_pairs={{0,24},{8,16},{16,8},{24,0},{1,25},{9,17},{17,9},{25,1},{2,26},{10... | collective-permute-start | bytes 688136 | tf_op jit(solution)/shard_map/ppermute | solution.py:104
  87.5 13.4 %copy-start.7 = (f32[32]{0:T(128)S(1)}, f32[32]{0:T(128)}, u32[]{:S(2)}) copy-start(f32[32]{0:T(128)} %param.8) | copy-start | bytes 388
  89.2 9.8 %collective-permute-start = (f32[1,32,1024]{2,1,0:T(8,128)S(1)}, f32[1,32,1024]{2,1,0:T(8,128)S(1)}, u32[]{:S(2)}, u32[]{:S(2)}) collective-permute-start(f32[1,32,1024]{2,1,0:T(8,128)S(1)} %get-tuple-element.42), channel_id=1, source_target_pairs={{0,8},{8,16},{16,24},{1,9},{9,17},{17,25},{2,10},{10,18},{18,26},{... | collective-permute-start | bytes 393224 | tf_op jit(solution)/shard_map/ppermute | solution.py:168
  92.6 8.3 %collective-permute-start.1 = (f32[1,32,1024]{2,1,0:T(8,128)S(1)}, f32[1,32,1024]{2,1,0:T(8,128)S(1)}, u32[]{:S(2)}, u32[]{:S(2)}) collective-permute-start(f32[1,32,1024]{2,1,0:T(8,128)S(1)} %get-tuple-element.43), channel_id=1, source_target_pairs={{8,0},{16,8},{24,16},{9,1},{17,9},{25,17},{10,2},{18,10},{26,18},{... | collective-permute-start | bytes 393224 | tf_op jit(solution)/shard_map/ppermute | solution.py:169
  94.0 22.6 %collective-permute-start.8 = (f32[224,256]{1,0:T(8,128)S(1)}, f32[224,256]{1,0:T(8,128)S(1)}, u32[]{:S(2)}, u32[]{:S(2)}) collective-permute-start(f32[224,256]{1,0:T(8,128)S(1)} %fusion.65), channel_id=1, source_target_pairs={{0,8},{8,0},{16,24},{24,16},{1,9},{9,1},{17,25},{25,17},{2,10},{10... | collective-permute-start | bytes 688136 | tf_op jit(solution)/shard_map/ppermute | solution.py:106
  96.7 19.9 %collective-permute-start.9 = (f32[224,256]{1,0:T(8,128)S(1)}, f32[224,256]{1,0:T(8,128)S(1)}, u32[]{:S(2)}, u32[]{:S(2)}) collective-permute-start(f32[224,256]{1,0:T(8,128)S(1)} %fusion.65), channel_id=1, source_target_pairs={{0,16},{8,24},{16,0},{24,8},{1,17},{9,25},{17,1},{25,9},{2,18},{10... | collective-permute-start | bytes 688136 | tf_op jit(solution)/shard_map/ppermute | solution.py:106
  98.2 18.4 %collective-permute-start.10 = (f32[224,256]{1,0:T(8,128)S(1)}, f32[224,256]{1,0:T(8,128)S(1)}, u32[]{:S(2)}, u32[]{:S(2)}) collective-permute-start(f32[224,256]{1,0:T(8,128)S(1)} %fusion.65), channel_id=1, source_target_pairs={{0,24},{8,16},{16,8},{24,0},{1,25},{9,17},{17,9},{25,1},{2,26},{10... | collective-permute-start | bytes 688136 | tf_op jit(solution)/shard_map/ppermute | solution.py:106
  115.3 3.1 %copy-start.5 = (f32[256,1024]{1,0:T(8,128)S(1)}, f32[256,1024]{1,0:T(8,128)}, u32[]{:S(2)}) copy-start(f32[256,1024]{1,0:T(8,128)} %reduce-scatter.2.cloned.1.call-done) | copy-start | bytes 3145732
  116.5 2.0 %collective-permute-start.4 = (f32[4,32,1024]{2,1,0:T(8,128)S(1)}, f32[4,32,1024]{2,1,0:T(8,128)S(1)}, u32[]{:S(2)}, u32[]{:S(2)}) collective-permute-start(f32[4,32,1024]{2,1,0:T(8,128)S(1)} %dynamic-slice_bitcast_fusion), channel_id=1, source_target_pairs={{0,1},{1,0},{2,3},{3,2},{4,5},{5,4},{6,7},{7,6},{8,9},{9,8},{10,11... | collective-permute-start | bytes 1572872 | tf_op jit(solution)/shard_map/ppermute | solution.py:123
Sparse Core Ops, SparseCore 0:
  17.1 54.7 all-gather.1
Sparse Core Ops, SparseCore 1:
  33.0 82.2 reduce-scatter.1

commit v16 on v11

--- a/solution.py
+++ b/solution.py
@@ -131,10 +131,8 @@
     depth_cells = inputs.shape[1]
     plane_cells = inputs.shape[2]
     grad_scale = 1.0 / math.sqrt(lax.axis_size("space") * depth_cells * plane_cells)
-    inputs_planes = jnp.transpose(inputs, (1, 0, 2))
-    inputs_planes, output_grad = lax.optimization_barrier((inputs_planes, output_grad))
     grad_planes = jnp.transpose(output_grad, (1, 0, 2))
-    gathered = lax.all_gather(inputs_planes, ("chips", "core"), axis=1, tiled=True)
+    gathered = jnp.transpose(lax.all_gather(inputs, ("chips", "core"), axis=0, tiled=True), (1, 0, 2))
 
     weight_grid = weight.reshape(3, 9, channels_in, block_out)
     forward_weight = jnp.transpose(weight_grid, (0, 1, 3, 2)).reshape(3, 9 * block_out, channels_in)

time: 112 us -> 111 us (level)
    unnamed x31 -> x34, local copies, waits for them, and re-layouts: 15.2 us -> 16.4 us
  transfers between devices with their start and end apart: 13 -> 13, of which waited for: 4 -> 4; matrix products, arithmetic and copies ran while one was open for 47% -> 48% of each run, Pallas kernels for 0% -> 0%
where the time goes in v16:
time: 111 us
  local copies, waits for them, and re-layouts  31.7 us (29%)
  starting transfers between devices  21.6 us (19%)
  matrix products  17.3 us (16%)
  between operations  16 us (14%)
  waiting for transfers between devices  14.8 us (13%)
  other arithmetic  9.19 us (8%)
    unnamed x34, local copies, waits for them, and re-layouts  16.4 us
    dot_general x6, matrix products, partial_sums(): jnp.einsum('cjk,zkn->czjn', core_weight[depth_index], grad_shifted[2 - de...  10.8 us
    ppermute x3, waiting for transfers between devices, all_reduce_direct(): lax.ppermute(reduced, axis, [(i, i ^ distance) for i in range(devices)])  7.51 us
    ppermute x3, starting transfers between devices, all_reduce_direct(): lax.ppermute(reduced, axis, [(i, i ^ distance) for i in range(devices)])  5.96 us
    reduce_scatter x1, waiting for transfers between devices, body(): lax.psum_scatter(spread.reshape(-1, plane_cells), 'chips', scatter_dimens...  5.47 us
    ppermute x3, starting transfers between devices, all_reduce_direct(): reduced = reduced + lax.ppermute(send, axis, pairs)  5.11 us
    ppermute x1, starting transfers between devices, padded_2(): before = lax.ppermute(last, axis, up)  4.85 us
    slice x1, local copies, waits for them, and re-layouts, partial_sums(): core_weight[depth_index]  4.62 us
  transfers between devices with their start and end apart: 13, of which 4 were waited for; matrix products, arithmetic and copies ran while one was open for 48% of the time, Pallas kernels for 0%

profile of v16, /device:TPU:0, one launch (start us, length us, event | category | flops | bytes accessed | tf_op | source)
XLA Modules:
  0.0 110.6 jit_solution(16154615487509877276)
XLA Ops:
  8.0 1.0 copy.67
  9.1 4.8 %collective-permute-start.2 = (bf16[1,32,1024]{2,1,0:T(8,128)(2,1)S(1)}, bf16[1,32,1024]{2,1,0:T(8,128)(2,1)S(1)}, u32[]{:S(2)}, u32[]{:S(2)}) collective-permute-start(bf16[1,32,1024]{2,1,0:T(8,128)(2,1)S(1)} %get-tuple-element.51), channel_id=1, source_target_pairs={{0,8},{8,16},{16,24},{1,9},{9,17},{17,25},{2,10},{10,18},{18,26},{... | collective-permute-start | bytes 196616 | tf_op jit(solution)/shard_map/ppermute | solution.py:28
  14.0 1.3 %collective-permute-start.3 = (bf16[1,32,1024]{2,1,0:T(8,128)(2,1)S(1)}, bf16[1,32,1024]{2,1,0:T(8,128)(2,1)S(1)}, u32[]{:S(2)}, u32[]{:S(2)}) collective-permute-start(bf16[1,32,1024]{2,1,0:T(8,128)(2,1)S(1)} %get-tuple-element.52), channel_id=1, source_target_pairs={{8,0},{16,8},{24,16},{9,1},{17,9},{25,17},{10,2},{18,10},{26,18},{... | collective-permute-start | bytes 196616 | tf_op jit(solution)/shard_map/ppermute | solution.py:29
  15.3 1.7 %copy.24 = bf16[32,4,1024]{2,0,1:T(8,128)(2,1)} copy(bf16[32,4,1024]{2,1,0:T(4,128)(2,1)} %param.6) | data formatting | bytes 524288 | tf_op args[0]
  17.1 4.4 %reshape.130 = bf16[3,4,2,32,288]{3,2,1,4,0:T(2,128)(2,1)S(1)} reshape(bf16[3,256,9,32]{1,3,2,0:T(8,128)(2,1)} %bitcast.262) | data formatting | bytes 884736 | tf_op jit(solution)/shard_map/reshape | solution.py:195
  21.5 4.6 %constant_dynamic-slice_fusion.4 = (bf16[1,4,1,32,288]{3,2,1,4,0:T(2,128)(2,1)S(1)}, bf16[1,4,1,32,288]{3,2,1,4,0:T(2,128)(2,1)}, bf16[1,4,1,32,288]{3,2,1,4,0:T...) fusion(bf16[3,4,2,32,288]{3,2,1,4,0:T(2,128)(2,1)S(1)} %reshape, ...), kind=kLoop, calls=%fused_computation.143 | loop fusion | bytes 884752 | tf_op jit(solution)/shard_map/slice | solution.py:204
  26.1 1.9 %copy.59 = bf16[1,4,1,32,288]{4,3,1,2,0:T(8,128)(2,1)} copy(bf16[1,4,1,32,288]{3,2,1,4,0:T(2,128)(2,1)} %get-tuple-element.34) | data formatting | bytes 147456
  28.0 1.9 %copy.58 = bf16[1,4,1,32,288]{4,3,1,2,0:T(8,128)(2,1)} copy(bf16[1,4,1,32,288]{3,2,1,4,0:T(2,128)(2,1)} %get-tuple-element.35) | data formatting | bytes 147456
  29.9 1.9 %copy.60 = bf16[1,4,1,32,288]{4,3,1,2,0:T(8,128)(2,1)} copy(bf16[1,4,1,32,288]{3,2,1,4,0:T(2,128)(2,1)} %get-tuple-element.36) | data formatting | bytes 147456
  33.3 1.0 fusion.88
  35.8 1.0 fusion.70
  36.9 1.0 fusion.72
  37.9 2.6 %add_bitcast_fusion = f32[4,4,32,1024]{3,2,0,1:T(8,128)} fusion(f32[4,1024,4,32]{1,3,2,0:T(8,128)S(1)} %fusion.72, f32[4,1024,4,32]{1,3,2,0:T(8,128)S(1)} %fusion.70, bf16[4,288,1024,1]{2,1,3,0:T(8,128)(2,1)S(1)} %bitcast.247, bf16[1,4,1,32,288]{4,3,1,2,0:T(8,128)(2,1)S(1)} %copy-done.7), kind=kOutput, calls=%fused_computation.16 | convolution fusion | flops 303038464 | bytes 8724480 | tf_op jit(solution)/shard_map/cjk,zkn->czjn/dot_general | solution.py:202
  40.5 1.9 %copy.63 = bf16[1,4,1,32,288]{4,3,1,2,0:T(8,128)(2,1)} copy(bf16[1,4,1,32,288]{3,2,1,4,0:T(2,128)(2,1)} %get-tuple-element.32) | data formatting | bytes 147456
  42.4 1.1 %copy.62 = bf16[1,4,1,32,288]{4,3,1,2,0:T(8,128)(2,1)} copy(bf16[1,4,1,32,288]{3,2,1,4,0:T(2,128)(2,1)S(1)} %get-tuple-element.33) | data formatting | bytes 147456
  43.5 0.7 copy.64
  44.3 1.3 %convert_reduce_fusion = f32[32]{0:T(128)S(1)} fusion(bf16[32,4,1024]{2,1,0:T(4,128)(2,1)} %param.9), kind=kLoop, calls=%fused_computation.71 | loop fusion | flops 262112 | bytes 262272 | tf_op jit(solution)/shard_map/reduce_sum | solution.py:182
  45.6 1.1 fusion.90
  46.7 2.1 %fusion.65 = f32[4,1024,4,32]{1,3,2,0:T(8,128)S(1)} fusion(bf16[4,288,1024,1]{2,1,3,0:T(8,128)(2,1)S(1)} %bitcast.245, bf16[1,4,1,32,288]{4,3,1,2,0:T(8,128)(2,1)} %copy.63), kind=kOutput, calls=%fused_computation.114 | convolution fusion | flops 301989888 | bytes 4530176 | tf_op jit(solution)/shard_map/cjk,zkn->czjn/dot_general | solution.py:202
  48.8 1.0 fusion.67
  50.5 3.1 %bitcast_add_fusion = f32[4,4,32,1024]{3,2,0,1:T(8,128)S(1)} fusion(f32[4,1024,4,32]{1,3,2,0:T(8,128)S(1)} %fusion.65, f32[4,4,32,1024]{3,2,0,1:T(8,128)} %collective-permute-done.4, f32[4,1024,4,32]{1,3,2,0:T(8,128)S(1)} %fusion.67, bf16[4,288,1024,1]{2,1,3,0:T(8,128)(2,1)S(1)} %bitcast.248, bf16[1,4,1,32,288]{4,3,1,2,0:T(8,128)(2,1)S(1)} %copy.64), kind=kOutput, calls=%fused_computation.4 | convolution fusion | flops 303562752 | bytes 10821632 | tf_op jit(solution)/shard_map/cjk,zkn->czjn/dot_general | solution.py:202
  53.5 1.5 %copy.42 = f32[4,4,32,1024]{3,2,1,0:T(8,128)} copy(f32[4,4,32,1024]{3,2,0,1:T(8,128)S(1)} %bitcast_add_fusion) | data formatting | bytes 4194304 | tf_op jit(solution)/shard_map/add | solution.py:208
  55.1 2.5 %fusion.12 = f32[1,288,256]{2,1,0:T(8,128)S(1)} fusion(bf16[4,288,1024]{2,1,0:T(8,128)(2,1)S(1)} %bitcast.246, bf16[256,4,1024]{2,0,1:T(8,128)(2,1)} %all-gather.2.cloned.1.call-done), kind=kOutput, calls=%fused_computation.20 | convolution fusion | flops 603979776 | bytes 4751360 | tf_op jit(solution)/shard_map/zkn,zin->ki/dot_general | solution.py:173
  58.1 0.8 fusion.15
  58.9 0.8 copy-done.5
  59.7 0.8 fusion.9
  60.7 2.8 %collective-permute-start.5 = (f32[224,256]{1,0:T(8,128)S(1)}, f32[224,256]{1,0:T(8,128)S(1)}, u32[]{:S(2)}, u32[]{:S(2)}) collective-permute-start(f32[224,256]{1,0:T(8,128)S(1)} %get-tuple-element.41), channel_id=1, source_target_pairs={{0,8},{8,0},{16,24},{24,16},{1,9},{9,1},{17,25},{25,17},{2,10},{10... | collective-permute-start | bytes 688136 | tf_op jit(solution)/shard_map/ppermute | solution.py:104
  63.5 1.5 %collective-permute-start.6 = (f32[224,256]{1,0:T(8,128)S(1)}, f32[224,256]{1,0:T(8,128)S(1)}, u32[]{:S(2)}, u32[]{:S(2)}) collective-permute-start(f32[224,256]{1,0:T(8,128)S(1)} %get-tuple-element.43), channel_id=1, source_target_pairs={{0,16},{8,24},{16,0},{24,8},{1,17},{9,25},{17,1},{25,9},{2,18},{10... | collective-permute-start | bytes 688136 | tf_op jit(solution)/shard_map/ppermute | solution.py:104
  65.0 0.8 collective-permute-start.7
  65.8 0.8 convolution_bitcast_fusion
  66.6 0.8 convolution_bitcast_fusion.1
  67.4 0.8 convolution_bitcast_fusion.2
  68.2 2.3 %pad_add_fusion = f32[6,288,1024]{2,1,0:T(8,128)S(1)} fusion(f32[4,288,1024]{2,1,0:T(8,128)S(1)} %convolution_bitcast_fusion, f32[4,288,1024]{2,1,0:T(8,128)S(1)} %convolution_bitcast_fusion.1, f32[4,288,1024]{2,1,0:T(8,128)S(1)} %convolution_bitcast_fusion.2), kind=kLoop, calls=%fused_computation | loop fusion | flops 3538944 | bytes 21233664 | tf_op jit(solution)/shard_map/add | solution.py:148
  70.5 1.1 %slice_bitcast_fusion = (f32[6,32,1024]{2,1,0:T(8,128)S(1)}, f32[6,32,1024]{2,1,0:T(8,128)S(1)}, f32[6,32,1024]{2,1,0:T(8,128)S(1)}, f32[6,32,1024]{2,1,0:T(8,12...) fusion(f32[6,9,32,1024]{3,2,1,0:T(8,128)S(1)} %bitcast.253), kind=kLoop, calls=%fused_computation.55 | loop fusion | bytes 12582912 | tf_op jit(solution)/shard_map/squeeze | solution.py:152
  71.7 1.7 %fusion.28 = f32[6,32,1024]{2,1,0:T(8,128)S(1)} fusion(f32[6,32,1024]{2,1,0:T(8,128)S(1)} %get-tuple-element.27, f32[6,32,1024]{2,1,0:T(8,128)S(1)} %get-tuple-element.26, f32[6,32,1024]{2,1,0:T(8,128)S(1)} %get-tuple-element.25, f32[6,32,1024]{2,1,0:T(8,128)S(1)} %get-tuple-element.24, f32[6,32,1024]{2,1,0:T(8,128)S(1)} %get-tuple-element.23, ...), kind=kLoop, calls=%fused_computation.47 | loop fusion | flops 3342336 | bytes 7867392 | tf_op jit(solution)/shard_map/add | solution.py:153
  73.4 3.0 %collective-permute-start = (f32[1,32,1024]{2,1,0:T(8,128)S(1)}, f32[1,32,1024]{2,1,0:T(8,128)S(1)}, u32[]{:S(2)}, u32[]{:S(2)}) collective-permute-start(f32[1,32,1024]{2,1,0:T(8,128)S(1)} %get-tuple-element.44), channel_id=1, source_target_pairs={{0,8},{8,16},{16,24},{1,9},{9,17},{17,25},{2,10},{10,18},{18,26},{... | collective-permute-start | bytes 393224 | tf_op jit(solution)/shard_map/ppermute | solution.py:157
  76.4 1.3 %collective-permute-start.1 = (f32[1,32,1024]{2,1,0:T(8,128)S(1)}, f32[1,32,1024]{2,1,0:T(8,128)S(1)}, u32[]{:S(2)}, u32[]{:S(2)}) collective-permute-start(f32[1,32,1024]{2,1,0:T(8,128)S(1)} %get-tuple-element.45), channel_id=1, source_target_pairs={{8,0},{16,8},{24,16},{9,1},{17,9},{25,17},{10,2},{18,10},{26,18},{... | collective-permute-start | bytes 393224 | tf_op jit(solution)/shard_map/ppermute | solution.py:158
  77.8 3.0 %collective-permute-start.8 = (f32[224,256]{1,0:T(8,128)S(1)}, f32[224,256]{1,0:T(8,128)S(1)}, u32[]{:S(2)}, u32[]{:S(2)}) collective-permute-start(f32[224,256]{1,0:T(8,128)S(1)} %fusion.63), channel_id=1, source_target_pairs={{0,8},{8,0},{16,24},{24,16},{1,9},{9,1},{17,25},{25,17},{2,10},{10... | collective-permute-start | bytes 688136 | tf_op jit(solution)/shard_map/ppermute | solution.py:106
  80.9 1.5 %collective-permute-start.9 = (f32[224,256]{1,0:T(8,128)S(1)}, f32[224,256]{1,0:T(8,128)S(1)}, u32[]{:S(2)}, u32[]{:S(2)}) collective-permute-start(f32[224,256]{1,0:T(8,128)S(1)} %fusion.63), channel_id=1, source_target_pairs={{0,16},{8,24},{16,0},{24,8},{1,17},{9,25},{17,1},{25,9},{2,18},{10... | collective-permute-start | bytes 688136 | tf_op jit(solution)/shard_map/ppermute | solution.py:106
  82.4 1.4 %collective-permute-start.10 = (f32[224,256]{1,0:T(8,128)S(1)}, f32[224,256]{1,0:T(8,128)S(1)}, u32[]{:S(2)}, u32[]{:S(2)}) collective-permute-start(f32[224,256]{1,0:T(8,128)S(1)} %fusion.63), channel_id=1, source_target_pairs={{0,24},{8,16},{16,8},{24,0},{1,25},{9,17},{17,9},{25,1},{2,26},{10... | collective-permute-start | bytes 688136 | tf_op jit(solution)/shard_map/ppermute | solution.py:106
  83.8 1.7 %collective-permute-done.1 = f32[1,32,1024]{2,1,0:T(8,128)S(1)} collective-permute-done((f32[1,32,1024]{2,1,0:T(8,128)S(1)}, f32[1,32,1024]{2,1,0:T(8,128)S(1)}, u32[]{:S(2)}, u32[]{:S(2)}) %collective-permute-start.1) | collective-permute-done | bytes 131104 | tf_op jit(solution)/shard_map/ppermute | solution.py:158
  85.7 0.9 copy.43
  86.6 3.9 %collective-permute-done.8 = f32[224,256]{1,0:T(8,128)S(1)} collective-permute-done((f32[224,256]{1,0:T(8,128)S(1)}, f32[224,256]{1,0:T(8,128)S(1)}, u32[]{:S(2)}, u32[]{:S(2)}) %collective-permute-start.8) | collective-permute-done | bytes 229408 | tf_op jit(solution)/shard_map/ppermute | solution.py:106
  90.4 3.6 %collective-permute-done.10 = f32[224,256]{1,0:T(8,128)S(1)} collective-permute-done((f32[224,256]{1,0:T(8,128)S(1)}, f32[224,256]{1,0:T(8,128)S(1)}, u32[]{:S(2)}, u32[]{:S(2)}) %collective-permute-start.10) | collective-permute-done | bytes 229408 | tf_op jit(solution)/shard_map/ppermute | solution.py:106
  94.2 1.0 pad_maximum_fusion.1
  95.7 5.5 %reduce-scatter.2.cloned.1.call-done = f32[128,1024]{1,0:T(8,128)} async-done(((f32[512,1024]{1,0:T(8,128)}), f32[128,1024]{1,0:T(8,128)}) %reduce-scatter.2.cloned.1.call-update) | async-done | bytes 524304 | tf_op jit(solution)/shard_map/reduce_scatter | solution.py:214
  101.2 1.1 convert_element_type.39
  102.3 0.9 copy.44
  (64 shorter events, 5.2 us)
Async XLA Ops:
  8.0 47.1 %all-gather.2.cloned.1.call-start = ((), (), s32[]{:S(2)}) async-start(), calls=%async_computation.1 | async-start | bytes 2359296 | tf_op jit(solution)/shard_map/all_gather | solution.py:135
  9.1 22.6 %collective-permute-start.2 = (bf16[1,32,1024]{2,1,0:T(8,128)(2,1)S(1)}, bf16[1,32,1024]{2,1,0:T(8,128)(2,1)S(1)}, u32[]{:S(2)}, u32[]{:S(2)}) collective-permute-start(bf16[1,32,1024]{2,1,0:T(8,128)(2,1)S(1)} %get-tuple-element.51), channel_id=1, source_target_pairs={{0,8},{8,16},{16,24},{1,9},{9,17},{17,25},{2,10},{10,18},{18,26},{... | collective-permute-start | bytes 196616 | tf_op jit(solution)/shard_map/ppermute | solution.py:28
  14.0 17.8 %collective-permute-start.3 = (bf16[1,32,1024]{2,1,0:T(8,128)(2,1)S(1)}, bf16[1,32,1024]{2,1,0:T(8,128)(2,1)S(1)}, u32[]{:S(2)}, u32[]{:S(2)}) collective-permute-start(bf16[1,32,1024]{2,1,0:T(8,128)(2,1)S(1)} %get-tuple-element.52), channel_id=1, source_target_pairs={{8,0},{16,8},{24,16},{9,1},{17,9},{25,17},{10,2},{18,10},{26,18},{... | collective-permute-start | bytes 196616 | tf_op jit(solution)/shard_map/ppermute | solution.py:29
  17.0 84.2 %reduce-scatter.2.cloned.1.call-start = ((), (), s32[]{:S(2)}) async-start(), calls=%async_computation.2 | async-start | bytes 2621440 | tf_op jit(solution)/shard_map/reduce_scatter | solution.py:214
  34.8 3.1 %copy-start = (bf16[4,9,32,1024]{3,2,1,0:T(8,128)(2,1)}, bf16[4,9,32,1024]{3,2,1,0:T(8,128)(2,1)S(1)}, u32[]{:S(2)}) copy-start(bf16[4,9,32,1024]{3,2,1,0:T(8,128)(2,1)S(1)} %copy.40) | copy-start | bytes 7077892
  34.8 1.0 copy-start.8
  35.2 1.7 %copy-start.3 = (bf16[4,9,32,1024]{3,2,1,0:T(8,128)(2,1)}, bf16[4,9,32,1024]{3,2,1,0:T(8,128)(2,1)S(1)}, u32[]{:S(2)}) copy-start(bf16[4,9,32,1024]{3,2,1,0:T(8,128)(2,1)S(1)} %copy.37) | copy-start | bytes 7077892
  35.8 1.0 copy-start.9
  36.9 1.0 copy-start.7
  40.5 9.3 %collective-permute-start.4 = (f32[4,4,32,1024]{3,2,0,1:T(8,128)}, f32[4,4,32,1024]{3,2,0,1:T(8,128)}, u32[]{:S(2)}, u32[]{:S(2)}) collective-permute-start(f32[4,4,32,1024]{3,2,0,1:T(8,128)} %add_bitcast_fusion), channel_id=1, source_target_pairs={{0,1},{1,0},{2,3},{3,2},{4,5},{5,4},{6,7},{7,6},{8,9},{9,8},{10,11... | collective-permute-start | bytes 6291464 | tf_op jit(solution)/shard_map/ppermute | solution.py:212
  46.7 2.1 %copy-start.4 = (bf16[4,9,32,1024]{3,2,1,0:T(8,128)(2,1)S(1)}, bf16[4,9,32,1024]{3,2,1,0:T(8,128)(2,1)}, u32[]{:S(2)}) copy-start(bf16[4,9,32,1024]{3,2,1,0:T(8,128)(2,1)} %copy-done.3) | copy-start | bytes 7077892
  46.7 2.1 %copy-start.10 = (bf16[1,4,1,32,288]{4,3,1,2,0:T(8,128)(2,1)S(1)}, bf16[1,4,1,32,288]{4,3,1,2,0:T(8,128)(2,1)}, u32[]{:S(2)}) copy-start(bf16[1,4,1,32,288]{4,3,1,2,0:T(8,128)(2,1)} %copy.62) | copy-start | bytes 221188
  48.8 1.7 %copy-start.1 = (bf16[4,9,32,1024]{3,2,1,0:T(8,128)(2,1)S(1)}, bf16[4,9,32,1024]{3,2,1,0:T(8,128)(2,1)}, u32[]{:S(2)}) copy-start(bf16[4,9,32,1024]{3,2,1,0:T(8,128)(2,1)} %copy-done) | copy-start | bytes 7077892
  55.1 2.6 %copy-start.2 = (bf16[4,9,32,1024]{3,2,1,0:T(8,128)(2,1)S(1)}, bf16[4,9,32,1024]{3,2,1,0:T(8,128)(2,1)}, u32[]{:S(2)}) copy-start(bf16[4,9,32,1024]{3,2,1,0:T(8,128)(2,1)} %copy-done) | copy-start | bytes 7077892
  55.1 2.9 %copy-start.6 = (bf16[256,4,1024]{2,0,1:T(8,128)(2,1)S(1)}, bf16[256,4,1024]{2,0,1:T(8,128)(2,1)}, u32[]{:S(2)}) copy-start(bf16[256,4,1024]{2,0,1:T(8,128)(2,1)} %all-gather.2.cloned.1.call-done) | copy-start | bytes 6291460
  58.1 1.7 %copy-start.5 = (bf16[4,9,32,1024]{3,2,1,0:T(8,128)(2,1)S(1)}, bf16[4,9,32,1024]{3,2,1,0:T(8,128)(2,1)}, u32[]{:S(2)}) copy-start(bf16[4,9,32,1024]{3,2,1,0:T(8,128)(2,1)} %copy-done.3) | copy-start | bytes 7077892
  60.7 17.0 %collective-permute-start.5 = (f32[224,256]{1,0:T(8,128)S(1)}, f32[224,256]{1,0:T(8,128)S(1)}, u32[]{:S(2)}, u32[]{:S(2)}) collective-permute-start(f32[224,256]{1,0:T(8,128)S(1)} %get-tuple-element.41), channel_id=1, source_target_pairs={{0,8},{8,0},{16,24},{24,16},{1,9},{9,1},{17,25},{25,17},{2,10},{10... | collective-permute-start | bytes 688136 | tf_op jit(solution)/shard_map/ppermute | solution.py:104
  63.5 14.2 %collective-permute-start.6 = (f32[224,256]{1,0:T(8,128)S(1)}, f32[224,256]{1,0:T(8,128)S(1)}, u32[]{:S(2)}, u32[]{:S(2)}) collective-permute-start(f32[224,256]{1,0:T(8,128)S(1)} %get-tuple-element.43), channel_id=1, source_target_pairs={{0,16},{8,24},{16,0},{24,8},{1,17},{9,25},{17,1},{25,9},{2,18},{10... | collective-permute-start | bytes 688136 | tf_op jit(solution)/shard_map/ppermute | solution.py:104
  65.0 12.7 %collective-permute-start.7 = (f32[224,256]{1,0:T(8,128)S(1)}, f32[224,256]{1,0:T(8,128)S(1)}, u32[]{:S(2)}, u32[]{:S(2)}) collective-permute-start(f32[224,256]{1,0:T(8,128)S(1)} %get-tuple-element.42), channel_id=1, source_target_pairs={{0,24},{8,16},{16,8},{24,0},{1,25},{9,17},{17,9},{25,1},{2,26},{10... | collective-permute-start | bytes 688136 | tf_op jit(solution)/shard_map/ppermute | solution.py:104
  71.6 13.9 %copy-start.11 = (f32[32]{0:T(128)S(1)}, f32[32]{0:T(128)}, u32[]{:S(2)}) copy-start(f32[32]{0:T(128)} %param.8) | copy-start | bytes 388
  73.4 10.4 %collective-permute-start = (f32[1,32,1024]{2,1,0:T(8,128)S(1)}, f32[1,32,1024]{2,1,0:T(8,128)S(1)}, u32[]{:S(2)}, u32[]{:S(2)}) collective-permute-start(f32[1,32,1024]{2,1,0:T(8,128)S(1)} %get-tuple-element.44), channel_id=1, source_target_pairs={{0,8},{8,16},{16,24},{1,9},{9,17},{17,25},{2,10},{10,18},{18,26},{... | collective-permute-start | bytes 393224 | tf_op jit(solution)/shard_map/ppermute | solution.py:157
  76.4 9.1 %collective-permute-start.1 = (f32[1,32,1024]{2,1,0:T(8,128)S(1)}, f32[1,32,1024]{2,1,0:T(8,128)S(1)}, u32[]{:S(2)}, u32[]{:S(2)}) collective-permute-start(f32[1,32,1024]{2,1,0:T(8,128)S(1)} %get-tuple-element.45), channel_id=1, source_target_pairs={{8,0},{16,8},{24,16},{9,1},{17,9},{25,17},{10,2},{18,10},{26,18},{... | collective-permute-start | bytes 393224 | tf_op jit(solution)/shard_map/ppermute | solution.py:158
  77.8 12.6 %collective-permute-start.8 = (f32[224,256]{1,0:T(8,128)S(1)}, f32[224,256]{1,0:T(8,128)S(1)}, u32[]{:S(2)}, u32[]{:S(2)}) collective-permute-start(f32[224,256]{1,0:T(8,128)S(1)} %fusion.63), channel_id=1, source_target_pairs={{0,8},{8,0},{16,24},{24,16},{1,9},{9,1},{17,25},{25,17},{2,10},{10... | collective-permute-start | bytes 688136 | tf_op jit(solution)/shard_map/ppermute | solution.py:106
  80.9 9.6 %collective-permute-start.9 = (f32[224,256]{1,0:T(8,128)S(1)}, f32[224,256]{1,0:T(8,128)S(1)}, u32[]{:S(2)}, u32[]{:S(2)}) collective-permute-start(f32[224,256]{1,0:T(8,128)S(1)} %fusion.63), channel_id=1, source_target_pairs={{0,16},{8,24},{16,0},{24,8},{1,17},{9,25},{17,1},{25,9},{2,18},{10... | collective-permute-start | bytes 688136 | tf_op jit(solution)/shard_map/ppermute | solution.py:106
  82.4 11.7 %collective-permute-start.10 = (f32[224,256]{1,0:T(8,128)S(1)}, f32[224,256]{1,0:T(8,128)S(1)}, u32[]{:S(2)}, u32[]{:S(2)}) collective-permute-start(f32[224,256]{1,0:T(8,128)S(1)} %fusion.63), channel_id=1, source_target_pairs={{0,24},{8,16},{16,8},{24,0},{1,25},{9,17},{17,9},{25,1},{2,26},{10... | collective-permute-start | bytes 688136 | tf_op jit(solution)/shard_map/ppermute | solution.py:106
Sparse Core Ops, SparseCore 0:
  17.1 31.4 all-gather.1
Sparse Core Ops, SparseCore 1:
  55.2 46.0 reduce-scatter.1

commit v17 on v14

--- a/solution.py
+++ b/solution.py
@@ -192,15 +192,15 @@
     bias_grad = reduced[taps_total * block_out, :block_out]
 
     chan_devices = lax.axis_size("chips") * lax.axis_size("core")
-    backward_weight = jnp.transpose(weight_grid, (0, 2, 1, 3)).reshape(
-        3, chan_devices, channels_in // chan_devices, 9 * block_out
-    )
+    backward_weight = weight.reshape(3, 9, chan_devices, channels_in // chan_devices, block_out)
     spread = None
     for depth_index in range(3):
         part = jnp.einsum(
-            "bjk,zkn->bzjn",
+            "sbjo,zson->bzjn",
             backward_weight[depth_index],
-            grad_shifted[2 - depth_index : 2 - depth_index + depth_cells],
+            grad_shifted[2 - depth_index : 2 - depth_index + depth_cells].reshape(
+                depth_cells, 9, block_out, plane_cells
+            ),
             preferred_element_type=jnp.float32,
         )
         spread = part if spread is None else spread + part

time: 98.4 us -> 102 us (1.037)
  local copies, waits for them, and re-layouts: 16.3 us -> 22.2 us
  waiting for transfers between devices: 20.6 us -> 16.4 us
  other arithmetic: 12.4 us -> 13.6 us
    ppermute x1, waiting for transfers between devices: 4.05 us -> 0.01 us  [scatter_channels(): partial = keep + lax.ppermute(send, 'core', [(0, 1), (1, 0)])]
    all_gather x1, waiting for transfers between devices: 6.14 us -> 2.69 us  [body(): lax.all_gather(inputs, ('chips', 'core'), axis=0, tiled=True)]
    reduce_scatter x1, waiting for transfers between devices: 0.77 us -> 4.04 us  [scatter_channels(): lax.psum_scatter(partial.reshape(-1, blocks.shape[-1]), 'chips', scatter_...]
    squeeze x6, local copies, waits for them, and re-layouts: 1.91 us -> 4.47 us  [body(): backward_weight[depth_index]]
    slice x1, local copies, waits for them, and re-layouts: 0.03 us -> 1.8 us  [body(): forward_weight[depth_index]]
    slice x4 -> x1, local copies, waits for them, and re-layouts: 1.77 us -> 3.21 us  [body(): grad_shifted[2 - depth_index:2 - depth_index + depth_cells]]
    unnamed x18 -> x34, local copies, waits for them, and re-layouts: 6.14 us -> 5.79 us
  transfers between devices with their start and end apart: 13 -> 13, of which waited for: 6 -> 5; matrix products, arithmetic and copies ran while one was open for 38% -> 45% of each run, Pallas kernels for 0% -> 0%
where the time goes in v17:
time: 102 us
  local copies, waits for them, and re-layouts  22.2 us (22%)
  starting transfers between devices  19.5 us (19%)
  waiting for transfers between devices  16.4 us (16%)
  between operations  16 us (16%)
  matrix products  13.8 us (14%)
  other arithmetic  13.6 us (13%)
    ppermute x3, waiting for transfers between devices, all_reduce_direct(): lax.ppermute(reduced, axis, [(i, i ^ distance) for i in range(devices)])  7.78 us
    dot_general x3, matrix products, body(): jnp.einsum('sbjo,zson->bzjn', backward_weight[depth_index], grad_shifted[...  6.43 us
    unnamed x34, local copies, waits for them, and re-layouts  5.79 us
    ppermute x3, starting transfers between devices, all_reduce_direct(): lax.ppermute(reduced, axis, [(i, i ^ distance) for i in range(devices)])  5.08 us
    dot_general x3, matrix products, body(): jnp.einsum('zkn,zin->ki', grad_shifted[2 - depth_index:2 - depth_index +...  5.07 us
    ppermute x1, starting transfers between devices, padded_2(): before = lax.ppermute(last, axis, up)  4.85 us
    squeeze x6, local copies, waits for them, and re-layouts, body(): backward_weight[depth_index]  4.47 us
    reduce_scatter x1, waiting for transfers between devices, scatter_channels(): lax.psum_scatter(partial.reshape(-1, blocks.shape[-1]), 'chips', scatter_...  4.04 us
  transfers between devices with their start and end apart: 13, of which 5 were waited for; matrix products, arithmetic and copies ran while one was open for 45% of the time, Pallas kernels for 0%

profile of v17, /device:TPU:0, one launch (start us, length us, event | category | flops | bytes accessed | tf_op | source)
XLA Modules:
  0.0 101.5 jit_solution(18430660320304169187)
XLA Ops:
  8.0 1.0 %copy.76 = bf16[32,4,1024]{2,0,1:T(8,128)(2,1)S(1)} copy(bf16[32,4,1024]{2,1,0:T(4,128)(2,1)} %param.9) | data formatting | bytes 524288 | tf_op args[3]
  9.1 4.8 %collective-permute-start.2 = (bf16[1,32,1024]{2,1,0:T(8,128)(2,1)S(1)}, bf16[1,32,1024]{2,1,0:T(8,128)(2,1)S(1)}, u32[]{:S(2)}, u32[]{:S(2)}) collective-permute-start(bf16[1,32,1024]{2,1,0:T(8,128)(2,1)S(1)} %get-tuple-element.54), channel_id=1, source_target_pairs={{0,8},{8,16},{16,24},{1,9},{9,17},{17,25},{2,10},{10,18},{18,26},{... | collective-permute-start | bytes 196616 | tf_op jit(solution)/shard_map/ppermute | solution.py:28
  14.0 1.3 %collective-permute-start.3 = (bf16[1,32,1024]{2,1,0:T(8,128)(2,1)S(1)}, bf16[1,32,1024]{2,1,0:T(8,128)(2,1)S(1)}, u32[]{:S(2)}, u32[]{:S(2)}) collective-permute-start(bf16[1,32,1024]{2,1,0:T(8,128)(2,1)S(1)} %get-tuple-element.55), channel_id=1, source_target_pairs={{8,0},{16,8},{24,16},{9,1},{17,9},{25,17},{10,2},{18,10},{26,18},{... | collective-permute-start | bytes 196616 | tf_op jit(solution)/shard_map/ppermute | solution.py:29
  15.3 1.7 %copy.29 = bf16[32,4,1024]{2,0,1:T(8,128)(2,1)} copy(bf16[32,4,1024]{2,1,0:T(4,128)(2,1)} %param.6) | data formatting | bytes 524288 | tf_op args[0]
  17.1 1.1 %fusion.95 = (bf16[9,256,32]{1,2,0:T(8,128)(2,1)S(1)}, bf16[9,256,32]{1,2,0:T(8,128)(2,1)S(1)}, bf16[9,256,32]{1,2,0:T(8,128)(2,1)S(1)}) fusion(bf16[27,256,32]{1,2,0:T(8,128)(2,1)} %param.7), kind=kLoop, calls=%fused_computation.147 | loop fusion | bytes 884736 | tf_op jit(solution)/shard_map/slice | solution.py:200
  18.4 1.2 %copy.51 = bf16[9,8,32,32]{3,2,0,1:T(8,128)(2,1)} copy(bf16[9,8,32,32]{2,1,3,0:T(8,128)(2,1)S(1)} %squeeze.94) | data formatting | bytes 294912 | tf_op jit(solution)/shard_map/squeeze | solution.py:200
  19.9 1.2 %copy.50 = bf16[9,8,32,32]{3,2,0,1:T(8,128)(2,1)} copy(bf16[9,8,32,32]{2,1,3,0:T(8,128)(2,1)S(1)} %squeeze.93) | data formatting | bytes 294912 | tf_op jit(solution)/shard_map/squeeze | solution.py:200
  21.4 1.3 %copy.49 = bf16[9,8,32,32]{3,2,0,1:T(8,128)(2,1)} copy(bf16[9,8,32,32]{2,1,3,0:T(8,128)(2,1)S(1)} %squeeze.92) | data formatting | bytes 294912 | tf_op jit(solution)/shard_map/squeeze | solution.py:200
  22.9 0.4 copy-done.11
  24.0 1.1 %fusion.72 = bf16[6,9,32,1024]{3,2,1,0:T(8,128)(2,1)S(1)} fusion(bf16[6,9,32,1024]{3,2,1,0:T(8,128)(2,1)S(1)} %fusion.64, bf16[1,1,32,1024]{3,2,0,1:T(8,128)(2,1)} %bitcast.266, bf16[4,1,32,1024]{3,2,0,1:T(8,128)(2,1)} %bitcast.254, bf16[1,1,32,1024]{3,2,0,1:T(8,128)(2,1)} %bitcast.265, pred[1024]{0:T(1024)(128)(4,1)S(1)} %fusion.88), kind=kLoop, calls=%fused_computation.109 | loop fusion | flops 1376256 | bytes 787456
  25.7 1.8 %fusion = f32[4,1024,8,32,1]{1,3,4,2,0:T(8,128)S(1)} fusion(bf16[9,8,32,32]{3,2,0,1:T(8,128)(2,1)S(1)} %copy-done.8, bf16[6,9,32,1024]{3,2,1,0:T(8,128)(2,1)S(1)} %fusion.56), kind=kOutput, calls=%fused_computation.3 | convolution fusion | flops 603979776 | bytes 7143424 | tf_op jit(solution)/shard_map/sbjo,zson->bzjn/dot_general | solution.py:198
  27.6 1.8 %fusion.2 = f32[4,1024,8,32,1]{1,3,4,2,0:T(8,128)S(1)} fusion(bf16[9,8,32,32]{3,2,0,1:T(8,128)(2,1)S(1)} %copy-done.9, bf16[6,9,32,1024]{3,2,1,0:T(8,128)(2,1)S(1)} %fusion.56), kind=kOutput, calls=%fused_computation.5 | convolution fusion | flops 603979776 | bytes 7143424 | tf_op jit(solution)/shard_map/sbjo,zson->bzjn/dot_general | solution.py:198
  29.4 2.8 %bitcast_add_fusion = f32[4,1024,8,32]{1,3,2,0:T(8,128)S(1)} fusion(f32[4,1024,8,32,1]{1,3,4,2,0:T(8,128)S(1)} %fusion, f32[4,1024,8,32,1]{1,3,4,2,0:T(8,128)S(1)} %fusion.2, bf16[9,8,32,32]{3,2,0,1:T(8,128)(2,1)S(1)} %copy-done.10, bf16[6,9,32,1024]{3,2,1,0:T(8,128)(2,1)S(1)} %fusion.56), kind=kOutput, calls=%fused_computation.1 | convolution fusion | flops 606076928 | bytes 15532032 | tf_op jit(solution)/shard_map/sbjo,zson->bzjn/dot_general | solution.py:198
  32.2 1.9 %constant_dynamic-slice_fusion.1 = (f32[4,1,4,32,1024]{4,3,1,0,2:T(8,128)}, f32[4,1,4,32,1024]{4,3,1,0,2:T(8,128)S(1)}) fusion(f32[4,2,4,32,1024]{4,3,1,0,2:T(8,128)S(1)} %bitcast.248, s32[]{:T(128)S(6)} %select_n.181, s32[]{:T(128)S(6)} %select_n.182), kind=kLoop, calls=%fused_computation.140 | loop fusion | bytes 8388616 | tf_op jit(solution)/shard_map/jit(dynamic_index_in_dim)/dynamic_slice | solution.py:118
  34.1 1.6 %copy.75 = f32[4,1,4,32,1024]{4,3,2,0,1:T(8,128)} copy(f32[4,1,4,32,1024]{4,3,1,0,2:T(8,128)S(1)} %get-tuple-element.33) | data formatting | bytes 4194304 | tf_op jit(solution)/shard_map/jit(dynamic_index_in_dim)/dynamic_slice | solution.py:119
  35.7 0.6 pad.87.clone
  36.3 1.3 %convert_reduce_fusion = f32[32]{0:T(128)S(1)} fusion(bf16[32,4,1024]{2,1,0:T(4,128)(2,1)} %param.9), kind=kLoop, calls=%fused_computation.80 | loop fusion | flops 262112 | bytes 262272 | tf_op jit(solution)/shard_map/reduce_sum | solution.py:182
  37.6 1.8 %fusion.96 = (bf16[1,9,32,256]{3,2,1,0:T(8,128)(2,1)}, bf16[1,9,32,256]{3,2,1,0:T(8,128)(2,1)}, bf16[1,9,32,256]{3,2,1,0:T(8,128)(2,1)}) fusion(bf16[3,9,32,256]{3,2,1,0:T(8,128)(2,1)} %bitcast.258), kind=kLoop, calls=%fused_computation.148 | loop fusion | bytes 884736 | tf_op jit(solution)/shard_map/slice | solution.py:143
  39.4 3.2 %fusion.93 = (bf16[4,9,32,1024]{3,2,1,0:T(8,128)(2,1)}, bf16[4,9,32,1024]{3,2,1,0:T(8,128)(2,1)}, bf16[4,9,32,1024]{3,2,1,0:T(8,128)(2,1)}) fusion(bf16[6,9,32,1024]{3,2,1,0:T(8,128)(2,1)S(1)} %fusion.56), kind=kLoop, calls=%fused_computation.145 | loop fusion | bytes 14155776 | tf_op jit(solution)/shard_map/slice | solution.py:201
  42.6 3.4 %bitcast_add_fusion.2 = f32[4,4,32,1024]{3,2,1,0:T(8,128)} fusion(f32[4,4,32,1024]{3,2,1,0:T(8,128)} %collective-permute-done.4, f32[4,1,4,32,1024]{4,3,1,0,2:T(8,128)S(1)} %copy-done.1), kind=kLoop, calls=%fused_computation.12 | loop fusion | flops 524288 | bytes 6291456 | tf_op jit(solution)/shard_map/add | solution.py:120
  46.0 2.7 %all-gather.2.cloned.1.call-done = bf16[256,4,1024]{2,0,1:T(8,128)(2,1)} async-done(((bf16[32,4,1024]{2,0,1:T(8,128)(2,1)}), bf16[256,4,1024]{2,0,1:T(8,128)(2,1)}) %all-gather.2.cloned.1.call-update) | async-done | bytes 2097168 | tf_op jit(solution)/shard_map/all_gather | solution.py:135
  48.7 3.3 %fusion.17 = f32[1,288,256]{2,1,0:T(8,128)S(1)} fusion(bf16[4,288,1024]{2,1,0:T(8,128)(2,1)} %bitcast.257, bf16[256,4,1024]{2,0,1:T(8,128)(2,1)} %all-gather.2.cloned.1.call-done), kind=kOutput, calls=%fused_computation.25 | convolution fusion | flops 603979776 | bytes 4751360 | tf_op jit(solution)/shard_map/zkn,zin->ki/dot_general | solution.py:173
  52.0 1.0 fusion.20
  53.0 0.6 copy-done.3
  53.6 0.8 fusion.23
  54.7 1.5 %collective-permute-start.5 = (f32[224,256]{1,0:T(8,128)S(1)}, f32[224,256]{1,0:T(8,128)S(1)}, u32[]{:S(2)}, u32[]{:S(2)}) collective-permute-start(f32[224,256]{1,0:T(8,128)S(1)} %get-tuple-element.41), channel_id=1, source_target_pairs={{0,8},{8,0},{16,24},{24,16},{1,9},{9,1},{17,25},{25,17},{2,10},{10... | collective-permute-start | bytes 688136 | tf_op jit(solution)/shard_map/ppermute | solution.py:104
  56.2 1.5 %collective-permute-start.6 = (f32[224,256]{1,0:T(8,128)S(1)}, f32[224,256]{1,0:T(8,128)S(1)}, u32[]{:S(2)}, u32[]{:S(2)}) collective-permute-start(f32[224,256]{1,0:T(8,128)S(1)} %get-tuple-element.43), channel_id=1, source_target_pairs={{0,16},{8,24},{16,0},{24,8},{1,17},{9,25},{17,1},{25,9},{2,18},{10... | collective-permute-start | bytes 688136 | tf_op jit(solution)/shard_map/ppermute | solution.py:104
  57.7 0.5 collective-permute-start.7
  58.2 0.8 convolution_bitcast_fusion
  59.0 0.8 convolution_bitcast_fusion.1
  59.9 0.8 convolution_bitcast_fusion.2
  60.7 2.3 %pad_add_fusion = f32[6,288,1024]{2,1,0:T(8,128)S(1)} fusion(f32[4,288,1024]{2,1,0:T(8,128)S(1)} %convolution_bitcast_fusion, f32[4,288,1024]{2,1,0:T(8,128)S(1)} %convolution_bitcast_fusion.1, f32[4,288,1024]{2,1,0:T(8,128)S(1)} %convolution_bitcast_fusion.2), kind=kLoop, calls=%fused_computation | loop fusion | flops 3538944 | bytes 21233664 | tf_op jit(solution)/shard_map/add | solution.py:148
  63.0 1.1 %slice_bitcast_fusion = (f32[6,32,1024]{2,1,0:T(8,128)S(1)}, f32[6,32,1024]{2,1,0:T(8,128)S(1)}, f32[6,32,1024]{2,1,0:T(8,128)S(1)}, f32[6,32,1024]{2,1,0:T(8,12...) fusion(f32[6,9,32,1024]{3,2,1,0:T(8,128)S(1)} %bitcast.245), kind=kLoop, calls=%fused_computation.61 | loop fusion | bytes 12582912 | tf_op jit(solution)/shard_map/squeeze | solution.py:152
  64.1 1.7 %fusion.36 = f32[6,32,1024]{2,1,0:T(8,128)S(1)} fusion(f32[6,32,1024]{2,1,0:T(8,128)S(1)} %get-tuple-element.31, f32[6,32,1024]{2,1,0:T(8,128)S(1)} %get-tuple-element.30, f32[6,32,1024]{2,1,0:T(8,128)S(1)} %get-tuple-element.29, f32[6,32,1024]{2,1,0:T(8,128)S(1)} %get-tuple-element.28, f32[6,32,1024]{2,1,0:T(8,128)S(1)} %get-tuple-element.27, ...), kind=kLoop, calls=%fused_computation.53 | loop fusion | flops 3342336 | bytes 7867392 | tf_op jit(solution)/shard_map/add | solution.py:153
  65.8 3.4 %collective-permute-start = (f32[1,32,1024]{2,1,0:T(8,128)S(1)}, f32[1,32,1024]{2,1,0:T(8,128)S(1)}, u32[]{:S(2)}, u32[]{:S(2)}) collective-permute-start(f32[1,32,1024]{2,1,0:T(8,128)S(1)} %get-tuple-element.44), channel_id=1, source_target_pairs={{0,8},{8,16},{16,24},{1,9},{9,17},{17,25},{2,10},{10,18},{18,26},{... | collective-permute-start | bytes 393224 | tf_op jit(solution)/shard_map/ppermute | solution.py:157
  69.2 1.3 %collective-permute-start.1 = (f32[1,32,1024]{2,1,0:T(8,128)S(1)}, f32[1,32,1024]{2,1,0:T(8,128)S(1)}, u32[]{:S(2)}, u32[]{:S(2)}) collective-permute-start(f32[1,32,1024]{2,1,0:T(8,128)S(1)} %get-tuple-element.45), channel_id=1, source_target_pairs={{8,0},{16,8},{24,16},{9,1},{17,9},{25,17},{10,2},{18,10},{26,18},{... | collective-permute-start | bytes 393224 | tf_op jit(solution)/shard_map/ppermute | solution.py:158
  70.6 2.7 %collective-permute-start.8 = (f32[224,256]{1,0:T(8,128)S(1)}, f32[224,256]{1,0:T(8,128)S(1)}, u32[]{:S(2)}, u32[]{:S(2)}) collective-permute-start(f32[224,256]{1,0:T(8,128)S(1)} %fusion.75), channel_id=1, source_target_pairs={{0,8},{8,0},{16,24},{24,16},{1,9},{9,1},{17,25},{25,17},{2,10},{10... | collective-permute-start | bytes 688136 | tf_op jit(solution)/shard_map/ppermute | solution.py:106
  73.4 1.5 %collective-permute-start.9 = (f32[224,256]{1,0:T(8,128)S(1)}, f32[224,256]{1,0:T(8,128)S(1)}, u32[]{:S(2)}, u32[]{:S(2)}) collective-permute-start(f32[224,256]{1,0:T(8,128)S(1)} %fusion.75), channel_id=1, source_target_pairs={{0,16},{8,24},{16,0},{24,8},{1,17},{9,25},{17,1},{25,9},{2,18},{10... | collective-permute-start | bytes 688136 | tf_op jit(solution)/shard_map/ppermute | solution.py:106
  74.8 0.9 collective-permute-start.10
  75.7 1.8 %collective-permute-done.1 = f32[1,32,1024]{2,1,0:T(8,128)S(1)} collective-permute-done((f32[1,32,1024]{2,1,0:T(8,128)S(1)}, f32[1,32,1024]{2,1,0:T(8,128)S(1)}, u32[]{:S(2)}, u32[]{:S(2)}) %collective-permute-start.1) | collective-permute-done | bytes 131104 | tf_op jit(solution)/shard_map/ppermute | solution.py:158
  77.7 0.9 copy.54
  78.6 3.9 %collective-permute-done.8 = f32[224,256]{1,0:T(8,128)S(1)} collective-permute-done((f32[224,256]{1,0:T(8,128)S(1)}, f32[224,256]{1,0:T(8,128)S(1)}, u32[]{:S(2)}, u32[]{:S(2)}) %collective-permute-start.8) | collective-permute-done | bytes 229408 | tf_op jit(solution)/shard_map/ppermute | solution.py:106
  82.5 3.9 %collective-permute-done.10 = f32[224,256]{1,0:T(8,128)S(1)} collective-permute-done((f32[224,256]{1,0:T(8,128)S(1)}, f32[224,256]{1,0:T(8,128)S(1)}, u32[]{:S(2)}, u32[]{:S(2)}) %collective-permute-start.10) | collective-permute-done | bytes 229408 | tf_op jit(solution)/shard_map/ppermute | solution.py:106
  86.6 1.0 pad_maximum_fusion.1
  87.5 0.5 slice_bitcast_fusion.9
  88.0 4.0 %reduce-scatter.2.cloned.1.call-done = f32[128,1024]{1,0:T(8,128)} async-done(((f32[512,1024]{1,0:T(8,128)}), f32[128,1024]{1,0:T(8,128)}) %reduce-scatter.2.cloned.1.call-update) | async-done | bytes 524304 | tf_op jit(solution)/shard_map/reduce_scatter | solution.py:121
  92.1 1.1 %convert_element_type.39 = bf16[128,1024]{1,0:T(8,128)(2,1)S(1)} convert(f32[128,1024]{1,0:T(8,128)} %reduce-scatter.2.cloned.1.call-done) | non-fusion elementwise | flops 131072 | bytes 786432 | tf_op jit(solution)/shard_map/convert_element_type | solution.py:208
  93.2 0.9 copy.55
  (65 shorter events, 3.1 us)
Async XLA Ops:
  8.0 40.7 %all-gather.2.cloned.1.call-start = ((), (), s32[]{:S(2)}) async-start(), calls=%async_computation.1 | async-start | bytes 2359296 | tf_op jit(solution)/shard_map/all_gather | solution.py:135
  9.1 13.6 %copy-start.2 = (bf16[32,4,1024]{2,0,1:T(8,128)(2,1)}, bf16[32,4,1024]{2,0,1:T(8,128)(2,1)S(1)}, u32[]{:S(2)}) copy-start(bf16[32,4,1024]{2,0,1:T(8,128)(2,1)S(1)} %copy.76) | copy-start | bytes 786436
  9.1 13.6 %collective-permute-start.2 = (bf16[1,32,1024]{2,1,0:T(8,128)(2,1)S(1)}, bf16[1,32,1024]{2,1,0:T(8,128)(2,1)S(1)}, u32[]{:S(2)}, u32[]{:S(2)}) collective-permute-start(bf16[1,32,1024]{2,1,0:T(8,128)(2,1)S(1)} %get-tuple-element.54), channel_id=1, source_target_pairs={{0,8},{8,16},{16,24},{1,9},{9,17},{17,25},{2,10},{10,18},{18,26},{... | collective-permute-start | bytes 196616 | tf_op jit(solution)/shard_map/ppermute | solution.py:28
  14.0 8.7 %collective-permute-start.3 = (bf16[1,32,1024]{2,1,0:T(8,128)(2,1)S(1)}, bf16[1,32,1024]{2,1,0:T(8,128)(2,1)S(1)}, u32[]{:S(2)}, u32[]{:S(2)}) collective-permute-start(bf16[1,32,1024]{2,1,0:T(8,128)(2,1)S(1)} %get-tuple-element.55), channel_id=1, source_target_pairs={{8,0},{16,8},{24,16},{9,1},{17,9},{25,17},{10,2},{18,10},{26,18},{... | collective-permute-start | bytes 196616 | tf_op jit(solution)/shard_map/ppermute | solution.py:29
  17.0 75.1 %reduce-scatter.2.cloned.1.call-start = ((), (), s32[]{:S(2)}) async-start(), calls=%async_computation.2 | async-start | bytes 2621440 | tf_op jit(solution)/shard_map/reduce_scatter | solution.py:121
  22.7 0.6 copy-start.11
  22.7 0.6 copy-start.12
  23.3 2.4 %copy-start.8 = (bf16[9,8,32,32]{3,2,0,1:T(8,128)(2,1)S(1)}, bf16[9,8,32,32]{3,2,0,1:T(8,128)(2,1)}, u32[]{:S(2)}) copy-start(bf16[9,8,32,32]{3,2,0,1:T(8,128)(2,1)} %copy.51) | copy-start | bytes 442372
  25.7 1.8 %copy-start.9 = (bf16[9,8,32,32]{3,2,0,1:T(8,128)(2,1)S(1)}, bf16[9,8,32,32]{3,2,0,1:T(8,128)(2,1)}, u32[]{:S(2)}) copy-start(bf16[9,8,32,32]{3,2,0,1:T(8,128)(2,1)} %copy.50) | copy-start | bytes 442372
  27.6 1.8 %copy-start.10 = (bf16[9,8,32,32]{3,2,0,1:T(8,128)(2,1)S(1)}, bf16[9,8,32,32]{3,2,0,1:T(8,128)(2,1)}, u32[]{:S(2)}) copy-start(bf16[9,8,32,32]{3,2,0,1:T(8,128)(2,1)} %copy.49) | copy-start | bytes 442372
  35.7 6.9 %collective-permute-start.4 = (f32[4,4,32,1024]{3,2,1,0:T(8,128)}, f32[4,4,32,1024]{3,2,1,0:T(8,128)}, u32[]{:S(2)}, u32[]{:S(2)}) collective-permute-start(f32[4,4,32,1024]{3,2,1,0:T(8,128)} %bitcast.243), channel_id=1, source_target_pairs={{0,1},{1,0},{2,3},{3,2},{4,5},{5,4},{6,7},{7,6},{8,9},{9,8},{10,11... | collective-permute-start | bytes 6291464 | tf_op jit(solution)/shard_map/ppermute | solution.py:120
  39.4 3.2 %copy-start.1 = (f32[4,1,4,32,1024]{4,3,1,0,2:T(8,128)S(1)}, f32[4,1,4,32,1024]{4,3,1,0,2:T(8,128)}, u32[]{:S(2)}) copy-start(f32[4,1,4,32,1024]{4,3,1,0,2:T(8,128)} %get-tuple-element.32) | copy-start | bytes 6291460
  46.0 6.0 %copy-start.4 = (bf16[4,9,32,1024]{3,2,1,0:T(8,128)(2,1)S(1)}, bf16[4,9,32,1024]{3,2,1,0:T(8,128)(2,1)}, u32[]{:S(2)}) copy-start(bf16[4,9,32,1024]{3,2,1,0:T(8,128)(2,1)} %get-tuple-element.36) | copy-start | bytes 7077892
  48.7 3.3 %copy-start = (bf16[256,4,1024]{2,0,1:T(8,128)(2,1)S(1)}, bf16[256,4,1024]{2,0,1:T(8,128)(2,1)}, u32[]{:S(2)}) copy-start(bf16[256,4,1024]{2,0,1:T(8,128)(2,1)} %all-gather.2.cloned.1.call-done) | copy-start | bytes 6291460
  51.9 1.7 %copy-start.3 = (bf16[4,9,32,1024]{3,2,1,0:T(8,128)(2,1)S(1)}, bf16[4,9,32,1024]{3,2,1,0:T(8,128)(2,1)}, u32[]{:S(2)}) copy-start(bf16[4,9,32,1024]{3,2,1,0:T(8,128)(2,1)} %get-tuple-element.35) | copy-start | bytes 7077892
  54.4 3.8 %copy-start.7 = (bf16[1,9,32,256]{3,2,1,0:T(8,128)(2,1)S(1)}, bf16[1,9,32,256]{3,2,1,0:T(8,128)(2,1)}, u32[]{:S(2)}) copy-start(bf16[1,9,32,256]{3,2,1,0:T(8,128)(2,1)} %get-tuple-element.50) | copy-start | bytes 442372
  54.6 4.4 %copy-start.6 = (bf16[1,9,32,256]{3,2,1,0:T(8,128)(2,1)S(1)}, bf16[1,9,32,256]{3,2,1,0:T(8,128)(2,1)}, u32[]{:S(2)}) copy-start(bf16[1,9,32,256]{3,2,1,0:T(8,128)(2,1)} %get-tuple-element.51) | copy-start | bytes 442372
  54.7 15.9 %collective-permute-start.5 = (f32[224,256]{1,0:T(8,128)S(1)}, f32[224,256]{1,0:T(8,128)S(1)}, u32[]{:S(2)}, u32[]{:S(2)}) collective-permute-start(f32[224,256]{1,0:T(8,128)S(1)} %get-tuple-element.41), channel_id=1, source_target_pairs={{0,8},{8,0},{16,24},{24,16},{1,9},{9,1},{17,25},{25,17},{2,10},{10... | collective-permute-start | bytes 688136 | tf_op jit(solution)/shard_map/ppermute | solution.py:104
  56.2 14.4 %collective-permute-start.6 = (f32[224,256]{1,0:T(8,128)S(1)}, f32[224,256]{1,0:T(8,128)S(1)}, u32[]{:S(2)}, u32[]{:S(2)}) collective-permute-start(f32[224,256]{1,0:T(8,128)S(1)} %get-tuple-element.43), channel_id=1, source_target_pairs={{0,16},{8,24},{16,0},{24,8},{1,17},{9,25},{17,1},{25,9},{2,18},{10... | collective-permute-start | bytes 688136 | tf_op jit(solution)/shard_map/ppermute | solution.py:104
  57.7 12.9 %collective-permute-start.7 = (f32[224,256]{1,0:T(8,128)S(1)}, f32[224,256]{1,0:T(8,128)S(1)}, u32[]{:S(2)}, u32[]{:S(2)}) collective-permute-start(f32[224,256]{1,0:T(8,128)S(1)} %get-tuple-element.42), channel_id=1, source_target_pairs={{0,24},{8,16},{16,8},{24,0},{1,25},{9,17},{17,9},{25,1},{2,26},{10... | collective-permute-start | bytes 688136 | tf_op jit(solution)/shard_map/ppermute | solution.py:104
  59.0 0.9 copy-start.5
  64.1 13.5 %copy-start.13 = (f32[32]{0:T(128)S(1)}, f32[32]{0:T(128)}, u32[]{:S(2)}) copy-start(f32[32]{0:T(128)} %param.8) | copy-start | bytes 388
  64.1 13.5 %copy-start.14 = (f32[4]{0:T(128)S(1)}, f32[4]{0:T(128)}, u32[]{:S(2)}) copy-start(f32[4]{0:T(128)} %pad.87.clone) | copy-start | bytes 52
  65.8 9.9 %collective-permute-start = (f32[1,32,1024]{2,1,0:T(8,128)S(1)}, f32[1,32,1024]{2,1,0:T(8,128)S(1)}, u32[]{:S(2)}, u32[]{:S(2)}) collective-permute-start(f32[1,32,1024]{2,1,0:T(8,128)S(1)} %get-tuple-element.44), channel_id=1, source_target_pairs={{0,8},{8,16},{16,24},{1,9},{9,17},{17,25},{2,10},{10,18},{18,26},{... | collective-permute-start | bytes 393224 | tf_op jit(solution)/shard_map/ppermute | solution.py:157
  69.2 8.3 %collective-permute-start.1 = (f32[1,32,1024]{2,1,0:T(8,128)S(1)}, f32[1,32,1024]{2,1,0:T(8,128)S(1)}, u32[]{:S(2)}, u32[]{:S(2)}) collective-permute-start(f32[1,32,1024]{2,1,0:T(8,128)S(1)} %get-tuple-element.45), channel_id=1, source_target_pairs={{8,0},{16,8},{24,16},{9,1},{17,9},{25,17},{10,2},{18,10},{26,18},{... | collective-permute-start | bytes 393224 | tf_op jit(solution)/shard_map/ppermute | solution.py:158
  70.6 11.8 %collective-permute-start.8 = (f32[224,256]{1,0:T(8,128)S(1)}, f32[224,256]{1,0:T(8,128)S(1)}, u32[]{:S(2)}, u32[]{:S(2)}) collective-permute-start(f32[224,256]{1,0:T(8,128)S(1)} %fusion.75), channel_id=1, source_target_pairs={{0,8},{8,0},{16,24},{24,16},{1,9},{9,1},{17,25},{25,17},{2,10},{10... | collective-permute-start | bytes 688136 | tf_op jit(solution)/shard_map/ppermute | solution.py:106
  73.4 9.1 %collective-permute-start.9 = (f32[224,256]{1,0:T(8,128)S(1)}, f32[224,256]{1,0:T(8,128)S(1)}, u32[]{:S(2)}, u32[]{:S(2)}) collective-permute-start(f32[224,256]{1,0:T(8,128)S(1)} %fusion.75), channel_id=1, source_target_pairs={{0,16},{8,24},{16,0},{24,8},{1,17},{9,25},{17,1},{25,9},{2,18},{10... | collective-permute-start | bytes 688136 | tf_op jit(solution)/shard_map/ppermute | solution.py:106
  74.8 11.6 %collective-permute-start.10 = (f32[224,256]{1,0:T(8,128)S(1)}, f32[224,256]{1,0:T(8,128)S(1)}, u32[]{:S(2)}, u32[]{:S(2)}) collective-permute-start(f32[224,256]{1,0:T(8,128)S(1)} %fusion.75), channel_id=1, source_target_pairs={{0,24},{8,16},{16,8},{24,0},{1,25},{9,17},{17,9},{25,1},{2,26},{10... | collective-permute-start | bytes 688136 | tf_op jit(solution)/shard_map/ppermute | solution.py:106
Sparse Core Ops, SparseCore 0:
  17.1 31.4 all-gather.1
Sparse Core Ops, SparseCore 1:
  46.1 46.0 reduce-scatter.1

commit v18 on v14

--- a/solution.py
+++ b/solution.py
@@ -164,10 +164,19 @@
     )
 
     grad_rimmed = padded_2(grad_planes, (("space", 0),), 1)
-    grad_shifted = jnp.stack(
-        [shift_cells(grad_rimmed, -row_step, -column_step) for row_step, column_step in plane_offsets],
-        axis=1,
-    ).reshape(depth_cells + 2, 9 * block_out, plane_cells)
+
+    def shifted_planes(planes):
+        return jnp.stack(
+            [shift_cells(planes, -row_step, -column_step) for row_step, column_step in plane_offsets], axis=1
+        ).reshape(planes.shape[0], 9 * block_out, plane_cells)
+
+    grad_shifted = jnp.concatenate(
+        [
+            shifted_planes(grad_rimmed[:1]),
+            shifted_planes(grad_planes),
+            shifted_planes(grad_rimmed[depth_cells + 1 :]),
+        ]
+    )
     weight_part = jnp.stack(
         [
             jnp.einsum(

time: 98.4 us -> 104 us (1.057)
  local copies, waits for them, and re-layouts: 16.3 us -> 21.9 us
  waiting for transfers between devices: 20.6 us -> 15.2 us
  other arithmetic: 12.4 us -> 14.9 us
  matrix products: 13.3 us -> 14.8 us
    all_gather x1, waiting for transfers between devices: 6.14 us -> 0.95 us  [body(): lax.all_gather(inputs, ('chips', 'core'), axis=0, tiled=True)]
    squeeze x6, local copies, waits for them, and re-layouts: 1.91 us -> 4.59 us  [body(): backward_weight[depth_index]]
    squeeze x1 -> x4, local copies, waits for them, and re-layouts: 1.12 us -> 3.79 us  [body(): term = shift_cells(in_plane[:, shift_index], row_step, column_step)]
    dot_general x3, matrix products: 5.84 us -> 8.13 us  [body(): jnp.einsum('bjk,zkn->bzjn', backward_weight[depth_index], grad_shifted[2...]
    ppermute x1, waiting for transfers between devices: 4.05 us -> 2.8 us  [scatter_channels(): partial = keep + lax.ppermute(send, 'core', [(0, 1), (1, 0)])]
    reduce_scatter x1, waiting for transfers between devices: 0.77 us -> 1.92 us  [scatter_channels(): lax.psum_scatter(partial.reshape(-1, blocks.shape[-1]), 'chips', scatter_...]
    unnamed x8 -> x21, other arithmetic: 1.24 us -> 2.12 us
    unnamed x18 -> x33, local copies, waits for them, and re-layouts: 6.14 us -> 5.4 us
  transfers between devices with their start and end apart: 13 -> 13, of which waited for: 6 -> 6; matrix products, arithmetic and copies ran while one was open for 38% -> 45% of each run, Pallas kernels for 0% -> 0%
where the time goes in v18:
time: 104 us; the launch traced here: 103 us
  local copies, waits for them, and re-layouts  21.9 us (21%)
  starting transfers between devices  20.1 us (19%)
  between operations  16.1 us (15%)
  waiting for transfers between devices  15.2 us (15%)
  other arithmetic  14.9 us (14%)
  matrix products  14.8 us (14%)
    dot_general x3, matrix products, body(): jnp.einsum('bjk,zkn->bzjn', backward_weight[depth_index], grad_shifted[2...  8.13 us
    ppermute x3, waiting for transfers between devices, all_reduce_direct(): lax.ppermute(reduced, axis, [(i, i ^ distance) for i in range(devices)])  7.11 us
    ppermute x1, starting transfers between devices, padded_2(): before = lax.ppermute(last, axis, up)  5.47 us
    unnamed x33, local copies, waits for them, and re-layouts  5.4 us
    squeeze x6, local copies, waits for them, and re-layouts, body(): backward_weight[depth_index]  4.59 us
    ppermute x3, starting transfers between devices, all_reduce_direct(): lax.ppermute(reduced, axis, [(i, i ^ distance) for i in range(devices)])  4.5 us
    dot_general x3, matrix products, body(): jnp.einsum('zkn,zin->ki', grad_shifted[2 - depth_index:2 - depth_index +...  4.36 us
    add x1, other arithmetic, scatter_channels(): partial = keep + lax.ppermute(send, 'core', [(0, 1), (1, 0)])  4.23 us
  transfers between devices with their start and end apart: 13, of which 6 were waited for; matrix products, arithmetic and copies ran while one was open for 45% of the time, Pallas kernels for 0%

profile of v18, /device:TPU:0, one launch (start us, length us, event | category | flops | bytes accessed | tf_op | source)
XLA Modules:
  0.0 103.1 jit_solution(14969632807222953632)
XLA Ops:
  8.1 1.1 %copy.75 = bf16[32,4,1024]{2,0,1:T(8,128)(2,1)S(1)} copy(bf16[32,4,1024]{2,1,0:T(4,128)(2,1)} %param.9) | data formatting | bytes 524288 | tf_op args[3]
  9.1 0.7 fusion.155
  9.8 1.3 %collective-permute-start.2 = (bf16[1,32,1024]{2,1,0:T(8,128)(2,1)}, bf16[1,32,1024]{2,1,0:T(8,128)(2,1)S(1)}, u32[]{:S(2)}, u32[]{:S(2)}) collective-permute-start(bf16[1,32,1024]{2,1,0:T(8,128)(2,1)} %get-tuple-element.46), channel_id=1, source_target_pairs={{8,0},{16,8},{24,16},{9,1},{17,9},{25,17},{10,2},{18,10},{26,18},{... | collective-permute-start | bytes 196616 | tf_op jit(solution)/shard_map/ppermute | solution.py:29
  11.1 5.5 %collective-permute-start.3 = (bf16[1,32,1024]{2,1,0:T(8,128)(2,1)}, bf16[1,32,1024]{2,1,0:T(8,128)(2,1)S(1)}, u32[]{:S(2)}, u32[]{:S(2)}) collective-permute-start(bf16[1,32,1024]{2,1,0:T(8,128)(2,1)} %get-tuple-element.47), channel_id=1, source_target_pairs={{0,8},{8,16},{16,24},{1,9},{9,17},{17,25},{2,10},{10,18},{18,26},{... | collective-permute-start | bytes 196616 | tf_op jit(solution)/shard_map/ppermute | solution.py:28
  16.5 1.7 %copy.26 = bf16[32,4,1024]{2,0,1:T(8,128)(2,1)} copy(bf16[32,4,1024]{2,1,0:T(4,128)(2,1)} %param.6) | data formatting | bytes 524288 | tf_op args[0]
  19.9 0.7 copy-done.3
  20.7 0.7 fusion.153
  22.1 3.7 %fusion.82 = f32[4,1024,8,32]{1,3,2,0:T(8,128)} fusion(bf16[4,288,1024,1]{2,1,3,0:T(8,128)(2,1)S(1)} %bitcast.269, bf16[8,32,288]{2,1,0:T(8,128)(2,1)S(1)} %copy.39), kind=kOutput, calls=%fused_computation.125 | convolution fusion | flops 603979776 | bytes 6701056 | tf_op jit(solution)/shard_map/bjk,zkn->bzjn/dot_general | solution.py:209
  25.8 1.3 %squeeze.94 = bf16[8,32,288]{1,0,2:T(8,128)(2,1)S(1)} reshape(bf16[1,256,9,32]{1,3,2,0:T(8,128)(2,1)} %get-tuple-element.41) | data formatting | bytes 294912 | tf_op jit(solution)/shard_map/squeeze | solution.py:211
  27.0 1.1 %copy.40 = bf16[8,32,288]{2,1,0:T(8,128)(2,1)} copy(bf16[8,32,288]{1,0,2:T(8,128)(2,1)S(1)} %squeeze.94) | data formatting | bytes 294912 | tf_op jit(solution)/shard_map/squeeze | solution.py:211
  28.1 1.3 %squeeze.92 = bf16[8,32,288]{1,0,2:T(8,128)(2,1)S(1)} reshape(bf16[1,256,9,32]{1,3,2,0:T(8,128)(2,1)} %get-tuple-element.40) | data formatting | bytes 294912 | tf_op jit(solution)/shard_map/squeeze | solution.py:211
  31.2 1.7 %fusion.8 = f32[4,1024,8,32]{1,3,2,0:T(8,128)S(1)} fusion(bf16[4,288,1024]{2,1,0:T(8,128)(2,1)S(1)} %bitcast.270, bf16[1,288,1024]{2,1,0:T(8,128)(2,1)S(1)} %bitcast.295, bf16[8,32,288]{2,1,0:T(8,128)(2,1)S(1)} %copy-done.5), kind=kOutput, calls=%fused_computation.11 | convolution fusion | flops 608698368 | bytes 7290880 | tf_op jit(solution)/shard_map/bjk,zkn->bzjn/dot_general | solution.py:209
  32.9 0.6 copy-done
  33.6 2.7 %add_add_fusion = f32[4,1024,8,32]{1,3,2,0:T(8,128)S(1)} fusion(f32[4,1024,8,32]{1,3,2,0:T(8,128)S(1)} %fusion.8, f32[4,1024,8,32]{1,3,2,0:T(8,128)S(1)} %copy-done, bf16[1,288,1024]{2,1,0:T(8,128)(2,1)S(1)} %bitcast.297, bf16[4,288,1024]{2,1,0:T(8,128)(2,1)S(1)} %bitcast.271, bf16[8,32,288]{2,1,0:T(8,128)(2,1)S(1)} %copy.38), kind=kOutput, calls=%fused_computation.1 | convolution fusion | flops 610795520 | bytes 15679488 | tf_op jit(solution)/shard_map/bjk,zkn->bzjn/dot_general | solution.py:209
  36.3 1.8 %constant_dynamic-slice_fusion.1 = (f32[4,1,4,32,1024]{4,3,1,0,2:T(8,128)}, f32[4,1,4,32,1024]{4,3,1,0,2:T(8,128)S(1)}) fusion(f32[4,2,4,32,1024]{4,3,1,0,2:T(8,128)S(1)} %bitcast.275, s32[]{:T(128)S(6)} %select_n.319, s32[]{:T(128)S(6)} %select_n.320), kind=kLoop, calls=%fused_computation.211 | loop fusion | bytes 8388616 | tf_op jit(solution)/shard_map/jit(dynamic_index_in_dim)/dynamic_slice | solution.py:118
  38.1 1.5 %copy.74 = f32[4,1,4,32,1024]{4,3,2,0,1:T(8,128)} copy(f32[4,1,4,32,1024]{4,3,1,0,2:T(8,128)S(1)} %get-tuple-element.30) | data formatting | bytes 4194304 | tf_op jit(solution)/shard_map/jit(dynamic_index_in_dim)/dynamic_slice | solution.py:119
  40.5 0.8 fusion.154
  41.3 2.8 %collective-permute-done.4 = f32[4,4,32,1024]{3,2,1,0:T(8,128)} collective-permute-done((f32[4,4,32,1024]{3,2,1,0:T(8,128)}, f32[4,4,32,1024]{3,2,1,0:T(8,128)}, u32[]{:S(2)}, u32[]{:S(2)}) %collective-permute-start.4) | collective-permute-done | bytes 2097184 | tf_op jit(solution)/shard_map/ppermute | solution.py:120
  44.1 4.2 %bitcast_add_fusion = f32[4,4,32,1024]{3,2,1,0:T(8,128)} fusion(f32[4,4,32,1024]{3,2,1,0:T(8,128)} %collective-permute-done.4, f32[4,1,4,32,1024]{4,3,1,0,2:T(8,128)} %get-tuple-element.29), kind=kLoop, calls=%fused_computation.21 | loop fusion | flops 524288 | bytes 6291456 | tf_op jit(solution)/shard_map/add | solution.py:120
  48.3 0.9 all-gather.2.cloned.1.call-done
  49.3 2.5 %fusion.24 = f32[1,288,256]{2,1,0:T(8,128)S(1)} fusion(bf16[256,4,1024]{2,0,1:T(8,128)(2,1)} %all-gather.2.cloned.1.call-done, bf16[4,288,1024]{2,1,0:T(8,128)(2,1)S(1)} %bitcast.272, bf16[1,288,1024]{2,1,0:T(8,128)(2,1)S(1)} %bitcast.296), kind=kOutput, calls=%fused_computation.39 | convolution fusion | flops 609878016 | bytes 5341184 | tf_op jit(solution)/shard_map/zkn,zin->ki/dot_general | solution.py:182
  51.9 0.8 fusion.29
  52.7 1.0 fusion.21
  53.9 2.1 %collective-permute-start.5 = (f32[224,256]{1,0:T(8,128)S(1)}, f32[224,256]{1,0:T(8,128)S(1)}, u32[]{:S(2)}, u32[]{:S(2)}) collective-permute-start(f32[224,256]{1,0:T(8,128)S(1)} %get-tuple-element.37), channel_id=1, source_target_pairs={{0,8},{8,0},{16,24},{24,16},{1,9},{9,1},{17,25},{25,17},{2,10},{10... | collective-permute-start | bytes 688136 | tf_op jit(solution)/shard_map/ppermute | solution.py:104
  56.0 0.9 collective-permute-start.6
  57.6 0.8 convolution_bitcast_fusion
  58.5 0.8 convolution_bitcast_fusion.1
  59.4 0.8 convolution_bitcast_fusion.2
  60.2 2.3 %pad_add_fusion = f32[6,288,1024]{2,1,0:T(8,128)S(1)} fusion(f32[4,288,1024]{2,1,0:T(8,128)S(1)} %convolution_bitcast_fusion, f32[4,288,1024]{2,1,0:T(8,128)S(1)} %convolution_bitcast_fusion.1, f32[4,288,1024]{2,1,0:T(8,128)S(1)} %convolution_bitcast_fusion.2), kind=kLoop, calls=%fused_computation | loop fusion | flops 3538944 | bytes 21233664 | tf_op jit(solution)/shard_map/add | solution.py:148
  62.4 0.9 fusion.151
  63.4 0.9 copy_bitcast_fusion.1
  64.3 0.9 copy_bitcast_fusion.3
  65.3 0.9 copy_bitcast_fusion.6
  66.3 0.9 copy_bitcast_fusion.8
  67.2 2.2 %fusion.42 = f32[6,32,1024]{2,0,1:T(8,128)S(1)} fusion(f32[6,32,1024]{2,0,1:T(8,128)S(1)} %get-tuple-element.61, f32[6,32,1024]{2,0,1:T(8,128)S(1)} %get-tuple-element.60, f32[6,32,1024]{2,0,1:T(8,128)S(1)} %get-tuple-element.59, f32[6,32,1024]{2,0,1:T(8,128)S(1)} %get-tuple-element.58, f32[6,32,1024]{2,0,1:T(8,128)S(1)} %get-tuple-element.57, ...), kind=kLoop, calls=%fused_computation.49 | loop fusion | flops 3342336 | bytes 7867392 | tf_op jit(solution)/shard_map/add | solution.py:153
  69.7 3.9 %collective-permute-start = (f32[1,32,1024]{2,0,1:T(1,128)S(1)}, f32[1,32,1024]{2,0,1:T(1,128)S(1)}, u32[]{:S(2)}, u32[]{:S(2)}) collective-permute-start(f32[1,32,1024]{2,0,1:T(1,128)S(1)} %get-tuple-element.31), channel_id=1, source_target_pairs={{0,8},{8,16},{16,24},{1,9},{9,17},{17,25},{2,10},{10,18},{18,26},{... | collective-permute-start | bytes 393224 | tf_op jit(solution)/shard_map/ppermute | solution.py:157
  73.5 1.3 %collective-permute-start.1 = (f32[1,32,1024]{2,0,1:T(1,128)S(1)}, f32[1,32,1024]{2,0,1:T(1,128)S(1)}, u32[]{:S(2)}, u32[]{:S(2)}) collective-permute-start(f32[1,32,1024]{2,0,1:T(1,128)S(1)} %get-tuple-element.32), channel_id=1, source_target_pairs={{8,0},{16,8},{24,16},{9,1},{17,9},{25,17},{10,2},{18,10},{26,18},{... | collective-permute-start | bytes 393224 | tf_op jit(solution)/shard_map/ppermute | solution.py:158
  74.9 2.7 %collective-permute-start.8 = (f32[224,256]{1,0:T(8,128)S(1)}, f32[224,256]{1,0:T(8,128)S(1)}, u32[]{:S(2)}, u32[]{:S(2)}) collective-permute-start(f32[224,256]{1,0:T(8,128)S(1)} %fusion.80), channel_id=1, source_target_pairs={{0,8},{8,0},{16,24},{24,16},{1,9},{9,1},{17,25},{25,17},{2,10},{10... | collective-permute-start | bytes 688136 | tf_op jit(solution)/shard_map/ppermute | solution.py:106
  77.7 0.9 collective-permute-start.9
  78.6 0.9 collective-permute-start.10
  79.5 2.4 %collective-permute-done.1 = f32[1,32,1024]{2,0,1:T(1,128)S(1)} collective-permute-done((f32[1,32,1024]{2,0,1:T(1,128)S(1)}, f32[1,32,1024]{2,0,1:T(1,128)S(1)}, u32[]{:S(2)}, u32[]{:S(2)}) %collective-permute-start.1) | collective-permute-done | bytes 131104 | tf_op jit(solution)/shard_map/ppermute | solution.py:158
  81.9 1.1 %fusion.78 = bf16[32,4,1024]{2,1,0:T(4,128)(2,1)} fusion(f32[32]{0:T(128)S(1)} %copy-done.13, f32[1,32,1024]{2,0,1:T(1,128)S(1)} %collective-permute-done.1, f32[4]{0:T(128)S(1)} %copy-done.14, f32[1,32,1024]{2,0,1:T(1,128)S(1)} %collective-permute-done, f32[6,32,1024]{2,0,1:T(8,128)S(1)} %fusion.42), kind=kLoop, calls=%fused_computation.113 | loop fusion | flops 655360 | bytes 1048720 | tf_op jit(solution)/shard_map/transpose | solution.py:162
  83.0 3.8 %collective-permute-done.8 = f32[224,256]{1,0:T(8,128)S(1)} collective-permute-done((f32[224,256]{1,0:T(8,128)S(1)}, f32[224,256]{1,0:T(8,128)S(1)}, u32[]{:S(2)}, u32[]{:S(2)}) %collective-permute-start.8) | collective-permute-done | bytes 229408 | tf_op jit(solution)/shard_map/ppermute | solution.py:106
  86.8 3.3 %collective-permute-done.10 = f32[224,256]{1,0:T(8,128)S(1)} collective-permute-done((f32[224,256]{1,0:T(8,128)S(1)}, f32[224,256]{1,0:T(8,128)S(1)}, u32[]{:S(2)}, u32[]{:S(2)}) %collective-permute-start.10) | collective-permute-done | bytes 229408 | tf_op jit(solution)/shard_map/ppermute | solution.py:106
  90.3 1.0 pad_maximum_fusion.1
  91.7 1.9 %reduce-scatter.2.cloned.1.call-done = f32[128,1024]{1,0:T(8,128)} async-done(((f32[512,1024]{1,0:T(8,128)}), f32[128,1024]{1,0:T(8,128)}) %reduce-scatter.2.cloned.1.call-update) | async-done | bytes 524304 | tf_op jit(solution)/shard_map/reduce_scatter | solution.py:121
  93.7 1.1 %convert_element_type.58 = bf16[128,1024]{1,0:T(8,128)(2,1)S(1)} convert(f32[128,1024]{1,0:T(8,128)} %reduce-scatter.2.cloned.1.call-done) | non-fusion elementwise | flops 131072 | bytes 786432 | tf_op jit(solution)/shard_map/convert_element_type | solution.py:217
  94.7 0.9 copy.43
  (82 shorter events, 6.8 us)
Async XLA Ops:
  8.0 11.0 %copy-start.2 = (bf16[32,4,1024]{2,1,0:T(4,128)(2,1)S(1)}, bf16[32,4,1024]{2,1,0:T(4,128)(2,1)}, u32[]{:S(2)}) copy-start(bf16[32,4,1024]{2,1,0:T(4,128)(2,1)} %param.9) | copy-start | bytes 786436
  8.0 41.3 %all-gather.2.cloned.1.call-start = ((), (), s32[]{:S(2)}) async-start(), calls=%async_computation.1 | async-start | bytes 2359296 | tf_op jit(solution)/shard_map/all_gather | solution.py:135
  9.8 20.0 %collective-permute-start.2 = (bf16[1,32,1024]{2,1,0:T(8,128)(2,1)}, bf16[1,32,1024]{2,1,0:T(8,128)(2,1)S(1)}, u32[]{:S(2)}, u32[]{:S(2)}) collective-permute-start(bf16[1,32,1024]{2,1,0:T(8,128)(2,1)} %get-tuple-element.46), channel_id=1, source_target_pairs={{8,0},{16,8},{24,16},{9,1},{17,9},{25,17},{10,2},{18,10},{26,18},{... | collective-permute-start | bytes 196616 | tf_op jit(solution)/shard_map/ppermute | solution.py:29
  11.1 19.2 %collective-permute-start.3 = (bf16[1,32,1024]{2,1,0:T(8,128)(2,1)}, bf16[1,32,1024]{2,1,0:T(8,128)(2,1)S(1)}, u32[]{:S(2)}, u32[]{:S(2)}) collective-permute-start(bf16[1,32,1024]{2,1,0:T(8,128)(2,1)} %get-tuple-element.47), channel_id=1, source_target_pairs={{0,8},{8,16},{16,24},{1,9},{9,17},{17,25},{2,10},{10,18},{18,26},{... | collective-permute-start | bytes 196616 | tf_op jit(solution)/shard_map/ppermute | solution.py:28
  18.3 75.4 %reduce-scatter.2.cloned.1.call-start = ((), (), s32[]{:S(2)}) async-start(), calls=%async_computation.2 | async-start | bytes 2621440 | tf_op jit(solution)/shard_map/reduce_scatter | solution.py:121
  19.7 1.0 copy-start.3
  29.7 1.4 %copy-start.5 = (bf16[8,32,288]{2,1,0:T(8,128)(2,1)S(1)}, bf16[8,32,288]{2,1,0:T(8,128)(2,1)}, u32[]{:S(2)}) copy-start(bf16[8,32,288]{2,1,0:T(8,128)(2,1)} %copy.40) | copy-start | bytes 442372
  30.6 2.3 %copy-start.8 = (bf16[1,9,32,1024]{3,2,1,0:T(8,128)(2,1)}, bf16[1,9,32,1024]{3,2,1,0:T(8,128)(2,1)S(1)}, u32[]{:S(2)}) copy-start(bf16[1,9,32,1024]{3,2,1,0:T(8,128)(2,1)S(1)} %get-tuple-element.48) | copy-start | bytes 1769476
  31.1 1.8 %copy-start.6 = (bf16[1,9,32,1024]{3,2,1,0:T(8,128)(2,1)}, bf16[1,9,32,1024]{3,2,1,0:T(8,128)(2,1)S(1)}, u32[]{:S(2)}) copy-start(bf16[1,9,32,1024]{3,2,1,0:T(8,128)(2,1)S(1)} %fusion.132) | copy-start | bytes 1769476
  31.1 2.4 %copy-start = (f32[4,1024,8,32]{1,3,2,0:T(8,128)S(1)}, f32[4,1024,8,32]{1,3,2,0:T(8,128)}, u32[]{:S(2)}) copy-start(f32[4,1024,8,32]{1,3,2,0:T(8,128)} %fusion.82) | copy-start | bytes 12582916
  38.1 2.4 %copy-start.4 = (bf16[27,256,32]{1,2,0:T(8,128)(2,1)S(1)}, bf16[27,256,32]{1,2,0:T(8,128)(2,1)}, u32[]{:S(2)}) copy-start(bf16[27,256,32]{1,2,0:T(8,128)(2,1)} %param.7) | copy-start | bytes 1327108
  39.6 4.5 %collective-permute-start.4 = (f32[4,4,32,1024]{3,2,1,0:T(8,128)}, f32[4,4,32,1024]{3,2,1,0:T(8,128)}, u32[]{:S(2)}, u32[]{:S(2)}) collective-permute-start(f32[4,4,32,1024]{3,2,1,0:T(8,128)} %bitcast.267), channel_id=1, source_target_pairs={{0,1},{1,0},{2,3},{3,2},{4,5},{5,4},{6,7},{7,6},{8,9},{9,8},{10,11... | collective-permute-start | bytes 6291464 | tf_op jit(solution)/shard_map/ppermute | solution.py:120
  44.1 5.2 %copy-start.7 = (bf16[1,9,32,1024]{3,2,1,0:T(8,128)(2,1)S(1)}, bf16[1,9,32,1024]{3,2,1,0:T(8,128)(2,1)}, u32[]{:S(2)}) copy-start(bf16[1,9,32,1024]{3,2,1,0:T(8,128)(2,1)} %copy-done.6) | copy-start | bytes 1769476
  48.3 3.5 %copy-start.9 = (bf16[1,9,32,1024]{3,2,1,0:T(8,128)(2,1)S(1)}, bf16[1,9,32,1024]{3,2,1,0:T(8,128)(2,1)}, u32[]{:S(2)}) copy-start(bf16[1,9,32,1024]{3,2,1,0:T(8,128)(2,1)} %copy-done.8) | copy-start | bytes 1769476
  49.3 2.6 %copy-start.1 = (bf16[256,4,1024]{2,0,1:T(8,128)(2,1)S(1)}, bf16[256,4,1024]{2,0,1:T(8,128)(2,1)}, u32[]{:S(2)}) copy-start(bf16[256,4,1024]{2,0,1:T(8,128)(2,1)} %all-gather.2.cloned.1.call-done) | copy-start | bytes 6291460
  53.7 3.9 %copy-start.12 = (bf16[1,9,32,256]{3,2,1,0:T(8,128)(2,1)S(1)}, bf16[1,9,32,256]{3,2,1,0:T(8,128)(2,1)}, u32[]{:S(2)}) copy-start(bf16[1,9,32,256]{3,2,1,0:T(8,128)(2,1)} %get-tuple-element.44) | copy-start | bytes 442372
  53.9 20.9 %collective-permute-start.5 = (f32[224,256]{1,0:T(8,128)S(1)}, f32[224,256]{1,0:T(8,128)S(1)}, u32[]{:S(2)}, u32[]{:S(2)}) collective-permute-start(f32[224,256]{1,0:T(8,128)S(1)} %get-tuple-element.37), channel_id=1, source_target_pairs={{0,8},{8,0},{16,24},{24,16},{1,9},{9,1},{17,25},{25,17},{2,10},{10... | collective-permute-start | bytes 688136 | tf_op jit(solution)/shard_map/ppermute | solution.py:104
  56.0 18.8 %collective-permute-start.6 = (f32[224,256]{1,0:T(8,128)S(1)}, f32[224,256]{1,0:T(8,128)S(1)}, u32[]{:S(2)}, u32[]{:S(2)}) collective-permute-start(f32[224,256]{1,0:T(8,128)S(1)} %get-tuple-element.39), channel_id=1, source_target_pairs={{0,16},{8,24},{16,0},{24,8},{1,17},{9,25},{17,1},{25,9},{2,18},{10... | collective-permute-start | bytes 688136 | tf_op jit(solution)/shard_map/ppermute | solution.py:104
  56.9 18.0 %collective-permute-start.7 = (f32[224,256]{1,0:T(8,128)S(1)}, f32[224,256]{1,0:T(8,128)S(1)}, u32[]{:S(2)}, u32[]{:S(2)}) collective-permute-start(f32[224,256]{1,0:T(8,128)S(1)} %get-tuple-element.38), channel_id=1, source_target_pairs={{0,24},{8,16},{16,8},{24,0},{1,25},{9,17},{17,9},{25,1},{2,26},{10... | collective-permute-start | bytes 688136 | tf_op jit(solution)/shard_map/ppermute | solution.py:104
  57.6 0.9 copy-start.11
  58.5 0.9 copy-start.10
  67.2 14.7 %copy-start.13 = (f32[32]{0:T(128)S(1)}, f32[32]{0:T(128)}, u32[]{:S(2)}) copy-start(f32[32]{0:T(128)} %param.8) | copy-start | bytes 388
  67.2 14.7 %copy-start.14 = (f32[4]{0:T(128)S(1)}, f32[4]{0:T(128)}, u32[]{:S(2)}) copy-start(f32[4]{0:T(128)} %pad.110.clone) | copy-start | bytes 52
  69.7 9.8 %collective-permute-start = (f32[1,32,1024]{2,0,1:T(1,128)S(1)}, f32[1,32,1024]{2,0,1:T(1,128)S(1)}, u32[]{:S(2)}, u32[]{:S(2)}) collective-permute-start(f32[1,32,1024]{2,0,1:T(1,128)S(1)} %get-tuple-element.31), channel_id=1, source_target_pairs={{0,8},{8,16},{16,24},{1,9},{9,17},{17,25},{2,10},{10,18},{18,26},{... | collective-permute-start | bytes 393224 | tf_op jit(solution)/shard_map/ppermute | solution.py:157
  73.5 8.3 %collective-permute-start.1 = (f32[1,32,1024]{2,0,1:T(1,128)S(1)}, f32[1,32,1024]{2,0,1:T(1,128)S(1)}, u32[]{:S(2)}, u32[]{:S(2)}) collective-permute-start(f32[1,32,1024]{2,0,1:T(1,128)S(1)} %get-tuple-element.32), channel_id=1, source_target_pairs={{8,0},{16,8},{24,16},{9,1},{17,9},{25,17},{10,2},{18,10},{26,18},{... | collective-permute-start | bytes 393224 | tf_op jit(solution)/shard_map/ppermute | solution.py:158
  74.9 11.8 %collective-permute-start.8 = (f32[224,256]{1,0:T(8,128)S(1)}, f32[224,256]{1,0:T(8,128)S(1)}, u32[]{:S(2)}, u32[]{:S(2)}) collective-permute-start(f32[224,256]{1,0:T(8,128)S(1)} %fusion.80), channel_id=1, source_target_pairs={{0,8},{8,0},{16,24},{24,16},{1,9},{9,1},{17,25},{25,17},{2,10},{10... | collective-permute-start | bytes 688136 | tf_op jit(solution)/shard_map/ppermute | solution.py:106
  77.7 9.1 %collective-permute-start.9 = (f32[224,256]{1,0:T(8,128)S(1)}, f32[224,256]{1,0:T(8,128)S(1)}, u32[]{:S(2)}, u32[]{:S(2)}) collective-permute-start(f32[224,256]{1,0:T(8,128)S(1)} %fusion.80), channel_id=1, source_target_pairs={{0,16},{8,24},{16,0},{24,8},{1,17},{9,25},{17,1},{25,9},{2,18},{10... | collective-permute-start | bytes 688136 | tf_op jit(solution)/shard_map/ppermute | solution.py:106
  78.6 11.6 %collective-permute-start.10 = (f32[224,256]{1,0:T(8,128)S(1)}, f32[224,256]{1,0:T(8,128)S(1)}, u32[]{:S(2)}, u32[]{:S(2)}) collective-permute-start(f32[224,256]{1,0:T(8,128)S(1)} %fusion.80), channel_id=1, source_target_pairs={{0,24},{8,16},{16,8},{24,0},{1,25},{9,17},{17,9},{25,1},{2,26},{10... | collective-permute-start | bytes 688136 | tf_op jit(solution)/shard_map/ppermute | solution.py:106
Sparse Core Ops, SparseCore 0:
  18.4 30.8 all-gather.1
Sparse Core Ops, SparseCore 1:
  48.4 45.2 reduce-scatter.1
